TPU v7x, 256 devices: a whole 4x4x8 slice. The times are simulated.
256 devices in a mesh: ctx: 64 (over z, x, y_lo), tp: 4 (over y_hi, core).
Axes of the slice: x: 4, y: 4 (y_hi: 2, y_lo: 2; y = y_hi * 2 + y_lo), z: 8, core: 2. Of those that a mesh axis runs over, the one named last changes fastest.
Arguments:
- query_rows: bfloat16 [32768, 2048], P('ctx', 'tp'), may hold values from -5 to 5
- key_rows: bfloat16 [32768, 512], P('ctx', 'tp'), may hold values from -5 to 5
- value_rows: bfloat16 [32768, 512], P('ctx', 'tp'), may hold values from -6 to 6
- out_weight: bfloat16 [2048, 4096], P('tp'), may hold values from -0.125 to 0.125
- out_grad: bfloat16 [32768, 4096], P(('ctx', 'tp')), may hold values from -24 to 24
- doc_ids: int32 [32768], replicated, may hold values from 0 to 7, never falling along the last dimension, each value on 1 to 16384 neighbouring positions
- window_blocks: int32 [256], replicated, may hold values from 1 to 12, as said below
Outputs:
- layer_out: bfloat16 [32768, 4096], P(('ctx', 'tp'))
- grad_queries: bfloat16 [32768, 2048], P('ctx', 'tp')
- grad_keys: bfloat16 [32768, 512], P('ctx', 'tp')
- grad_values: bfloat16 [32768, 512], P('ctx', 'tp')
- grad_weight: float32 [2048, 4096], P('tp', 'ctx')
Inputs may be any that keep to these rules, and one draw needn't show every extreme that they name: `window_blocks`: some query block has the full window of 12 blocks.
All inputs are finite; a program needn't handle non-finite values.
Results may differ from a plain program's by a relative error of at most 0.019.
Values may be sent and summed in bfloat16 or wider, within the bound.
No kernel may reach another device: no remote copies, remote signals or barrier semaphores. Data moves between devices by JAX's collectives and lax.ppermute only.
A program may use at most 128 MiB of HBM per device.

v0:
```python
import jax
import jax.numpy as jnp
from jax import lax
from jax.sharding import PartitionSpec as P

HEAD_DIM = 128
BLOCK = 128
REACH = 3


NEG_FILL = -1e30


def passed_along(block, axis, distance):
    devices = range(lax.axis_size(axis))
    route = [(i - distance, i) for i in devices if i - distance in devices]
    return lax.ppermute(block, axis, route)


def shifted(block, axis, distance):
    devices = range(lax.axis_size(axis))
    route = [((i - distance) % len(devices), i) for i in devices]
    return lax.ppermute(block, axis, route)


def allowed_tile(doc_ids, window_blocks, query_start, query_count, key_start, key_count):
    total_rows = doc_ids.shape[0]
    query_pos = query_start + jnp.arange(query_count, dtype=jnp.int32)
    key_pos = key_start + jnp.arange(key_count, dtype=jnp.int32)
    query_safe = jnp.clip(query_start, 0, total_rows - query_count)
    key_safe = jnp.clip(key_start, 0, total_rows - key_count)
    query_doc = lax.dynamic_slice_in_dim(doc_ids, query_safe, query_count)
    key_doc = lax.dynamic_slice_in_dim(doc_ids, key_safe, key_count)
    query_width = jnp.repeat(
        lax.dynamic_slice_in_dim(window_blocks, query_safe // BLOCK, query_count // BLOCK), BLOCK
    )
    inside = (
        (query_start >= 0)
        & (query_start + query_count <= total_rows)
        & (key_start >= 0)
        & (key_start + key_count <= total_rows)
    )
    return (
        inside
        & (key_pos[None, :] <= query_pos[:, None])
        & (query_doc[:, None] == key_doc[None, :])
        & (query_pos[:, None] // BLOCK - key_pos[None, :] // BLOCK < query_width[:, None])
    )


def split_heads(flat_rows, heads_here):
    return flat_rows.reshape(flat_rows.shape[0], heads_here, HEAD_DIM)


def forward_update(soft_state, query_four, key_heads, value_heads, allowed, score_scale):
    run_max, run_total, run_acc = soft_state
    scores = (
        jnp.einsum("qcgd,kcd->cgqk", query_four, key_heads, preferred_element_type=jnp.float32)
        * score_scale
    )
    masked = jnp.where(allowed, scores, NEG_FILL)
    new_max = jnp.maximum(run_max, jnp.max(masked, axis=-1))
    weights = jnp.where(allowed, jnp.exp(masked - new_max[..., None]), 0.0)
    factor = jnp.exp(run_max - new_max)
    new_total = run_total * factor + jnp.sum(weights, axis=-1)
    added = jnp.einsum(
        "cgqk,kcd->qcgd",
        weights.astype(jnp.bfloat16),
        value_heads,
        preferred_element_type=jnp.float32,
    )
    new_acc = run_acc * jnp.transpose(factor, (2, 0, 1))[..., None] + added
    return (new_max, new_total, new_acc)


def backward_tile(
    query_four, grad_four, log_sum, delta_rows, key_heads, value_heads, allowed, score_scale
):
    scores = (
        jnp.einsum("qcgd,kcd->cgqk", query_four, key_heads, preferred_element_type=jnp.float32)
        * score_scale
    )
    probs = jnp.exp(jnp.where(allowed, scores - log_sum[..., None], NEG_FILL))
    d_probs = jnp.einsum(
        "qcgd,kcd->cgqk", grad_four, value_heads, preferred_element_type=jnp.float32
    )
    d_scores = (probs * (d_probs - delta_rows[..., None]) * score_scale).astype(jnp.bfloat16)
    query_part = jnp.einsum(
        "cgqk,kcd->qcgd", d_scores, key_heads, preferred_element_type=jnp.float32
    )
    key_part = jnp.einsum(
        "cgqk,qcgd->kcd", d_scores, query_four, preferred_element_type=jnp.float32
    )
    value_part = jnp.einsum(
        "cgqk,qcgd->kcd", probs.astype(jnp.bfloat16), grad_four, preferred_element_type=jnp.float32
    )
    return (query_part, key_part, value_part)


def advance_keys(held_keys):
    return passed_along((held_keys[0], held_keys[1]), "ctx", 1)


def pass_grads(grad_pair, moved_by):
    return (
        shifted(grad_pair[0].astype(jnp.bfloat16), "ctx", moved_by).astype(jnp.float32),
        shifted(grad_pair[1].astype(jnp.bfloat16), "ctx", moved_by).astype(jnp.float32),
    )


def on_device(query_rows, key_rows, value_rows, out_weight, out_grad, doc_ids, window_blocks):
    tokens_here = query_rows.shape[0]
    kv_width = key_rows.shape[1]
    kv_here = kv_width // HEAD_DIM
    groups = query_rows.shape[1] // kv_width
    score_scale = HEAD_DIM ** (-0.5)
    ctx_count = lax.axis_size("ctx")
    ctx_place = lax.axis_index("ctx")
    my_start = ctx_place * tokens_here
    query_four = query_rows.reshape(tokens_here, kv_here, groups, HEAD_DIM)
    start_state = (
        jnp.full((kv_here, groups, tokens_here), NEG_FILL, jnp.float32),
        jnp.zeros((kv_here, groups, tokens_here), jnp.float32),
        jnp.zeros((tokens_here, kv_here, groups, HEAD_DIM), jnp.float32),
    )

    def absorb_keys(soft_state, key_block, value_block, key_start):
        allowed = allowed_tile(
            doc_ids, window_blocks, my_start, tokens_here, key_start, key_block.shape[0]
        )
        return forward_update(
            soft_state,
            query_four,
            split_heads(key_block, kv_here),
            split_heads(value_block, kv_here),
            allowed,
            score_scale,
        )

    first_state = absorb_keys(start_state, key_rows, value_rows, my_start)

    def forward_turn(distance, carried):
        held_keys, current = carried
        held_keys = advance_keys(held_keys)
        return (
            held_keys,
            absorb_keys(current, held_keys[0], held_keys[1], (ctx_place - distance) * tokens_here),
        )

    held_keys, soft_state = lax.fori_loop(
        1, REACH + 1, forward_turn, ((key_rows, value_rows), first_state)
    )
    run_max, run_total, run_acc = soft_state
    attn_four = run_acc / jnp.transpose(run_total, (2, 0, 1))[..., None]
    attn = attn_four.reshape(tokens_here, -1).astype(jnp.bfloat16)
    log_sum = run_max + jnp.log(run_total)
    layer_out = lax.psum_scatter(
        jnp.dot(attn, out_weight, preferred_element_type=jnp.float32).astype(jnp.bfloat16),
        "tp",
        scatter_dimension=0,
        tiled=True,
    )
    grad_piece = lax.all_gather(out_grad, "tp", axis=0, tiled=True)
    part_heads = lax.dot_general(
        grad_piece, out_weight, (((1,), (1,)), ((), ())), preferred_element_type=jnp.float32
    )
    head_grads = part_heads
    weight_part = lax.dot_general(
        attn, grad_piece, (((0,), (0,)), ((), ())), preferred_element_type=jnp.float32
    )
    head_grads, weight_part = (head_grads, weight_part)
    seq_total = ctx_count * tokens_here
    grad_weight = lax.psum_scatter(
        weight_part, "ctx", scatter_dimension=1, tiled=True
    ) * seq_total ** (-0.5)
    d_attn = head_grads.astype(jnp.bfloat16)
    grad_four = d_attn.reshape(tokens_here, kv_here, groups, HEAD_DIM)
    delta_rows = jnp.transpose(
        jnp.sum(
            grad_four.astype(jnp.float32)
            * attn.reshape(tokens_here, kv_here, groups, HEAD_DIM).astype(jnp.float32),
            axis=-1,
        ),
        (1, 2, 0),
    )
    zeros_query = jnp.zeros((tokens_here, kv_here, groups, HEAD_DIM), jnp.float32)
    zeros_keys = jnp.zeros((tokens_here, kv_width), jnp.float32)

    def back_visit(distance, held_keys, key_grads, query_grad):
        allowed = allowed_tile(
            doc_ids,
            window_blocks,
            my_start,
            tokens_here,
            (ctx_place - distance) * tokens_here,
            tokens_here,
        )
        query_part, key_part, value_part = backward_tile(
            query_four,
            grad_four,
            log_sum,
            delta_rows,
            split_heads(held_keys[0], kv_here),
            split_heads(held_keys[1], kv_here),
            allowed,
            score_scale,
        )
        return (
            query_grad + query_part,
            key_grads[0] + key_part.reshape(tokens_here, kv_width),
            key_grads[1] + value_part.reshape(tokens_here, kv_width),
        )

    first_sums = back_visit(0, (key_rows, value_rows), (zeros_keys, zeros_keys), zeros_query)

    def back_turn(distance, carried):
        held_keys, sums_now = carried
        held_keys = advance_keys(held_keys)
        moved = pass_grads((sums_now[1], sums_now[2]), 1)
        return (held_keys, back_visit(distance, held_keys, moved, sums_now[0]))

    held_keys, sums_now = lax.fori_loop(
        1, REACH + 1, back_turn, ((key_rows, value_rows), first_sums)
    )
    home_grads = pass_grads((sums_now[1], sums_now[2]), -REACH)
    query_grad, key_grad, value_grad = (sums_now[0], home_grads[0], home_grads[1])
    grad_queries = query_grad.reshape(tokens_here, -1).astype(jnp.bfloat16)
    grad_keys = key_grad.astype(jnp.bfloat16)
    grad_values = value_grad.astype(jnp.bfloat16)
    return (layer_out, grad_queries, grad_keys, grad_values, grad_weight)


def solution(mesh):
    placed = (
        P("ctx", "tp"),
        P("ctx", "tp"),
        P("ctx", "tp"),
        P("tp", None),
        P(("ctx", "tp"), None),
        P(),
        P(),
    )
    return jax.shard_map(
        on_device,
        mesh=mesh,
        in_specs=placed,
        out_specs=(
            P(("ctx", "tp"), None),
            P("ctx", "tp"),
            P("ctx", "tp"),
            P("ctx", "tp"),
            P("tp", "ctx"),
        ),
        check_vma=False,
    )
```

profile of v0, /device:TPU:96, one launch (start us, length us, event | category | flops | bytes accessed | tf_op | source)
XLA Modules:
  0.0 510.2 jit_solution(6499111236145695360)
XLA Ops:
  17.7 47.1 %while.48 = (s32[]{:T(128)}, bf16[512,128]{1,0:T(8,128)(2,1)S(1)}, bf16[512,128]{1,0:T(8,128)(2,1)S(1)}, f32[1,4,512]{2,1,0:T(4,128)S(1)}, f32[1,4,512]{2,1,0:T(...) while((s32[]{:T(128)}, bf16[512,128]{1,0:T(8,128)(2,1)S(1)}, ...), condition=%wide.region_5.6_spmd, body=%wide.region_2.5_spmd.sunk | while | flops 552884224 | bytes 18248036 | solution.py:150
  17.7 3.5 collective-permute-start
  21.2 3.3 collective-permute-start.1
  32.8 3.1 collective-permute-start
  39.7 3.8 collective-permute-done
  48.8 4.4 collective-permute-start
  56.7 3.4 collective-permute-done
  67.4 6.0 %convolution_convert_fusion.1 = bf16[512,512]{0,1:T(8,128)(2,1)S(1)} fusion(bf16[512,4096]{1,0:T(8,128)(2,1)} %all-gather.2.cloned.1.call-done, bf16[512,4096]{1,0:T(8,128)(2,1)} %param.14), kind=kOutput, calls=%fused_computation.121 | convolution fusion | flops 2147745792 | bytes 8912896 | tf_op jit(solution)/shard_map/dot_general | solution.py:164
  73.6 5.7 %fusion.131 = f32[512,4096]{0,1:T(8,128)} fusion(bf16[512,512]{0,1:T(8,128)(2,1)S(1)} %bitcast.362, bf16[512,4096]{1,0:T(8,128)(2,1)S(1)} %copy-done.2), kind=kOutput, calls=%fused_computation.160 | convolution fusion | flops 2147483648 | bytes 13107200 | tf_op jit(solution)/shard_map/dot_general | solution.py:168
  79.6 3.6 fusion.105
  83.2 3.0 fusion.77
  86.2 4.3 convolution_convert_fusion
  97.3 64.5 %while.49 = (s32[]{:T(128)}, bf16[512,128]{1,0:T(8,128)(2,1)S(1)}, bf16[512,128]{1,0:T(8,128)(2,1)S(1)}, f32[512,1,4,128]{3,0,2,1:T(8,128)S(1)}, bf16[512,128]{1...) while((s32[]{:T(128)}, bf16[512,128]{1,0:T(8,128)(2,1)S(1)}, ...), condition=%wide.region_9.10_spmd, body=%wide.region_8.9_spmd.sunk | while | flops 1356218368 | bytes 29544936 | solution.py:222
  97.5 3.3 collective-permute-start.2
  108.6 3.5 collective-permute-done.3
  118.1 3.2 collective-permute-start.2
  121.3 2.6 collective-permute-start.3
  130.0 2.6 collective-permute-done.3
  138.9 2.6 collective-permute-start.2
  141.5 2.9 collective-permute-start.3
  146.6 3.9 collective-permute-start.5
  163.9 4.6 collective-permute-done.6
  170.2 261.9 %reduce-scatter.5.cloned.1.call-done = f32[512,64]{0,1:T(8,128)} async-done(((f32[512,4096]{0,1:T(8,128)}), f32[512,64]{0,1:T(8,128)}) %reduce-scatter.5.cloned.1.call-update) | async-done | bytes 131088 | tf_op jit(solution)/shard_map/reduce_scatter | solution.py:173
  433.7 68.7 %reduce-scatter.3.cloned.1.call-done = bf16[128,4096]{1,0:T(8,128)(2,1)} async-done(((bf16[512,4096]{1,0:T(8,128)(2,1)}), bf16[128,4096]{1,0:T(8,128)(2,1)}) %reduce-scatter.3.cloned.1.call-update) | async-done | bytes 1048592 | tf_op jit(solution)/shard_map/reduce_scatter | solution.py:157
  (159 shorter events, 91.4 us)
Async XLA Ops:
  7.2 60.2 %all-gather.2.cloned.1.call-start = ((), (), s32[]{:S(2)}) async-start(), calls=%async_computation.3 | async-start | bytes 5242880 | tf_op jit(solution)/shard_map/all_gather | solution.py:163
  9.1 423.0 %reduce-scatter.5.cloned.1.call-start = ((), (), s32[]{:S(2)}) async-start(), calls=%async_computation.4 | async-start | bytes 8519680 | tf_op jit(solution)/shard_map/reduce_scatter | solution.py:173
  17.7 10.2 %collective-permute-start = (bf16[512,128]{1,0:T(8,128)(2,1)S(1)}, bf16[512,128]{1,0:T(8,128)(2,1)S(1)}, u32[]{:S(2)}, u32[]{:S(2)}) collective-permute-start(bf16[512,128]{1,0:T(8,128)(2,1)S(1)} %get-tuple-element.1159), channel_id=1, source_target_pairs={{0,4},{4,8},{8,12},{12,16},{16,20},{20,24},{24,28},{28,32},{32,36}... | collective-permute-start | bytes 393224 | tf_op jit(solution)/shard_map/while/body/eval_jaxpr/ppermute | solution.py:17
  21.2 9.9 %collective-permute-start.1 = (bf16[512,128]{1,0:T(8,128)(2,1)S(1)}, bf16[512,128]{1,0:T(8,128)(2,1)S(1)}, u32[]{:S(2)}, u32[]{:S(2)}) collective-permute-start(bf16[512,128]{1,0:T(8,128)(2,1)S(1)} %get-tuple-element.1160), channel_id=1, source_target_pairs={{0,4},{4,8},{8,12},{12,16},{16,20},{20,24},{24,28},{28,32},{32,36}... | collective-permute-start | bytes 393224 | tf_op jit(solution)/shard_map/while/body/eval_jaxpr/ppermute | solution.py:17
  32.8 10.7 %collective-permute-start = (bf16[512,128]{1,0:T(8,128)(2,1)S(1)}, bf16[512,128]{1,0:T(8,128)(2,1)S(1)}, u32[]{:S(2)}, u32[]{:S(2)}) collective-permute-start(bf16[512,128]{1,0:T(8,128)(2,1)S(1)} %get-tuple-element.1159), channel_id=1, source_target_pairs={{0,4},{4,8},{8,12},{12,16},{16,20},{20,24},{24,28},{28,32},{32,36}... | collective-permute-start | bytes 393224 | tf_op jit(solution)/shard_map/while/body/eval_jaxpr/ppermute | solution.py:17
  35.9 11.2 %collective-permute-start.1 = (bf16[512,128]{1,0:T(8,128)(2,1)S(1)}, bf16[512,128]{1,0:T(8,128)(2,1)S(1)}, u32[]{:S(2)}, u32[]{:S(2)}) collective-permute-start(bf16[512,128]{1,0:T(8,128)(2,1)S(1)} %get-tuple-element.1160), channel_id=1, source_target_pairs={{0,4},{4,8},{8,12},{12,16},{16,20},{20,24},{24,28},{28,32},{32,36}... | collective-permute-start | bytes 393224 | tf_op jit(solution)/shard_map/while/body/eval_jaxpr/ppermute | solution.py:17
  48.8 11.3 %collective-permute-start = (bf16[512,128]{1,0:T(8,128)(2,1)S(1)}, bf16[512,128]{1,0:T(8,128)(2,1)S(1)}, u32[]{:S(2)}, u32[]{:S(2)}) collective-permute-start(bf16[512,128]{1,0:T(8,128)(2,1)S(1)} %get-tuple-element.1159), channel_id=1, source_target_pairs={{0,4},{4,8},{8,12},{12,16},{16,20},{20,24},{24,28},{28,32},{32,36}... | collective-permute-start | bytes 393224 | tf_op jit(solution)/shard_map/while/body/eval_jaxpr/ppermute | solution.py:17
  53.2 10.0 %collective-permute-start.1 = (bf16[512,128]{1,0:T(8,128)(2,1)S(1)}, bf16[512,128]{1,0:T(8,128)(2,1)S(1)}, u32[]{:S(2)}, u32[]{:S(2)}) collective-permute-start(bf16[512,128]{1,0:T(8,128)(2,1)S(1)} %get-tuple-element.1160), channel_id=1, source_target_pairs={{0,4},{4,8},{8,12},{12,16},{16,20},{20,24},{24,28},{28,32},{32,36}... | collective-permute-start | bytes 393224 | tf_op jit(solution)/shard_map/while/body/eval_jaxpr/ppermute | solution.py:17
  79.3 423.1 %reduce-scatter.3.cloned.1.call-start = ((), (), s32[]{:S(2)}) async-start(), calls=%async_computation.2 | async-start | bytes 5242880 | tf_op jit(solution)/shard_map/reduce_scatter | solution.py:157
  97.5 10.4 %collective-permute-start.2 = (bf16[512,128]{1,0:T(8,128)(2,1)S(1)}, bf16[512,128]{1,0:T(8,128)(2,1)S(1)}, u32[]{:S(2)}, u32[]{:S(2)}) collective-permute-start(bf16[512,128]{1,0:T(8,128)(2,1)S(1)} %get-tuple-element.1216), channel_id=1, source_target_pairs={{0,4},{4,8},{8,12},{12,16},{16,20},{20,24},{24,28},{28,32},{32,36}... | collective-permute-start | bytes 393224 | tf_op jit(solution)/shard_map/while/body/eval_jaxpr/ppermute | solution.py:17
  100.8 11.3 %collective-permute-start.3 = (bf16[512,128]{1,0:T(8,128)(2,1)S(1)}, bf16[512,128]{1,0:T(8,128)(2,1)S(1)}, u32[]{:S(2)}, u32[]{:S(2)}) collective-permute-start(bf16[512,128]{1,0:T(8,128)(2,1)S(1)} %get-tuple-element.1217), channel_id=1, source_target_pairs={{0,4},{4,8},{8,12},{12,16},{16,20},{20,24},{24,28},{28,32},{32,36}... | collective-permute-start | bytes 393224 | tf_op jit(solution)/shard_map/while/body/eval_jaxpr/ppermute | solution.py:17
  102.8 12.2 %collective-permute-start.4 = (bf16[512,128]{1,0:T(8,128)(2,1)S(1)}, bf16[512,128]{1,0:T(8,128)(2,1)S(1)}, u32[]{:S(2)}, u32[]{:S(2)}) collective-permute-start(bf16[512,128]{1,0:T(8,128)(2,1)S(1)} %get-tuple-element.1219), channel_id=1, source_target_pairs={{252,0},{0,4},{4,8},{8,12},{12,16},{16,20},{20,24},{24,28},{28,32}... | collective-permute-start | bytes 393224 | tf_op jit(solution)/shard_map/while/body/eval_jaxpr/ppermute | solution.py:23
  105.2 11.6 %collective-permute-start.5 = (bf16[512,128]{1,0:T(8,128)(2,1)S(1)}, bf16[512,128]{1,0:T(8,128)(2,1)S(1)}, u32[]{:S(2)}, u32[]{:S(2)}) collective-permute-start(bf16[512,128]{1,0:T(8,128)(2,1)S(1)} %get-tuple-element.1220), channel_id=1, source_target_pairs={{252,0},{0,4},{4,8},{8,12},{12,16},{16,20},{20,24},{24,28},{28,32}... | collective-permute-start | bytes 393224 | tf_op jit(solution)/shard_map/while/body/eval_jaxpr/ppermute | solution.py:23
  118.1 11.2 %collective-permute-start.2 = (bf16[512,128]{1,0:T(8,128)(2,1)S(1)}, bf16[512,128]{1,0:T(8,128)(2,1)S(1)}, u32[]{:S(2)}, u32[]{:S(2)}) collective-permute-start(bf16[512,128]{1,0:T(8,128)(2,1)S(1)} %get-tuple-element.1216), channel_id=1, source_target_pairs={{0,4},{4,8},{8,12},{12,16},{16,20},{20,24},{24,28},{28,32},{32,36}... | collective-permute-start | bytes 393224 | tf_op jit(solution)/shard_map/while/body/eval_jaxpr/ppermute | solution.py:17
  121.3 11.4 %collective-permute-start.3 = (bf16[512,128]{1,0:T(8,128)(2,1)S(1)}, bf16[512,128]{1,0:T(8,128)(2,1)S(1)}, u32[]{:S(2)}, u32[]{:S(2)}) collective-permute-start(bf16[512,128]{1,0:T(8,128)(2,1)S(1)} %get-tuple-element.1217), channel_id=1, source_target_pairs={{0,4},{4,8},{8,12},{12,16},{16,20},{20,24},{24,28},{28,32},{32,36}... | collective-permute-start | bytes 393224 | tf_op jit(solution)/shard_map/while/body/eval_jaxpr/ppermute | solution.py:17
  123.9 11.5 %collective-permute-start.4 = (bf16[512,128]{1,0:T(8,128)(2,1)S(1)}, bf16[512,128]{1,0:T(8,128)(2,1)S(1)}, u32[]{:S(2)}, u32[]{:S(2)}) collective-permute-start(bf16[512,128]{1,0:T(8,128)(2,1)S(1)} %get-tuple-element.1219), channel_id=1, source_target_pairs={{252,0},{0,4},{4,8},{8,12},{12,16},{16,20},{20,24},{24,28},{28,32}... | collective-permute-start | bytes 393224 | tf_op jit(solution)/shard_map/while/body/eval_jaxpr/ppermute | solution.py:23
  124.6 13.0 %collective-permute-start.5 = (bf16[512,128]{1,0:T(8,128)(2,1)S(1)}, bf16[512,128]{1,0:T(8,128)(2,1)S(1)}, u32[]{:S(2)}, u32[]{:S(2)}) collective-permute-start(bf16[512,128]{1,0:T(8,128)(2,1)S(1)} %get-tuple-element.1220), channel_id=1, source_target_pairs={{252,0},{0,4},{4,8},{8,12},{12,16},{16,20},{20,24},{24,28},{28,32}... | collective-permute-start | bytes 393224 | tf_op jit(solution)/shard_map/while/body/eval_jaxpr/ppermute | solution.py:23
  138.9 16.0 %copy-start.9 = (bf16[512,1,4,128]{3,0,2,1:T(8,128)(2,1)S(1)}, bf16[512,1,4,128]{3,0,2,1:T(8,128)(2,1)}, u32[]{:S(2)}) copy-start(bf16[512,1,4,128]{3,0,2,1:T(8,128)(2,1)} %get-tuple-element.1250) | copy-start | bytes 1572868 | tf_op jit(solution)/shard_map/while
  138.9 13.2 %collective-permute-start.2 = (bf16[512,128]{1,0:T(8,128)(2,1)S(1)}, bf16[512,128]{1,0:T(8,128)(2,1)S(1)}, u32[]{:S(2)}, u32[]{:S(2)}) collective-permute-start(bf16[512,128]{1,0:T(8,128)(2,1)S(1)} %get-tuple-element.1216), channel_id=1, source_target_pairs={{0,4},{4,8},{8,12},{12,16},{16,20},{20,24},{24,28},{28,32},{32,36}... | collective-permute-start | bytes 393224 | tf_op jit(solution)/shard_map/while/body/eval_jaxpr/ppermute | solution.py:17
  141.5 13.4 %collective-permute-start.3 = (bf16[512,128]{1,0:T(8,128)(2,1)S(1)}, bf16[512,128]{1,0:T(8,128)(2,1)S(1)}, u32[]{:S(2)}, u32[]{:S(2)}) collective-permute-start(bf16[512,128]{1,0:T(8,128)(2,1)S(1)} %get-tuple-element.1217), channel_id=1, source_target_pairs={{0,4},{4,8},{8,12},{12,16},{16,20},{20,24},{24,28},{28,32},{32,36}... | collective-permute-start | bytes 393224 | tf_op jit(solution)/shard_map/while/body/eval_jaxpr/ppermute | solution.py:17
  144.5 13.3 %collective-permute-start.4 = (bf16[512,128]{1,0:T(8,128)(2,1)S(1)}, bf16[512,128]{1,0:T(8,128)(2,1)S(1)}, u32[]{:S(2)}, u32[]{:S(2)}) collective-permute-start(bf16[512,128]{1,0:T(8,128)(2,1)S(1)} %get-tuple-element.1219), channel_id=1, source_target_pairs={{252,0},{0,4},{4,8},{8,12},{12,16},{16,20},{20,24},{24,28},{28,32}... | collective-permute-start | bytes 393224 | tf_op jit(solution)/shard_map/while/body/eval_jaxpr/ppermute | solution.py:23
  146.6 13.9 %collective-permute-start.5 = (bf16[512,128]{1,0:T(8,128)(2,1)S(1)}, bf16[512,128]{1,0:T(8,128)(2,1)S(1)}, u32[]{:S(2)}, u32[]{:S(2)}) collective-permute-start(bf16[512,128]{1,0:T(8,128)(2,1)S(1)} %get-tuple-element.1220), channel_id=1, source_target_pairs={{252,0},{0,4},{4,8},{8,12},{12,16},{16,20},{20,24},{24,28},{28,32}... | collective-permute-start | bytes 393224 | tf_op jit(solution)/shard_map/while/body/eval_jaxpr/ppermute | solution.py:23
  161.8 6.6 %collective-permute-start.6 = (bf16[512,128]{1,0:T(8,128)(2,1)S(1)}, bf16[512,128]{1,0:T(8,128)(2,1)S(1)}, u32[]{:S(2)}, u32[]{:S(2)}) collective-permute-start(bf16[512,128]{1,0:T(8,128)(2,1)S(1)} %get-tuple-element.813), channel_id=1, source_target_pairs={{12,0},{16,4},{20,8},{24,12},{28,16},{32,20},{36,24},{40,28},{44,3... | collective-permute-start | bytes 393224 | tf_op jit(solution)/shard_map/ppermute | solution.py:23
  161.9 8.3 %collective-permute-start.7 = (bf16[512,128]{1,0:T(8,128)(2,1)S(1)}, bf16[512,128]{1,0:T(8,128)(2,1)S(1)}, u32[]{:S(2)}, u32[]{:S(2)}) collective-permute-start(bf16[512,128]{1,0:T(8,128)(2,1)S(1)} %get-tuple-element.814), channel_id=1, source_target_pairs={{12,0},{16,4},{20,8},{24,12},{28,16},{32,20},{36,24},{40,28},{44,3... | collective-permute-start | bytes 393224 | tf_op jit(solution)/shard_map/ppermute | solution.py:23
  (11 other events, 60.8 us)
Sparse Core Ops, SparseCore 0:
  9.8 54.3 all-gather.1
  79.4 352.6 reduce-scatter.4
  435.5 66.8 reduce-scatter.2
where the time goes:
time: 513 us; the launch traced here: 510 us
  waiting for transfers between devices  365 us (71%)
  matrix products  54.2 us (11%)
  starting transfers between devices  48.6 us (9%)
  local copies, waits for them, and re-layouts  17.3 us (3%)
  between operations  14 us (3%)
  other arithmetic  9.62 us (2%)
    reduce_scatter x1, waiting for transfers between devices, on_device(): lax.psum_scatter(weight_part, 'ctx', scatter_dimension=1, tiled=True)  262 us
    reduce_scatter x1, waiting for transfers between devices, on_device(): lax.psum_scatter(jnp.dot(attn, out_weight, preferred_element_type=jnp.flo...  68.7 us
    ppermute x12, starting transfers between devices, passed_along(): return lax.ppermute(block, axis, route)  35.4 us
    ppermute x12, waiting for transfers between devices, passed_along(): return lax.ppermute(block, axis, route)  23.2 us
    ppermute x8, starting transfers between devices, shifted(): return lax.ppermute(block, axis, route)  12.9 us
    ppermute x8, waiting for transfers between devices, shifted(): return lax.ppermute(block, axis, route)  11.6 us
  transfers between devices with their start and end apart: 23, of which 22 were waited for; matrix products, arithmetic and copies ran while one was open for 13% of the time, Pallas kernels for 0%

commit v1 on v0

v1 whole, which is shorter than its diff:
```python
import jax
import jax.numpy as jnp
import numpy as np
from jax import lax
from jax.sharding import Mesh
from jax.sharding import PartitionSpec as P

HEAD_DIM = 128
BLOCK = 128
REACH = 3
NEG_FILL = -1e30

CTX_PARTS = (("z", 8), ("x", 4), ("y_lo", 2))
TP_PARTS = (("y_hi", 2), ("core", 2))
CTX = tuple(name for name, _ in CTX_PARTS)
TP = tuple(name for name, _ in TP_PARTS)


def from_earlier(block, distance, count):
    route = [(i - distance, i) for i in range(count) if 0 <= i - distance < count]
    return lax.ppermute(block, CTX, route)


def to_earlier(block, distance, count):
    route = [(i, i - distance) for i in range(count) if 0 <= i - distance < count]
    return lax.ppermute(block, CTX, route)


def rotated(block, distance, count):
    route = [((i - distance) % count, i) for i in range(count)]
    return lax.ppermute(block, TP, route)


def on_device(query_rows, key_rows, value_rows, out_weight, out_grad, doc_ids, window_blocks):
    tokens_here = query_rows.shape[0]
    kv_width = key_rows.shape[1]
    kv_here = kv_width // HEAD_DIM
    groups = query_rows.shape[1] // kv_width
    score_scale = HEAD_DIM ** (-0.5)
    ctx_count = lax.axis_size(CTX)
    tp_count = lax.axis_size(TP)
    ctx_place = lax.axis_index(CTX)
    tp_place = lax.axis_index(TP)
    my_start = ctx_place * tokens_here
    span = REACH * tokens_here
    key_count = span + tokens_here

    grad_piece = lax.all_gather(out_grad, TP, axis=0, tiled=True)

    earlier = [
        from_earlier((key_rows, value_rows), distance, ctx_count)
        for distance in range(REACH, 0, -1)
    ]
    keys_all = jnp.concatenate([pair[0] for pair in earlier] + [key_rows], axis=0)
    values_all = jnp.concatenate([pair[1] for pair in earlier] + [value_rows], axis=0)
    key_heads = keys_all.reshape(key_count, kv_here, HEAD_DIM)
    value_heads = values_all.reshape(key_count, kv_here, HEAD_DIM)

    doc_pad = jnp.concatenate([jnp.full((span,), -1, jnp.int32), doc_ids.astype(jnp.int32)])
    query_pos = my_start + jnp.arange(tokens_here, dtype=jnp.int32)
    key_pos = my_start - span + jnp.arange(key_count, dtype=jnp.int32)
    query_doc = lax.dynamic_slice_in_dim(doc_ids, my_start, tokens_here)
    key_doc = lax.dynamic_slice_in_dim(doc_pad, my_start, key_count)
    query_width = jnp.repeat(
        lax.dynamic_slice_in_dim(window_blocks, my_start // BLOCK, tokens_here // BLOCK), BLOCK
    )
    allowed = (
        (key_pos[None, :] >= 0)
        & (key_pos[None, :] <= query_pos[:, None])
        & (query_doc[:, None] == key_doc[None, :])
        & (query_pos[:, None] // BLOCK - key_pos[None, :] // BLOCK < query_width[:, None])
    )

    query_four = query_rows.reshape(tokens_here, kv_here, groups, HEAD_DIM)
    scores = (
        jnp.einsum("qcgd,kcd->cgqk", query_four, key_heads, preferred_element_type=jnp.float32)
        * score_scale
    )
    masked = jnp.where(allowed, scores, NEG_FILL)
    row_max = jnp.max(masked, axis=-1)
    expo = jnp.where(allowed, jnp.exp(masked - row_max[..., None]), 0.0)
    total = jnp.sum(expo, axis=-1)
    summed = jnp.einsum(
        "cgqk,kcd->qcgd", expo.astype(jnp.bfloat16), value_heads, preferred_element_type=jnp.float32
    )
    attn_four = summed / jnp.transpose(total, (2, 0, 1))[..., None]
    attn = attn_four.reshape(tokens_here, -1).astype(jnp.bfloat16)
    log_sum = row_max + jnp.log(total)

    out_part = jnp.dot(attn, out_weight, preferred_element_type=jnp.float32)
    out_chunks = out_part.reshape(tp_count, tokens_here // tp_count, out_part.shape[1])
    layer_sum = lax.dynamic_index_in_dim(out_chunks, tp_place, 0, keepdims=False)
    for distance in range(1, tp_count):
        chunk = lax.dynamic_index_in_dim(
            out_chunks, (tp_place + distance) % tp_count, 0, keepdims=False
        )
        layer_sum = layer_sum + rotated(chunk.astype(jnp.bfloat16), distance, tp_count).astype(
            jnp.float32
        )
    layer_out = layer_sum.astype(jnp.bfloat16)

    weight_part = lax.dot_general(
        attn, grad_piece, (((0,), (0,)), ((), ())), preferred_element_type=jnp.float32
    )
    weight_sum = weight_part.astype(jnp.bfloat16)
    for stage, (name, _) in enumerate(CTX_PARTS):
        weight_sum = lax.psum_scatter(weight_sum, name, scatter_dimension=1, tiled=True)
        if stage == 0:
            weight_sum = weight_sum.astype(jnp.float32)
    seq_total = ctx_count * tokens_here
    grad_weight = weight_sum * seq_total ** (-0.5)

    d_attn = lax.dot_general(
        grad_piece, out_weight, (((1,), (1,)), ((), ())), preferred_element_type=jnp.float32
    ).astype(jnp.bfloat16)
    grad_four = d_attn.reshape(tokens_here, kv_here, groups, HEAD_DIM)
    delta_rows = jnp.transpose(
        jnp.sum(
            grad_four.astype(jnp.float32)
            * attn.reshape(tokens_here, kv_here, groups, HEAD_DIM).astype(jnp.float32),
            axis=-1,
        ),
        (1, 2, 0),
    )

    probs = jnp.exp(jnp.where(allowed, scores - log_sum[..., None], NEG_FILL))
    d_probs = jnp.einsum(
        "qcgd,kcd->cgqk", grad_four, value_heads, preferred_element_type=jnp.float32
    )
    d_scores = (probs * (d_probs - delta_rows[..., None]) * score_scale).astype(jnp.bfloat16)
    query_grad = jnp.einsum(
        "cgqk,kcd->qcgd", d_scores, key_heads, preferred_element_type=jnp.float32
    )
    key_grad_all = jnp.einsum(
        "cgqk,qcgd->kcd", d_scores, query_four, preferred_element_type=jnp.float32
    ).reshape(key_count, kv_width)
    value_grad_all = jnp.einsum(
        "cgqk,qcgd->kcd", probs.astype(jnp.bfloat16), grad_four, preferred_element_type=jnp.float32
    ).reshape(key_count, kv_width)

    key_grad = key_grad_all[span:]
    value_grad = value_grad_all[span:]
    for distance in range(1, REACH + 1):
        lo = span - distance * tokens_here
        sent = to_earlier(
            (
                key_grad_all[lo : lo + tokens_here].astype(jnp.bfloat16),
                value_grad_all[lo : lo + tokens_here].astype(jnp.bfloat16),
            ),
            distance,
            ctx_count,
        )
        key_grad = key_grad + sent[0].astype(jnp.float32)
        value_grad = value_grad + sent[1].astype(jnp.float32)

    grad_queries = query_grad.reshape(tokens_here, -1).astype(jnp.bfloat16)
    grad_keys = key_grad.astype(jnp.bfloat16)
    grad_values = value_grad.astype(jnp.bfloat16)
    return (layer_out, grad_queries, grad_keys, grad_values, grad_weight)


def solution(mesh):
    shape = tuple(size for _, size in CTX_PARTS + TP_PARTS)
    fine = Mesh(np.asarray(mesh.devices).reshape(shape), CTX + TP)
    placed = (
        P(CTX, TP),
        P(CTX, TP),
        P(CTX, TP),
        P(TP, None),
        P(CTX + TP, None),
        P(),
        P(),
    )
    return jax.shard_map(
        on_device,
        mesh=fine,
        in_specs=placed,
        out_specs=(
            P(CTX + TP, None),
            P(CTX, TP),
            P(CTX, TP),
            P(CTX, TP),
            P(TP, CTX),
        ),
        check_vma=False,
    )
```

time: 513 us -> 221 us (0.43)
  waiting for transfers between devices: 365 us -> 64.5 us
  local copies, waits for them, and re-layouts: 17.3 us -> 27 us
  other arithmetic: 9.62 us -> 15.4 us
    reduce_scatter x2, waiting for transfers between devices: 331 us -> 25.4 us  [on_device(): lax.psum_scatter(weight_sum, name, scatter_dimension=1, tiled=True)]
    unnamed x25 -> x30, local copies, waits for them, and re-layouts: 7.18 us -> 21.1 us
    all_gather x1, waiting for transfers between devices: 0.02 us -> 9.52 us  [on_device(): grad_piece = lax.all_gather(out_grad, TP, axis=0, tiled=True)]
    convert_element_type x1 -> x4, other arithmetic: 0.07 us -> 8.89 us  [the longest x1 4.09 us: on_device(): layer_out = layer_sum.astype(jnp.bfloat16)]
    ppermute x20 -> x15, waiting for transfers between devices: 34.8 us -> 28.9 us  [the longest x3 26.3 us: rotated(): return lax.ppermute(block, TP, route)]
    dot_general x28 -> x7, matrix products: 42.6 us -> 40.5 us  [the longest x1 10 us: on_device(): jnp.einsum('qcgd,kcd->cgqk', grad_four, value_heads, preferred_element_ty...]
    ppermute x20 -> x15, starting transfers between devices: 48.3 us -> 48.4 us  [the longest x6 23.5 us: from_earlier(): return lax.ppermute(block, CTX, route)]
  transfers between devices with their start and end apart: 23 -> 19, of which waited for: 22 -> 5; matrix products, arithmetic and copies ran while one was open for 13% -> 30% of each run, Pallas kernels for 0% -> 0%
where the time goes in v1:
time: 221 us
  waiting for transfers between devices  64.5 us (29%)
  matrix products  50.9 us (23%)
  starting transfers between devices  48.6 us (22%)
  local copies, waits for them, and re-layouts  27 us (12%)
  other arithmetic  15.4 us (7%)
  between operations  14.2 us (6%)
    ppermute x3, waiting for transfers between devices, rotated(): return lax.ppermute(block, TP, route)  26.3 us
    reduce_scatter x2, waiting for transfers between devices, on_device(): lax.psum_scatter(weight_sum, name, scatter_dimension=1, tiled=True)  25.4 us
    ppermute x6, starting transfers between devices, from_earlier(): return lax.ppermute(block, CTX, route)  23.5 us
    unnamed x30, local copies, waits for them, and re-layouts  21.1 us
    ppermute x6, starting transfers between devices, to_earlier(): return lax.ppermute(block, CTX, route)  18.7 us
    dot_general x1, matrix products, on_device(): jnp.einsum('qcgd,kcd->cgqk', grad_four, value_heads, preferred_element_ty...  10 us
    all_gather x1, waiting for transfers between devices, on_device(): grad_piece = lax.all_gather(out_grad, TP, axis=0, tiled=True)  9.52 us
    dot_general x1, matrix products, on_device(): jnp.einsum('cgqk,qcgd->kcd', probs.astype(jnp.bfloat16), grad_four, prefe...  9.45 us
  transfers between devices with their start and end apart: 19, of which 5 were waited for; matrix products, arithmetic and copies ran while one was open for 30% of the time, Pallas kernels for 0%

profile of v1, /device:TPU:96, one launch (start us, length us, event | category | flops | bytes accessed | tf_op | source)
XLA Modules:
  0.0 220.5 jit_solution(11239289833931936468)
XLA Ops:
  9.0 3.5 %collective-permute-start.2 = (bf16[512,128]{0,1:T(8,128)(2,1)S(1)}, bf16[512,128]{0,1:T(8,128)(2,1)S(1)}, u32[]{:S(2)}, u32[]{:S(2)}) collective-permute-start(bf16[512,128]{0,1:T(8,128)(2,1)S(1)} %copy.28), channel_id=1, source_target_pairs={{0,4},{4,8},{8,12},{12,16},{16,20},{20,24},{24,28},{28,32},{32,36}... | collective-permute-start | bytes 393224 | tf_op jit(solution)/shard_map/ppermute | solution.py:21
  12.5 3.4 %collective-permute-start.1 = (bf16[512,128]{0,1:T(8,128)(2,1)S(1)}, bf16[512,128]{0,1:T(8,128)(2,1)S(1)}, u32[]{:S(2)}, u32[]{:S(2)}) collective-permute-start(bf16[512,128]{0,1:T(8,128)(2,1)S(1)} %copy.28), channel_id=1, source_target_pairs={{0,8},{4,12},{8,16},{12,20},{16,24},{20,28},{24,32},{28,36},{32,40... | collective-permute-start | bytes 393224 | tf_op jit(solution)/shard_map/ppermute | solution.py:21
  15.9 3.4 %collective-permute-start.4 = (bf16[512,128]{1,0:T(8,128)(2,1)}, bf16[512,128]{1,0:T(8,128)(2,1)S(1)}, u32[]{:S(2)}, u32[]{:S(2)}) collective-permute-start(bf16[512,128]{1,0:T(8,128)(2,1)} %param.8), channel_id=1, source_target_pairs={{0,8},{4,12},{8,16},{12,20},{16,24},{20,28},{24,32},{28,36},{32,40... | collective-permute-start | bytes 393224 | tf_op jit(solution)/shard_map/ppermute | solution.py:21
  19.3 5.5 %collective-permute-start.3 = (bf16[512,128]{1,0:T(8,128)(2,1)}, bf16[512,128]{1,0:T(8,128)(2,1)S(1)}, u32[]{:S(2)}, u32[]{:S(2)}) collective-permute-start(bf16[512,128]{1,0:T(8,128)(2,1)} %param.8), channel_id=1, source_target_pairs={{0,12},{4,16},{8,20},{12,24},{16,28},{20,32},{24,36},{28,40},{32,4... | collective-permute-start | bytes 393224 | tf_op jit(solution)/shard_map/ppermute | solution.py:21
  24.8 4.1 %collective-permute-start.5 = (bf16[512,128]{1,0:T(8,128)(2,1)}, bf16[512,128]{1,0:T(8,128)(2,1)S(1)}, u32[]{:S(2)}, u32[]{:S(2)}) collective-permute-start(bf16[512,128]{1,0:T(8,128)(2,1)} %param.8), channel_id=1, source_target_pairs={{0,4},{4,8},{8,12},{12,16},{16,20},{20,24},{24,28},{28,32},{32,36}... | collective-permute-start | bytes 393224 | tf_op jit(solution)/shard_map/ppermute | solution.py:21
  33.6 3.6 %collective-permute-start = (bf16[512,128]{0,1:T(8,128)(2,1)S(1)}, bf16[512,128]{0,1:T(8,128)(2,1)S(1)}, u32[]{:S(2)}, u32[]{:S(2)}) collective-permute-start(bf16[512,128]{0,1:T(8,128)(2,1)S(1)} %copy.28), channel_id=1, source_target_pairs={{0,12},{4,16},{8,20},{12,24},{16,28},{20,32},{24,36},{28,40},{32,4... | collective-permute-start | bytes 393224 | tf_op jit(solution)/shard_map/ppermute | solution.py:21
  37.3 4.1 %fusion.5 = (f32[4,512]{1,0:T(4,128)S(1)}, f32[2048,512,4]{1,0,2:T(8,128)S(1)}) fusion(pred[512,2048]{0,1:T(8,128)(4,1)S(1)} %fusion.20, bf16[512,128]{1,0:T(8,128)(2,1)} %param.8, bf16[512,128]{1,0:T(8,128)(2,1)S(1)} %collective-permute-done.5, bf16[512,128]{1,0:T(8,128)(2,1)S(1)} %collective-permute-done.4, ...), kind=kOutput, calls=%fused_computation.9 | convolution fusion | flops 1088419840 | bytes 18882560 | tf_op jit(solution)/shard_map/qcgd,kcd->cgqk/dot_general | solution.py:76
  41.4 5.7 %copy-done.3 = f32[2048,512,4]{1,0,2:T(8,128)} copy-done((f32[2048,512,4]{1,0,2:T(8,128)}, f32[2048,512,4]{1,0,2:T(8,128)S(1)}, u32[]{:S(2)}) %copy-start.3) | copy-done | bytes 16777240
  47.1 4.2 %fusion.7 = f32[4,512]{1,0:T(4,128)S(1)} fusion(f32[2048,512,4]{1,0,2:T(8,128)S(1)} %get-tuple-element.25, f32[4,512]{1,0:T(4,128)S(1)} %get-tuple-element.24, pred[512,2048]{0,1:T(8,128)(4,1)S(1)} %fusion.20), kind=kLoop, calls=%fused_computation.11 | loop fusion | flops 20969472 | bytes 17842176 | tf_op jit(solution)/shard_map/reduce_sum | solution.py:82
  51.2 9.5 %all-gather.2.cloned.1.call-done = bf16[512,4096]{1,0:T(8,128)(2,1)} async-done(((bf16[128,4096]{1,0:T(8,128)(2,1)}), bf16[512,4096]{1,0:T(8,128)(2,1)}) %all-gather.2.cloned.1.call-update) | async-done | bytes 4194320 | tf_op jit(solution)/shard_map/all_gather | solution.py:48
  60.8 6.0 %convolution_convert_fusion.1 = bf16[512,512]{0,1:T(8,128)(2,1)S(1)} fusion(bf16[512,4096]{1,0:T(8,128)(2,1)} %all-gather.2.cloned.1.call-done, bf16[512,4096]{1,0:T(8,128)(2,1)} %param.10), kind=kOutput, calls=%fused_computation.35 | convolution fusion | flops 2147745792 | bytes 8912896 | tf_op jit(solution)/shard_map/dot_general | solution.py:113
  69.2 5.2 %fusion.33 = (f32[512,4]{0,1:T(4,128)S(1)}, bf16[512,1,4,128]{0,3,2,1:T(8,128)(2,1)S(1)}) fusion(bf16[512,1,4,128]{0,3,2,1:T(8,128)(2,1)S(1)} %bitcast.207, f32[512,4]{0,1:T(4,128)S(1)} %bitcast.206, f32[2048,512,4]{1,0,2:T(8,128)S(1)} %copy-done.4, f32[4,512]{1,0:T(4,128)S(1)} %get-tuple-element.24, pred[512,2048]{0,1:T(8,128)(4,1)S(1)} %fusion.20, ...), kind=kOutput, calls=%fused_computation.41 | convolution fusion | flops 1098381312 | bytes 19423232 | tf_op jit(solution)/shard_map/cgqk,kcd->qcgd/dot_general | solution.py:83
  74.4 4.4 %convolution_convert_fusion = bf16[512,4096]{1,0:T(8,128)(2,1)} fusion(bf16[512,512]{0,1:T(8,128)(2,1)S(1)} %bitcast.204, bf16[512,4096]{1,0:T(8,128)(2,1)S(1)} %copy-done.8), kind=kOutput, calls=%fused_computation.20 | convolution fusion | flops 2149580800 | bytes 8912896 | tf_op jit(solution)/shard_map/dot_general | solution.py:102
  79.1 10.0 %fusion.11 = bf16[4,512,2048]{1,2,0:T(8,128)(2,1)S(1)} fusion(f32[2048,512,4]{1,0,2:T(8,128)} %copy-done.3, f32[4,512]{1,0:T(4,128)S(1)} %bitcast.210, f32[4,512]{1,0:T(4,128)S(1)} %log_add_fusion, pred[512,2048]{0,1:T(8,128)(4,1)S(1)} %fusion.20, bf16[512,4,128]{0,2,1:T(8,128)(2,1)} %bitcast.208, bf16[512,128]{0,1:T(8,128)(2,1)S(1)} %copy.28, ...), kind=kOutput, calls=%fused_computation.15 | convolution fusion | flops 1105199104 | bytes 27279360 | tf_op jit(solution)/shard_map/qcgd,kcd->cgqk/dot_general | solution.py:127
  89.2 3.3 %copy-done.1 = bf16[4,512,2048]{1,2,0:T(8,128)(2,1)} copy-done((bf16[4,512,2048]{1,2,0:T(8,128)(2,1)}, bf16[4,512,2048]{1,2,0:T(8,128)(2,1)S(1)}, u32[]{:S(2)}) %copy-start.1) | copy-done | bytes 8388632
  95.6 3.6 %collective-permute-start.9 = (bf16[512,128]{1,0:T(8,128)(2,1)}, bf16[512,128]{1,0:T(8,128)(2,1)}, u32[]{:S(2)}, u32[]{:S(2)}) collective-permute-start(bf16[512,128]{1,0:T(8,128)(2,1)} %get-tuple-element.21), channel_id=1, source_target_pairs={{4,0},{8,4},{12,8},{16,12},{20,16},{24,20},{28,24},{32,28},{36,32}... | collective-permute-start | bytes 393224 | tf_op jit(solution)/shard_map/ppermute | solution.py:26
  99.2 9.4 %fusion.67 = (bf16[2048,1,128]{0,2,1:T(8,128)(2,1)S(1)}, f32[2048,1,128]{0,2,1:T(8,128)}) fusion(bf16[512,4,128]{0,2,1:T(8,128)(2,1)S(1)} %bitcast.209, f32[2048,512,4]{1,0,2:T(8,128)} %copy-done.3, f32[4,512]{1,0:T(4,128)S(1)} %log_add_fusion, pred[512,2048]{0,1:T(8,128)(4,1)S(1)} %fusion.20), kind=kOutput, calls=%fused_computation.100 | convolution fusion | flops 1090781184 | bytes 19931136 | tf_op jit(solution)/shard_map/cgqk,qcgd->kcd/dot_general | solution.py:137
  112.5 25.4 %reduce-scatter.6.cloned.1.call-done = bf16[512,512]{1,0:T(8,128)(2,1)} async-done(((bf16[512,4096]{1,0:T(8,128)(2,1)}), bf16[512,512]{1,0:T(8,128)(2,1)}) %reduce-scatter.6.cloned.1.call-update) | async-done | bytes 524304 | tf_op jit(solution)/shard_map/reduce_scatter | solution.py:107
  140.1 4.7 %fusion.18 = f32[4,128,4096]{2,1,0:T(8,128)S(1)} fusion(bf16[512,4096]{1,0:T(8,128)(2,1)} %param.10, bf16[4,128,512]{1,0,2:T(4,128)(2,1)S(1)} %convert_element_type.141), kind=kOutput, calls=%fused_computation.21 | convolution fusion | flops 2147483648 | bytes 13107200 | tf_op jit(solution)/shard_map/dot_general | solution.py:90
  144.8 3.3 %copy-done.2 = f32[4,128,4096]{2,1,0:T(8,128)} copy-done((f32[4,128,4096]{2,1,0:T(8,128)}, f32[4,128,4096]{2,1,0:T(8,128)S(1)}, u32[]{:S(2)}) %copy-start.2) | copy-done | bytes 8388632
  160.0 4.7 %convolution_convert_fusion.2 = bf16[128,4,512]{2,0,1:T(8,128)(2,1)S(1)} fusion(bf16[4,512,2048]{1,2,0:T(8,128)(2,1)} %copy-done.1, bf16[512,128]{1,0:T(8,128)(2,1)S(1)} %copy-done.5, bf16[512,128]{1,0:T(8,128)(2,1)S(1)} %collective-permute-done.5, bf16[512,128]{1,0:T(8,128)(2,1)S(1)} %collective-permute-done.4, bf16[512,128]{1,0:T(8,128)(2,1)S(1)} %collective-permute-done.3), kind=kOutput, calls=%fused_computation.36 | convolution fusion | flops 1076101120 | bytes 9437184 | tf_op jit(solution)/shard_map/cgqk,kcd->qcgd/dot_general | solution.py:131
  165.7 5.7 %collective-permute-start.11 = (bf16[512,128]{1,0:T(8,128)(2,1)S(1)}, bf16[512,128]{1,0:T(8,128)(2,1)S(1)}, u32[]{:S(2)}, u32[]{:S(2)}) collective-permute-start(bf16[512,128]{1,0:T(8,128)(2,1)S(1)} %copy-done.7), channel_id=1, source_target_pairs={{12,0},{16,4},{20,8},{24,12},{28,16},{32,20},{36,24},{40,28},{44,3... | collective-permute-start | bytes 393224 | tf_op jit(solution)/shard_map/ppermute | solution.py:26
  182.2 25.9 %collective-permute-done.7 = bf16[128,4096]{1,0:T(8,128)(2,1)} collective-permute-done((bf16[128,4096]{1,0:T(8,128)(2,1)}, bf16[128,4096]{1,0:T(8,128)(2,1)}, u32[]{:S(2)}, u32[]{:S(2)}) %collective-permute-start.7) | collective-permute-done | bytes 1048608 | tf_op jit(solution)/shard_map/ppermute | solution.py:31
  208.1 4.1 %fusion.26 = bf16[128,4096]{1,0:T(8,128)(2,1)} fusion(bf16[128,4096]{1,0:T(8,128)(2,1)} %collective-permute-done.8, bf16[128,4096]{1,0:T(8,128)(2,1)} %collective-permute-done.7, bf16[128,4096]{1,0:T(8,128)(2,1)} %collective-permute-done.6, f32[4,128,4096]{2,1,0:T(8,128)} %copy-done.2, s32[]{:T(128)S(6)} %select_n.79), kind=kLoop, calls=%fused_computation.30 | loop fusion | flops 3670016 | bytes 6291460 | tf_op jit(solution)/shard_map/convert_element_type | solution.py:100
  (76 shorter events, 43.9 us)
Async XLA Ops:
  7.2 30.1 %copy-start = (bf16[512,512]{1,0:T(8,128)(2,1)S(1)}, bf16[512,512]{1,0:T(8,128)(2,1)}, u32[]{:S(2)}) copy-start(bf16[512,512]{1,0:T(8,128)(2,1)} %param.7) | copy-start | bytes 1572868
  7.2 53.6 %all-gather.2.cloned.1.call-start = ((), (), s32[]{:S(2)}) async-start(), calls=%async_computation.3 | async-start | bytes 5242880 | tf_op jit(solution)/shard_map/all_gather | solution.py:48
  7.9 129.9 %reduce-scatter.6.cloned.1.call-start = ((), (), s32[]{:S(2)}) async-start(), calls=%async_computation.4 | async-start | bytes 4718592 | tf_op jit(solution)/shard_map/reduce_scatter | solution.py:107
  9.0 57.8 %collective-permute-start.2 = (bf16[512,128]{0,1:T(8,128)(2,1)S(1)}, bf16[512,128]{0,1:T(8,128)(2,1)S(1)}, u32[]{:S(2)}, u32[]{:S(2)}) collective-permute-start(bf16[512,128]{0,1:T(8,128)(2,1)S(1)} %copy.28), channel_id=1, source_target_pairs={{0,4},{4,8},{8,12},{12,16},{16,20},{20,24},{24,28},{28,32},{32,36}... | collective-permute-start | bytes 393224 | tf_op jit(solution)/shard_map/ppermute | solution.py:21
  12.5 54.3 %collective-permute-start.1 = (bf16[512,128]{0,1:T(8,128)(2,1)S(1)}, bf16[512,128]{0,1:T(8,128)(2,1)S(1)}, u32[]{:S(2)}, u32[]{:S(2)}) collective-permute-start(bf16[512,128]{0,1:T(8,128)(2,1)S(1)} %copy.28), channel_id=1, source_target_pairs={{0,8},{4,12},{8,16},{12,20},{16,24},{20,28},{24,32},{28,36},{32,40... | collective-permute-start | bytes 393224 | tf_op jit(solution)/shard_map/ppermute | solution.py:21
  15.9 17.8 %collective-permute-start.4 = (bf16[512,128]{1,0:T(8,128)(2,1)}, bf16[512,128]{1,0:T(8,128)(2,1)S(1)}, u32[]{:S(2)}, u32[]{:S(2)}) collective-permute-start(bf16[512,128]{1,0:T(8,128)(2,1)} %param.8), channel_id=1, source_target_pairs={{0,8},{4,12},{8,16},{12,20},{16,24},{20,28},{24,32},{28,36},{32,40... | collective-permute-start | bytes 393224 | tf_op jit(solution)/shard_map/ppermute | solution.py:21
  19.3 18.0 %collective-permute-start.3 = (bf16[512,128]{1,0:T(8,128)(2,1)}, bf16[512,128]{1,0:T(8,128)(2,1)S(1)}, u32[]{:S(2)}, u32[]{:S(2)}) collective-permute-start(bf16[512,128]{1,0:T(8,128)(2,1)} %param.8), channel_id=1, source_target_pairs={{0,12},{4,16},{8,20},{12,24},{16,28},{20,32},{24,36},{28,40},{32,4... | collective-permute-start | bytes 393224 | tf_op jit(solution)/shard_map/ppermute | solution.py:21
  24.8 12.5 %collective-permute-start.5 = (bf16[512,128]{1,0:T(8,128)(2,1)}, bf16[512,128]{1,0:T(8,128)(2,1)S(1)}, u32[]{:S(2)}, u32[]{:S(2)}) collective-permute-start(bf16[512,128]{1,0:T(8,128)(2,1)} %param.8), channel_id=1, source_target_pairs={{0,4},{4,8},{8,12},{12,16},{16,20},{20,24},{24,28},{28,32},{32,36}... | collective-permute-start | bytes 393224 | tf_op jit(solution)/shard_map/ppermute | solution.py:21
  33.6 33.1 %collective-permute-start = (bf16[512,128]{0,1:T(8,128)(2,1)S(1)}, bf16[512,128]{0,1:T(8,128)(2,1)S(1)}, u32[]{:S(2)}, u32[]{:S(2)}) collective-permute-start(bf16[512,128]{0,1:T(8,128)(2,1)S(1)} %copy.28), channel_id=1, source_target_pairs={{0,12},{4,16},{8,20},{12,24},{16,28},{20,32},{24,36},{28,40},{32,4... | collective-permute-start | bytes 393224 | tf_op jit(solution)/shard_map/ppermute | solution.py:21
  60.7 8.5 %copy-start.4 = (f32[2048,512,4]{1,0,2:T(8,128)S(1)}, f32[2048,512,4]{1,0,2:T(8,128)}, u32[]{:S(2)}) copy-start(f32[2048,512,4]{1,0,2:T(8,128)} %copy-done.3) | copy-start | bytes 50331652
  78.9 101.1 %reduce-scatter.8.cloned.1.call-start = ((), (), s32[]{:S(2)}) async-start(), calls=%async_computation.5 | async-start | bytes 1310720 | tf_op jit(solution)/shard_map/reduce_scatter | solution.py:107
  95.6 60.6 %collective-permute-start.9 = (bf16[512,128]{1,0:T(8,128)(2,1)}, bf16[512,128]{1,0:T(8,128)(2,1)}, u32[]{:S(2)}, u32[]{:S(2)}) collective-permute-start(bf16[512,128]{1,0:T(8,128)(2,1)} %get-tuple-element.21), channel_id=1, source_target_pairs={{4,0},{8,4},{12,8},{16,12},{20,16},{24,20},{28,24},{32,28},{36,32}... | collective-permute-start | bytes 393224 | tf_op jit(solution)/shard_map/ppermute | solution.py:26
  109.4 48.7 %collective-permute-start.12 = (bf16[512,128]{0,1:T(8,128)(2,1)S(1)}, bf16[512,128]{0,1:T(8,128)(2,1)S(1)}, u32[]{:S(2)}, u32[]{:S(2)}) collective-permute-start(bf16[512,128]{0,1:T(8,128)(2,1)S(1)} %get-tuple-element.18), channel_id=1, source_target_pairs={{4,0},{8,4},{12,8},{16,12},{20,16},{24,20},{28,24},{32,28},{36,32}... | collective-permute-start | bytes 393224 | tf_op jit(solution)/shard_map/ppermute | solution.py:26
  140.0 20.0 %copy-start.5 = (bf16[512,128]{1,0:T(8,128)(2,1)S(1)}, bf16[512,128]{1,0:T(8,128)(2,1)}, u32[]{:S(2)}) copy-start(bf16[512,128]{1,0:T(8,128)(2,1)} %param.8) | copy-start | bytes 393220
  140.0 72.1 %reduce-scatter.10.cloned.1.call-start = ((), (), s32[]{:S(2)}) async-start(), calls=%async_computation.6 | async-start | bytes 393216
  148.0 17.7 %copy-start.7 = (bf16[512,128]{1,0:T(8,128)(2,1)S(1)}, bf16[512,128]{1,0:T(8,128)(2,1)}, u32[]{:S(2)}) copy-start(bf16[512,128]{1,0:T(8,128)(2,1)} %get-tuple-element.22) | copy-start | bytes 393220
  148.0 23.4 %copy-start.6 = (bf16[512,128]{1,0:T(8,128)(2,1)S(1)}, bf16[512,128]{1,0:T(8,128)(2,1)}, u32[]{:S(2)}) copy-start(bf16[512,128]{1,0:T(8,128)(2,1)} %get-tuple-element.23) | copy-start | bytes 393220
  149.9 31.9 %collective-permute-start.6 = (bf16[128,4096]{1,0:T(8,128)(2,1)}, bf16[128,4096]{1,0:T(8,128)(2,1)}, u32[]{:S(2)}, u32[]{:S(2)}) collective-permute-start(bf16[128,4096]{1,0:T(8,128)(2,1)} %get-tuple-element.15), channel_id=1, source_target_pairs={{3,0},{0,1},{1,2},{2,3},{7,4},{4,5},{5,6},{6,7},{11,8},{8,9},{9,10... | collective-permute-start | bytes 3145736 | tf_op jit(solution)/shard_map/ppermute | solution.py:31
  149.9 32.3 %collective-permute-start.8 = (bf16[128,4096]{1,0:T(8,128)(2,1)}, bf16[128,4096]{1,0:T(8,128)(2,1)}, u32[]{:S(2)}, u32[]{:S(2)}) collective-permute-start(bf16[128,4096]{1,0:T(8,128)(2,1)} %get-tuple-element.16), channel_id=1, source_target_pairs={{1,0},{2,1},{3,2},{0,3},{5,4},{6,5},{7,6},{4,7},{9,8},{10,9},{11,1... | collective-permute-start | bytes 3145736 | tf_op jit(solution)/shard_map/ppermute | solution.py:31
  153.1 54.9 %collective-permute-start.7 = (bf16[128,4096]{1,0:T(8,128)(2,1)}, bf16[128,4096]{1,0:T(8,128)(2,1)}, u32[]{:S(2)}, u32[]{:S(2)}) collective-permute-start(bf16[128,4096]{1,0:T(8,128)(2,1)} %get-tuple-element.17), channel_id=1, source_target_pairs={{2,0},{3,1},{0,2},{1,3},{6,4},{7,5},{4,6},{5,7},{10,8},{11,9},{8,1... | collective-permute-start | bytes 3145736 | tf_op jit(solution)/shard_map/ppermute | solution.py:31
  156.1 9.6 %collective-permute-start.14 = (bf16[512,128]{0,1:T(8,128)(2,1)}, bf16[512,128]{0,1:T(8,128)(2,1)S(1)}, u32[]{:S(2)}, u32[]{:S(2)}) collective-permute-start(bf16[512,128]{0,1:T(8,128)(2,1)} %get-tuple-element.19), channel_id=1, source_target_pairs={{12,0},{16,4},{20,8},{24,12},{28,16},{32,20},{36,24},{40,28},{44,3... | collective-permute-start | bytes 393224 | tf_op jit(solution)/shard_map/ppermute | solution.py:26
  158.1 13.4 %collective-permute-start.13 = (bf16[512,128]{0,1:T(8,128)(2,1)}, bf16[512,128]{0,1:T(8,128)(2,1)S(1)}, u32[]{:S(2)}, u32[]{:S(2)}) collective-permute-start(bf16[512,128]{0,1:T(8,128)(2,1)} %get-tuple-element.20), channel_id=1, source_target_pairs={{8,0},{12,4},{16,8},{20,12},{24,16},{28,20},{32,24},{36,28},{40,32... | collective-permute-start | bytes 393224 | tf_op jit(solution)/shard_map/ppermute | solution.py:26
  165.7 10.1 %collective-permute-start.11 = (bf16[512,128]{1,0:T(8,128)(2,1)S(1)}, bf16[512,128]{1,0:T(8,128)(2,1)S(1)}, u32[]{:S(2)}, u32[]{:S(2)}) collective-permute-start(bf16[512,128]{1,0:T(8,128)(2,1)S(1)} %copy-done.7), channel_id=1, source_target_pairs={{12,0},{16,4},{20,8},{24,12},{28,16},{32,20},{36,24},{40,28},{44,3... | collective-permute-start | bytes 393224 | tf_op jit(solution)/shard_map/ppermute | solution.py:26
  171.5 6.9 %collective-permute-start.10 = (bf16[512,128]{1,0:T(8,128)(2,1)S(1)}, bf16[512,128]{1,0:T(8,128)(2,1)S(1)}, u32[]{:S(2)}, u32[]{:S(2)}) collective-permute-start(bf16[512,128]{1,0:T(8,128)(2,1)S(1)} %copy-done.6), channel_id=1, source_target_pairs={{8,0},{12,4},{16,8},{20,12},{24,16},{28,20},{32,24},{36,28},{40,32... | collective-permute-start | bytes 393224 | tf_op jit(solution)/shard_map/ppermute | solution.py:26
  (7 other events, 39.6 us)
Sparse Core Ops, SparseCore 0:
  9.8 50.9 all-gather.1
  79.0 58.7 reduce-scatter.5
  140.4 25.0 reduce-scatter.7
  181.9 18.7 reduce-scatter.9

commit v2 on v1

--- a/solution.py
+++ b/solution.py
@@ -47,12 +47,11 @@
 
     grad_piece = lax.all_gather(out_grad, TP, axis=0, tiled=True)
 
-    earlier = [
-        from_earlier((key_rows, value_rows), distance, ctx_count)
-        for distance in range(REACH, 0, -1)
-    ]
-    keys_all = jnp.concatenate([pair[0] for pair in earlier] + [key_rows], axis=0)
-    values_all = jnp.concatenate([pair[1] for pair in earlier] + [value_rows], axis=0)
+    own_pair = jnp.concatenate([key_rows, value_rows], axis=1)
+    earlier = [from_earlier(own_pair, distance, ctx_count) for distance in range(REACH, 0, -1)]
+    pairs_all = jnp.concatenate(earlier + [own_pair], axis=0)
+    keys_all = pairs_all[:, :kv_width]
+    values_all = pairs_all[:, kv_width:]
     key_heads = keys_all.reshape(key_count, kv_here, HEAD_DIM)
     value_heads = values_all.reshape(key_count, kv_here, HEAD_DIM)
 
@@ -102,11 +101,12 @@
     weight_part = lax.dot_general(
         attn, grad_piece, (((0,), (0,)), ((), ())), preferred_element_type=jnp.float32
     )
-    weight_sum = weight_part.astype(jnp.bfloat16)
-    for stage, (name, _) in enumerate(CTX_PARTS):
-        weight_sum = lax.psum_scatter(weight_sum, name, scatter_dimension=1, tiled=True)
-        if stage == 0:
-            weight_sum = weight_sum.astype(jnp.float32)
+    weight_sum = lax.psum_scatter(
+        weight_part.astype(jnp.bfloat16), CTX[0], scatter_dimension=1, tiled=True
+    )
+    weight_sum = lax.psum_scatter(
+        weight_sum.astype(jnp.float32), CTX[1:], scatter_dimension=1, tiled=True
+    )
     seq_total = ctx_count * tokens_here
     grad_weight = weight_sum * seq_total ** (-0.5)
 
@@ -138,20 +138,16 @@
         "cgqk,qcgd->kcd", probs.astype(jnp.bfloat16), grad_four, preferred_element_type=jnp.float32
     ).reshape(key_count, kv_width)
 
-    key_grad = key_grad_all[span:]
-    value_grad = value_grad_all[span:]
+    pair_grad_all = jnp.concatenate([key_grad_all, value_grad_all], axis=1)
+    pair_grad = pair_grad_all[span:]
     for distance in range(1, REACH + 1):
         lo = span - distance * tokens_here
         sent = to_earlier(
-            (
-                key_grad_all[lo : lo + tokens_here].astype(jnp.bfloat16),
-                value_grad_all[lo : lo + tokens_here].astype(jnp.bfloat16),
-            ),
-            distance,
-            ctx_count,
+            pair_grad_all[lo : lo + tokens_here].astype(jnp.bfloat16), distance, ctx_count
         )
-        key_grad = key_grad + sent[0].astype(jnp.float32)
-        value_grad = value_grad + sent[1].astype(jnp.float32)
+        pair_grad = pair_grad + sent.astype(jnp.float32)
+    key_grad = pair_grad[:, :kv_width]
+    value_grad = pair_grad[:, kv_width:]
 
     grad_queries = query_grad.reshape(tokens_here, -1).astype(jnp.bfloat16)
     grad_keys = key_grad.astype(jnp.bfloat16)

time: 221 us -> 231 us (1.045)
  waiting for transfers between devices: 64.5 us -> 100 us
  starting transfers between devices: 48.6 us -> 23.3 us
  local copies, waits for them, and re-layouts: 27 us -> 31.2 us
  other arithmetic: 15.4 us -> 11.9 us
    ppermute x3, waiting for transfers between devices: 26.3 us -> 52.7 us  [rotated(): return lax.ppermute(block, TP, route)]
    ppermute x6 -> x3, starting transfers between devices: 18.7 us -> 5.96 us  [to_earlier(): return lax.ppermute(block, CTX, route)]
    ppermute x6 -> x3, starting transfers between devices: 23.5 us -> 10.8 us  [from_earlier(): return lax.ppermute(block, CTX, route)]
    ppermute x6 -> x3, waiting for transfers between devices: 0.02 us -> 8.09 us  [from_earlier(): return lax.ppermute(block, CTX, route)]
    convert_element_type x3 -> x0, other arithmetic: 4.81 us -> none  [the longest x1 2.17 us: on_device(): weight_sum = weight_sum.astype(jnp.float32)]
    convert_element_type x1, local copies, waits for them, and re-layouts: 1.86 us -> 4.68 us  [on_device(): chunk.astype(jnp.bfloat16)]
    unnamed x30 -> x31, local copies, waits for them, and re-layouts: 21.1 us -> 19.8 us
    reduce_scatter x2 -> x1, waiting for transfers between devices: 25.4 us -> 25.3 us  [on_device(): lax.psum_scatter(weight_part.astype(jnp.bfloat16), CTX[0], scatter_dimens...]
  transfers between devices with their start and end apart: 19 -> 12, of which waited for: 5 -> 9; matrix products, arithmetic and copies ran while one was open for 30% -> 28% of each run, Pallas kernels for 0% -> 0%
where the time goes in v2:
time: 231 us; the launch traced here: 230 us
  waiting for transfers between devices  100 us (43%)
  matrix products  49.5 us (21%)
  local copies, waits for them, and re-layouts  31.2 us (14%)
  starting transfers between devices  23.3 us (10%)
  between operations  14.1 us (6%)
  other arithmetic  11.9 us (5%)
    ppermute x3, waiting for transfers between devices, rotated(): return lax.ppermute(block, TP, route)  52.7 us
    reduce_scatter x1, waiting for transfers between devices, on_device(): lax.psum_scatter(weight_part.astype(jnp.bfloat16), CTX[0], scatter_dimens...  25.3 us
    unnamed x31, local copies, waits for them, and re-layouts  19.8 us
    ppermute x3, starting transfers between devices, from_earlier(): return lax.ppermute(block, CTX, route)  10.8 us
    dot_general x1, matrix products, on_device(): jnp.einsum('qcgd,kcd->cgqk', grad_four, value_heads, preferred_element_ty...  9.58 us
    all_gather x1, waiting for transfers between devices, on_device(): grad_piece = lax.all_gather(out_grad, TP, axis=0, tiled=True)  8.84 us
    dot_general x1, matrix products, on_device(): jnp.einsum('cgqk,qcgd->kcd', probs.astype(jnp.bfloat16), grad_four, prefe...  8.57 us
    ppermute x3, waiting for transfers between devices, from_earlier(): return lax.ppermute(block, CTX, route)  8.09 us
  transfers between devices with their start and end apart: 12, of which 9 were waited for; matrix products, arithmetic and copies ran while one was open for 28% of the time, Pallas kernels for 0%

profile of v2, /device:TPU:96, one launch (start us, length us, event | category | flops | bytes accessed | tf_op | source)
XLA Modules:
  0.0 230.2 jit_solution(4342639491603659621)
XLA Ops:
  9.8 3.5 %collective-permute-start.2 = (bf16[512,256]{1,0:T(8,128)(2,1)S(1)}, bf16[512,256]{1,0:T(8,128)(2,1)S(1)}, u32[]{:S(2)}, u32[]{:S(2)}) collective-permute-start(bf16[512,256]{1,0:T(8,128)(2,1)S(1)} %constant_dynamic-update-slice_fusion), channel_id=1, source_target_pairs={{0,4},{4,8},{8,12},{12,16},{16,20},{20,24},{24,28},{28,32},{32,36}... | collective-permute-start | bytes 786440 | tf_op jit(solution)/shard_map/ppermute | solution.py:21
  13.3 3.4 %collective-permute-start.1 = (bf16[512,256]{1,0:T(8,128)(2,1)S(1)}, bf16[512,256]{1,0:T(8,128)(2,1)S(1)}, u32[]{:S(2)}, u32[]{:S(2)}) collective-permute-start(bf16[512,256]{1,0:T(8,128)(2,1)S(1)} %constant_dynamic-update-slice_fusion), channel_id=1, source_target_pairs={{0,8},{4,12},{8,16},{12,20},{16,24},{20,28},{24,32},{28,36},{32,40... | collective-permute-start | bytes 786440 | tf_op jit(solution)/shard_map/ppermute | solution.py:21
  16.7 3.9 %collective-permute-start = (bf16[512,256]{1,0:T(8,128)(2,1)S(1)}, bf16[512,256]{1,0:T(8,128)(2,1)}, u32[]{:S(2)}, u32[]{:S(2)}) collective-permute-start(bf16[512,256]{1,0:T(8,128)(2,1)S(1)} %constant_dynamic-update-slice_fusion), channel_id=1, source_target_pairs={{0,12},{4,16},{8,20},{12,24},{16,28},{20,32},{24,36},{28,40},{32,4... | collective-permute-start | bytes 786440 | tf_op jit(solution)/shard_map/ppermute | solution.py:21
  26.5 7.6 %collective-permute-done = bf16[512,256]{1,0:T(8,128)(2,1)} collective-permute-done((bf16[512,256]{1,0:T(8,128)(2,1)S(1)}, bf16[512,256]{1,0:T(8,128)(2,1)}, u32[]{:S(2)}, u32[]{:S(2)}) %collective-permute-start) | collective-permute-done | bytes 262176 | tf_op jit(solution)/shard_map/ppermute | solution.py:21
  35.2 3.2 %fusion.5 = (f32[4,512]{1,0:T(4,128)S(1)}, f32[2048,512,4]{1,0,2:T(8,128)S(1)}) fusion(pred[512,2048]{0,1:T(8,128)(4,1)S(1)} %fusion.20, bf16[512,4,128]{0,2,1:T(8,128)(2,1)S(1)} %bitcast.151, bf16[2048,256]{1,0:T(8,128)(2,1)S(1)} %pad_maximum_fusion.1), kind=kOutput, calls=%fused_computation.9 | convolution fusion | flops 1086322688 | bytes 18882560 | tf_op jit(solution)/shard_map/qcgd,kcd->cgqk/dot_general | solution.py:75
  38.4 5.7 %copy-done.3 = f32[2048,512,4]{1,0,2:T(8,128)} copy-done((f32[2048,512,4]{1,0,2:T(8,128)}, f32[2048,512,4]{1,0,2:T(8,128)S(1)}, u32[]{:S(2)}) %copy-start.3) | copy-done | bytes 16777240
  44.1 4.2 %fusion.7 = f32[4,512]{1,0:T(4,128)S(1)} fusion(f32[2048,512,4]{1,0,2:T(8,128)S(1)} %get-tuple-element.24, f32[4,512]{1,0:T(4,128)S(1)} %get-tuple-element.23, pred[512,2048]{0,1:T(8,128)(4,1)S(1)} %fusion.20), kind=kLoop, calls=%fused_computation.11 | loop fusion | flops 20969472 | bytes 17842176 | tf_op jit(solution)/shard_map/reduce_sum | solution.py:81
  48.2 8.8 %all-gather.2.cloned.1.call-done = bf16[512,4096]{1,0:T(8,128)(2,1)} async-done(((bf16[128,4096]{1,0:T(8,128)(2,1)}), bf16[512,4096]{1,0:T(8,128)(2,1)}) %all-gather.2.cloned.1.call-update) | async-done | bytes 4194320 | tf_op jit(solution)/shard_map/all_gather | solution.py:48
  57.1 6.0 %convolution_convert_fusion.1 = bf16[512,512]{0,1:T(8,128)(2,1)S(1)} fusion(bf16[512,4096]{1,0:T(8,128)(2,1)} %all-gather.2.cloned.1.call-done, bf16[512,4096]{1,0:T(8,128)(2,1)} %param.10), kind=kOutput, calls=%fused_computation.39 | convolution fusion | flops 2147745792 | bytes 8912896 | tf_op jit(solution)/shard_map/dot_general | solution.py:113
  65.5 4.5 %fusion.34 = (f32[512,4]{0,1:T(4,128)S(1)}, bf16[512,1,4,128]{0,3,2,1:T(8,128)(2,1)S(1)}) fusion(bf16[512,1,4,128]{0,3,2,1:T(8,128)(2,1)S(1)} %bitcast.156, f32[512,4]{0,1:T(4,128)S(1)} %bitcast.155, f32[2048,512,4]{1,0,2:T(8,128)S(1)} %copy-done.4, f32[4,512]{1,0:T(4,128)S(1)} %get-tuple-element.23, pred[512,2048]{0,1:T(8,128)(4,1)S(1)} %fusion.20, ...), kind=kOutput, calls=%fused_computation.46 | convolution fusion | flops 1096284160 | bytes 19423232 | tf_op jit(solution)/shard_map/cgqk,kcd->qcgd/dot_general | solution.py:82
  70.8 4.3 %convolution_convert_fusion = bf16[512,4096]{1,0:T(8,128)(2,1)} fusion(bf16[512,512]{0,1:T(8,128)(2,1)S(1)} %bitcast.153, bf16[512,4096]{1,0:T(8,128)(2,1)S(1)} %copy-done.9), kind=kOutput, calls=%fused_computation.20 | convolution fusion | flops 2149580800 | bytes 8912896 | tf_op jit(solution)/shard_map/dot_general | solution.py:101
  77.5 9.6 %fusion.11 = bf16[4,512,2048]{1,2,0:T(8,128)(2,1)S(1)} fusion(f32[2048,512,4]{1,0,2:T(8,128)} %copy-done.3, f32[4,512]{1,0:T(4,128)S(1)} %bitcast.159, f32[4,512]{1,0:T(4,128)S(1)} %log_add_fusion, pred[512,2048]{0,1:T(8,128)(4,1)S(1)} %fusion.20, bf16[512,4,128]{0,2,1:T(8,128)(2,1)} %bitcast.157, bf16[2048,256]{1,0:T(8,128)(2,1)S(1)} %pad_maximum_fusion.1), kind=kOutput, calls=%fused_computation.15 | convolution fusion | flops 1103101952 | bytes 27279360 | tf_op jit(solution)/shard_map/qcgd,kcd->cgqk/dot_general | solution.py:127
  87.1 3.2 %copy-done.2 = bf16[4,512,2048]{1,2,0:T(8,128)(2,1)} copy-done((bf16[4,512,2048]{1,2,0:T(8,128)(2,1)}, bf16[4,512,2048]{1,2,0:T(8,128)(2,1)S(1)}, u32[]{:S(2)}) %copy-start.2) | copy-done | bytes 8388632
  93.1 8.6 %fusion.21 = f32[2048,128]{0,1:T(8,128)S(1)} fusion(bf16[512,4,128]{0,2,1:T(8,128)(2,1)S(1)} %bitcast.158, f32[2048,512,4]{1,0,2:T(8,128)} %copy-done.3, f32[4,512]{1,0:T(4,128)S(1)} %log_add_fusion, pred[512,2048]{0,1:T(8,128)(4,1)S(1)} %fusion.20), kind=kOutput, calls=%fused_computation.29 | convolution fusion | flops 1090519040 | bytes 19406848 | tf_op jit(solution)/shard_map/cgqk,qcgd->kcd/dot_general | solution.py:137
  104.7 5.7 %fusion.18 = f32[4,128,4096]{2,1,0:T(8,128)} fusion(bf16[512,4096]{1,0:T(8,128)(2,1)S(1)} %copy-done.5, bf16[4,128,512]{1,0,2:T(4,128)(2,1)S(1)} %copy-done.7), kind=kOutput, calls=%fused_computation.21 | convolution fusion | flops 2147483648 | bytes 13107200 | tf_op jit(solution)/shard_map/dot_general | solution.py:89
  110.4 25.3 %reduce-scatter.5.cloned.1.call-done = bf16[512,512]{1,0:T(8,128)(2,1)} async-done(((bf16[512,4096]{1,0:T(8,128)(2,1)}), bf16[512,512]{1,0:T(8,128)(2,1)}) %reduce-scatter.5.cloned.1.call-update) | async-done | bytes 524304 | tf_op jit(solution)/shard_map/reduce_scatter | solution.py:104
  138.0 4.7 %fusion.31 = (bf16[128,4096]{1,0:T(8,128)(2,1)}, bf16[128,4096]{1,0:T(8,128)(2,1)}, bf16[128,4096]{1,0:T(8,128)(2,1)}) fusion(f32[4,128,4096]{2,1,0:T(8,128)} %fusion.18, s32[]{:T(128)S(6)} %select_n.81, s32[]{:T(128)S(6)} %select_n.85, s32[]{:T(128)S(6)} %select_n.83), kind=kLoop, calls=%fused_computation.41 | loop fusion | bytes 6291468 | tf_op jit(solution)/shard_map/convert_element_type | solution.py:96
  142.7 3.2 %collective-permute-start.5 = (bf16[128,4096]{1,0:T(8,128)(2,1)}, bf16[128,4096]{1,0:T(8,128)(2,1)}, u32[]{:S(2)}, u32[]{:S(2)}) collective-permute-start(bf16[128,4096]{1,0:T(8,128)(2,1)} %get-tuple-element.16), channel_id=1, source_target_pairs={{1,0},{2,1},{3,2},{0,3},{5,4},{6,5},{7,6},{4,7},{9,8},{10,9},{11,1... | collective-permute-start | bytes 3145736 | tf_op jit(solution)/shard_map/ppermute | solution.py:31
  145.9 3.0 %collective-permute-start.4 = (bf16[128,4096]{1,0:T(8,128)(2,1)}, bf16[128,4096]{1,0:T(8,128)(2,1)}, u32[]{:S(2)}, u32[]{:S(2)}) collective-permute-start(bf16[128,4096]{1,0:T(8,128)(2,1)} %get-tuple-element.17), channel_id=1, source_target_pairs={{2,0},{3,1},{0,2},{1,3},{6,4},{7,5},{4,6},{5,7},{10,8},{11,9},{8,1... | collective-permute-start | bytes 3145736 | tf_op jit(solution)/shard_map/ppermute | solution.py:31
  153.0 4.9 %convolution_convert_fusion.2 = bf16[128,4,512]{2,0,1:T(8,128)(2,1)S(1)} fusion(bf16[4,512,2048]{1,2,0:T(8,128)(2,1)} %copy-done.2, bf16[2048,256]{1,0:T(8,128)(2,1)} %copy-done.6), kind=kOutput, calls=%fused_computation.40 | convolution fusion | flops 1074003968 | bytes 9437184 | tf_op jit(solution)/shard_map/cgqk,kcd->qcgd/dot_general | solution.py:131
  160.4 2.9 %collective-permute-done.7 = bf16[512,256]{0,1:T(8,128)(2,1)S(1)} collective-permute-done((bf16[512,256]{0,1:T(8,128)(2,1)}, bf16[512,256]{0,1:T(8,128)(2,1)S(1)}, u32[]{:S(2)}, u32[]{:S(2)}) %collective-permute-start.7) | collective-permute-done | bytes 262176 | tf_op jit(solution)/shard_map/ppermute | solution.py:26
  165.0 28.0 %collective-permute-done.3 = bf16[128,4096]{1,0:T(8,128)(2,1)} collective-permute-done((bf16[128,4096]{1,0:T(8,128)(2,1)}, bf16[128,4096]{1,0:T(8,128)(2,1)}, u32[]{:S(2)}, u32[]{:S(2)}) %collective-permute-start.3) | collective-permute-done | bytes 1048608 | tf_op jit(solution)/shard_map/ppermute | solution.py:31
  194.0 23.7 %collective-permute-done.4 = bf16[128,4096]{1,0:T(8,128)(2,1)} collective-permute-done((bf16[128,4096]{1,0:T(8,128)(2,1)}, bf16[128,4096]{1,0:T(8,128)(2,1)}, u32[]{:S(2)}, u32[]{:S(2)}) %collective-permute-start.4) | collective-permute-done | bytes 1048608 | tf_op jit(solution)/shard_map/ppermute | solution.py:31
  217.7 4.1 %fusion.27 = bf16[128,4096]{1,0:T(8,128)(2,1)} fusion(bf16[128,4096]{1,0:T(8,128)(2,1)} %collective-permute-done.5, bf16[128,4096]{1,0:T(8,128)(2,1)} %collective-permute-done.4, bf16[128,4096]{1,0:T(8,128)(2,1)} %collective-permute-done.3, f32[4,128,4096]{2,1,0:T(8,128)} %fusion.18, s32[]{:T(128)S(6)} %select_n.79), kind=kLoop, calls=%fused_computation.34 | loop fusion | flops 3670016 | bytes 6291460 | tf_op jit(solution)/shard_map/convert_element_type | solution.py:99
  (64 shorter events, 34.0 us)
Async XLA Ops:
  7.2 14.8 %copy-start = (s32[256]{0:T(256)S(1)}, s32[256]{0:T(256)}, u32[]{:S(2)}) copy-start(s32[256]{0:T(256)} %param.13) | copy-start | bytes 3076
  7.2 49.9 %all-gather.2.cloned.1.call-start = ((), (), s32[]{:S(2)}) async-start(), calls=%async_computation.2 | async-start | bytes 5242880 | tf_op jit(solution)/shard_map/all_gather | solution.py:48
  7.9 127.8 %reduce-scatter.5.cloned.1.call-start = ((), (), s32[]{:S(2)}) async-start(), calls=%async_computation.3 | async-start | bytes 4718592 | tf_op jit(solution)/shard_map/reduce_scatter | solution.py:104
  9.8 16.2 %collective-permute-start.2 = (bf16[512,256]{1,0:T(8,128)(2,1)S(1)}, bf16[512,256]{1,0:T(8,128)(2,1)S(1)}, u32[]{:S(2)}, u32[]{:S(2)}) collective-permute-start(bf16[512,256]{1,0:T(8,128)(2,1)S(1)} %constant_dynamic-update-slice_fusion), channel_id=1, source_target_pairs={{0,4},{4,8},{8,12},{12,16},{16,20},{20,24},{24,28},{28,32},{32,36}... | collective-permute-start | bytes 786440 | tf_op jit(solution)/shard_map/ppermute | solution.py:21
  13.3 13.2 %collective-permute-start.1 = (bf16[512,256]{1,0:T(8,128)(2,1)S(1)}, bf16[512,256]{1,0:T(8,128)(2,1)S(1)}, u32[]{:S(2)}, u32[]{:S(2)}) collective-permute-start(bf16[512,256]{1,0:T(8,128)(2,1)S(1)} %constant_dynamic-update-slice_fusion), channel_id=1, source_target_pairs={{0,8},{4,12},{8,16},{12,20},{16,24},{20,28},{24,32},{28,36},{32,40... | collective-permute-start | bytes 786440 | tf_op jit(solution)/shard_map/ppermute | solution.py:21
  16.7 17.4 %collective-permute-start = (bf16[512,256]{1,0:T(8,128)(2,1)S(1)}, bf16[512,256]{1,0:T(8,128)(2,1)}, u32[]{:S(2)}, u32[]{:S(2)}) collective-permute-start(bf16[512,256]{1,0:T(8,128)(2,1)S(1)} %constant_dynamic-update-slice_fusion), channel_id=1, source_target_pairs={{0,12},{4,16},{8,20},{12,24},{16,28},{20,32},{24,36},{28,40},{32,4... | collective-permute-start | bytes 786440 | tf_op jit(solution)/shard_map/ppermute | solution.py:21
  35.1 42.3 %copy-start.6 = (bf16[2048,256]{1,0:T(8,128)(2,1)}, bf16[2048,256]{1,0:T(8,128)(2,1)S(1)}, u32[]{:S(2)}) copy-start(bf16[2048,256]{1,0:T(8,128)(2,1)S(1)} %pad_maximum_fusion.1) | copy-start | bytes 3145732
  38.4 5.7 %copy-start.3 = (f32[2048,512,4]{1,0,2:T(8,128)}, f32[2048,512,4]{1,0,2:T(8,128)S(1)}, u32[]{:S(2)}) copy-start(f32[2048,512,4]{1,0,2:T(8,128)S(1)} %get-tuple-element.24) | copy-start | bytes 50331652
  57.1 8.4 %copy-start.4 = (f32[2048,512,4]{1,0,2:T(8,128)S(1)}, f32[2048,512,4]{1,0,2:T(8,128)}, u32[]{:S(2)}) copy-start(f32[2048,512,4]{1,0,2:T(8,128)} %copy-done.3) | copy-start | bytes 50331652
  63.0 7.0 %copy-start.10 = (bf16[512,512]{0,1:T(8,128)(2,1)}, bf16[512,512]{0,1:T(8,128)(2,1)S(1)}, u32[]{:S(2)}) copy-start(bf16[512,512]{0,1:T(8,128)(2,1)S(1)} %convolution_convert_fusion.1) | copy-start | bytes 1572868
  65.5 5.3 %copy-start.9 = (bf16[512,4096]{1,0:T(8,128)(2,1)S(1)}, bf16[512,4096]{1,0:T(8,128)(2,1)}, u32[]{:S(2)}) copy-start(bf16[512,4096]{1,0:T(8,128)(2,1)} %all-gather.2.cloned.1.call-done) | copy-start | bytes 12582916
  70.0 0.8 copy-start.8
  75.2 146.6 %reduce-scatter.7.cloned.1.call-start = ((), (), s32[]{:S(2)}) async-start(), calls=%async_computation.4 | async-start | bytes 1179648
  87.0 3.3 %copy-start.2 = (bf16[4,512,2048]{1,2,0:T(8,128)(2,1)}, bf16[4,512,2048]{1,2,0:T(8,128)(2,1)S(1)}, u32[]{:S(2)}) copy-start(bf16[4,512,2048]{1,2,0:T(8,128)(2,1)S(1)} %fusion.11) | copy-start | bytes 25165828
  90.3 2.8 %copy-start.11 = (bf16[512,512]{0,1:T(8,128)(2,1)S(1)}, bf16[512,512]{0,1:T(8,128)(2,1)}, u32[]{:S(2)}) copy-start(bf16[512,512]{0,1:T(8,128)(2,1)} %copy-done.10) | copy-start | bytes 1572868
  93.1 11.5 %copy-start.5 = (bf16[512,4096]{1,0:T(8,128)(2,1)S(1)}, bf16[512,4096]{1,0:T(8,128)(2,1)}, u32[]{:S(2)}) copy-start(bf16[512,4096]{1,0:T(8,128)(2,1)} %param.10) | copy-start | bytes 12582916
  93.1 11.5 %copy-start.7 = (bf16[4,128,512]{1,0,2:T(4,128)(2,1)S(1)}, bf16[4,128,512]{1,0,2:T(4,128)(2,1)}, u32[]{:S(2)}) copy-start(bf16[4,128,512]{1,0,2:T(4,128)(2,1)} %convert_element_type.107) | copy-start | bytes 1572868
  102.7 48.1 %collective-permute-start.6 = (bf16[512,256]{0,1:T(8,128)(2,1)S(1)}, bf16[512,256]{0,1:T(8,128)(2,1)S(1)}, u32[]{:S(2)}, u32[]{:S(2)}) collective-permute-start(bf16[512,256]{0,1:T(8,128)(2,1)S(1)} %get-tuple-element.18), channel_id=1, source_target_pairs={{4,0},{8,4},{12,8},{16,12},{20,16},{24,20},{28,24},{32,28},{36,32}... | collective-permute-start | bytes 786440 | tf_op jit(solution)/shard_map/ppermute | solution.py:26
  142.7 50.3 %collective-permute-start.3 = (bf16[128,4096]{1,0:T(8,128)(2,1)}, bf16[128,4096]{1,0:T(8,128)(2,1)}, u32[]{:S(2)}, u32[]{:S(2)}) collective-permute-start(bf16[128,4096]{1,0:T(8,128)(2,1)} %get-tuple-element.15), channel_id=1, source_target_pairs={{3,0},{0,1},{1,2},{2,3},{7,4},{4,5},{5,6},{6,7},{11,8},{8,9},{9,10... | collective-permute-start | bytes 3145736 | tf_op jit(solution)/shard_map/ppermute | solution.py:31
  142.7 51.3 %collective-permute-start.5 = (bf16[128,4096]{1,0:T(8,128)(2,1)}, bf16[128,4096]{1,0:T(8,128)(2,1)}, u32[]{:S(2)}, u32[]{:S(2)}) collective-permute-start(bf16[128,4096]{1,0:T(8,128)(2,1)} %get-tuple-element.16), channel_id=1, source_target_pairs={{1,0},{2,1},{3,2},{0,3},{5,4},{6,5},{7,6},{4,7},{9,8},{10,9},{11,1... | collective-permute-start | bytes 3145736 | tf_op jit(solution)/shard_map/ppermute | solution.py:31
  145.9 71.8 %collective-permute-start.4 = (bf16[128,4096]{1,0:T(8,128)(2,1)}, bf16[128,4096]{1,0:T(8,128)(2,1)}, u32[]{:S(2)}, u32[]{:S(2)}) collective-permute-start(bf16[128,4096]{1,0:T(8,128)(2,1)} %get-tuple-element.17), channel_id=1, source_target_pairs={{2,0},{3,1},{0,2},{1,3},{6,4},{7,5},{4,6},{5,7},{10,8},{11,9},{8,1... | collective-permute-start | bytes 3145736 | tf_op jit(solution)/shard_map/ppermute | solution.py:31
  149.0 11.5 %collective-permute-start.8 = (bf16[512,256]{0,1:T(8,128)(2,1)}, bf16[512,256]{0,1:T(8,128)(2,1)S(1)}, u32[]{:S(2)}, u32[]{:S(2)}) collective-permute-start(bf16[512,256]{0,1:T(8,128)(2,1)} %get-tuple-element.19), channel_id=1, source_target_pairs={{12,0},{16,4},{20,8},{24,12},{28,16},{32,20},{36,24},{40,28},{44,3... | collective-permute-start | bytes 786440 | tf_op jit(solution)/shard_map/ppermute | solution.py:26
  150.9 12.5 %collective-permute-start.7 = (bf16[512,256]{0,1:T(8,128)(2,1)}, bf16[512,256]{0,1:T(8,128)(2,1)S(1)}, u32[]{:S(2)}, u32[]{:S(2)}) collective-permute-start(bf16[512,256]{0,1:T(8,128)(2,1)} %get-tuple-element.20), channel_id=1, source_target_pairs={{8,0},{12,4},{16,8},{20,12},{24,16},{28,20},{32,24},{36,28},{40,32... | collective-permute-start | bytes 786440 | tf_op jit(solution)/shard_map/ppermute | solution.py:26
  153.0 70.6 %copy-start.1 = (s32[256]{0:T(256)S(1)}, s32[256]{0:T(256)}, u32[]{:S(2)}) copy-start(s32[256]{0:T(256)} %param.13) | copy-start | bytes 3076
Sparse Core Ops, SparseCore 0:
  9.8 47.2 all-gather.1
  75.3 60.3 reduce-scatter.4
  138.2 49.4 reduce-scatter.6

commit v3 on v2

--- a/solution.py
+++ b/solution.py
@@ -26,9 +26,34 @@
     return lax.ppermute(block, CTX, route)
 
 
-def rotated(block, distance, count):
-    route = [((i - distance) % count, i) for i in range(count)]
-    return lax.ppermute(block, TP, route)
+def swapped(block, axis):
+    return lax.ppermute(block, axis, [(0, 1), (1, 0)])
+
+
+def in_order(own, other, place):
+    first = jnp.where(place == 0, own, other)
+    second = jnp.where(place == 0, other, own)
+    return jnp.stack([first, second])
+
+
+def gathered_over_tp(piece):
+    high = lax.axis_index(TP[0])
+    low = lax.axis_index(TP[1])
+    by_high = in_order(piece, swapped(piece, TP[0]), high)
+    both = in_order(by_high, swapped(by_high, TP[1]), low)
+    return jnp.transpose(both, (1, 0, 2, 3)).reshape(-1, piece.shape[1])
+
+
+def summed_over_tp(part):
+    high = lax.axis_index(TP[0])
+    low = lax.axis_index(TP[1])
+    quarters = part.reshape(2, 2, part.shape[0] // 4, part.shape[1])
+    kept = lax.dynamic_index_in_dim(quarters, low, 1, keepdims=False)
+    given = lax.dynamic_index_in_dim(quarters, 1 - low, 1, keepdims=False)
+    halves = kept + swapped(given.astype(jnp.bfloat16), TP[1]).astype(jnp.float32)
+    kept = lax.dynamic_index_in_dim(halves, high, 0, keepdims=False)
+    given = lax.dynamic_index_in_dim(halves, 1 - high, 0, keepdims=False)
+    return kept + swapped(given.astype(jnp.bfloat16), TP[0]).astype(jnp.float32)
 
 
 def on_device(query_rows, key_rows, value_rows, out_weight, out_grad, doc_ids, window_blocks):
@@ -38,14 +63,12 @@
     groups = query_rows.shape[1] // kv_width
     score_scale = HEAD_DIM ** (-0.5)
     ctx_count = lax.axis_size(CTX)
-    tp_count = lax.axis_size(TP)
     ctx_place = lax.axis_index(CTX)
-    tp_place = lax.axis_index(TP)
     my_start = ctx_place * tokens_here
     span = REACH * tokens_here
     key_count = span + tokens_here
 
-    grad_piece = lax.all_gather(out_grad, TP, axis=0, tiled=True)
+    grad_piece = gathered_over_tp(out_grad)
 
     own_pair = jnp.concatenate([key_rows, value_rows], axis=1)
     earlier = [from_earlier(own_pair, distance, ctx_count) for distance in range(REACH, 0, -1)]
@@ -87,16 +110,7 @@
     log_sum = row_max + jnp.log(total)
 
     out_part = jnp.dot(attn, out_weight, preferred_element_type=jnp.float32)
-    out_chunks = out_part.reshape(tp_count, tokens_here // tp_count, out_part.shape[1])
-    layer_sum = lax.dynamic_index_in_dim(out_chunks, tp_place, 0, keepdims=False)
-    for distance in range(1, tp_count):
-        chunk = lax.dynamic_index_in_dim(
-            out_chunks, (tp_place + distance) % tp_count, 0, keepdims=False
-        )
-        layer_sum = layer_sum + rotated(chunk.astype(jnp.bfloat16), distance, tp_count).astype(
-            jnp.float32
-        )
-    layer_out = layer_sum.astype(jnp.bfloat16)
+    layer_out = summed_over_tp(out_part).astype(jnp.bfloat16)
 
     weight_part = lax.dot_general(
         attn, grad_piece, (((0,), (0,)), ((), ())), preferred_element_type=jnp.float32
@@ -104,9 +118,10 @@
     weight_sum = lax.psum_scatter(
         weight_part.astype(jnp.bfloat16), CTX[0], scatter_dimension=1, tiled=True
     )
-    weight_sum = lax.psum_scatter(
-        weight_sum.astype(jnp.float32), CTX[1:], scatter_dimension=1, tiled=True
-    )
+    rest_count = ctx_count // lax.axis_size(CTX[0])
+    weight_cols = weight_sum.reshape(weight_sum.shape[0], rest_count, -1).transpose(1, 0, 2)
+    weight_cols = lax.all_to_all(weight_cols, CTX[1:], 0, 0, tiled=True)
+    weight_sum = jnp.sum(weight_cols.astype(jnp.float32), axis=0)
     seq_total = ctx_count * tokens_here
     grad_weight = weight_sum * seq_total ** (-0.5)
 

time: 231 us -> 181 us (0.78)
  waiting for transfers between devices: 100 us -> 48.3 us
  local copies, waits for them, and re-layouts: 31.2 us -> 16.5 us
  starting transfers between devices: 23.3 us -> 33 us
  other arithmetic: 11.9 us -> 18.5 us
    ppermute x3 -> x4, waiting for transfers between devices: 52.7 us -> 16.9 us  [swapped(): return lax.ppermute(block, axis, [(0, 1), (1, 0)])]
    reduce_scatter x1, waiting for transfers between devices: 25.3 us -> 0.01 us  [on_device(): lax.psum_scatter(weight_part.astype(jnp.bfloat16), CTX[0], scatter_dimens...]
    ppermute x3, waiting for transfers between devices: 4.44 us -> 22.4 us  [to_earlier(): return lax.ppermute(block, CTX, route)]
    unnamed x31 -> x38, local copies, waits for them, and re-layouts: 19.8 us -> 7.32 us
    all_gather x1 -> x0, waiting for transfers between devices: 8.84 us -> none  [on_device(): grad_piece = lax.all_gather(out_grad, TP, axis=0, tiled=True)]
    all_to_all x0 -> x1, waiting for transfers between devices: none -> 6.23 us  [on_device(): weight_cols = lax.all_to_all(weight_cols, CTX[1:], 0, 0, tiled=True)]
    ppermute x3, waiting for transfers between devices: 8.09 us -> 2.64 us  [from_earlier(): return lax.ppermute(block, CTX, route)]
    all_to_all x0 -> x1, starting transfers between devices: none -> 5.12 us  [on_device(): weight_cols = lax.all_to_all(weight_cols, CTX[1:], 0, 0, tiled=True)]
  transfers between devices with their start and end apart: 12 -> 12, of which waited for: 9 -> 4; matrix products, arithmetic and copies ran while one was open for 28% -> 33% of each run, Pallas kernels for 0% -> 0%
where the time goes in v3:
time: 181 us; the launch traced here: 180 us
  matrix products  49.1 us (27%)
  waiting for transfers between devices  48.3 us (27%)
  starting transfers between devices  33 us (18%)
  other arithmetic  18.5 us (10%)
  local copies, waits for them, and re-layouts  16.5 us (9%)
  between operations  14.5 us (8%)
    ppermute x3, waiting for transfers between devices, to_earlier(): return lax.ppermute(block, CTX, route)  22.4 us
    ppermute x4, waiting for transfers between devices, swapped(): return lax.ppermute(block, axis, [(0, 1), (1, 0)])  16.9 us
    dot_general x1, matrix products, on_device(): jnp.einsum('qcgd,kcd->cgqk', grad_four, value_heads, preferred_element_ty...  11.7 us
    ppermute x3, starting transfers between devices, from_earlier(): return lax.ppermute(block, CTX, route)  10.8 us
    ppermute x3, starting transfers between devices, to_earlier(): return lax.ppermute(block, CTX, route)  10.2 us
    dot_general x1, matrix products, on_device(): jnp.einsum('cgqk,qcgd->kcd', probs.astype(jnp.bfloat16), grad_four, prefe...  8.39 us
    unnamed x38, local copies, waits for them, and re-layouts  7.32 us
    ppermute x4, starting transfers between devices, swapped(): return lax.ppermute(block, axis, [(0, 1), (1, 0)])  6.8 us
  transfers between devices with their start and end apart: 12, of which 4 were waited for; matrix products, arithmetic and copies ran while one was open for 33% of the time, Pallas kernels for 0%

profile of v3, /device:TPU:96, one launch (start us, length us, event | category | flops | bytes accessed | tf_op | source)
XLA Modules:
  0.0 179.9 jit_solution(4943815723597866321)
XLA Ops:
  9.2 3.5 %collective-permute-start.2 = (bf16[512,256]{1,0:T(8,128)(2,1)S(1)}, bf16[512,256]{1,0:T(8,128)(2,1)S(1)}, u32[]{:S(2)}, u32[]{:S(2)}) collective-permute-start(bf16[512,256]{1,0:T(8,128)(2,1)S(1)} %constant_dynamic-update-slice_fusion), channel_id=1, source_target_pairs={{0,4},{4,8},{8,12},{12,16},{16,20},{20,24},{24,28},{28,32},{32,36}... | collective-permute-start | bytes 786440 | tf_op jit(solution)/shard_map/ppermute | solution.py:21
  12.7 3.4 %collective-permute-start.1 = (bf16[512,256]{1,0:T(8,128)(2,1)S(1)}, bf16[512,256]{1,0:T(8,128)(2,1)S(1)}, u32[]{:S(2)}, u32[]{:S(2)}) collective-permute-start(bf16[512,256]{1,0:T(8,128)(2,1)S(1)} %constant_dynamic-update-slice_fusion), channel_id=1, source_target_pairs={{0,8},{4,12},{8,16},{12,20},{16,24},{20,28},{24,32},{28,36},{32,40... | collective-permute-start | bytes 786440 | tf_op jit(solution)/shard_map/ppermute | solution.py:21
  16.1 3.9 %collective-permute-start = (bf16[512,256]{1,0:T(8,128)(2,1)S(1)}, bf16[512,256]{1,0:T(8,128)(2,1)}, u32[]{:S(2)}, u32[]{:S(2)}) collective-permute-start(bf16[512,256]{1,0:T(8,128)(2,1)S(1)} %constant_dynamic-update-slice_fusion), channel_id=1, source_target_pairs={{0,12},{4,16},{8,20},{12,24},{16,28},{20,32},{24,36},{28,40},{32,4... | collective-permute-start | bytes 786440 | tf_op jit(solution)/shard_map/ppermute | solution.py:21
  20.0 3.3 %collective-permute-start.5 = (bf16[128,4096]{1,0:T(8,128)(2,1)}, bf16[128,4096]{1,0:T(8,128)(2,1)}, u32[]{:S(2)}, u32[]{:S(2)}) collective-permute-start(bf16[128,4096]{1,0:T(8,128)(2,1)} %param.11), channel_id=1, source_target_pairs={{0,2},{2,0},{1,3},{3,1},{4,6},{6,4},{5,7},{7,5},{8,10},{10,8},{9,1... | collective-permute-start | bytes 3145736 | tf_op jit(solution)/shard_map/ppermute | solution.py:30
  30.8 2.6 %collective-permute-done = bf16[512,256]{1,0:T(8,128)(2,1)} collective-permute-done((bf16[512,256]{1,0:T(8,128)(2,1)S(1)}, bf16[512,256]{1,0:T(8,128)(2,1)}, u32[]{:S(2)}, u32[]{:S(2)}) %collective-permute-start) | collective-permute-done | bytes 262176 | tf_op jit(solution)/shard_map/ppermute | solution.py:21
  34.7 16.9 %collective-permute-done.5 = bf16[128,4096]{1,0:T(8,128)(2,1)} collective-permute-done((bf16[128,4096]{1,0:T(8,128)(2,1)}, bf16[128,4096]{1,0:T(8,128)(2,1)}, u32[]{:S(2)}, u32[]{:S(2)}) %collective-permute-start.5) | collective-permute-done | bytes 1048608 | tf_op jit(solution)/shard_map/ppermute | solution.py:30
  53.3 3.2 %fusion.5 = (f32[4,512]{1,0:T(4,128)S(1)}, f32[2048,512,4]{1,0,2:T(8,128)S(1)}) fusion(pred[512,2048]{0,1:T(8,128)(4,1)S(1)} %fusion.20, bf16[512,4,128]{0,2,1:T(8,128)(2,1)S(1)} %bitcast.166, bf16[2048,256]{1,0:T(8,128)(2,1)S(1)} %pad_maximum_fusion.3), kind=kOutput, calls=%fused_computation.9 | convolution fusion | flops 1086322688 | bytes 18882560 | tf_op jit(solution)/shard_map/qcgd,kcd->cgqk/dot_general | solution.py:98
  56.5 4.4 %fusion.7 = f32[4,512]{1,0:T(4,128)S(1)} fusion(f32[2048,512,4]{1,0,2:T(8,128)S(1)} %get-tuple-element.25, f32[4,512]{1,0:T(4,128)S(1)} %get-tuple-element.24, pred[512,2048]{0,1:T(8,128)(4,1)S(1)} %fusion.20), kind=kLoop, calls=%fused_computation.11 | loop fusion | flops 20969472 | bytes 17842176 | tf_op jit(solution)/shard_map/reduce_sum | solution.py:104
  61.2 2.4 %pad_maximum_fusion = bf16[2,2,128,4096]{3,2,0,1:T(8,128)(2,1)} fusion(bf16[1,2,128,4096]{3,2,0,1:T(8,128)(2,1)S(1)} %get-tuple-element.16, bf16[1,2,128,4096]{3,2,0,1:T(8,128)(2,1)S(1)} %get-tuple-element.15), kind=kLoop, calls=%fused_computation.21 | loop fusion | flops 2097152 | bytes 8388608 | tf_op jit(solution)/shard_map/stack | solution.py:36
  65.7 4.7 %convolution_convert_fusion.1 = bf16[512,512]{0,1:T(8,128)(2,1)S(1)} fusion(bf16[512,4096]{1,0:T(8,128)(2,1)} %bitcast.163, bf16[512,4096]{1,0:T(8,128)(2,1)S(1)} %copy-done.4), kind=kOutput, calls=%fused_computation.42 | convolution fusion | flops 2147745792 | bytes 8912896 | tf_op jit(solution)/shard_map/dot_general | solution.py:128
  70.5 4.5 %fusion.31 = (f32[512,4]{0,1:T(4,128)S(1)}, bf16[512,1,4,128]{0,3,2,1:T(8,128)(2,1)S(1)}) fusion(bf16[512,1,4,128]{0,3,2,1:T(8,128)(2,1)S(1)} %bitcast.170, f32[512,4]{0,1:T(4,128)S(1)} %bitcast.169, f32[2048,512,4]{1,0,2:T(8,128)S(1)} %get-tuple-element.25, f32[4,512]{1,0:T(4,128)S(1)} %get-tuple-element.24, pred[512,2048]{0,1:T(8,128)(4,1)S(1)} %fusion.20, ...), kind=kOutput, calls=%fused_computation.47 | convolution fusion | flops 1096284160 | bytes 19423232 | tf_op jit(solution)/shard_map/cgqk,kcd->qcgd/dot_general | solution.py:105
  75.0 4.4 %convolution_convert_fusion = bf16[512,4096]{1,0:T(8,128)(2,1)} fusion(bf16[512,512]{0,1:T(8,128)(2,1)S(1)} %bitcast.168, bf16[512,4096]{1,0:T(8,128)(2,1)S(1)} %bitcast.164), kind=kOutput, calls=%fused_computation.20 | convolution fusion | flops 2149580800 | bytes 8912896 | tf_op jit(solution)/shard_map/dot_general | solution.py:115
  79.6 4.6 %fusion.18 = f32[2,2,128,4096]{3,2,1,0:T(8,128)S(1)} fusion(bf16[512,4096]{1,0:T(8,128)(2,1)} %param.10, bf16[2,2,128,512]{2,1,0,3:T(2,128)(2,1)S(1)} %convert_element_type.98), kind=kOutput, calls=%fused_computation.22 | convolution fusion | flops 2147483648 | bytes 13107200 | tf_op jit(solution)/shard_map/dot_general | solution.py:112
  85.3 11.7 %fusion.11 = bf16[4,512,2048]{1,2,0:T(8,128)(2,1)} fusion(f32[2048,512,4]{1,0,2:T(8,128)} %copy-done.2, f32[4,512]{1,0:T(4,128)S(1)} %bitcast.173, f32[4,512]{1,0:T(4,128)S(1)} %log_add_fusion, pred[512,2048]{0,1:T(8,128)(4,1)S(1)} %fusion.20, bf16[512,4,128]{0,2,1:T(8,128)(2,1)S(1)} %bitcast.171, bf16[2048,256]{1,0:T(8,128)(2,1)S(1)} %pad_maximum_fusion.3), kind=kOutput, calls=%fused_computation.15 | convolution fusion | flops 1103101952 | bytes 27279360 | tf_op jit(solution)/shard_map/qcgd,kcd->cgqk/dot_general | solution.py:142
  97.0 6.3 %convolution_bitcast_fusion = f32[2048,128]{0,1:T(8,128)S(1)} fusion(bf16[4,512,2048]{1,2,0:T(8,128)(2,1)} %fusion.11, bf16[512,4,128]{0,2,1:T(8,128)(2,1)S(1)} %bitcast.167), kind=kOutput, calls=%fused_computation.31 | convolution fusion | flops 1073741824 | bytes 9961472 | tf_op jit(solution)/shard_map/cgqk,qcgd->kcd/dot_general | solution.py:149
  103.3 8.4 %fusion.21 = f32[2048,128]{0,1:T(8,128)S(1)} fusion(bf16[512,4,128]{0,2,1:T(8,128)(2,1)S(1)} %bitcast.172, f32[2048,512,4]{1,0,2:T(8,128)} %copy-done.2, f32[4,512]{1,0:T(4,128)S(1)} %log_add_fusion, pred[512,2048]{0,1:T(8,128)(4,1)S(1)} %fusion.20), kind=kOutput, calls=%fused_computation.32 | convolution fusion | flops 1090519040 | bytes 19406848 | tf_op jit(solution)/shard_map/cgqk,qcgd->kcd/dot_general | solution.py:152
  115.3 2.9 %collective-permute-start.4 = (bf16[128,4096]{1,0:T(8,128)(2,1)}, bf16[128,4096]{1,0:T(8,128)(2,1)}, u32[]{:S(2)}, u32[]{:S(2)}) collective-permute-start(bf16[128,4096]{1,0:T(8,128)(2,1)} %fusion.30), channel_id=1, source_target_pairs={{0,2},{2,0},{1,3},{3,1},{4,6},{6,4},{5,7},{7,5},{8,10},{10,8},{9,1... | collective-permute-start | bytes 3145736 | tf_op jit(solution)/shard_map/ppermute | solution.py:30
  119.1 3.5 %collective-permute-start.7 = (bf16[512,256]{0,1:T(8,128)(2,1)}, bf16[512,256]{0,1:T(8,128)(2,1)S(1)}, u32[]{:S(2)}, u32[]{:S(2)}) collective-permute-start(bf16[512,256]{0,1:T(8,128)(2,1)} %get-tuple-element.19), channel_id=1, source_target_pairs={{4,0},{8,4},{12,8},{16,12},{20,16},{24,20},{28,24},{32,28},{36,32}... | collective-permute-start | bytes 786440 | tf_op jit(solution)/shard_map/ppermute | solution.py:26
  122.5 3.4 %collective-permute-start.9 = (bf16[512,256]{0,1:T(8,128)(2,1)}, bf16[512,256]{0,1:T(8,128)(2,1)S(1)}, u32[]{:S(2)}, u32[]{:S(2)}) collective-permute-start(bf16[512,256]{0,1:T(8,128)(2,1)} %get-tuple-element.20), channel_id=1, source_target_pairs={{12,0},{16,4},{20,8},{24,12},{28,16},{32,20},{36,24},{40,28},{44,3... | collective-permute-start | bytes 786440 | tf_op jit(solution)/shard_map/ppermute | solution.py:26
  125.9 3.3 %collective-permute-start.8 = (bf16[512,256]{0,1:T(8,128)(2,1)}, bf16[512,256]{0,1:T(8,128)(2,1)S(1)}, u32[]{:S(2)}, u32[]{:S(2)}) collective-permute-start(bf16[512,256]{0,1:T(8,128)(2,1)} %get-tuple-element.21), channel_id=1, source_target_pairs={{8,0},{12,4},{16,8},{20,12},{24,16},{28,20},{32,24},{36,28},{40,32... | collective-permute-start | bytes 786440 | tf_op jit(solution)/shard_map/ppermute | solution.py:26
  131.6 22.4 %collective-permute-done.7 = bf16[512,256]{0,1:T(8,128)(2,1)S(1)} collective-permute-done((bf16[512,256]{0,1:T(8,128)(2,1)}, bf16[512,256]{0,1:T(8,128)(2,1)S(1)}, u32[]{:S(2)}, u32[]{:S(2)}) %collective-permute-start.7) | collective-permute-done | bytes 262176 | tf_op jit(solution)/shard_map/ppermute | solution.py:26
  157.8 5.1 %all-to-all-start = ((bf16[8,512,64]{1,2,0:T(8,128)(2,1)}), bf16[8,512,64]{1,2,0:T(8,128)(2,1)S(1)}, u32[]{:S(2)}, u32[]{:S(2)}) async-start(bf16[8,512,64]{1,2,0:T(8,128)(2,1)} %bitcast.47), calls=%async_computation.1 | async-start | bytes 1048576 | tf_op jit(solution)/shard_map/all_to_all | solution.py:123
  163.0 3.1 %fusion.26 = bf16[128,4096]{1,0:T(8,128)(2,1)} fusion(bf16[128,4096]{1,0:T(8,128)(2,1)} %collective-permute-done.4, f32[2,128,4096]{2,1,0:T(8,128)} %copy-done.3, s32[]{:T(128)S(6)} %select_n.92), kind=kLoop, calls=%fused_computation.37 | loop fusion | flops 1572864 | bytes 4194308 | tf_op jit(solution)/shard_map/convert_element_type | solution.py:113
  166.1 6.2 %all-to-all-done = bf16[8,512,64]{1,2,0:T(8,128)(2,1)S(1)} async-done(((bf16[8,512,64]{1,2,0:T(8,128)(2,1)}), bf16[8,512,64]{1,2,0:T(8,128)(2,1)S(1)}, u32[]{:S(2)}, u32[]{:S(2)}) %all-to-all-start) | async-done | bytes 524320 | tf_op jit(solution)/shard_map/all_to_all | solution.py:123
  (78 shorter events, 27.2 us)
Async XLA Ops:
  7.2 19.8 %copy-start = (s32[256]{0:T(256)S(1)}, s32[256]{0:T(256)}, u32[]{:S(2)}) copy-start(s32[256]{0:T(256)} %param.13) | copy-start | bytes 3076
  7.2 44.4 %copy-start.8 = (bf16[128,4096]{1,0:T(8,128)(2,1)S(1)}, bf16[128,4096]{1,0:T(8,128)(2,1)}, u32[]{:S(2)}) copy-start(bf16[128,4096]{1,0:T(8,128)(2,1)} %param.11) | copy-start | bytes 3145732
  7.2 148.6 %reduce-scatter.2.cloned.1.call-start = ((), (), s32[]{:S(2)}) async-start(), calls=%async_computation.2 | async-start | bytes 4718592 | tf_op jit(solution)/shard_map/reduce_scatter | solution.py:118
  9.2 20.2 %collective-permute-start.2 = (bf16[512,256]{1,0:T(8,128)(2,1)S(1)}, bf16[512,256]{1,0:T(8,128)(2,1)S(1)}, u32[]{:S(2)}, u32[]{:S(2)}) collective-permute-start(bf16[512,256]{1,0:T(8,128)(2,1)S(1)} %constant_dynamic-update-slice_fusion), channel_id=1, source_target_pairs={{0,4},{4,8},{8,12},{12,16},{16,20},{20,24},{24,28},{28,32},{32,36}... | collective-permute-start | bytes 786440 | tf_op jit(solution)/shard_map/ppermute | solution.py:21
  12.7 16.8 %collective-permute-start.1 = (bf16[512,256]{1,0:T(8,128)(2,1)S(1)}, bf16[512,256]{1,0:T(8,128)(2,1)S(1)}, u32[]{:S(2)}, u32[]{:S(2)}) collective-permute-start(bf16[512,256]{1,0:T(8,128)(2,1)S(1)} %constant_dynamic-update-slice_fusion), channel_id=1, source_target_pairs={{0,8},{4,12},{8,16},{12,20},{16,24},{20,28},{24,32},{28,36},{32,40... | collective-permute-start | bytes 786440 | tf_op jit(solution)/shard_map/ppermute | solution.py:21
  16.1 17.4 %collective-permute-start = (bf16[512,256]{1,0:T(8,128)(2,1)S(1)}, bf16[512,256]{1,0:T(8,128)(2,1)}, u32[]{:S(2)}, u32[]{:S(2)}) collective-permute-start(bf16[512,256]{1,0:T(8,128)(2,1)S(1)} %constant_dynamic-update-slice_fusion), channel_id=1, source_target_pairs={{0,12},{4,16},{8,20},{12,24},{16,28},{20,32},{24,36},{28,40},{32,4... | collective-permute-start | bytes 786440 | tf_op jit(solution)/shard_map/ppermute | solution.py:21
  20.0 31.6 %collective-permute-start.5 = (bf16[128,4096]{1,0:T(8,128)(2,1)}, bf16[128,4096]{1,0:T(8,128)(2,1)}, u32[]{:S(2)}, u32[]{:S(2)}) collective-permute-start(bf16[128,4096]{1,0:T(8,128)(2,1)} %param.11), channel_id=1, source_target_pairs={{0,2},{2,0},{1,3},{3,1},{4,6},{6,4},{5,7},{7,5},{8,10},{10,8},{9,1... | collective-permute-start | bytes 3145736 | tf_op jit(solution)/shard_map/ppermute | solution.py:30
  34.7 50.4 %copy-start.6 = (bf16[2048,256]{1,0:T(8,128)(2,1)}, bf16[2048,256]{1,0:T(8,128)(2,1)S(1)}, u32[]{:S(2)}) copy-start(bf16[2048,256]{1,0:T(8,128)(2,1)S(1)} %pad_maximum_fusion.3) | copy-start | bytes 3145732
  34.7 18.6 %copy-start.9 = (bf16[512,512]{0,1:T(8,128)(2,1)S(1)}, bf16[512,512]{0,1:T(8,128)(2,1)}, u32[]{:S(2)}) copy-start(bf16[512,512]{0,1:T(8,128)(2,1)} %copy.50) | copy-start | bytes 1572868
  53.2 7.7 %collective-permute-start.6 = (bf16[2,128,4096]{2,1,0:T(8,128)(2,1)S(1)}, bf16[2,128,4096]{2,1,0:T(8,128)(2,1)S(1)}, u32[]{:S(2)}, u32[]{:S(2)}) collective-permute-start(bf16[2,128,4096]{2,1,0:T(8,128)(2,1)S(1)} %pad_maximum_fusion.2), channel_id=1, source_target_pairs={{0,1},{1,0},{2,3},{3,2},{4,5},{5,4},{6,7},{7,6},{8,9},{9,8},{10,11... | collective-permute-start | bytes 6291464 | tf_op jit(solution)/shard_map/ppermute | solution.py:30
  56.5 14.0 %copy-start.2 = (f32[2048,512,4]{1,0,2:T(8,128)}, f32[2048,512,4]{1,0,2:T(8,128)S(1)}, u32[]{:S(2)}) copy-start(f32[2048,512,4]{1,0,2:T(8,128)S(1)} %get-tuple-element.25) | copy-start | bytes 50331652
  70.4 4.6 %copy-start.13 = (bf16[512,512]{0,1:T(8,128)(2,1)}, bf16[512,512]{0,1:T(8,128)(2,1)S(1)}, u32[]{:S(2)}) copy-start(bf16[512,512]{0,1:T(8,128)(2,1)S(1)} %convolution_convert_fusion.1) | copy-start | bytes 1572868
  84.5 27.3 %collective-permute-start.3 = (bf16[2,128,4096]{2,1,0:T(8,128)(2,1)S(1)}, bf16[2,128,4096]{2,1,0:T(8,128)(2,1)}, u32[]{:S(2)}, u32[]{:S(2)}) collective-permute-start(bf16[2,128,4096]{2,1,0:T(8,128)(2,1)S(1)} %fusion.25), channel_id=1, source_target_pairs={{0,1},{1,0},{2,3},{3,2},{4,5},{5,4},{6,7},{7,6},{8,9},{9,8},{10,11... | collective-permute-start | bytes 6291464 | tf_op jit(solution)/shard_map/ppermute | solution.py:30
  85.3 11.7 %copy-start.10 = (bf16[512,512]{0,1:T(8,128)(2,1)S(1)}, bf16[512,512]{0,1:T(8,128)(2,1)}, u32[]{:S(2)}) copy-start(bf16[512,512]{0,1:T(8,128)(2,1)} %copy.50) | copy-start | bytes 1572868
  111.7 17.6 %slice-start = ((s8[8388608]{0:T(1024)(128)(4,1)}), s8[4194304]{0:T(1024)(128)(4,1)S(1)}, s32[]{:S(2)}) async-start(s8[8388608]{0:T(1024)(128)(4,1)} %bitcast.161), calls=%async_computation.3 | async-start | bytes 8388608
  111.8 17.5 %slice-start.1 = ((s8[8388608]{0:T(1024)(128)(4,1)}), s8[4194304]{0:T(1024)(128)(4,1)S(1)}, s32[]{:S(2)}) async-start(s8[8388608]{0:T(1024)(128)(4,1)} %bitcast.161), calls=%async_computation.4 | async-start | bytes 8388608
  111.8 17.5 %copy-start.7 = (bf16[2048,256]{1,0:T(8,128)(2,1)S(1)}, bf16[2048,256]{1,0:T(8,128)(2,1)}, u32[]{:S(2)}) copy-start(bf16[2048,256]{1,0:T(8,128)(2,1)} %copy-done.6) | copy-start | bytes 3145732
  114.2 16.5 %copy-start.3 = (f32[2,128,4096]{2,1,0:T(8,128)}, f32[2,128,4096]{2,1,0:T(8,128)S(1)}, u32[]{:S(2)}) copy-start(f32[2,128,4096]{2,1,0:T(8,128)S(1)} %bitcast_add_fusion) | copy-start | bytes 12582916
  115.3 47.7 %collective-permute-start.4 = (bf16[128,4096]{1,0:T(8,128)(2,1)}, bf16[128,4096]{1,0:T(8,128)(2,1)}, u32[]{:S(2)}, u32[]{:S(2)}) collective-permute-start(bf16[128,4096]{1,0:T(8,128)(2,1)} %fusion.30), channel_id=1, source_target_pairs={{0,2},{2,0},{1,3},{3,1},{4,6},{6,4},{5,7},{7,5},{8,10},{10,8},{9,1... | collective-permute-start | bytes 3145736 | tf_op jit(solution)/shard_map/ppermute | solution.py:30
  119.1 35.0 %collective-permute-start.7 = (bf16[512,256]{0,1:T(8,128)(2,1)}, bf16[512,256]{0,1:T(8,128)(2,1)S(1)}, u32[]{:S(2)}, u32[]{:S(2)}) collective-permute-start(bf16[512,256]{0,1:T(8,128)(2,1)} %get-tuple-element.19), channel_id=1, source_target_pairs={{4,0},{8,4},{12,8},{16,12},{20,16},{24,20},{28,24},{32,28},{36,32}... | collective-permute-start | bytes 786440 | tf_op jit(solution)/shard_map/ppermute | solution.py:26
  122.5 31.5 %collective-permute-start.9 = (bf16[512,256]{0,1:T(8,128)(2,1)}, bf16[512,256]{0,1:T(8,128)(2,1)S(1)}, u32[]{:S(2)}, u32[]{:S(2)}) collective-permute-start(bf16[512,256]{0,1:T(8,128)(2,1)} %get-tuple-element.20), channel_id=1, source_target_pairs={{12,0},{16,4},{20,8},{24,12},{28,16},{32,20},{36,24},{40,28},{44,3... | collective-permute-start | bytes 786440 | tf_op jit(solution)/shard_map/ppermute | solution.py:26
  125.9 28.2 %collective-permute-start.8 = (bf16[512,256]{0,1:T(8,128)(2,1)}, bf16[512,256]{0,1:T(8,128)(2,1)S(1)}, u32[]{:S(2)}, u32[]{:S(2)}) collective-permute-start(bf16[512,256]{0,1:T(8,128)(2,1)} %get-tuple-element.21), channel_id=1, source_target_pairs={{8,0},{12,4},{16,8},{20,12},{24,16},{28,20},{32,24},{36,28},{40,32... | collective-permute-start | bytes 786440 | tf_op jit(solution)/shard_map/ppermute | solution.py:26
  154.1 19.0 %copy-start.1 = (s32[256]{0:T(256)S(1)}, s32[256]{0:T(256)}, u32[]{:S(2)}) copy-start(s32[256]{0:T(256)} %param.13) | copy-start | bytes 3076
  157.8 14.5 %all-to-all-start = ((bf16[8,512,64]{1,2,0:T(8,128)(2,1)}), bf16[8,512,64]{1,2,0:T(8,128)(2,1)S(1)}, u32[]{:S(2)}, u32[]{:S(2)}) async-start(bf16[8,512,64]{1,2,0:T(8,128)(2,1)} %bitcast.47), calls=%async_computation.1 | async-start | bytes 1048576 | tf_op jit(solution)/shard_map/all_to_all | solution.py:123
  (5 other events, 11.6 us)
Sparse Core Ops, SparseCore 0:
  79.6 61.4 reduce-scatter.1

commit v4 on v3

--- a/solution.py
+++ b/solution.py
@@ -109,15 +109,14 @@
     attn = attn_four.reshape(tokens_here, -1).astype(jnp.bfloat16)
     log_sum = row_max + jnp.log(total)
 
+    weight_part = lax.dot_general(
+        attn, grad_piece, (((0,), (0,)), ((), ())), preferred_element_type=jnp.float32
+    ).astype(jnp.bfloat16)
+    weight_part, attn, grad_piece = lax.optimization_barrier((weight_part, attn, grad_piece))
+    weight_sum = lax.psum_scatter(weight_part, CTX[0], scatter_dimension=1, tiled=True)
+
     out_part = jnp.dot(attn, out_weight, preferred_element_type=jnp.float32)
     layer_out = summed_over_tp(out_part).astype(jnp.bfloat16)
-
-    weight_part = lax.dot_general(
-        attn, grad_piece, (((0,), (0,)), ((), ())), preferred_element_type=jnp.float32
-    )
-    weight_sum = lax.psum_scatter(
-        weight_part.astype(jnp.bfloat16), CTX[0], scatter_dimension=1, tiled=True
-    )
     rest_count = ctx_count // lax.axis_size(CTX[0])
     weight_cols = weight_sum.reshape(weight_sum.shape[0], rest_count, -1).transpose(1, 0, 2)
     weight_cols = lax.all_to_all(weight_cols, CTX[1:], 0, 0, tiled=True)

time: 181 us -> 178 us (0.983)
  waiting for transfers between devices: 48.3 us -> 45.9 us
    ppermute x4, waiting for transfers between devices: 16.9 us -> 13.6 us  [swapped(): return lax.ppermute(block, axis, [(0, 1), (1, 0)])]
    dot_general x1, matrix products: 4.74 us -> 2.37 us  [on_device(): lax.dot_general(grad_piece, out_weight, (((1,), (1,)), ((), ())), preferr...]
    unnamed x38 -> x32, local copies, waits for them, and re-layouts: 7.32 us -> 6.25 us
  transfers between devices with their start and end apart: 12 -> 12, of which waited for: 4 -> 4; matrix products, arithmetic and copies ran while one was open for 33% -> 39% of each run, Pallas kernels for 0% -> 0%
where the time goes in v4:
time: 178 us; the launch traced here: 177 us
  matrix products  48.9 us (27%)
  waiting for transfers between devices  45.9 us (26%)
  starting transfers between devices  32.9 us (18%)
  other arithmetic  18.2 us (10%)
  local copies, waits for them, and re-layouts  16.7 us (9%)
  between operations  14.4 us (8%)
    ppermute x3, waiting for transfers between devices, to_earlier(): return lax.ppermute(block, CTX, route)  22.3 us
    ppermute x4, waiting for transfers between devices, swapped(): return lax.ppermute(block, axis, [(0, 1), (1, 0)])  13.6 us
    dot_general x1, matrix products, on_device(): jnp.einsum('qcgd,kcd->cgqk', grad_four, value_heads, preferred_element_ty...  12.1 us
    ppermute x3, starting transfers between devices, from_earlier(): return lax.ppermute(block, CTX, route)  10.8 us
    ppermute x3, starting transfers between devices, to_earlier(): return lax.ppermute(block, CTX, route)  10.4 us
    dot_general x1, matrix products, on_device(): jnp.einsum('cgqk,qcgd->kcd', probs.astype(jnp.bfloat16), grad_four, prefe...  8.59 us
    ppermute x4, starting transfers between devices, swapped(): return lax.ppermute(block, axis, [(0, 1), (1, 0)])  6.77 us
    dot_general x1, matrix products, on_device(): jnp.einsum('cgqk,qcgd->kcd', d_scores, query_four, preferred_element_type...  6.26 us
  transfers between devices with their start and end apart: 12, of which 4 were waited for; matrix products, arithmetic and copies ran while one was open for 39% of the time, Pallas kernels for 0%

profile of v4, /device:TPU:96, one launch (start us, length us, event | category | flops | bytes accessed | tf_op | source)
XLA Modules:
  0.0 176.9 jit_solution(17791752441945187424)
XLA Ops:
  9.1 3.5 %collective-permute-start.2 = (bf16[512,256]{1,0:T(8,128)(2,1)S(1)}, bf16[512,256]{1,0:T(8,128)(2,1)S(1)}, u32[]{:S(2)}, u32[]{:S(2)}) collective-permute-start(bf16[512,256]{1,0:T(8,128)(2,1)S(1)} %constant_dynamic-update-slice_fusion), channel_id=1, source_target_pairs={{0,4},{4,8},{8,12},{12,16},{16,20},{20,24},{24,28},{28,32},{32,36}... | collective-permute-start | bytes 786440 | tf_op jit(solution)/shard_map/ppermute | solution.py:21
  12.6 3.4 %collective-permute-start.1 = (bf16[512,256]{1,0:T(8,128)(2,1)S(1)}, bf16[512,256]{1,0:T(8,128)(2,1)S(1)}, u32[]{:S(2)}, u32[]{:S(2)}) collective-permute-start(bf16[512,256]{1,0:T(8,128)(2,1)S(1)} %constant_dynamic-update-slice_fusion), channel_id=1, source_target_pairs={{0,8},{4,12},{8,16},{12,20},{16,24},{20,28},{24,32},{28,36},{32,40... | collective-permute-start | bytes 786440 | tf_op jit(solution)/shard_map/ppermute | solution.py:21
  16.0 3.9 %collective-permute-start = (bf16[512,256]{1,0:T(8,128)(2,1)S(1)}, bf16[512,256]{1,0:T(8,128)(2,1)S(1)}, u32[]{:S(2)}, u32[]{:S(2)}) collective-permute-start(bf16[512,256]{1,0:T(8,128)(2,1)S(1)} %constant_dynamic-update-slice_fusion), channel_id=1, source_target_pairs={{0,12},{4,16},{8,20},{12,24},{16,28},{20,32},{24,36},{28,40},{32,4... | collective-permute-start | bytes 786440 | tf_op jit(solution)/shard_map/ppermute | solution.py:21
  19.9 3.3 %collective-permute-start.3 = (bf16[128,4096]{1,0:T(8,128)(2,1)}, bf16[128,4096]{1,0:T(8,128)(2,1)}, u32[]{:S(2)}, u32[]{:S(2)}) collective-permute-start(bf16[128,4096]{1,0:T(8,128)(2,1)} %param.11), channel_id=1, source_target_pairs={{0,2},{2,0},{1,3},{3,1},{4,6},{6,4},{5,7},{7,5},{8,10},{10,8},{9,1... | collective-permute-start | bytes 3145736 | tf_op jit(solution)/shard_map/ppermute | solution.py:30
  29.4 3.9 %collective-permute-done = bf16[512,256]{1,0:T(8,128)(2,1)S(1)} collective-permute-done((bf16[512,256]{1,0:T(8,128)(2,1)S(1)}, bf16[512,256]{1,0:T(8,128)(2,1)S(1)}, u32[]{:S(2)}, u32[]{:S(2)}) %collective-permute-start) | collective-permute-done | bytes 262176 | tf_op jit(solution)/shard_map/ppermute | solution.py:21
  33.4 4.5 %fusion.5 = (f32[4,512]{1,0:T(4,128)S(1)}, f32[2048,512,4]{1,0,2:T(8,128)S(1)}) fusion(pred[512,2048]{0,1:T(8,128)(4,1)S(1)} %fusion.18, bf16[512,4,128]{0,2,1:T(8,128)(2,1)} %bitcast.163, bf16[2048,256]{1,0:T(8,128)(2,1)S(1)} %pad_maximum_fusion.3), kind=kOutput, calls=%fused_computation.9 | convolution fusion | flops 1086322688 | bytes 18882560 | tf_op jit(solution)/shard_map/qcgd,kcd->cgqk/dot_general | solution.py:98
  37.9 13.6 %collective-permute-done.3 = bf16[128,4096]{1,0:T(8,128)(2,1)} collective-permute-done((bf16[128,4096]{1,0:T(8,128)(2,1)}, bf16[128,4096]{1,0:T(8,128)(2,1)}, u32[]{:S(2)}, u32[]{:S(2)}) %collective-permute-start.3) | collective-permute-done | bytes 1048608 | tf_op jit(solution)/shard_map/ppermute | solution.py:30
  54.4 4.2 %fusion.7 = f32[4,512]{1,0:T(4,128)S(1)} fusion(f32[2048,512,4]{1,0,2:T(8,128)S(1)} %get-tuple-element.31, f32[4,512]{1,0:T(4,128)S(1)} %get-tuple-element.30, pred[512,2048]{0,1:T(8,128)(4,1)S(1)} %fusion.18), kind=kLoop, calls=%fused_computation.11 | loop fusion | flops 20969472 | bytes 17842176 | tf_op jit(solution)/shard_map/reduce_sum | solution.py:104
  58.6 4.6 %divide_convert_fusion = bf16[512,1,4,128]{0,3,2,1:T(8,128)(2,1)S(1)} fusion(f32[2048,512,4]{1,0,2:T(8,128)S(1)} %get-tuple-element.31, f32[4,512]{1,0:T(4,128)S(1)} %get-tuple-element.30, pred[512,2048]{0,1:T(8,128)(4,1)S(1)} %fusion.18, f32[512,4]{0,1:T(4,128)S(1)} %bitcast.165, bf16[2048,256]{1,0:T(8,128)(2,1)S(1)} %pad_maximum_fusion.3), kind=kOutput, calls=%fused_computation.49 | convolution fusion | flops 1095237632 | bytes 18890752 | tf_op jit(solution)/shard_map/cgqk,kcd->qcgd/dot_general | solution.py:105
  67.4 4.3 %convolution_convert_fusion = bf16[512,4096]{1,0:T(8,128)(2,1)} fusion(bf16[512,512]{0,1:T(8,128)(2,1)S(1)} %bitcast.160, bf16[512,4096]{1,0:T(8,128)(2,1)S(1)} %bitcast.157), kind=kOutput, calls=%fused_computation.20 | convolution fusion | flops 2149580800 | bytes 8912896 | tf_op jit(solution)/shard_map/dot_general | solution.py:112
  71.8 4.8 %fusion.51 = f32[512,4096]{1,0:T(8,128)S(1)} fusion(bf16[512,512]{0,1:T(8,128)(2,1)S(1)} %bitcast.161, bf16[512,4096]{1,0:T(8,128)(2,1)} %param.10), kind=kOutput, calls=%fused_computation.90 | convolution fusion | flops 2147483648 | bytes 13107200 | tf_op jit(solution)/shard_map/dot_general | solution.py:118
  79.6 2.4 %bitcast_reduce_fusion = (f32[512,4]{0,1:T(4,128)S(1)}, bf16[512,512]{0,1:T(8,128)(2,1)S(1)}) fusion(bf16[512,512]{0,1:T(8,128)(2,1)S(1)} %bitcast.162, bf16[512,4096]{1,0:T(8,128)(2,1)S(1)} %bitcast.158, bf16[512,4096]{1,0:T(8,128)(2,1)S(1)} %copy-done.4), kind=kOutput, calls=%fused_computation.44 | convolution fusion | flops 2148792320 | bytes 9445376 | tf_op jit(solution)/shard_map/dot_general | solution.py:127
  82.0 12.1 %fusion.11 = bf16[4,512,2048]{1,2,0:T(8,128)(2,1)} fusion(f32[2048,512,4]{1,0,2:T(8,128)} %copy-done.2, f32[4,512]{1,0:T(4,128)S(1)} %bitcast.168, f32[4,512]{1,0:T(4,128)S(1)} %log_add_fusion, pred[512,2048]{0,1:T(8,128)(4,1)S(1)} %fusion.18, bf16[512,4,128]{0,2,1:T(8,128)(2,1)S(1)} %bitcast.166, bf16[2048,256]{1,0:T(8,128)(2,1)S(1)} %pad_maximum_fusion.3), kind=kOutput, calls=%fused_computation.15 | convolution fusion | flops 1103101952 | bytes 27279360 | tf_op jit(solution)/shard_map/qcgd,kcd->cgqk/dot_general | solution.py:141
  94.1 6.3 %convolution_bitcast_fusion = f32[2048,128]{0,1:T(8,128)S(1)} fusion(bf16[4,512,2048]{1,2,0:T(8,128)(2,1)} %fusion.11, bf16[512,4,128]{0,2,1:T(8,128)(2,1)S(1)} %bitcast.164), kind=kOutput, calls=%fused_computation.29 | convolution fusion | flops 1073741824 | bytes 9961472 | tf_op jit(solution)/shard_map/cgqk,qcgd->kcd/dot_general | solution.py:148
  100.4 8.6 %fusion.19 = f32[2048,128]{0,1:T(8,128)S(1)} fusion(bf16[512,4,128]{0,2,1:T(8,128)(2,1)} %bitcast.167, f32[2048,512,4]{1,0,2:T(8,128)} %copy-done.2, f32[4,512]{1,0:T(4,128)S(1)} %log_add_fusion, pred[512,2048]{0,1:T(8,128)(4,1)S(1)} %fusion.18), kind=kOutput, calls=%fused_computation.30 | convolution fusion | flops 1090519040 | bytes 19406848 | tf_op jit(solution)/shard_map/cgqk,qcgd->kcd/dot_general | solution.py:151
  109.1 2.3 %bitcast_add_fusion = f32[2,128,4096]{2,1,0:T(8,128)S(1)} fusion(bf16[2,128,4096]{2,1,0:T(8,128)(2,1)} %collective-permute-done.5, f32[2,2,128,4096]{3,2,1,0:T(8,128)S(1)} %bitcast.154, s32[]{:T(128)S(6)} %select_n.96), kind=kLoop, calls=%fused_computation.23 | loop fusion | flops 2097152 | bytes 10485764 | tf_op jit(solution)/shard_map/add | solution.py:53
  112.6 3.0 %collective-permute-start.6 = (bf16[128,4096]{1,0:T(8,128)(2,1)}, bf16[128,4096]{1,0:T(8,128)(2,1)}, u32[]{:S(2)}, u32[]{:S(2)}) collective-permute-start(bf16[128,4096]{1,0:T(8,128)(2,1)} %fusion.28), channel_id=1, source_target_pairs={{0,2},{2,0},{1,3},{3,1},{4,6},{6,4},{5,7},{7,5},{8,10},{10,8},{9,1... | collective-permute-start | bytes 3145736 | tf_op jit(solution)/shard_map/ppermute | solution.py:30
  116.4 3.4 %collective-permute-start.7 = (bf16[512,256]{0,1:T(8,128)(2,1)}, bf16[512,256]{0,1:T(8,128)(2,1)S(1)}, u32[]{:S(2)}, u32[]{:S(2)}) collective-permute-start(bf16[512,256]{0,1:T(8,128)(2,1)} %get-tuple-element.25), channel_id=1, source_target_pairs={{4,0},{8,4},{12,8},{16,12},{20,16},{24,20},{28,24},{32,28},{36,32}... | collective-permute-start | bytes 786440 | tf_op jit(solution)/shard_map/ppermute | solution.py:26
  119.8 3.1 %collective-permute-start.9 = (bf16[512,256]{0,1:T(8,128)(2,1)}, bf16[512,256]{0,1:T(8,128)(2,1)S(1)}, u32[]{:S(2)}, u32[]{:S(2)}) collective-permute-start(bf16[512,256]{0,1:T(8,128)(2,1)} %get-tuple-element.26), channel_id=1, source_target_pairs={{12,0},{16,4},{20,8},{24,12},{28,16},{32,20},{36,24},{40,28},{44,3... | collective-permute-start | bytes 786440 | tf_op jit(solution)/shard_map/ppermute | solution.py:26
  122.9 3.9 %collective-permute-start.8 = (bf16[512,256]{0,1:T(8,128)(2,1)}, bf16[512,256]{0,1:T(8,128)(2,1)S(1)}, u32[]{:S(2)}, u32[]{:S(2)}) collective-permute-start(bf16[512,256]{0,1:T(8,128)(2,1)} %get-tuple-element.27), channel_id=1, source_target_pairs={{8,0},{12,4},{16,8},{20,12},{24,16},{28,20},{32,24},{36,28},{40,32... | collective-permute-start | bytes 786440 | tf_op jit(solution)/shard_map/ppermute | solution.py:26
  129.2 22.3 %collective-permute-done.7 = bf16[512,256]{0,1:T(8,128)(2,1)S(1)} collective-permute-done((bf16[512,256]{0,1:T(8,128)(2,1)}, bf16[512,256]{0,1:T(8,128)(2,1)S(1)}, u32[]{:S(2)}, u32[]{:S(2)}) %collective-permute-start.7) | collective-permute-done | bytes 262176 | tf_op jit(solution)/shard_map/ppermute | solution.py:26
  155.2 4.8 %all-to-all-start = ((bf16[8,512,64]{1,2,0:T(8,128)(2,1)}), bf16[8,512,64]{1,2,0:T(8,128)(2,1)S(1)}, u32[]{:S(2)}, u32[]{:S(2)}) async-start(bf16[8,512,64]{1,2,0:T(8,128)(2,1)} %bitcast.45), calls=%async_computation.1 | async-start | bytes 1048576 | tf_op jit(solution)/shard_map/all_to_all | solution.py:122
  160.1 3.1 %fusion.24 = bf16[128,4096]{1,0:T(8,128)(2,1)} fusion(bf16[128,4096]{1,0:T(8,128)(2,1)} %collective-permute-done.6, f32[2,128,4096]{2,1,0:T(8,128)} %copy-done.3, s32[]{:T(128)S(6)} %select_n.98), kind=kLoop, calls=%fused_computation.35 | loop fusion | flops 1572864 | bytes 4194308 | tf_op jit(solution)/shard_map/convert_element_type | solution.py:119
  163.2 6.1 %all-to-all-done = bf16[8,512,64]{1,2,0:T(8,128)(2,1)S(1)} async-done(((bf16[8,512,64]{1,2,0:T(8,128)(2,1)}), bf16[8,512,64]{1,2,0:T(8,128)(2,1)S(1)}, u32[]{:S(2)}, u32[]{:S(2)}) %all-to-all-start) | async-done | bytes 524320 | tf_op jit(solution)/shard_map/all_to_all | solution.py:122
  (71 shorter events, 27.1 us)
Async XLA Ops:
  7.2 16.1 %copy-start = (s32[256]{0:T(256)S(1)}, s32[256]{0:T(256)}, u32[]{:S(2)}) copy-start(s32[256]{0:T(256)} %param.13) | copy-start | bytes 3076
  7.2 146.0 %reduce-scatter.2.cloned.1.call-start = ((), (), s32[]{:S(2)}) async-start(), calls=%async_computation.2 | async-start | bytes 4718592 | tf_op jit(solution)/shard_map/reduce_scatter | solution.py:116
  9.1 20.3 %collective-permute-start.2 = (bf16[512,256]{1,0:T(8,128)(2,1)S(1)}, bf16[512,256]{1,0:T(8,128)(2,1)S(1)}, u32[]{:S(2)}, u32[]{:S(2)}) collective-permute-start(bf16[512,256]{1,0:T(8,128)(2,1)S(1)} %constant_dynamic-update-slice_fusion), channel_id=1, source_target_pairs={{0,4},{4,8},{8,12},{12,16},{16,20},{20,24},{24,28},{28,32},{32,36}... | collective-permute-start | bytes 786440 | tf_op jit(solution)/shard_map/ppermute | solution.py:21
  12.6 16.8 %collective-permute-start.1 = (bf16[512,256]{1,0:T(8,128)(2,1)S(1)}, bf16[512,256]{1,0:T(8,128)(2,1)S(1)}, u32[]{:S(2)}, u32[]{:S(2)}) collective-permute-start(bf16[512,256]{1,0:T(8,128)(2,1)S(1)} %constant_dynamic-update-slice_fusion), channel_id=1, source_target_pairs={{0,8},{4,12},{8,16},{12,20},{16,24},{20,28},{24,32},{28,36},{32,40... | collective-permute-start | bytes 786440 | tf_op jit(solution)/shard_map/ppermute | solution.py:21
  16.0 17.3 %collective-permute-start = (bf16[512,256]{1,0:T(8,128)(2,1)S(1)}, bf16[512,256]{1,0:T(8,128)(2,1)S(1)}, u32[]{:S(2)}, u32[]{:S(2)}) collective-permute-start(bf16[512,256]{1,0:T(8,128)(2,1)S(1)} %constant_dynamic-update-slice_fusion), channel_id=1, source_target_pairs={{0,12},{4,16},{8,20},{12,24},{16,28},{20,32},{24,36},{28,40},{32,4... | collective-permute-start | bytes 786440 | tf_op jit(solution)/shard_map/ppermute | solution.py:21
  19.9 31.6 %collective-permute-start.3 = (bf16[128,4096]{1,0:T(8,128)(2,1)}, bf16[128,4096]{1,0:T(8,128)(2,1)}, u32[]{:S(2)}, u32[]{:S(2)}) collective-permute-start(bf16[128,4096]{1,0:T(8,128)(2,1)} %param.11), channel_id=1, source_target_pairs={{0,2},{2,0},{1,3},{3,1},{4,6},{6,4},{5,7},{7,5},{8,10},{10,8},{9,1... | collective-permute-start | bytes 3145736 | tf_op jit(solution)/shard_map/ppermute | solution.py:30
  33.4 48.6 %copy-start.7 = (bf16[2048,256]{1,0:T(8,128)(2,1)}, bf16[2048,256]{1,0:T(8,128)(2,1)S(1)}, u32[]{:S(2)}) copy-start(bf16[2048,256]{1,0:T(8,128)(2,1)S(1)} %pad_maximum_fusion.3) | copy-start | bytes 3145732
  33.4 18.1 %copy-start.9 = (bf16[128,4096]{1,0:T(8,128)(2,1)S(1)}, bf16[128,4096]{1,0:T(8,128)(2,1)}, u32[]{:S(2)}) copy-start(bf16[128,4096]{1,0:T(8,128)(2,1)} %param.11) | copy-start | bytes 3145732
  37.9 20.6 %copy-start.2 = (f32[2048,512,4]{1,0,2:T(8,128)}, f32[2048,512,4]{1,0,2:T(8,128)S(1)}, u32[]{:S(2)}) copy-start(f32[2048,512,4]{1,0,2:T(8,128)S(1)} %get-tuple-element.31) | copy-start | bytes 50331652
  54.4 8.8 %collective-permute-start.4 = (bf16[2,128,4096]{2,1,0:T(8,128)(2,1)}, bf16[2,128,4096]{2,1,0:T(8,128)(2,1)}, u32[]{:S(2)}, u32[]{:S(2)}) collective-permute-start(bf16[2,128,4096]{2,1,0:T(8,128)(2,1)} %pad_maximum_fusion.2), channel_id=1, source_target_pairs={{0,1},{1,0},{2,3},{3,2},{4,5},{5,4},{6,7},{7,6},{8,9},{9,8},{10,11... | collective-permute-start | bytes 6291464 | tf_op jit(solution)/shard_map/ppermute | solution.py:30
  71.8 6.9 %copy-start.6 = (bf16[2,2,128,4096]{3,2,0,1:T(8,128)(2,1)S(1)}, bf16[2,2,128,4096]{3,2,0,1:T(8,128)(2,1)}, u32[]{:S(2)}) copy-start(bf16[2,2,128,4096]{3,2,0,1:T(8,128)(2,1)} %copy-done.5) | copy-start | bytes 12582916
  78.2 30.9 %collective-permute-start.5 = (bf16[2,128,4096]{2,1,0:T(8,128)(2,1)}, bf16[2,128,4096]{2,1,0:T(8,128)(2,1)}, u32[]{:S(2)}, u32[]{:S(2)}) collective-permute-start(bf16[2,128,4096]{2,1,0:T(8,128)(2,1)} %fusion.23), channel_id=1, source_target_pairs={{0,1},{1,0},{2,3},{3,2},{4,5},{5,4},{6,7},{7,6},{8,9},{9,8},{10,11... | collective-permute-start | bytes 6291464 | tf_op jit(solution)/shard_map/ppermute | solution.py:30
  81.9 12.1 %copy-start.11 = (bf16[512,512]{0,1:T(8,128)(2,1)}, bf16[512,512]{0,1:T(8,128)(2,1)S(1)}, u32[]{:S(2)}) copy-start(bf16[512,512]{0,1:T(8,128)(2,1)S(1)} %get-tuple-element.33) | copy-start | bytes 1572868
  82.0 12.1 %copy-start.10 = (bf16[512,512]{0,1:T(8,128)(2,1)S(1)}, bf16[512,512]{0,1:T(8,128)(2,1)}, u32[]{:S(2)}) copy-start(bf16[512,512]{0,1:T(8,128)(2,1)} %copy.50) | copy-start | bytes 1572868
  108.9 17.9 %slice-start = ((s8[8388608]{0:T(1024)(128)(4,1)}), s8[4194304]{0:T(1024)(128)(4,1)S(1)}, s32[]{:S(2)}) async-start(s8[8388608]{0:T(1024)(128)(4,1)} %bitcast.155), calls=%async_computation.3 | async-start | bytes 8388608
  109.1 17.8 %slice-start.1 = ((s8[8388608]{0:T(1024)(128)(4,1)}), s8[4194304]{0:T(1024)(128)(4,1)S(1)}, s32[]{:S(2)}) async-start(s8[8388608]{0:T(1024)(128)(4,1)} %bitcast.155), calls=%async_computation.4 | async-start | bytes 8388608
  109.1 17.8 %copy-start.8 = (bf16[2048,256]{1,0:T(8,128)(2,1)S(1)}, bf16[2048,256]{1,0:T(8,128)(2,1)}, u32[]{:S(2)}) copy-start(bf16[2048,256]{1,0:T(8,128)(2,1)} %copy-done.7) | copy-start | bytes 3145732
  111.5 16.8 %copy-start.3 = (f32[2,128,4096]{2,1,0:T(8,128)}, f32[2,128,4096]{2,1,0:T(8,128)S(1)}, u32[]{:S(2)}) copy-start(f32[2,128,4096]{2,1,0:T(8,128)S(1)} %bitcast_add_fusion) | copy-start | bytes 12582916
  112.6 47.5 %collective-permute-start.6 = (bf16[128,4096]{1,0:T(8,128)(2,1)}, bf16[128,4096]{1,0:T(8,128)(2,1)}, u32[]{:S(2)}, u32[]{:S(2)}) collective-permute-start(bf16[128,4096]{1,0:T(8,128)(2,1)} %fusion.28), channel_id=1, source_target_pairs={{0,2},{2,0},{1,3},{3,1},{4,6},{6,4},{5,7},{7,5},{8,10},{10,8},{9,1... | collective-permute-start | bytes 3145736 | tf_op jit(solution)/shard_map/ppermute | solution.py:30
  116.4 35.0 %collective-permute-start.7 = (bf16[512,256]{0,1:T(8,128)(2,1)}, bf16[512,256]{0,1:T(8,128)(2,1)S(1)}, u32[]{:S(2)}, u32[]{:S(2)}) collective-permute-start(bf16[512,256]{0,1:T(8,128)(2,1)} %get-tuple-element.25), channel_id=1, source_target_pairs={{4,0},{8,4},{12,8},{16,12},{20,16},{24,20},{28,24},{32,28},{36,32}... | collective-permute-start | bytes 786440 | tf_op jit(solution)/shard_map/ppermute | solution.py:26
  119.8 31.7 %collective-permute-start.9 = (bf16[512,256]{0,1:T(8,128)(2,1)}, bf16[512,256]{0,1:T(8,128)(2,1)S(1)}, u32[]{:S(2)}, u32[]{:S(2)}) collective-permute-start(bf16[512,256]{0,1:T(8,128)(2,1)} %get-tuple-element.26), channel_id=1, source_target_pairs={{12,0},{16,4},{20,8},{24,12},{28,16},{32,20},{36,24},{40,28},{44,3... | collective-permute-start | bytes 786440 | tf_op jit(solution)/shard_map/ppermute | solution.py:26
  122.9 28.5 %collective-permute-start.8 = (bf16[512,256]{0,1:T(8,128)(2,1)}, bf16[512,256]{0,1:T(8,128)(2,1)S(1)}, u32[]{:S(2)}, u32[]{:S(2)}) collective-permute-start(bf16[512,256]{0,1:T(8,128)(2,1)} %get-tuple-element.27), channel_id=1, source_target_pairs={{8,0},{12,4},{16,8},{20,12},{24,16},{28,20},{32,24},{36,28},{40,32... | collective-permute-start | bytes 786440 | tf_op jit(solution)/shard_map/ppermute | solution.py:26
  151.5 18.6 %copy-start.1 = (s32[256]{0:T(256)S(1)}, s32[256]{0:T(256)}, u32[]{:S(2)}) copy-start(s32[256]{0:T(256)} %param.13) | copy-start | bytes 3076
  155.2 14.0 %all-to-all-start = ((bf16[8,512,64]{1,2,0:T(8,128)(2,1)}), bf16[8,512,64]{1,2,0:T(8,128)(2,1)S(1)}, u32[]{:S(2)}, u32[]{:S(2)}) async-start(bf16[8,512,64]{1,2,0:T(8,128)(2,1)} %bitcast.45), calls=%async_computation.1 | async-start | bytes 1048576 | tf_op jit(solution)/shard_map/all_to_all | solution.py:122
  (2 other events, 4.9 us)
Sparse Core Ops, SparseCore 0:
  71.9 56.5 reduce-scatter.1

commit v5 on v4

--- a/solution.py
+++ b/solution.py
@@ -36,12 +36,13 @@
     return jnp.stack([first, second])
 
 
-def gathered_over_tp(piece):
+def gathered_over_tp(piece, after):
     high = lax.axis_index(TP[0])
     low = lax.axis_index(TP[1])
-    by_high = in_order(piece, swapped(piece, TP[0]), high)
+    other, after = lax.optimization_barrier((swapped(piece, TP[0]), after))
+    by_high = in_order(piece, other, high)
     both = in_order(by_high, swapped(by_high, TP[1]), low)
-    return jnp.transpose(both, (1, 0, 2, 3)).reshape(-1, piece.shape[1])
+    return jnp.transpose(both, (1, 0, 2, 3)).reshape(-1, piece.shape[1]), after
 
 
 def summed_over_tp(part):
@@ -68,8 +69,6 @@
     span = REACH * tokens_here
     key_count = span + tokens_here
 
-    grad_piece = gathered_over_tp(out_grad)
-
     own_pair = jnp.concatenate([key_rows, value_rows], axis=1)
     earlier = [from_earlier(own_pair, distance, ctx_count) for distance in range(REACH, 0, -1)]
     pairs_all = jnp.concatenate(earlier + [own_pair], axis=0)
@@ -108,6 +107,7 @@
     attn_four = summed / jnp.transpose(total, (2, 0, 1))[..., None]
     attn = attn_four.reshape(tokens_here, -1).astype(jnp.bfloat16)
     log_sum = row_max + jnp.log(total)
+    grad_piece, attn = gathered_over_tp(out_grad, attn)
 
     weight_part = lax.dot_general(
         attn, grad_piece, (((0,), (0,)), ((), ())), preferred_element_type=jnp.float32
@@ -142,23 +142,31 @@
         "qcgd,kcd->cgqk", grad_four, value_heads, preferred_element_type=jnp.float32
     )
     d_scores = (probs * (d_probs - delta_rows[..., None]) * score_scale).astype(jnp.bfloat16)
+    probs_half = probs.astype(jnp.bfloat16)
+
+    def key_side(score_part, prob_part):
+        key_part = jnp.einsum(
+            "cgqk,qcgd->kcd", score_part, query_four, preferred_element_type=jnp.float32
+        )
+        value_part = jnp.einsum(
+            "cgqk,qcgd->kcd", prob_part, grad_four, preferred_element_type=jnp.float32
+        )
+        rows = score_part.shape[-1]
+        return jnp.concatenate(
+            [key_part.reshape(rows, kv_width), value_part.reshape(rows, kv_width)], axis=1
+        )
+
+    early_grad = key_side(d_scores[..., :span], probs_half[..., :span]).astype(jnp.bfloat16)
+    early_grad, d_scores, probs_half = lax.optimization_barrier((early_grad, d_scores, probs_half))
+    returned = []
+    for distance in range(1, REACH + 1):
+        lo = span - distance * tokens_here
+        returned.append(to_earlier(early_grad[lo : lo + tokens_here], distance, ctx_count))
     query_grad = jnp.einsum(
         "cgqk,kcd->qcgd", d_scores, key_heads, preferred_element_type=jnp.float32
     )
-    key_grad_all = jnp.einsum(
-        "cgqk,qcgd->kcd", d_scores, query_four, preferred_element_type=jnp.float32
-    ).reshape(key_count, kv_width)
-    value_grad_all = jnp.einsum(
-        "cgqk,qcgd->kcd", probs.astype(jnp.bfloat16), grad_four, preferred_element_type=jnp.float32
-    ).reshape(key_count, kv_width)
-
-    pair_grad_all = jnp.concatenate([key_grad_all, value_grad_all], axis=1)
-    pair_grad = pair_grad_all[span:]
-    for distance in range(1, REACH + 1):
-        lo = span - distance * tokens_here
-        sent = to_earlier(
-            pair_grad_all[lo : lo + tokens_here].astype(jnp.bfloat16), distance, ctx_count
-        )
+    pair_grad = key_side(d_scores[..., span:], probs_half[..., span:])
+    for sent in returned:
         pair_grad = pair_grad + sent.astype(jnp.float32)
     key_grad = pair_grad[:, :kv_width]
     value_grad = pair_grad[:, kv_width:]

time: 178 us -> 180 us (1.011)
  other arithmetic: 18.2 us -> 31 us
  waiting for transfers between devices: 45.9 us -> 36.5 us
  matrix products: 48.9 us -> 41.1 us
  local copies, waits for them, and re-layouts: 16.7 us -> 22.8 us
    convert_element_type x0 -> x1, other arithmetic: none -> 10.8 us  [on_device(): probs_half = probs.astype(jnp.bfloat16)]
    unnamed x32 -> x50, local copies, waits for them, and re-layouts: 6.25 us -> 14.3 us
    ppermute x4, waiting for transfers between devices: 13.6 us -> 7.38 us  [swapped(): return lax.ppermute(block, axis, [(0, 1), (1, 0)])]
    ppermute x3, waiting for transfers between devices: 22.3 us -> 18.3 us  [to_earlier(): return lax.ppermute(block, CTX, route)]
    dot_general x2 -> x4, matrix products: 14.9 us -> 11.5 us  [the longest x2 7.85 us: key_side(): jnp.einsum('cgqk,qcgd->kcd', prob_part, grad_four, preferred_element_type...]
    dot_general x1, matrix products: 12.1 us -> 9.47 us  [on_device(): jnp.einsum('qcgd,kcd->cgqk', grad_four, value_heads, preferred_element_ty...]
    dot_general x1, matrix products: 4.78 us -> 2.38 us  [on_device(): out_part = jnp.dot(attn, out_weight, preferred_element_type=jnp.float32)]
  transfers between devices with their start and end apart: 12 -> 12, of which waited for: 4 -> 5; matrix products, arithmetic and copies ran while one was open for 39% -> 40% of each run, Pallas kernels for 0% -> 0%
where the time goes in v5:
time: 180 us; the launch traced here: 179 us
  matrix products  41.1 us (23%)
  waiting for transfers between devices  36.5 us (20%)
  starting transfers between devices  33.1 us (18%)
  other arithmetic  31 us (17%)
  local copies, waits for them, and re-layouts  22.8 us (13%)
  between operations  14.4 us (8%)
    ppermute x3, waiting for transfers between devices, to_earlier(): return lax.ppermute(block, CTX, route)  18.3 us
    unnamed x50, local copies, waits for them, and re-layouts  14.3 us
    ppermute x3, starting transfers between devices, to_earlier(): return lax.ppermute(block, CTX, route)  11.3 us
    convert_element_type x1, other arithmetic, on_device(): probs_half = probs.astype(jnp.bfloat16)  10.8 us
    ppermute x3, starting transfers between devices, from_earlier(): return lax.ppermute(block, CTX, route)  10.8 us
    dot_general x1, matrix products, on_device(): jnp.einsum('qcgd,kcd->cgqk', grad_four, value_heads, preferred_element_ty...  9.47 us
    dot_general x2, matrix products, key_side(): jnp.einsum('cgqk,qcgd->kcd', prob_part, grad_four, preferred_element_type...  7.85 us
    ppermute x4, waiting for transfers between devices, swapped(): return lax.ppermute(block, axis, [(0, 1), (1, 0)])  7.38 us
  transfers between devices with their start and end apart: 12, of which 5 were waited for; matrix products, arithmetic and copies ran while one was open for 40% of the time, Pallas kernels for 0%

profile of v5, /device:TPU:96, one launch (start us, length us, event | category | flops | bytes accessed | tf_op | source)
XLA Modules:
  0.0 178.9 jit_solution(3108560571948670618)
XLA Ops:
  9.1 3.5 %collective-permute-start.3 = (bf16[512,256]{1,0:T(8,128)(2,1)S(1)}, bf16[512,256]{1,0:T(8,128)(2,1)S(1)}, u32[]{:S(2)}, u32[]{:S(2)}) collective-permute-start(bf16[512,256]{1,0:T(8,128)(2,1)S(1)} %constant_dynamic-update-slice_fusion), channel_id=1, source_target_pairs={{0,4},{4,8},{8,12},{12,16},{16,20},{20,24},{24,28},{28,32},{32,36}... | collective-permute-start | bytes 786440 | tf_op jit(solution)/shard_map/ppermute | solution.py:21
  12.6 3.4 %collective-permute-start.2 = (bf16[512,256]{1,0:T(8,128)(2,1)S(1)}, bf16[512,256]{1,0:T(8,128)(2,1)S(1)}, u32[]{:S(2)}, u32[]{:S(2)}) collective-permute-start(bf16[512,256]{1,0:T(8,128)(2,1)S(1)} %constant_dynamic-update-slice_fusion), channel_id=1, source_target_pairs={{0,8},{4,12},{8,16},{12,20},{16,24},{20,28},{24,32},{28,36},{32,40... | collective-permute-start | bytes 786440 | tf_op jit(solution)/shard_map/ppermute | solution.py:21
  16.0 3.9 %collective-permute-start.1 = (bf16[512,256]{1,0:T(8,128)(2,1)S(1)}, bf16[512,256]{1,0:T(8,128)(2,1)}, u32[]{:S(2)}, u32[]{:S(2)}) collective-permute-start(bf16[512,256]{1,0:T(8,128)(2,1)S(1)} %constant_dynamic-update-slice_fusion), channel_id=1, source_target_pairs={{0,12},{4,16},{8,20},{12,24},{16,28},{20,32},{24,36},{28,40},{32,4... | collective-permute-start | bytes 786440 | tf_op jit(solution)/shard_map/ppermute | solution.py:21
  19.9 3.3 %collective-permute-start = (bf16[128,4096]{1,0:T(8,128)(2,1)}, bf16[128,4096]{1,0:T(8,128)(2,1)S(1)}, u32[]{:S(2)}, u32[]{:S(2)}) collective-permute-start(bf16[128,4096]{1,0:T(8,128)(2,1)} %param.11), channel_id=1, source_target_pairs={{0,2},{2,0},{1,3},{3,1},{4,6},{6,4},{5,7},{7,5},{8,10},{10,8},{9,1... | collective-permute-start | bytes 3145736 | tf_op jit(solution)/shard_map/ppermute | solution.py:30
  28.6 4.8 %collective-permute-done.1 = bf16[512,256]{1,0:T(8,128)(2,1)} collective-permute-done((bf16[512,256]{1,0:T(8,128)(2,1)S(1)}, bf16[512,256]{1,0:T(8,128)(2,1)}, u32[]{:S(2)}, u32[]{:S(2)}) %collective-permute-start.1) | collective-permute-done | bytes 262176 | tf_op jit(solution)/shard_map/ppermute | solution.py:21
  34.4 3.1 %fusion.5 = (f32[4,512]{1,0:T(4,128)S(1)}, f32[2048,512,4]{1,0,2:T(8,128)S(1)}) fusion(pred[512,2048]{0,1:T(8,128)(4,1)S(1)} %fusion.17, bf16[512,4,128]{0,2,1:T(8,128)(2,1)S(1)} %bitcast.196, bf16[2048,256]{1,0:T(8,128)(2,1)S(1)} %pad_maximum_fusion.2), kind=kOutput, calls=%fused_computation.9 | convolution fusion | flops 1086322688 | bytes 18882560 | tf_op jit(solution)/shard_map/qcgd,kcd->cgqk/dot_general | solution.py:97
  37.6 4.2 %fusion.7 = f32[4,512]{1,0:T(4,128)S(1)} fusion(f32[2048,512,4]{1,0,2:T(8,128)S(1)} %get-tuple-element.41, f32[4,512]{1,0:T(4,128)S(1)} %get-tuple-element.40, pred[512,2048]{0,1:T(8,128)(4,1)S(1)} %fusion.17), kind=kLoop, calls=%fused_computation.11 | loop fusion | flops 20969472 | bytes 17842176 | tf_op jit(solution)/shard_map/reduce_sum | solution.py:103
  43.3 5.2 %divide_convert_fusion = bf16[512,1,4,128]{0,3,2,1:T(8,128)(2,1)} fusion(f32[2048,512,4]{1,0,2:T(8,128)S(1)} %get-tuple-element.41, f32[4,512]{1,0:T(4,128)S(1)} %get-tuple-element.40, pred[512,2048]{0,1:T(8,128)(4,1)S(1)} %fusion.17, f32[512,4]{0,1:T(4,128)S(1)} %bitcast.199, bf16[2048,256]{1,0:T(8,128)(2,1)S(1)} %pad_maximum_fusion.2), kind=kOutput, calls=%fused_computation.58 | convolution fusion | flops 1095237632 | bytes 18890752 | tf_op jit(solution)/shard_map/cgqk,kcd->qcgd/dot_general | solution.py:104
  48.5 2.9 %collective-permute-done = bf16[128,4096]{1,0:T(8,128)(2,1)S(1)} collective-permute-done((bf16[128,4096]{1,0:T(8,128)(2,1)}, bf16[128,4096]{1,0:T(8,128)(2,1)S(1)}, u32[]{:S(2)}, u32[]{:S(2)}) %collective-permute-start) | collective-permute-done | bytes 1048608 | tf_op jit(solution)/shard_map/ppermute | solution.py:30
  55.3 4.5 %collective-permute-done.4 = bf16[2,128,4096]{2,1,0:T(8,128)(2,1)} collective-permute-done((bf16[2,128,4096]{2,1,0:T(8,128)(2,1)}, bf16[2,128,4096]{2,1,0:T(8,128)(2,1)}, u32[]{:S(2)}, u32[]{:S(2)}) %collective-permute-start.4) | collective-permute-done | bytes 2097184 | tf_op jit(solution)/shard_map/ppermute | solution.py:30
  64.3 4.4 %convolution_convert_fusion = bf16[512,4096]{1,0:T(8,128)(2,1)} fusion(bf16[512,512]{0,1:T(8,128)(2,1)S(1)} %bitcast.193, bf16[512,4096]{1,0:T(8,128)(2,1)S(1)} %bitcast.190), kind=kOutput, calls=%fused_computation.22 | convolution fusion | flops 2149580800 | bytes 8912896 | tf_op jit(solution)/shard_map/dot_general | solution.py:112
  68.8 10.8 %fusion.6 = bf16[1,4,512,2048]{2,3,1,0:T(8,128)(2,1)} fusion(f32[2048,512,4]{1,0,2:T(8,128)} %copy-done.2, f32[4,512]{1,0:T(4,128)S(1)} %log_add_fusion, pred[512,2048]{0,1:T(8,128)(4,1)S(1)} %fusion.17), kind=kLoop, calls=%fused_computation.10 | loop fusion | flops 16777216 | bytes 26222592 | tf_op jit(solution)/shard_map/convert_element_type | solution.py:145
  83.8 3.8 %bitcast_reduce_fusion = (f32[512,4]{0,1:T(4,128)}, bf16[512,512]{0,1:T(8,128)(2,1)}) fusion(bf16[512,512]{0,1:T(8,128)(2,1)S(1)} %bitcast.195, bf16[512,4096]{1,0:T(8,128)(2,1)S(1)} %bitcast.191, bf16[512,4096]{1,0:T(8,128)(2,1)S(1)} %copy-done.6), kind=kOutput, calls=%fused_computation.53 | convolution fusion | flops 2148792320 | bytes 9445376 | tf_op jit(solution)/shard_map/dot_general | solution.py:127
  91.4 9.5 %fusion.2 = bf16[1,4,512,2048]{2,3,1,0:T(8,128)(2,1)} fusion(f32[2048,512,4]{1,0,2:T(8,128)S(1)} %bitcast.185, f32[4,512]{1,0:T(4,128)} %bitcast.203, f32[4,512]{1,0:T(4,128)S(1)} %log_add_fusion, pred[512,2048]{0,1:T(8,128)(4,1)S(1)} %fusion.17, bf16[512,4,128]{0,2,1:T(8,128)(2,1)} %bitcast.200, bf16[2048,256]{1,0:T(8,128)(2,1)} %copy-done.9), kind=kOutput, calls=%fused_computation.3 | convolution fusion | flops 1103101952 | bytes 27279360 | tf_op jit(solution)/shard_map/qcgd,kcd->cgqk/dot_general | solution.py:141
  100.9 5.3 %fusion.22 = bf16[1536,128]{0,1:T(8,128)(2,1)S(1)} fusion(bf16[512,4,128]{0,2,1:T(8,128)(2,1)} %bitcast.201, bf16[1,4,512,2048]{2,3,1,0:T(8,128)(2,1)} %fusion.6), kind=kOutput, calls=%fused_computation.32 | convolution fusion | flops 805502976 | bytes 7208960 | tf_op jit(solution)/shard_map/cgqk,qcgd->kcd/dot_general | solution.py:151
  114.6 3.0 %collective-permute-start.6 = (bf16[128,4096]{1,0:T(8,128)(2,1)S(1)}, bf16[128,4096]{1,0:T(8,128)(2,1)S(1)}, u32[]{:S(2)}, u32[]{:S(2)}) collective-permute-start(bf16[128,4096]{1,0:T(8,128)(2,1)S(1)} %fusion.43), channel_id=1, source_target_pairs={{0,2},{2,0},{1,3},{3,1},{4,6},{6,4},{5,7},{7,5},{8,10},{10,8},{9,1... | collective-permute-start | bytes 3145736 | tf_op jit(solution)/shard_map/ppermute | solution.py:30
  118.3 3.5 %collective-permute-start.7 = (bf16[512,256]{0,1:T(8,128)(2,1)}, bf16[512,256]{0,1:T(8,128)(2,1)S(1)}, u32[]{:S(2)}, u32[]{:S(2)}) collective-permute-start(bf16[512,256]{0,1:T(8,128)(2,1)} %get-tuple-element.35), channel_id=1, source_target_pairs={{4,0},{8,4},{12,8},{16,12},{20,16},{24,20},{28,24},{32,28},{36,32}... | collective-permute-start | bytes 786440 | tf_op jit(solution)/shard_map/ppermute | solution.py:26
  121.8 3.4 %collective-permute-start.9 = (bf16[512,256]{0,1:T(8,128)(2,1)S(1)}, bf16[512,256]{0,1:T(8,128)(2,1)}, u32[]{:S(2)}, u32[]{:S(2)}) collective-permute-start(bf16[512,256]{0,1:T(8,128)(2,1)S(1)} %get-tuple-element.36), channel_id=1, source_target_pairs={{12,0},{16,4},{20,8},{24,12},{28,16},{32,20},{36,24},{40,28},{44,3... | collective-permute-start | bytes 786440 | tf_op jit(solution)/shard_map/ppermute | solution.py:26
  125.2 4.4 %collective-permute-start.8 = (bf16[512,256]{0,1:T(8,128)(2,1)S(1)}, bf16[512,256]{0,1:T(8,128)(2,1)}, u32[]{:S(2)}, u32[]{:S(2)}) collective-permute-start(bf16[512,256]{0,1:T(8,128)(2,1)S(1)} %get-tuple-element.37), channel_id=1, source_target_pairs={{8,0},{12,4},{16,8},{20,12},{24,16},{28,20},{32,24},{36,28},{40,32... | collective-permute-start | bytes 786440 | tf_op jit(solution)/shard_map/ppermute | solution.py:26
  132.2 2.6 %fusion.40 = f32[512,128]{0,1:T(8,128)S(1)} fusion(bf16[512,4,128]{0,2,1:T(8,128)(2,1)} %bitcast.202, bf16[1,4,512,2048]{2,3,1,0:T(8,128)(2,1)} %fusion.6), kind=kOutput, calls=%fused_computation.50 | convolution fusion | flops 268435456 | bytes 2883584 | tf_op jit(solution)/shard_map/cgqk,qcgd->kcd/dot_general | solution.py:151
  134.7 18.3 %collective-permute-done.7 = bf16[512,256]{0,1:T(8,128)(2,1)S(1)} collective-permute-done((bf16[512,256]{0,1:T(8,128)(2,1)}, bf16[512,256]{0,1:T(8,128)(2,1)S(1)}, u32[]{:S(2)}, u32[]{:S(2)}) %collective-permute-start.7) | collective-permute-done | bytes 262176 | tf_op jit(solution)/shard_map/ppermute | solution.py:26
  157.9 4.6 %all-to-all-start = ((bf16[8,512,64]{1,2,0:T(8,128)(2,1)}), bf16[8,512,64]{1,2,0:T(8,128)(2,1)S(1)}, u32[]{:S(2)}, u32[]{:S(2)}) async-start(bf16[8,512,64]{1,2,0:T(8,128)(2,1)} %bitcast.53), calls=%async_computation.1 | async-start | bytes 1048576 | tf_op jit(solution)/shard_map/all_to_all | solution.py:122
  162.5 2.8 %fusion.28 = bf16[128,4096]{1,0:T(8,128)(2,1)} fusion(bf16[128,4096]{1,0:T(8,128)(2,1)S(1)} %collective-permute-done.6, f32[2,128,4096]{2,1,0:T(8,128)} %copy-done.5, s32[]{:T(128)S(6)} %select_n.98), kind=kLoop, calls=%fused_computation.40 | loop fusion | flops 1572864 | bytes 4194308 | tf_op jit(solution)/shard_map/convert_element_type | solution.py:119
  165.3 6.0 %all-to-all-done = bf16[8,512,64]{1,2,0:T(8,128)(2,1)S(1)} async-done(((bf16[8,512,64]{1,2,0:T(8,128)(2,1)}), bf16[8,512,64]{1,2,0:T(8,128)(2,1)S(1)}, u32[]{:S(2)}, u32[]{:S(2)}) %all-to-all-start) | async-done | bytes 524320 | tf_op jit(solution)/shard_map/all_to_all | solution.py:122
  (93 shorter events, 43.5 us)
Async XLA Ops:
  7.2 16.1 %copy-start = (s32[256]{0:T(256)S(1)}, s32[256]{0:T(256)}, u32[]{:S(2)}) copy-start(s32[256]{0:T(256)} %param.13) | copy-start | bytes 3076
  7.2 148.7 %reduce-scatter.2.cloned.1.call-start = ((), (), s32[]{:S(2)}) async-start(), calls=%async_computation.2 | async-start | bytes 4718592 | tf_op jit(solution)/shard_map/reduce_scatter | solution.py:116
  9.1 19.5 %collective-permute-start.3 = (bf16[512,256]{1,0:T(8,128)(2,1)S(1)}, bf16[512,256]{1,0:T(8,128)(2,1)S(1)}, u32[]{:S(2)}, u32[]{:S(2)}) collective-permute-start(bf16[512,256]{1,0:T(8,128)(2,1)S(1)} %constant_dynamic-update-slice_fusion), channel_id=1, source_target_pairs={{0,4},{4,8},{8,12},{12,16},{16,20},{20,24},{24,28},{28,32},{32,36}... | collective-permute-start | bytes 786440 | tf_op jit(solution)/shard_map/ppermute | solution.py:21
  12.6 16.0 %collective-permute-start.2 = (bf16[512,256]{1,0:T(8,128)(2,1)S(1)}, bf16[512,256]{1,0:T(8,128)(2,1)S(1)}, u32[]{:S(2)}, u32[]{:S(2)}) collective-permute-start(bf16[512,256]{1,0:T(8,128)(2,1)S(1)} %constant_dynamic-update-slice_fusion), channel_id=1, source_target_pairs={{0,8},{4,12},{8,16},{12,20},{16,24},{20,28},{24,32},{28,36},{32,40... | collective-permute-start | bytes 786440 | tf_op jit(solution)/shard_map/ppermute | solution.py:21
  16.0 17.4 %collective-permute-start.1 = (bf16[512,256]{1,0:T(8,128)(2,1)S(1)}, bf16[512,256]{1,0:T(8,128)(2,1)}, u32[]{:S(2)}, u32[]{:S(2)}) collective-permute-start(bf16[512,256]{1,0:T(8,128)(2,1)S(1)} %constant_dynamic-update-slice_fusion), channel_id=1, source_target_pairs={{0,12},{4,16},{8,20},{12,24},{16,28},{20,32},{24,36},{28,40},{32,4... | collective-permute-start | bytes 786440 | tf_op jit(solution)/shard_map/ppermute | solution.py:21
  19.9 31.5 %collective-permute-start = (bf16[128,4096]{1,0:T(8,128)(2,1)}, bf16[128,4096]{1,0:T(8,128)(2,1)S(1)}, u32[]{:S(2)}, u32[]{:S(2)}) collective-permute-start(bf16[128,4096]{1,0:T(8,128)(2,1)} %param.11), channel_id=1, source_target_pairs={{0,2},{2,0},{1,3},{3,1},{4,6},{6,4},{5,7},{7,5},{8,10},{10,8},{9,1... | collective-permute-start | bytes 3145736 | tf_op jit(solution)/shard_map/ppermute | solution.py:30
  26.3 11.3 %copy-start.15 = (bf16[512,512]{0,1:T(8,128)(2,1)}, bf16[512,512]{0,1:T(8,128)(2,1)S(1)}, u32[]{:S(2)}) copy-start(bf16[512,512]{0,1:T(8,128)(2,1)S(1)} %copy.58) | copy-start | bytes 1572868
  34.4 7.3 %copy-start.9 = (bf16[2048,256]{1,0:T(8,128)(2,1)}, bf16[2048,256]{1,0:T(8,128)(2,1)S(1)}, u32[]{:S(2)}) copy-start(bf16[2048,256]{1,0:T(8,128)(2,1)S(1)} %pad_maximum_fusion.2) | copy-start | bytes 3145732
  37.5 5.8 %copy-start.2 = (f32[2048,512,4]{1,0,2:T(8,128)}, f32[2048,512,4]{1,0,2:T(8,128)S(1)}, u32[]{:S(2)}) copy-start(f32[2048,512,4]{1,0,2:T(8,128)S(1)} %get-tuple-element.41) | copy-start | bytes 50331652
  43.3 9.1 %copy-start.11 = (bf16[128,4096]{1,0:T(8,128)(2,1)S(1)}, bf16[128,4096]{1,0:T(8,128)(2,1)}, u32[]{:S(2)}) copy-start(bf16[128,4096]{1,0:T(8,128)(2,1)} %param.11) | copy-start | bytes 3145732
  55.3 4.5 %collective-permute-start.4 = (bf16[2,128,4096]{2,1,0:T(8,128)(2,1)}, bf16[2,128,4096]{2,1,0:T(8,128)(2,1)}, u32[]{:S(2)}, u32[]{:S(2)}) collective-permute-start(bf16[2,128,4096]{2,1,0:T(8,128)(2,1)} %pad_maximum_fusion.1), channel_id=1, source_target_pairs={{0,1},{1,0},{2,3},{3,2},{4,5},{5,4},{6,7},{7,6},{8,9},{9,8},{10,11... | collective-permute-start | bytes 6291464 | tf_op jit(solution)/shard_map/ppermute | solution.py:30
  68.7 10.9 %copy-start.6 = (bf16[512,4096]{1,0:T(8,128)(2,1)S(1)}, bf16[512,4096]{1,0:T(8,128)(2,1)}, u32[]{:S(2)}) copy-start(bf16[512,4096]{1,0:T(8,128)(2,1)} %param.10) | copy-start | bytes 12582916
  79.6 8.0 %slice-start = ((s8[16777216]{0:T(1024)(128)(4,1)}), s8[4194304]{0:T(1024)(128)(4,1)S(1)}, s32[]{:S(2)}) async-start(s8[16777216]{0:T(1024)(128)(4,1)} %bitcast.184), calls=%async_computation.3 | async-start | bytes 8388608
  79.6 9.2 %slice-start.1 = ((s8[16777216]{0:T(1024)(128)(4,1)}), s8[4194304]{0:T(1024)(128)(4,1)S(1)}, s32[]{:S(2)}) async-start(s8[16777216]{0:T(1024)(128)(4,1)} %bitcast.184), calls=%async_computation.4 | async-start | bytes 8388608
  83.7 6.5 %slice-start.2 = ((s8[16777216]{0:T(1024)(128)(4,1)}), s8[4194304]{0:T(1024)(128)(4,1)S(1)}, s32[]{:S(2)}) async-start(s8[16777216]{0:T(1024)(128)(4,1)} %bitcast.184), calls=%async_computation.5 | async-start | bytes 8388608
  83.7 7.8 %slice-start.3 = ((s8[16777216]{0:T(1024)(128)(4,1)}), s8[4194304]{0:T(1024)(128)(4,1)S(1)}, s32[]{:S(2)}) async-start(s8[16777216]{0:T(1024)(128)(4,1)} %bitcast.184), calls=%async_computation.6 | async-start | bytes 8388608
  83.7 26.3 %collective-permute-start.5 = (bf16[2,128,4096]{2,1,0:T(8,128)(2,1)}, bf16[2,128,4096]{2,1,0:T(8,128)(2,1)}, u32[]{:S(2)}, u32[]{:S(2)}) collective-permute-start(bf16[2,128,4096]{2,1,0:T(8,128)(2,1)} %fusion.23), channel_id=1, source_target_pairs={{0,1},{1,0},{2,3},{3,2},{4,5},{5,4},{6,7},{7,6},{8,9},{9,8},{10,11... | collective-permute-start | bytes 6291464 | tf_op jit(solution)/shard_map/ppermute | solution.py:30
  114.4 16.7 %copy-start.5 = (f32[2,128,4096]{2,1,0:T(8,128)}, f32[2,128,4096]{2,1,0:T(8,128)S(1)}, u32[]{:S(2)}) copy-start(f32[2,128,4096]{2,1,0:T(8,128)S(1)} %bitcast_add_fusion) | copy-start | bytes 12582916
  114.6 47.9 %collective-permute-start.6 = (bf16[128,4096]{1,0:T(8,128)(2,1)S(1)}, bf16[128,4096]{1,0:T(8,128)(2,1)S(1)}, u32[]{:S(2)}, u32[]{:S(2)}) collective-permute-start(bf16[128,4096]{1,0:T(8,128)(2,1)S(1)} %fusion.43), channel_id=1, source_target_pairs={{0,2},{2,0},{1,3},{3,1},{4,6},{6,4},{5,7},{7,5},{8,10},{10,8},{9,1... | collective-permute-start | bytes 3145736 | tf_op jit(solution)/shard_map/ppermute | solution.py:30
  118.3 34.7 %collective-permute-start.7 = (bf16[512,256]{0,1:T(8,128)(2,1)}, bf16[512,256]{0,1:T(8,128)(2,1)S(1)}, u32[]{:S(2)}, u32[]{:S(2)}) collective-permute-start(bf16[512,256]{0,1:T(8,128)(2,1)} %get-tuple-element.35), channel_id=1, source_target_pairs={{4,0},{8,4},{12,8},{16,12},{20,16},{24,20},{28,24},{32,28},{36,32}... | collective-permute-start | bytes 786440 | tf_op jit(solution)/shard_map/ppermute | solution.py:26
  121.8 31.2 %collective-permute-start.9 = (bf16[512,256]{0,1:T(8,128)(2,1)S(1)}, bf16[512,256]{0,1:T(8,128)(2,1)}, u32[]{:S(2)}, u32[]{:S(2)}) collective-permute-start(bf16[512,256]{0,1:T(8,128)(2,1)S(1)} %get-tuple-element.36), channel_id=1, source_target_pairs={{12,0},{16,4},{20,8},{24,12},{28,16},{32,20},{36,24},{40,28},{44,3... | collective-permute-start | bytes 786440 | tf_op jit(solution)/shard_map/ppermute | solution.py:26
  125.2 27.8 %collective-permute-start.8 = (bf16[512,256]{0,1:T(8,128)(2,1)S(1)}, bf16[512,256]{0,1:T(8,128)(2,1)}, u32[]{:S(2)}, u32[]{:S(2)}) collective-permute-start(bf16[512,256]{0,1:T(8,128)(2,1)S(1)} %get-tuple-element.37), channel_id=1, source_target_pairs={{8,0},{12,4},{16,8},{20,12},{24,16},{28,20},{32,24},{36,28},{40,32... | collective-permute-start | bytes 786440 | tf_op jit(solution)/shard_map/ppermute | solution.py:26
  131.2 40.9 %copy-start.1 = (s32[256]{0:T(256)S(1)}, s32[256]{0:T(256)}, u32[]{:S(2)}) copy-start(s32[256]{0:T(256)} %param.13) | copy-start | bytes 3076
  157.9 13.4 %all-to-all-start = ((bf16[8,512,64]{1,2,0:T(8,128)(2,1)}), bf16[8,512,64]{1,2,0:T(8,128)(2,1)S(1)}, u32[]{:S(2)}, u32[]{:S(2)}) async-start(bf16[8,512,64]{1,2,0:T(8,128)(2,1)} %bitcast.53), calls=%async_computation.1 | async-start | bytes 1048576 | tf_op jit(solution)/shard_map/all_to_all | solution.py:122
  (11 other events, 38.3 us)
Sparse Core Ops, SparseCore 0:
  68.9 55.2 reduce-scatter.1

commit v6 on v5

--- a/solution.py
+++ b/solution.py
@@ -54,7 +54,7 @@
     halves = kept + swapped(given.astype(jnp.bfloat16), TP[1]).astype(jnp.float32)
     kept = lax.dynamic_index_in_dim(halves, high, 0, keepdims=False)
     given = lax.dynamic_index_in_dim(halves, 1 - high, 0, keepdims=False)
-    return kept + swapped(given.astype(jnp.bfloat16), TP[0]).astype(jnp.float32)
+    return kept, swapped(given.astype(jnp.bfloat16), TP[0])
 
 
 def on_device(query_rows, key_rows, value_rows, out_weight, out_grad, doc_ids, window_blocks):
@@ -116,7 +116,7 @@
     weight_sum = lax.psum_scatter(weight_part, CTX[0], scatter_dimension=1, tiled=True)
 
     out_part = jnp.dot(attn, out_weight, preferred_element_type=jnp.float32)
-    layer_out = summed_over_tp(out_part).astype(jnp.bfloat16)
+    layer_kept, layer_received = summed_over_tp(out_part)
     rest_count = ctx_count // lax.axis_size(CTX[0])
     weight_cols = weight_sum.reshape(weight_sum.shape[0], rest_count, -1).transpose(1, 0, 2)
     weight_cols = lax.all_to_all(weight_cols, CTX[1:], 0, 0, tiled=True)
@@ -142,6 +142,8 @@
         "qcgd,kcd->cgqk", grad_four, value_heads, preferred_element_type=jnp.float32
     )
     d_scores = (probs * (d_probs - delta_rows[..., None]) * score_scale).astype(jnp.bfloat16)
+    layer_received, d_scores = lax.optimization_barrier((layer_received, d_scores))
+    layer_out = (layer_kept + layer_received.astype(jnp.float32)).astype(jnp.bfloat16)
     probs_half = probs.astype(jnp.bfloat16)
 
     def key_side(score_part, prob_part):

time: 180 us -> 184 us (1.022)
  matrix products: 41.1 us -> 49.7 us
  starting transfers between devices: 33.1 us -> 29.8 us
  other arithmetic: 31 us -> 28.2 us
    ppermute x3, waiting for transfers between devices: 18.3 us -> 0.01 us  [to_earlier(): return lax.ppermute(block, CTX, route)]
    ppermute x4, waiting for transfers between devices: 7.38 us -> 24.7 us  [swapped(): return lax.ppermute(block, axis, [(0, 1), (1, 0)])]
    dot_general x1, matrix products: 3.75 us -> 9.27 us  [on_device(): lax.dot_general(grad_piece, out_weight, (((1,), (1,)), ((), ())), preferr...]
    ppermute x4, starting transfers between devices: 6.37 us -> 4.07 us  [swapped(): return lax.ppermute(block, axis, [(0, 1), (1, 0)])]
    dot_general x1, matrix products: 2.38 us -> 4.65 us  [on_device(): out_part = jnp.dot(attn, out_weight, preferred_element_type=jnp.float32)]
    dot_general x2, matrix products: 3.65 us -> 5.77 us  [key_side(): jnp.einsum('cgqk,qcgd->kcd', score_part, query_four, preferred_element_ty...]
    unnamed x50 -> x56, local copies, waits for them, and re-layouts: 14.3 us -> 14.2 us
  transfers between devices with their start and end apart: 12 -> 12, of which waited for: 5 -> 5; matrix products, arithmetic and copies ran while one was open for 40% -> 39% of each run, Pallas kernels for 0% -> 0%
where the time goes in v6:
time: 184 us; the launch traced here: 183 us
  matrix products  49.7 us (27%)
  waiting for transfers between devices  37.4 us (20%)
  starting transfers between devices  29.8 us (16%)
  other arithmetic  28.2 us (15%)
  local copies, waits for them, and re-layouts  22.9 us (12%)
  between operations  14.6 us (8%)
    ppermute x4, waiting for transfers between devices, swapped(): return lax.ppermute(block, axis, [(0, 1), (1, 0)])  24.7 us
    unnamed x56, local copies, waits for them, and re-layouts  14.2 us
    ppermute x3, starting transfers between devices, from_earlier(): return lax.ppermute(block, CTX, route)  10.8 us
    ppermute x3, starting transfers between devices, to_earlier(): return lax.ppermute(block, CTX, route)  9.57 us
    dot_general x1, matrix products, on_device(): jnp.einsum('qcgd,kcd->cgqk', grad_four, value_heads, preferred_element_ty...  9.47 us
    convert_element_type x1, other arithmetic, on_device(): probs_half = probs.astype(jnp.bfloat16)  9.33 us
    dot_general x1, matrix products, on_device(): lax.dot_general(grad_piece, out_weight, (((1,), (1,)), ((), ())), preferr...  9.27 us
    all_to_all x1, waiting for transfers between devices, on_device(): weight_cols = lax.all_to_all(weight_cols, CTX[1:], 0, 0, tiled=True)  6.86 us
  transfers between devices with their start and end apart: 12, of which 5 were waited for; matrix products, arithmetic and copies ran while one was open for 39% of the time, Pallas kernels for 0%

profile of v6, /device:TPU:96, one launch (start us, length us, event | category | flops | bytes accessed | tf_op | source)
XLA Modules:
  0.0 182.5 jit_solution(12644729407409662495)
XLA Ops:
  9.1 4.4 %collective-permute-start.1 = (bf16[512,256]{1,0:T(8,128)(2,1)S(1)}, bf16[512,256]{1,0:T(8,128)(2,1)S(1)}, u32[]{:S(2)}, u32[]{:S(2)}) collective-permute-start(bf16[512,256]{1,0:T(8,128)(2,1)S(1)} %constant_dynamic-update-slice_fusion), channel_id=1, source_target_pairs={{0,12},{4,16},{8,20},{12,24},{16,28},{20,32},{24,36},{28,40},{32,4... | collective-permute-start | bytes 786440 | tf_op jit(solution)/shard_map/ppermute | solution.py:21
  13.5 3.4 %collective-permute-start.2 = (bf16[512,256]{1,0:T(8,128)(2,1)S(1)}, bf16[512,256]{1,0:T(8,128)(2,1)S(1)}, u32[]{:S(2)}, u32[]{:S(2)}) collective-permute-start(bf16[512,256]{1,0:T(8,128)(2,1)S(1)} %constant_dynamic-update-slice_fusion), channel_id=1, source_target_pairs={{0,8},{4,12},{8,16},{12,20},{16,24},{20,28},{24,32},{28,36},{32,40... | collective-permute-start | bytes 786440 | tf_op jit(solution)/shard_map/ppermute | solution.py:21
  16.9 3.0 %collective-permute-start.3 = (bf16[512,256]{1,0:T(8,128)(2,1)S(1)}, bf16[512,256]{1,0:T(8,128)(2,1)}, u32[]{:S(2)}, u32[]{:S(2)}) collective-permute-start(bf16[512,256]{1,0:T(8,128)(2,1)S(1)} %constant_dynamic-update-slice_fusion), channel_id=1, source_target_pairs={{0,4},{4,8},{8,12},{12,16},{16,20},{20,24},{24,28},{28,32},{32,36}... | collective-permute-start | bytes 786440 | tf_op jit(solution)/shard_map/ppermute | solution.py:21
  19.9 3.3 %collective-permute-start = (bf16[128,4096]{1,0:T(8,128)(2,1)}, bf16[128,4096]{1,0:T(8,128)(2,1)S(1)}, u32[]{:S(2)}, u32[]{:S(2)}) collective-permute-start(bf16[128,4096]{1,0:T(8,128)(2,1)} %param.11), channel_id=1, source_target_pairs={{0,2},{2,0},{1,3},{3,1},{4,6},{6,4},{5,7},{7,5},{8,10},{10,8},{9,1... | collective-permute-start | bytes 3145736 | tf_op jit(solution)/shard_map/ppermute | solution.py:30
  28.6 5.8 %collective-permute-done.3 = bf16[512,256]{1,0:T(8,128)(2,1)} collective-permute-done((bf16[512,256]{1,0:T(8,128)(2,1)S(1)}, bf16[512,256]{1,0:T(8,128)(2,1)}, u32[]{:S(2)}, u32[]{:S(2)}) %collective-permute-start.3) | collective-permute-done | bytes 262176 | tf_op jit(solution)/shard_map/ppermute | solution.py:21
  35.5 3.1 %fusion.5 = (f32[4,512]{1,0:T(4,128)S(1)}, f32[2048,512,4]{1,0,2:T(8,128)S(1)}) fusion(pred[512,2048]{0,1:T(8,128)(4,1)S(1)} %fusion.19, bf16[512,4,128]{0,2,1:T(8,128)(2,1)S(1)} %bitcast.196, bf16[2048,256]{1,0:T(8,128)(2,1)S(1)} %pad_maximum_fusion.2), kind=kOutput, calls=%fused_computation.9 | convolution fusion | flops 1086322688 | bytes 18882560 | tf_op jit(solution)/shard_map/qcgd,kcd->cgqk/dot_general | solution.py:97
  38.6 4.2 %fusion.7 = f32[4,512]{1,0:T(4,128)S(1)} fusion(f32[2048,512,4]{1,0,2:T(8,128)S(1)} %get-tuple-element.45, f32[4,512]{1,0:T(4,128)S(1)} %get-tuple-element.44, pred[512,2048]{0,1:T(8,128)(4,1)S(1)} %fusion.19), kind=kLoop, calls=%fused_computation.11 | loop fusion | flops 20969472 | bytes 17842176 | tf_op jit(solution)/shard_map/reduce_sum | solution.py:103
  44.3 5.2 %divide_convert_fusion = bf16[512,1,4,128]{0,3,2,1:T(8,128)(2,1)} fusion(f32[2048,512,4]{1,0,2:T(8,128)S(1)} %get-tuple-element.45, f32[4,512]{1,0:T(4,128)S(1)} %get-tuple-element.44, pred[512,2048]{0,1:T(8,128)(4,1)S(1)} %fusion.19, f32[512,4]{0,1:T(4,128)S(1)} %bitcast.199, bf16[2048,256]{1,0:T(8,128)(2,1)S(1)} %pad_maximum_fusion.2), kind=kOutput, calls=%fused_computation.59 | convolution fusion | flops 1095237632 | bytes 18890752 | tf_op jit(solution)/shard_map/cgqk,kcd->qcgd/dot_general | solution.py:104
  49.5 3.0 %collective-permute-done = bf16[128,4096]{1,0:T(8,128)(2,1)S(1)} collective-permute-done((bf16[128,4096]{1,0:T(8,128)(2,1)}, bf16[128,4096]{1,0:T(8,128)(2,1)S(1)}, u32[]{:S(2)}, u32[]{:S(2)}) %collective-permute-start) | collective-permute-done | bytes 1048608 | tf_op jit(solution)/shard_map/ppermute | solution.py:30
  56.5 4.5 %collective-permute-done.4 = bf16[2,128,4096]{2,1,0:T(8,128)(2,1)} collective-permute-done((bf16[2,128,4096]{2,1,0:T(8,128)(2,1)}, bf16[2,128,4096]{2,1,0:T(8,128)(2,1)}, u32[]{:S(2)}, u32[]{:S(2)}) %collective-permute-start.4) | collective-permute-done | bytes 2097184 | tf_op jit(solution)/shard_map/ppermute | solution.py:30
  65.5 4.4 %convolution_convert_fusion = bf16[512,4096]{1,0:T(8,128)(2,1)} fusion(bf16[512,512]{0,1:T(8,128)(2,1)S(1)} %bitcast.193, bf16[512,4096]{1,0:T(8,128)(2,1)S(1)} %bitcast.190), kind=kOutput, calls=%fused_computation.23 | convolution fusion | flops 2149580800 | bytes 8912896 | tf_op jit(solution)/shard_map/dot_general | solution.py:112
  69.9 4.7 %fusion.68 = f32[512,4096]{1,0:T(8,128)S(1)} fusion(bf16[512,512]{0,1:T(8,128)(2,1)S(1)} %bitcast.194, bf16[512,4096]{1,0:T(8,128)(2,1)} %param.10), kind=kOutput, calls=%fused_computation.98 | convolution fusion | flops 2147483648 | bytes 13107200 | tf_op jit(solution)/shard_map/dot_general | solution.py:118
  74.6 3.2 %copy-done.3 = f32[512,4096]{1,0:T(8,128)} copy-done((f32[512,4096]{1,0:T(8,128)}, f32[512,4096]{1,0:T(8,128)S(1)}, u32[]{:S(2)}) %copy-start.3) | copy-done | bytes 8388632
  79.6 9.3 %fusion.6 = bf16[1,4,512,2048]{2,3,1,0:T(8,128)(2,1)S(1)} fusion(f32[2048,512,4]{1,0,2:T(8,128)} %copy-done.2, f32[4,512]{1,0:T(4,128)S(1)} %log_add_fusion, pred[512,2048]{0,1:T(8,128)(4,1)S(1)} %fusion.19), kind=kLoop, calls=%fused_computation.10 | loop fusion | flops 16777216 | bytes 26222592 | tf_op jit(solution)/shard_map/convert_element_type | solution.py:147
  89.1 9.3 %bitcast_reduce_fusion = (f32[512,4]{0,1:T(4,128)}, bf16[512,512]{0,1:T(8,128)(2,1)}) fusion(bf16[512,512]{0,1:T(8,128)(2,1)S(1)} %bitcast.195, bf16[512,4096]{1,0:T(8,128)(2,1)} %bitcast.191, bf16[512,4096]{1,0:T(8,128)(2,1)S(1)} %copy-done.8), kind=kOutput, calls=%fused_computation.54 | convolution fusion | flops 2148792320 | bytes 9445376 | tf_op jit(solution)/shard_map/dot_general | solution.py:127
  98.3 4.1 %fusion.28 = bf16[1536,128]{0,1:T(8,128)(2,1)} fusion(bf16[512,4,128]{0,2,1:T(8,128)(2,1)} %bitcast.200, bf16[1,4,512,2048]{2,3,1,0:T(8,128)(2,1)S(1)} %fusion.6), kind=kOutput, calls=%fused_computation.33 | convolution fusion | flops 805502976 | bytes 7208960 | tf_op jit(solution)/shard_map/cgqk,qcgd->kcd/dot_general | solution.py:153
  102.5 2.4 %bitcast_add_fusion = f32[2,128,4096]{2,1,0:T(8,128)S(1)} fusion(bf16[2,128,4096]{2,1,0:T(8,128)(2,1)} %collective-permute-done.5, f32[2,2,128,4096]{3,2,1,0:T(8,128)S(1)} %bitcast.189, s32[]{:T(128)S(6)} %select_n.96), kind=kLoop, calls=%fused_computation.26 | loop fusion | flops 2097152 | bytes 10485764 | tf_op jit(solution)/shard_map/add | solution.py:54
  108.7 9.5 %fusion.2 = bf16[1,4,512,2048]{2,3,1,0:T(8,128)(2,1)} fusion(f32[2048,512,4]{1,0,2:T(8,128)S(1)} %bitcast.185, f32[4,512]{1,0:T(4,128)} %bitcast.203, f32[4,512]{1,0:T(4,128)S(1)} %log_add_fusion, pred[512,2048]{0,1:T(8,128)(4,1)S(1)} %fusion.19, bf16[512,4,128]{0,2,1:T(8,128)(2,1)} %bitcast.201, bf16[2048,256]{1,0:T(8,128)(2,1)} %copy-done.10), kind=kOutput, calls=%fused_computation.3 | convolution fusion | flops 1103101952 | bytes 27279360 | tf_op jit(solution)/shard_map/qcgd,kcd->cgqk/dot_general | solution.py:141
  118.2 17.2 %collective-permute-done.6 = bf16[128,4096]{1,0:T(8,128)(2,1)} collective-permute-done((bf16[128,4096]{1,0:T(8,128)(2,1)}, bf16[128,4096]{1,0:T(8,128)(2,1)}, u32[]{:S(2)}, u32[]{:S(2)}) %collective-permute-start.6) | collective-permute-done | bytes 1048608 | tf_op jit(solution)/shard_map/ppermute | solution.py:30
  135.3 5.0 %fusion.25 = bf16[1536,128]{0,1:T(8,128)(2,1)S(1)} fusion(bf16[512,4,128]{0,2,1:T(8,128)(2,1)} %bitcast.197, bf16[1,4,512,2048]{2,3,1,0:T(8,128)(2,1)} %fusion.2), kind=kOutput, calls=%fused_computation.32 | convolution fusion | flops 805502976 | bytes 7208960 | tf_op jit(solution)/shard_map/cgqk,qcgd->kcd/dot_general | solution.py:150
  140.5 4.8 %collective-permute-start.7 = (bf16[512,256]{0,1:T(8,128)(2,1)S(1)}, bf16[512,256]{0,1:T(8,128)(2,1)S(1)}, u32[]{:S(2)}, u32[]{:S(2)}) collective-permute-start(bf16[512,256]{0,1:T(8,128)(2,1)S(1)} %get-tuple-element.39), channel_id=1, source_target_pairs={{4,0},{8,4},{12,8},{16,12},{20,16},{24,20},{28,24},{32,28},{36,32}... | collective-permute-start | bytes 786440 | tf_op jit(solution)/shard_map/ppermute | solution.py:26
  150.8 2.5 %fusion.34 = bf16[128,4096]{1,0:T(8,128)(2,1)} fusion(bf16[128,4096]{1,0:T(8,128)(2,1)} %collective-permute-done.6, f32[2,128,4096]{2,1,0:T(8,128)S(1)} %copy-done.6, s32[]{:T(128)S(6)} %select_n.98), kind=kLoop, calls=%fused_computation.41 | loop fusion | flops 1572864 | bytes 4194308 | tf_op jit(solution)/shard_map/convert_element_type | solution.py:146
  161.0 5.3 %all-to-all-start = ((bf16[8,512,64]{1,2,0:T(8,128)(2,1)}), bf16[8,512,64]{1,2,0:T(8,128)(2,1)S(1)}, u32[]{:S(2)}, u32[]{:S(2)}) async-start(bf16[8,512,64]{1,2,0:T(8,128)(2,1)} %bitcast.53), calls=%async_computation.1 | async-start | bytes 1048576 | tf_op jit(solution)/shard_map/all_to_all | solution.py:122
  168.1 6.9 %all-to-all-done = bf16[8,512,64]{1,2,0:T(8,128)(2,1)S(1)} async-done(((bf16[8,512,64]{1,2,0:T(8,128)(2,1)}), bf16[8,512,64]{1,2,0:T(8,128)(2,1)S(1)}, u32[]{:S(2)}, u32[]{:S(2)}) %all-to-all-start) | async-done | bytes 524320 | tf_op jit(solution)/shard_map/all_to_all | solution.py:122
  (99 shorter events, 39.6 us)
Async XLA Ops:
  7.2 16.1 %copy-start = (s32[256]{0:T(256)S(1)}, s32[256]{0:T(256)}, u32[]{:S(2)}) copy-start(s32[256]{0:T(256)} %param.13) | copy-start | bytes 3076
  7.2 151.8 %reduce-scatter.2.cloned.1.call-start = ((), (), s32[]{:S(2)}) async-start(), calls=%async_computation.2 | async-start | bytes 4718592 | tf_op jit(solution)/shard_map/reduce_scatter | solution.py:116
  9.1 19.5 %collective-permute-start.1 = (bf16[512,256]{1,0:T(8,128)(2,1)S(1)}, bf16[512,256]{1,0:T(8,128)(2,1)S(1)}, u32[]{:S(2)}, u32[]{:S(2)}) collective-permute-start(bf16[512,256]{1,0:T(8,128)(2,1)S(1)} %constant_dynamic-update-slice_fusion), channel_id=1, source_target_pairs={{0,12},{4,16},{8,20},{12,24},{16,28},{20,32},{24,36},{28,40},{32,4... | collective-permute-start | bytes 786440 | tf_op jit(solution)/shard_map/ppermute | solution.py:21
  13.5 15.1 %collective-permute-start.2 = (bf16[512,256]{1,0:T(8,128)(2,1)S(1)}, bf16[512,256]{1,0:T(8,128)(2,1)S(1)}, u32[]{:S(2)}, u32[]{:S(2)}) collective-permute-start(bf16[512,256]{1,0:T(8,128)(2,1)S(1)} %constant_dynamic-update-slice_fusion), channel_id=1, source_target_pairs={{0,8},{4,12},{8,16},{12,20},{16,24},{20,28},{24,32},{28,36},{32,40... | collective-permute-start | bytes 786440 | tf_op jit(solution)/shard_map/ppermute | solution.py:21
  16.9 17.5 %collective-permute-start.3 = (bf16[512,256]{1,0:T(8,128)(2,1)S(1)}, bf16[512,256]{1,0:T(8,128)(2,1)}, u32[]{:S(2)}, u32[]{:S(2)}) collective-permute-start(bf16[512,256]{1,0:T(8,128)(2,1)S(1)} %constant_dynamic-update-slice_fusion), channel_id=1, source_target_pairs={{0,4},{4,8},{8,12},{12,16},{16,20},{20,24},{24,28},{28,32},{32,36}... | collective-permute-start | bytes 786440 | tf_op jit(solution)/shard_map/ppermute | solution.py:21
  19.9 32.7 %collective-permute-start = (bf16[128,4096]{1,0:T(8,128)(2,1)}, bf16[128,4096]{1,0:T(8,128)(2,1)S(1)}, u32[]{:S(2)}, u32[]{:S(2)}) collective-permute-start(bf16[128,4096]{1,0:T(8,128)(2,1)} %param.11), channel_id=1, source_target_pairs={{0,2},{2,0},{1,3},{3,1},{4,6},{6,4},{5,7},{7,5},{8,10},{10,8},{9,1... | collective-permute-start | bytes 3145736 | tf_op jit(solution)/shard_map/ppermute | solution.py:30
  26.2 12.3 %copy-start.16 = (bf16[512,512]{0,1:T(8,128)(2,1)}, bf16[512,512]{0,1:T(8,128)(2,1)S(1)}, u32[]{:S(2)}) copy-start(bf16[512,512]{0,1:T(8,128)(2,1)S(1)} %copy.58) | copy-start | bytes 1572868
  56.5 4.5 %collective-permute-start.4 = (bf16[2,128,4096]{2,1,0:T(8,128)(2,1)}, bf16[2,128,4096]{2,1,0:T(8,128)(2,1)}, u32[]{:S(2)}, u32[]{:S(2)}) collective-permute-start(bf16[2,128,4096]{2,1,0:T(8,128)(2,1)} %pad_maximum_fusion.1), channel_id=1, source_target_pairs={{0,1},{1,0},{2,3},{3,2},{4,5},{5,4},{6,7},{7,6},{8,9},{9,8},{10,11... | collective-permute-start | bytes 6291464 | tf_op jit(solution)/shard_map/ppermute | solution.py:30
  79.5 23.0 %collective-permute-start.5 = (bf16[2,128,4096]{2,1,0:T(8,128)(2,1)}, bf16[2,128,4096]{2,1,0:T(8,128)(2,1)}, u32[]{:S(2)}, u32[]{:S(2)}) collective-permute-start(bf16[2,128,4096]{2,1,0:T(8,128)(2,1)} %fusion.29), channel_id=1, source_target_pairs={{0,1},{1,0},{2,3},{3,2},{4,5},{5,4},{6,7},{7,6},{8,9},{9,8},{10,11... | collective-permute-start | bytes 6291464 | tf_op jit(solution)/shard_map/ppermute | solution.py:30
  79.6 22.8 %slice-start.4 = ((s8[8388608]{0:T(1024)(128)(4,1)}), s8[4194304]{0:T(1024)(128)(4,1)S(1)}, s32[]{:S(2)}) async-start(s8[8388608]{0:T(1024)(128)(4,1)} %bitcast.187), calls=%async_computation.7 | async-start | bytes 8388608
  89.0 13.4 %copy-start.7 = (bf16[1,4,512,2048]{2,3,1,0:T(8,128)(2,1)}, bf16[1,4,512,2048]{2,3,1,0:T(8,128)(2,1)S(1)}, u32[]{:S(2)}) copy-start(bf16[1,4,512,2048]{2,3,1,0:T(8,128)(2,1)S(1)} %fusion.6) | copy-start | bytes 25165828
  89.0 13.4 %slice-start.5 = ((s8[8388608]{0:T(1024)(128)(4,1)}), s8[4194304]{0:T(1024)(128)(4,1)S(1)}, s32[]{:S(2)}) async-start(s8[8388608]{0:T(1024)(128)(4,1)} %bitcast.187), calls=%async_computation.8 | async-start | bytes 8388608
  89.0 19.7 %slice-start = ((s8[16777216]{0:T(1024)(128)(4,1)}), s8[4194304]{0:T(1024)(128)(4,1)S(1)}, s32[]{:S(2)}) async-start(s8[16777216]{0:T(1024)(128)(4,1)} %bitcast.184), calls=%async_computation.3 | async-start | bytes 8388608
  89.0 19.6 %slice-start.1 = ((s8[16777216]{0:T(1024)(128)(4,1)}), s8[4194304]{0:T(1024)(128)(4,1)S(1)}, s32[]{:S(2)}) async-start(s8[16777216]{0:T(1024)(128)(4,1)} %bitcast.184), calls=%async_computation.4 | async-start | bytes 8388608
  89.0 19.6 %slice-start.2 = ((s8[16777216]{0:T(1024)(128)(4,1)}), s8[4194304]{0:T(1024)(128)(4,1)S(1)}, s32[]{:S(2)}) async-start(s8[16777216]{0:T(1024)(128)(4,1)} %bitcast.184), calls=%async_computation.5 | async-start | bytes 8388608
  108.0 27.3 %collective-permute-start.6 = (bf16[128,4096]{1,0:T(8,128)(2,1)}, bf16[128,4096]{1,0:T(8,128)(2,1)}, u32[]{:S(2)}, u32[]{:S(2)}) collective-permute-start(bf16[128,4096]{1,0:T(8,128)(2,1)} %fusion.49), channel_id=1, source_target_pairs={{0,2},{2,0},{1,3},{3,1},{4,6},{6,4},{5,7},{7,5},{8,10},{10,8},{9,1... | collective-permute-start | bytes 3145736 | tf_op jit(solution)/shard_map/ppermute | solution.py:30
  118.2 22.2 %copy-start.18 = (bf16[1536,128]{0,1:T(8,128)(2,1)S(1)}, bf16[1536,128]{0,1:T(8,128)(2,1)}, u32[]{:S(2)}) copy-start(bf16[1536,128]{0,1:T(8,128)(2,1)} %fusion.28) | copy-start | bytes 1179652
  118.2 29.6 %copy-start.4 = (bf16[1,4,512,2048]{2,3,1,0:T(8,128)(2,1)S(1)}, bf16[1,4,512,2048]{2,3,1,0:T(8,128)(2,1)}, u32[]{:S(2)}) copy-start(bf16[1,4,512,2048]{2,3,1,0:T(8,128)(2,1)} %fusion.2) | copy-start | bytes 25165828
  118.2 29.6 %copy-start.17 = (bf16[512,512]{0,1:T(8,128)(2,1)S(1)}, bf16[512,512]{0,1:T(8,128)(2,1)}, u32[]{:S(2)}) copy-start(bf16[512,512]{0,1:T(8,128)(2,1)} %copy-done.16) | copy-start | bytes 1572868
  140.5 25.9 %collective-permute-start.7 = (bf16[512,256]{0,1:T(8,128)(2,1)S(1)}, bf16[512,256]{0,1:T(8,128)(2,1)S(1)}, u32[]{:S(2)}, u32[]{:S(2)}) collective-permute-start(bf16[512,256]{0,1:T(8,128)(2,1)S(1)} %get-tuple-element.39), channel_id=1, source_target_pairs={{4,0},{8,4},{12,8},{16,12},{20,16},{24,20},{28,24},{32,28},{36,32}... | collective-permute-start | bytes 786440 | tf_op jit(solution)/shard_map/ppermute | solution.py:26
  145.3 21.1 %collective-permute-start.8 = (bf16[512,256]{0,1:T(8,128)(2,1)S(1)}, bf16[512,256]{0,1:T(8,128)(2,1)S(1)}, u32[]{:S(2)}, u32[]{:S(2)}) collective-permute-start(bf16[512,256]{0,1:T(8,128)(2,1)S(1)} %get-tuple-element.41), channel_id=1, source_target_pairs={{8,0},{12,4},{16,8},{20,12},{24,16},{28,20},{32,24},{36,28},{40,32... | collective-permute-start | bytes 786440 | tf_op jit(solution)/shard_map/ppermute | solution.py:26
  148.6 27.1 %copy-start.1 = (s32[256]{0:T(256)S(1)}, s32[256]{0:T(256)}, u32[]{:S(2)}) copy-start(s32[256]{0:T(256)} %param.13) | copy-start | bytes 3076
  153.2 13.2 %collective-permute-start.9 = (bf16[512,256]{0,1:T(8,128)(2,1)S(1)}, bf16[512,256]{0,1:T(8,128)(2,1)S(1)}, u32[]{:S(2)}, u32[]{:S(2)}) collective-permute-start(bf16[512,256]{0,1:T(8,128)(2,1)S(1)} %get-tuple-element.40), channel_id=1, source_target_pairs={{12,0},{16,4},{20,8},{24,12},{28,16},{32,20},{36,24},{40,28},{44,3... | collective-permute-start | bytes 786440 | tf_op jit(solution)/shard_map/ppermute | solution.py:26
  161.0 13.9 %all-to-all-start = ((bf16[8,512,64]{1,2,0:T(8,128)(2,1)}), bf16[8,512,64]{1,2,0:T(8,128)(2,1)S(1)}, u32[]{:S(2)}, u32[]{:S(2)}) async-start(bf16[8,512,64]{1,2,0:T(8,128)(2,1)} %bitcast.53), calls=%async_computation.1 | async-start | bytes 1048576 | tf_op jit(solution)/shard_map/all_to_all | solution.py:122
  (14 other events, 76.4 us)
Sparse Core Ops, SparseCore 0:
  79.7 54.7 reduce-scatter.1

commit v7 on v5

--- a/solution.py
+++ b/solution.py
@@ -166,6 +166,7 @@
         "cgqk,kcd->qcgd", d_scores, key_heads, preferred_element_type=jnp.float32
     )
     pair_grad = key_side(d_scores[..., span:], probs_half[..., span:])
+    returned, grad_weight = lax.optimization_barrier((returned, grad_weight))
     for sent in returned:
         pair_grad = pair_grad + sent.astype(jnp.float32)
     key_grad = pair_grad[:, :kv_width]

time: 180 us -> 168 us (0.933)
  waiting for transfers between devices: 36.5 us -> 25.7 us
  matrix products: 41.1 us -> 43.6 us
  local copies, waits for them, and re-layouts: 22.8 us -> 21 us
    ppermute x3, waiting for transfers between devices: 18.3 us -> 0.01 us  [to_earlier(): return lax.ppermute(block, CTX, route)]
    ppermute x4, waiting for transfers between devices: 7.38 us -> 21 us  [swapped(): return lax.ppermute(block, axis, [(0, 1), (1, 0)])]
    all_to_all x1, waiting for transfers between devices: 6.03 us -> 0.01 us  [on_device(): weight_cols = lax.all_to_all(weight_cols, CTX[1:], 0, 0, tiled=True)]
    dot_general x2, matrix products: 3.65 us -> 8.38 us  [key_side(): jnp.einsum('cgqk,qcgd->kcd', score_part, query_four, preferred_element_ty...]
    convert_element_type x1, other arithmetic: 10.8 us -> 8.4 us  [on_device(): probs_half = probs.astype(jnp.bfloat16)]
    unnamed x50 -> x54, local copies, waits for them, and re-layouts: 14.3 us -> 12.3 us
  transfers between devices with their start and end apart: 12 -> 12, of which waited for: 5 -> 4; matrix products, arithmetic and copies ran while one was open for 40% -> 43% of each run, Pallas kernels for 0% -> 0%
where the time goes in v7:
time: 168 us; the launch traced here: 166 us
  matrix products  43.6 us (26%)
  starting transfers between devices  31.9 us (19%)
  other arithmetic  29.3 us (17%)
  waiting for transfers between devices  25.7 us (15%)
  local copies, waits for them, and re-layouts  21 us (12%)
  between operations  14.5 us (9%)
    ppermute x4, waiting for transfers between devices, swapped(): return lax.ppermute(block, axis, [(0, 1), (1, 0)])  21 us
    unnamed x54, local copies, waits for them, and re-layouts  12.3 us
    ppermute x3, starting transfers between devices, from_earlier(): return lax.ppermute(block, CTX, route)  10.8 us
    ppermute x3, starting transfers between devices, to_earlier(): return lax.ppermute(block, CTX, route)  10.6 us
    dot_general x1, matrix products, on_device(): jnp.einsum('qcgd,kcd->cgqk', grad_four, value_heads, preferred_element_ty...  9.44 us
    convert_element_type x1, other arithmetic, on_device(): probs_half = probs.astype(jnp.bfloat16)  8.4 us
    dot_general x2, matrix products, key_side(): jnp.einsum('cgqk,qcgd->kcd', score_part, query_four, preferred_element_ty...  8.38 us
    ppermute x4, starting transfers between devices, swapped(): return lax.ppermute(block, axis, [(0, 1), (1, 0)])  6.4 us
  transfers between devices with their start and end apart: 12, of which 4 were waited for; matrix products, arithmetic and copies ran while one was open for 43% of the time, Pallas kernels for 0%

profile of v7, /device:TPU:96, one launch (start us, length us, event | category | flops | bytes accessed | tf_op | source)
XLA Modules:
  0.0 166.0 jit_solution(9137153790094784625)
XLA Ops:
  9.1 3.5 %collective-permute-start.3 = (bf16[512,256]{1,0:T(8,128)(2,1)S(1)}, bf16[512,256]{1,0:T(8,128)(2,1)S(1)}, u32[]{:S(2)}, u32[]{:S(2)}) collective-permute-start(bf16[512,256]{1,0:T(8,128)(2,1)S(1)} %constant_dynamic-update-slice_fusion), channel_id=1, source_target_pairs={{0,4},{4,8},{8,12},{12,16},{16,20},{20,24},{24,28},{28,32},{32,36}... | collective-permute-start | bytes 786440 | tf_op jit(solution)/shard_map/ppermute | solution.py:21
  12.6 3.4 %collective-permute-start.2 = (bf16[512,256]{1,0:T(8,128)(2,1)S(1)}, bf16[512,256]{1,0:T(8,128)(2,1)S(1)}, u32[]{:S(2)}, u32[]{:S(2)}) collective-permute-start(bf16[512,256]{1,0:T(8,128)(2,1)S(1)} %constant_dynamic-update-slice_fusion), channel_id=1, source_target_pairs={{0,8},{4,12},{8,16},{12,20},{16,24},{20,28},{24,32},{28,36},{32,40... | collective-permute-start | bytes 786440 | tf_op jit(solution)/shard_map/ppermute | solution.py:21
  16.0 3.9 %collective-permute-start.1 = (bf16[512,256]{1,0:T(8,128)(2,1)S(1)}, bf16[512,256]{1,0:T(8,128)(2,1)}, u32[]{:S(2)}, u32[]{:S(2)}) collective-permute-start(bf16[512,256]{1,0:T(8,128)(2,1)S(1)} %constant_dynamic-update-slice_fusion), channel_id=1, source_target_pairs={{0,12},{4,16},{8,20},{12,24},{16,28},{20,32},{24,36},{28,40},{32,4... | collective-permute-start | bytes 786440 | tf_op jit(solution)/shard_map/ppermute | solution.py:21
  19.9 3.3 %collective-permute-start = (bf16[128,4096]{1,0:T(8,128)(2,1)}, bf16[128,4096]{1,0:T(8,128)(2,1)S(1)}, u32[]{:S(2)}, u32[]{:S(2)}) collective-permute-start(bf16[128,4096]{1,0:T(8,128)(2,1)} %param.11), channel_id=1, source_target_pairs={{0,2},{2,0},{1,3},{3,1},{4,6},{6,4},{5,7},{7,5},{8,10},{10,8},{9,1... | collective-permute-start | bytes 3145736 | tf_op jit(solution)/shard_map/ppermute | solution.py:30
  28.6 4.8 %collective-permute-done.1 = bf16[512,256]{1,0:T(8,128)(2,1)} collective-permute-done((bf16[512,256]{1,0:T(8,128)(2,1)S(1)}, bf16[512,256]{1,0:T(8,128)(2,1)}, u32[]{:S(2)}, u32[]{:S(2)}) %collective-permute-start.1) | collective-permute-done | bytes 262176 | tf_op jit(solution)/shard_map/ppermute | solution.py:21
  34.4 3.1 %fusion.5 = (f32[4,512]{1,0:T(4,128)S(1)}, f32[2048,512,4]{1,0,2:T(8,128)S(1)}) fusion(pred[512,2048]{0,1:T(8,128)(4,1)S(1)} %fusion.17, bf16[512,4,128]{0,2,1:T(8,128)(2,1)S(1)} %bitcast.196, bf16[2048,256]{1,0:T(8,128)(2,1)S(1)} %pad_maximum_fusion.2), kind=kOutput, calls=%fused_computation.9 | convolution fusion | flops 1086322688 | bytes 18882560 | tf_op jit(solution)/shard_map/qcgd,kcd->cgqk/dot_general | solution.py:97
  37.6 4.2 %fusion.7 = f32[4,512]{1,0:T(4,128)S(1)} fusion(f32[2048,512,4]{1,0,2:T(8,128)S(1)} %get-tuple-element.49, f32[4,512]{1,0:T(4,128)S(1)} %get-tuple-element.48, pred[512,2048]{0,1:T(8,128)(4,1)S(1)} %fusion.17), kind=kLoop, calls=%fused_computation.11 | loop fusion | flops 20969472 | bytes 17842176 | tf_op jit(solution)/shard_map/reduce_sum | solution.py:103
  43.3 5.2 %divide_convert_fusion = bf16[512,1,4,128]{0,3,2,1:T(8,128)(2,1)} fusion(f32[2048,512,4]{1,0,2:T(8,128)S(1)} %get-tuple-element.49, f32[4,512]{1,0:T(4,128)S(1)} %get-tuple-element.48, pred[512,2048]{0,1:T(8,128)(4,1)S(1)} %fusion.17, f32[512,4]{0,1:T(4,128)S(1)} %bitcast.199, bf16[2048,256]{1,0:T(8,128)(2,1)S(1)} %pad_maximum_fusion.2), kind=kOutput, calls=%fused_computation.58 | convolution fusion | flops 1095237632 | bytes 18890752 | tf_op jit(solution)/shard_map/cgqk,kcd->qcgd/dot_general | solution.py:104
  48.5 2.9 %collective-permute-done = bf16[128,4096]{1,0:T(8,128)(2,1)S(1)} collective-permute-done((bf16[128,4096]{1,0:T(8,128)(2,1)}, bf16[128,4096]{1,0:T(8,128)(2,1)S(1)}, u32[]{:S(2)}, u32[]{:S(2)}) %collective-permute-start) | collective-permute-done | bytes 1048608 | tf_op jit(solution)/shard_map/ppermute | solution.py:30
  55.3 4.5 %collective-permute-done.4 = bf16[2,128,4096]{2,1,0:T(8,128)(2,1)} collective-permute-done((bf16[2,128,4096]{2,1,0:T(8,128)(2,1)}, bf16[2,128,4096]{2,1,0:T(8,128)(2,1)}, u32[]{:S(2)}, u32[]{:S(2)}) %collective-permute-start.4) | collective-permute-done | bytes 2097184 | tf_op jit(solution)/shard_map/ppermute | solution.py:30
  64.3 4.4 %convolution_convert_fusion = bf16[512,4096]{1,0:T(8,128)(2,1)} fusion(bf16[512,512]{0,1:T(8,128)(2,1)S(1)} %bitcast.193, bf16[512,4096]{1,0:T(8,128)(2,1)S(1)} %bitcast.190), kind=kOutput, calls=%fused_computation.22 | convolution fusion | flops 2149580800 | bytes 8912896 | tf_op jit(solution)/shard_map/dot_general | solution.py:112
  68.8 8.4 %fusion.6 = bf16[1,4,512,2048]{2,3,1,0:T(8,128)(2,1)S(1)} fusion(f32[2048,512,4]{1,0,2:T(8,128)} %copy-done.2, f32[4,512]{1,0:T(4,128)S(1)} %log_add_fusion, pred[512,2048]{0,1:T(8,128)(4,1)S(1)} %fusion.17), kind=kLoop, calls=%fused_computation.10 | loop fusion | flops 16777216 | bytes 26222592 | tf_op jit(solution)/shard_map/convert_element_type | solution.py:145
  82.5 3.2 %bitcast_reduce_fusion = (f32[512,4]{0,1:T(4,128)}, bf16[512,512]{0,1:T(8,128)(2,1)S(1)}) fusion(bf16[512,512]{0,1:T(8,128)(2,1)S(1)} %bitcast.195, bf16[512,4096]{1,0:T(8,128)(2,1)S(1)} %bitcast.191, bf16[512,4096]{1,0:T(8,128)(2,1)S(1)} %copy-done.7), kind=kOutput, calls=%fused_computation.53 | convolution fusion | flops 2148792320 | bytes 9445376 | tf_op jit(solution)/shard_map/dot_general | solution.py:127
  86.0 2.9 %fusion.22 = bf16[1536,128]{0,1:T(8,128)(2,1)} fusion(bf16[512,4,128]{0,2,1:T(8,128)(2,1)S(1)} %bitcast.200, bf16[1,4,512,2048]{2,3,1,0:T(8,128)(2,1)S(1)} %fusion.6), kind=kOutput, calls=%fused_computation.32 | convolution fusion | flops 805502976 | bytes 7208960 | tf_op jit(solution)/shard_map/cgqk,qcgd->kcd/dot_general | solution.py:151
  91.5 9.4 %fusion.2 = bf16[1,4,512,2048]{2,3,1,0:T(8,128)(2,1)} fusion(f32[2048,512,4]{1,0,2:T(8,128)S(1)} %bitcast.185, f32[4,512]{1,0:T(4,128)} %bitcast.203, f32[4,512]{1,0:T(4,128)S(1)} %log_add_fusion, pred[512,2048]{0,1:T(8,128)(4,1)S(1)} %fusion.17, bf16[512,4,128]{0,2,1:T(8,128)(2,1)} %bitcast.201, bf16[2048,256]{1,0:T(8,128)(2,1)} %copy-done.10), kind=kOutput, calls=%fused_computation.3 | convolution fusion | flops 1103101952 | bytes 27279360 | tf_op jit(solution)/shard_map/qcgd,kcd->cgqk/dot_general | solution.py:141
  101.0 5.2 %fusion.21 = bf16[1536,128]{0,1:T(8,128)(2,1)S(1)} fusion(bf16[512,4,128]{0,2,1:T(8,128)(2,1)} %bitcast.197, bf16[1,4,512,2048]{2,3,1,0:T(8,128)(2,1)} %fusion.2), kind=kOutput, calls=%fused_computation.31 | convolution fusion | flops 805502976 | bytes 7208960 | tf_op jit(solution)/shard_map/cgqk,qcgd->kcd/dot_general | solution.py:148
  106.6 3.1 %bitcast_add_fusion = f32[2,128,4096]{2,1,0:T(8,128)S(1)} fusion(bf16[2,128,4096]{2,1,0:T(8,128)(2,1)} %collective-permute-done.5, f32[2,2,128,4096]{3,2,1,0:T(8,128)S(1)} %bitcast.187, s32[]{:T(128)S(6)} %select_n.96), kind=kLoop, calls=%fused_computation.25 | loop fusion | flops 2097152 | bytes 10485764 | tf_op jit(solution)/shard_map/add | solution.py:54
  109.8 3.0 %collective-permute-start.6 = (bf16[128,4096]{1,0:T(8,128)(2,1)S(1)}, bf16[128,4096]{1,0:T(8,128)(2,1)S(1)}, u32[]{:S(2)}, u32[]{:S(2)}) collective-permute-start(bf16[128,4096]{1,0:T(8,128)(2,1)S(1)} %fusion.43), channel_id=1, source_target_pairs={{0,2},{2,0},{1,3},{3,1},{4,6},{6,4},{5,7},{7,5},{8,10},{10,8},{9,1... | collective-permute-start | bytes 3145736 | tf_op jit(solution)/shard_map/ppermute | solution.py:30
  116.1 4.7 %collective-permute-start.9 = (bf16[512,256]{0,1:T(8,128)(2,1)}, bf16[512,256]{0,1:T(8,128)(2,1)S(1)}, u32[]{:S(2)}, u32[]{:S(2)}) collective-permute-start(bf16[512,256]{0,1:T(8,128)(2,1)} %get-tuple-element.43), channel_id=1, source_target_pairs={{12,0},{16,4},{20,8},{24,12},{28,16},{32,20},{36,24},{40,28},{44,3... | collective-permute-start | bytes 786440 | tf_op jit(solution)/shard_map/ppermute | solution.py:26
  120.7 3.6 %collective-permute-start.8 = (bf16[512,256]{0,1:T(8,128)(2,1)}, bf16[512,256]{0,1:T(8,128)(2,1)S(1)}, u32[]{:S(2)}, u32[]{:S(2)}) collective-permute-start(bf16[512,256]{0,1:T(8,128)(2,1)} %get-tuple-element.44), channel_id=1, source_target_pairs={{8,0},{12,4},{16,8},{20,12},{24,16},{28,20},{32,24},{36,28},{40,32... | collective-permute-start | bytes 786440 | tf_op jit(solution)/shard_map/ppermute | solution.py:26
  126.7 3.3 %fusion.40 = f32[512,128]{0,1:T(8,128)} fusion(bf16[512,4,128]{0,2,1:T(8,128)(2,1)} %bitcast.202, bf16[1,4,512,2048]{2,3,1,0:T(8,128)(2,1)} %copy-done.6), kind=kOutput, calls=%fused_computation.50 | convolution fusion | flops 268435456 | bytes 2883584 | tf_op jit(solution)/shard_map/cgqk,qcgd->kcd/dot_general | solution.py:151
  130.0 3.2 %fusion.37 = f32[512,128]{0,1:T(8,128)} fusion(bf16[512,4,128]{0,2,1:T(8,128)(2,1)} %bitcast.198, bf16[1,4,512,2048]{2,3,1,0:T(8,128)(2,1)} %fusion.2), kind=kOutput, calls=%fused_computation.49 | convolution fusion | flops 268435456 | bytes 2883584 | tf_op jit(solution)/shard_map/cgqk,qcgd->kcd/dot_general | solution.py:148
  135.2 4.0 %all-to-all-start = ((bf16[8,512,64]{1,2,0:T(8,128)(2,1)}), bf16[8,512,64]{1,2,0:T(8,128)(2,1)S(1)}, u32[]{:S(2)}, u32[]{:S(2)}) async-start(bf16[8,512,64]{1,2,0:T(8,128)(2,1)} %bitcast.53), calls=%async_computation.1 | async-start | bytes 1048576 | tf_op jit(solution)/shard_map/all_to_all | solution.py:122
  139.3 13.6 %collective-permute-done.6 = bf16[128,4096]{1,0:T(8,128)(2,1)S(1)} collective-permute-done((bf16[128,4096]{1,0:T(8,128)(2,1)S(1)}, bf16[128,4096]{1,0:T(8,128)(2,1)S(1)}, u32[]{:S(2)}, u32[]{:S(2)}) %collective-permute-start.6) | collective-permute-done | bytes 1048608 | tf_op jit(solution)/shard_map/ppermute | solution.py:30
  (97 shorter events, 40.9 us)
Async XLA Ops:
  7.2 16.1 %copy-start = (s32[256]{0:T(256)S(1)}, s32[256]{0:T(256)}, u32[]{:S(2)}) copy-start(s32[256]{0:T(256)} %param.13) | copy-start | bytes 3076
  7.2 126.0 %reduce-scatter.2.cloned.1.call-start = ((), (), s32[]{:S(2)}) async-start(), calls=%async_computation.2 | async-start | bytes 4718592 | tf_op jit(solution)/shard_map/reduce_scatter | solution.py:116
  9.1 19.5 %collective-permute-start.3 = (bf16[512,256]{1,0:T(8,128)(2,1)S(1)}, bf16[512,256]{1,0:T(8,128)(2,1)S(1)}, u32[]{:S(2)}, u32[]{:S(2)}) collective-permute-start(bf16[512,256]{1,0:T(8,128)(2,1)S(1)} %constant_dynamic-update-slice_fusion), channel_id=1, source_target_pairs={{0,4},{4,8},{8,12},{12,16},{16,20},{20,24},{24,28},{28,32},{32,36}... | collective-permute-start | bytes 786440 | tf_op jit(solution)/shard_map/ppermute | solution.py:21
  12.6 16.0 %collective-permute-start.2 = (bf16[512,256]{1,0:T(8,128)(2,1)S(1)}, bf16[512,256]{1,0:T(8,128)(2,1)S(1)}, u32[]{:S(2)}, u32[]{:S(2)}) collective-permute-start(bf16[512,256]{1,0:T(8,128)(2,1)S(1)} %constant_dynamic-update-slice_fusion), channel_id=1, source_target_pairs={{0,8},{4,12},{8,16},{12,20},{16,24},{20,28},{24,32},{28,36},{32,40... | collective-permute-start | bytes 786440 | tf_op jit(solution)/shard_map/ppermute | solution.py:21
  16.0 17.4 %collective-permute-start.1 = (bf16[512,256]{1,0:T(8,128)(2,1)S(1)}, bf16[512,256]{1,0:T(8,128)(2,1)}, u32[]{:S(2)}, u32[]{:S(2)}) collective-permute-start(bf16[512,256]{1,0:T(8,128)(2,1)S(1)} %constant_dynamic-update-slice_fusion), channel_id=1, source_target_pairs={{0,12},{4,16},{8,20},{12,24},{16,28},{20,32},{24,36},{28,40},{32,4... | collective-permute-start | bytes 786440 | tf_op jit(solution)/shard_map/ppermute | solution.py:21
  19.9 31.5 %collective-permute-start = (bf16[128,4096]{1,0:T(8,128)(2,1)}, bf16[128,4096]{1,0:T(8,128)(2,1)S(1)}, u32[]{:S(2)}, u32[]{:S(2)}) collective-permute-start(bf16[128,4096]{1,0:T(8,128)(2,1)} %param.11), channel_id=1, source_target_pairs={{0,2},{2,0},{1,3},{3,1},{4,6},{6,4},{5,7},{7,5},{8,10},{10,8},{9,1... | collective-permute-start | bytes 3145736 | tf_op jit(solution)/shard_map/ppermute | solution.py:30
  26.3 11.3 %copy-start.16 = (bf16[512,512]{0,1:T(8,128)(2,1)}, bf16[512,512]{0,1:T(8,128)(2,1)S(1)}, u32[]{:S(2)}) copy-start(bf16[512,512]{0,1:T(8,128)(2,1)S(1)} %copy.58) | copy-start | bytes 1572868
  34.4 7.3 %copy-start.10 = (bf16[2048,256]{1,0:T(8,128)(2,1)}, bf16[2048,256]{1,0:T(8,128)(2,1)S(1)}, u32[]{:S(2)}) copy-start(bf16[2048,256]{1,0:T(8,128)(2,1)S(1)} %pad_maximum_fusion.2) | copy-start | bytes 3145732
  43.3 9.1 %copy-start.12 = (bf16[128,4096]{1,0:T(8,128)(2,1)S(1)}, bf16[128,4096]{1,0:T(8,128)(2,1)}, u32[]{:S(2)}) copy-start(bf16[128,4096]{1,0:T(8,128)(2,1)} %param.11) | copy-start | bytes 3145732
  55.3 4.5 %collective-permute-start.4 = (bf16[2,128,4096]{2,1,0:T(8,128)(2,1)}, bf16[2,128,4096]{2,1,0:T(8,128)(2,1)}, u32[]{:S(2)}, u32[]{:S(2)}) collective-permute-start(bf16[2,128,4096]{2,1,0:T(8,128)(2,1)} %pad_maximum_fusion.1), channel_id=1, source_target_pairs={{0,1},{1,0},{2,3},{3,2},{4,5},{5,4},{6,7},{7,6},{8,9},{9,8},{10,11... | collective-permute-start | bytes 6291464 | tf_op jit(solution)/shard_map/ppermute | solution.py:30
  68.8 8.4 %copy-start.7 = (bf16[512,4096]{1,0:T(8,128)(2,1)S(1)}, bf16[512,4096]{1,0:T(8,128)(2,1)}, u32[]{:S(2)}) copy-start(bf16[512,4096]{1,0:T(8,128)(2,1)} %param.10) | copy-start | bytes 12582916
  68.8 8.4 %copy-start.15 = (bf16[512,1,4,128]{0,3,2,1:T(8,128)(2,1)S(1)}, bf16[512,1,4,128]{0,3,2,1:T(8,128)(2,1)}, u32[]{:S(2)}) copy-start(bf16[512,1,4,128]{0,3,2,1:T(8,128)(2,1)} %divide_convert_fusion) | copy-start | bytes 1572868
  77.2 8.7 %copy-start.6 = (bf16[1,4,512,2048]{2,3,1,0:T(8,128)(2,1)}, bf16[1,4,512,2048]{2,3,1,0:T(8,128)(2,1)S(1)}, u32[]{:S(2)}) copy-start(bf16[1,4,512,2048]{2,3,1,0:T(8,128)(2,1)S(1)} %fusion.6) | copy-start | bytes 25165828
  81.4 24.9 %collective-permute-start.5 = (bf16[2,128,4096]{2,1,0:T(8,128)(2,1)}, bf16[2,128,4096]{2,1,0:T(8,128)(2,1)}, u32[]{:S(2)}, u32[]{:S(2)}) collective-permute-start(bf16[2,128,4096]{2,1,0:T(8,128)(2,1)} %fusion.23), channel_id=1, source_target_pairs={{0,1},{1,0},{2,3},{3,2},{4,5},{5,4},{6,7},{7,6},{8,9},{9,8},{10,11... | collective-permute-start | bytes 6291464 | tf_op jit(solution)/shard_map/ppermute | solution.py:30
  82.5 7.5 %slice-start.2 = ((s8[16777216]{0:T(1024)(128)(4,1)}), s8[4194304]{0:T(1024)(128)(4,1)S(1)}, s32[]{:S(2)}) async-start(s8[16777216]{0:T(1024)(128)(4,1)} %bitcast.184), calls=%async_computation.5 | async-start | bytes 8388608
  101.0 11.9 %slice-start.4 = ((s8[8388608]{0:T(1024)(128)(4,1)}), s8[4194304]{0:T(1024)(128)(4,1)S(1)}, s32[]{:S(2)}) async-start(s8[8388608]{0:T(1024)(128)(4,1)} %bitcast.188), calls=%async_computation.7 | async-start | bytes 8388608
  106.2 6.7 %slice-start.5 = ((s8[8388608]{0:T(1024)(128)(4,1)}), s8[4194304]{0:T(1024)(128)(4,1)S(1)}, s32[]{:S(2)}) async-start(s8[8388608]{0:T(1024)(128)(4,1)} %bitcast.188), calls=%async_computation.8 | async-start | bytes 8388608
  106.2 6.6 %copy-start.11 = (bf16[2048,256]{1,0:T(8,128)(2,1)S(1)}, bf16[2048,256]{1,0:T(8,128)(2,1)}, u32[]{:S(2)}) copy-start(bf16[2048,256]{1,0:T(8,128)(2,1)} %copy-done.10) | copy-start | bytes 3145732
  109.8 43.0 %collective-permute-start.6 = (bf16[128,4096]{1,0:T(8,128)(2,1)S(1)}, bf16[128,4096]{1,0:T(8,128)(2,1)S(1)}, u32[]{:S(2)}, u32[]{:S(2)}) collective-permute-start(bf16[128,4096]{1,0:T(8,128)(2,1)S(1)} %fusion.43), channel_id=1, source_target_pairs={{0,2},{2,0},{1,3},{3,1},{4,6},{6,4},{5,7},{7,5},{8,10},{10,8},{9,1... | collective-permute-start | bytes 3145736 | tf_op jit(solution)/shard_map/ppermute | solution.py:30
  116.1 40.3 %collective-permute-start.9 = (bf16[512,256]{0,1:T(8,128)(2,1)}, bf16[512,256]{0,1:T(8,128)(2,1)S(1)}, u32[]{:S(2)}, u32[]{:S(2)}) collective-permute-start(bf16[512,256]{0,1:T(8,128)(2,1)} %get-tuple-element.43), channel_id=1, source_target_pairs={{12,0},{16,4},{20,8},{24,12},{28,16},{32,20},{36,24},{40,28},{44,3... | collective-permute-start | bytes 786440 | tf_op jit(solution)/shard_map/ppermute | solution.py:26
  120.7 35.6 %collective-permute-start.8 = (bf16[512,256]{0,1:T(8,128)(2,1)}, bf16[512,256]{0,1:T(8,128)(2,1)S(1)}, u32[]{:S(2)}, u32[]{:S(2)}) collective-permute-start(bf16[512,256]{0,1:T(8,128)(2,1)} %get-tuple-element.44), channel_id=1, source_target_pairs={{8,0},{12,4},{16,8},{20,12},{24,16},{28,20},{32,24},{36,28},{40,32... | collective-permute-start | bytes 786440 | tf_op jit(solution)/shard_map/ppermute | solution.py:26
  124.3 32.0 %collective-permute-start.7 = (bf16[512,256]{0,1:T(8,128)(2,1)}, bf16[512,256]{0,1:T(8,128)(2,1)S(1)}, u32[]{:S(2)}, u32[]{:S(2)}) collective-permute-start(bf16[512,256]{0,1:T(8,128)(2,1)} %get-tuple-element.45), channel_id=1, source_target_pairs={{4,0},{8,4},{12,8},{16,12},{20,16},{24,20},{28,24},{32,28},{36,32}... | collective-permute-start | bytes 786440 | tf_op jit(solution)/shard_map/ppermute | solution.py:26
  126.7 32.4 %copy-start.1 = (s32[256]{0:T(256)S(1)}, s32[256]{0:T(256)}, u32[]{:S(2)}) copy-start(s32[256]{0:T(256)} %param.13) | copy-start | bytes 3076
  135.2 20.4 %all-to-all-start = ((bf16[8,512,64]{1,2,0:T(8,128)(2,1)}), bf16[8,512,64]{1,2,0:T(8,128)(2,1)S(1)}, u32[]{:S(2)}, u32[]{:S(2)}) async-start(bf16[8,512,64]{1,2,0:T(8,128)(2,1)} %bitcast.53), calls=%async_computation.1 | async-start | bytes 1048576 | tf_op jit(solution)/shard_map/all_to_all | solution.py:122
  (13 other events, 59.1 us)
Sparse Core Ops, SparseCore 0:
  68.9 55.2 reduce-scatter.1

commit v8 on v7

--- a/solution.py
+++ b/solution.py
@@ -45,16 +45,17 @@
     return jnp.transpose(both, (1, 0, 2, 3)).reshape(-1, piece.shape[1]), after
 
 
-def summed_over_tp(part):
+def summed_over_tp(part, after):
     high = lax.axis_index(TP[0])
     low = lax.axis_index(TP[1])
     quarters = part.reshape(2, 2, part.shape[0] // 4, part.shape[1])
     kept = lax.dynamic_index_in_dim(quarters, low, 1, keepdims=False)
     given = lax.dynamic_index_in_dim(quarters, 1 - low, 1, keepdims=False)
     halves = kept + swapped(given.astype(jnp.bfloat16), TP[1]).astype(jnp.float32)
+    halves, after = lax.optimization_barrier((halves, after))
     kept = lax.dynamic_index_in_dim(halves, high, 0, keepdims=False)
     given = lax.dynamic_index_in_dim(halves, 1 - high, 0, keepdims=False)
-    return kept + swapped(given.astype(jnp.bfloat16), TP[0]).astype(jnp.float32)
+    return kept + swapped(given.astype(jnp.bfloat16), TP[0]).astype(jnp.float32), after
 
 
 def on_device(query_rows, key_rows, value_rows, out_weight, out_grad, doc_ids, window_blocks):
@@ -116,7 +117,6 @@
     weight_sum = lax.psum_scatter(weight_part, CTX[0], scatter_dimension=1, tiled=True)
 
     out_part = jnp.dot(attn, out_weight, preferred_element_type=jnp.float32)
-    layer_out = summed_over_tp(out_part).astype(jnp.bfloat16)
     rest_count = ctx_count // lax.axis_size(CTX[0])
     weight_cols = weight_sum.reshape(weight_sum.shape[0], rest_count, -1).transpose(1, 0, 2)
     weight_cols = lax.all_to_all(weight_cols, CTX[1:], 0, 0, tiled=True)
@@ -127,6 +127,8 @@
     d_attn = lax.dot_general(
         grad_piece, out_weight, (((1,), (1,)), ((), ())), preferred_element_type=jnp.float32
     ).astype(jnp.bfloat16)
+    layer_sum, d_attn = summed_over_tp(out_part, d_attn)
+    layer_out = layer_sum.astype(jnp.bfloat16)
     grad_four = d_attn.reshape(tokens_here, kv_here, groups, HEAD_DIM)
     delta_rows = jnp.transpose(
         jnp.sum(

time: 168 us -> 174 us (1.036)
  waiting for transfers between devices: 25.7 us -> 18.4 us
  matrix products: 43.6 us -> 48.1 us
  other arithmetic: 29.3 us -> 33.6 us
  local copies, waits for them, and re-layouts: 21 us -> 25.1 us
    ppermute x4, waiting for transfers between devices: 21 us -> 7.43 us  [swapped(): return lax.ppermute(block, axis, [(0, 1), (1, 0)])]
    all_to_all x1, waiting for transfers between devices: 0.01 us -> 6.21 us  [on_device(): weight_cols = lax.all_to_all(weight_cols, CTX[1:], 0, 0, tiled=True)]
    dot_general x2, matrix products: 8.38 us -> 5.24 us  [key_side(): jnp.einsum('cgqk,qcgd->kcd', score_part, query_four, preferred_element_ty...]
    convert_element_type x1 -> x2, local copies, waits for them, and re-layouts: 1.64 us -> 4.39 us  [summed_over_tp(): given.astype(jnp.bfloat16)]
    dot_general x1, matrix products: 3.17 us -> 5.92 us  [on_device(): lax.dot_general(grad_piece, out_weight, (((1,), (1,)), ((), ())), preferr...]
    add x1, other arithmetic: 3.08 us -> 5.57 us  [summed_over_tp(): kept + swapped(given.astype(jnp.bfloat16), TP[1]).astype(jnp.float32)]
    dot_general x2, matrix products: 6.18 us -> 8.45 us  [key_side(): jnp.einsum('cgqk,qcgd->kcd', prob_part, grad_four, preferred_element_type...]
    dot_general x1, matrix products: 2.45 us -> 4.65 us  [on_device(): out_part = jnp.dot(attn, out_weight, preferred_element_type=jnp.float32)]
  transfers between devices with their start and end apart: 12 -> 12, of which waited for: 4 -> 4; matrix products, arithmetic and copies ran while one was open for 43% -> 49% of each run, Pallas kernels for 0% -> 0%
where the time goes in v8:
time: 174 us; the launch traced here: 172 us
  matrix products  48.1 us (28%)
  other arithmetic  33.6 us (19%)
  starting transfers between devices  32.1 us (18%)
  local copies, waits for them, and re-layouts  25.1 us (14%)
  waiting for transfers between devices  18.4 us (11%)
  between operations  14.5 us (8%)
    unnamed x40, local copies, waits for them, and re-layouts  12.3 us
    ppermute x3, starting transfers between devices, from_earlier(): return lax.ppermute(block, CTX, route)  10.8 us
    ppermute x3, starting transfers between devices, to_earlier(): return lax.ppermute(block, CTX, route)  10.5 us
    convert_element_type x1, other arithmetic, on_device(): probs_half = probs.astype(jnp.bfloat16)  10.5 us
    dot_general x1, matrix products, on_device(): jnp.einsum('qcgd,kcd->cgqk', grad_four, value_heads, preferred_element_ty...  9.77 us
    dot_general x2, matrix products, key_side(): jnp.einsum('cgqk,qcgd->kcd', prob_part, grad_four, preferred_element_type...  8.45 us
    ppermute x4, waiting for transfers between devices, swapped(): return lax.ppermute(block, axis, [(0, 1), (1, 0)])  7.43 us
    ppermute x4, starting transfers between devices, swapped(): return lax.ppermute(block, axis, [(0, 1), (1, 0)])  6.32 us
  transfers between devices with their start and end apart: 12, of which 4 were waited for; matrix products, arithmetic and copies ran while one was open for 49% of the time, Pallas kernels for 0%

profile of v8, /device:TPU:96, one launch (start us, length us, event | category | flops | bytes accessed | tf_op | source)
XLA Modules:
  0.0 171.7 jit_solution(4406669400410624608)
XLA Ops:
  9.1 3.5 %collective-permute-start.3 = (bf16[512,256]{1,0:T(8,128)(2,1)S(1)}, bf16[512,256]{1,0:T(8,128)(2,1)S(1)}, u32[]{:S(2)}, u32[]{:S(2)}) collective-permute-start(bf16[512,256]{1,0:T(8,128)(2,1)S(1)} %constant_dynamic-update-slice_fusion), channel_id=1, source_target_pairs={{0,4},{4,8},{8,12},{12,16},{16,20},{20,24},{24,28},{28,32},{32,36}... | collective-permute-start | bytes 786440 | tf_op jit(solution)/shard_map/ppermute | solution.py:21
  12.6 3.4 %collective-permute-start.2 = (bf16[512,256]{1,0:T(8,128)(2,1)S(1)}, bf16[512,256]{1,0:T(8,128)(2,1)S(1)}, u32[]{:S(2)}, u32[]{:S(2)}) collective-permute-start(bf16[512,256]{1,0:T(8,128)(2,1)S(1)} %constant_dynamic-update-slice_fusion), channel_id=1, source_target_pairs={{0,8},{4,12},{8,16},{12,20},{16,24},{20,28},{24,32},{28,36},{32,40... | collective-permute-start | bytes 786440 | tf_op jit(solution)/shard_map/ppermute | solution.py:21
  16.0 3.9 %collective-permute-start.1 = (bf16[512,256]{1,0:T(8,128)(2,1)S(1)}, bf16[512,256]{1,0:T(8,128)(2,1)}, u32[]{:S(2)}, u32[]{:S(2)}) collective-permute-start(bf16[512,256]{1,0:T(8,128)(2,1)S(1)} %constant_dynamic-update-slice_fusion), channel_id=1, source_target_pairs={{0,12},{4,16},{8,20},{12,24},{16,28},{20,32},{24,36},{28,40},{32,4... | collective-permute-start | bytes 786440 | tf_op jit(solution)/shard_map/ppermute | solution.py:21
  19.9 3.3 %collective-permute-start = (bf16[128,4096]{1,0:T(8,128)(2,1)}, bf16[128,4096]{1,0:T(8,128)(2,1)S(1)}, u32[]{:S(2)}, u32[]{:S(2)}) collective-permute-start(bf16[128,4096]{1,0:T(8,128)(2,1)} %param.11), channel_id=1, source_target_pairs={{0,2},{2,0},{1,3},{3,1},{4,6},{6,4},{5,7},{7,5},{8,10},{10,8},{9,1... | collective-permute-start | bytes 3145736 | tf_op jit(solution)/shard_map/ppermute | solution.py:30
  28.6 4.8 %collective-permute-done.1 = bf16[512,256]{1,0:T(8,128)(2,1)} collective-permute-done((bf16[512,256]{1,0:T(8,128)(2,1)S(1)}, bf16[512,256]{1,0:T(8,128)(2,1)}, u32[]{:S(2)}, u32[]{:S(2)}) %collective-permute-start.1) | collective-permute-done | bytes 262176 | tf_op jit(solution)/shard_map/ppermute | solution.py:21
  34.4 3.1 %fusion.5 = (f32[4,512]{1,0:T(4,128)S(1)}, f32[2048,512,4]{1,0,2:T(8,128)S(1)}) fusion(pred[512,2048]{0,1:T(8,128)(4,1)S(1)} %fusion.17, bf16[512,4,128]{0,2,1:T(8,128)(2,1)S(1)} %bitcast.191, bf16[2048,256]{1,0:T(8,128)(2,1)S(1)} %pad_maximum_fusion.2), kind=kOutput, calls=%fused_computation.9 | convolution fusion | flops 1086322688 | bytes 18882560 | tf_op jit(solution)/shard_map/qcgd,kcd->cgqk/dot_general | solution.py:98
  37.6 4.2 %fusion.7 = f32[4,512]{1,0:T(4,128)S(1)} fusion(f32[2048,512,4]{1,0,2:T(8,128)S(1)} %get-tuple-element.58, f32[4,512]{1,0:T(4,128)S(1)} %get-tuple-element.57, pred[512,2048]{0,1:T(8,128)(4,1)S(1)} %fusion.17), kind=kLoop, calls=%fused_computation.11 | loop fusion | flops 20969472 | bytes 17842176 | tf_op jit(solution)/shard_map/reduce_sum | solution.py:104
  43.3 5.2 %divide_convert_fusion = bf16[512,1,4,128]{0,3,2,1:T(8,128)(2,1)} fusion(f32[2048,512,4]{1,0,2:T(8,128)S(1)} %get-tuple-element.58, f32[4,512]{1,0:T(4,128)S(1)} %get-tuple-element.57, pred[512,2048]{0,1:T(8,128)(4,1)S(1)} %fusion.17, f32[512,4]{0,1:T(4,128)S(1)} %bitcast.197, bf16[2048,256]{1,0:T(8,128)(2,1)S(1)} %pad_maximum_fusion.2), kind=kOutput, calls=%fused_computation.57 | convolution fusion | flops 1095237632 | bytes 18890752 | tf_op jit(solution)/shard_map/cgqk,kcd->qcgd/dot_general | solution.py:105
  48.5 2.9 %collective-permute-done = bf16[128,4096]{1,0:T(8,128)(2,1)S(1)} collective-permute-done((bf16[128,4096]{1,0:T(8,128)(2,1)}, bf16[128,4096]{1,0:T(8,128)(2,1)S(1)}, u32[]{:S(2)}, u32[]{:S(2)}) %collective-permute-start) | collective-permute-done | bytes 1048608 | tf_op jit(solution)/shard_map/ppermute | solution.py:30
  55.3 4.5 %collective-permute-done.4 = bf16[2,128,4096]{2,1,0:T(8,128)(2,1)} collective-permute-done((bf16[2,128,4096]{2,1,0:T(8,128)(2,1)}, bf16[2,128,4096]{2,1,0:T(8,128)(2,1)}, u32[]{:S(2)}, u32[]{:S(2)}) %collective-permute-start.4) | collective-permute-done | bytes 2097184 | tf_op jit(solution)/shard_map/ppermute | solution.py:30
  64.3 4.4 %convolution_convert_fusion = bf16[512,4096]{1,0:T(8,128)(2,1)} fusion(bf16[512,512]{0,1:T(8,128)(2,1)S(1)} %bitcast.187, bf16[512,4096]{1,0:T(8,128)(2,1)S(1)} %bitcast.184), kind=kOutput, calls=%fused_computation.22 | convolution fusion | flops 2149580800 | bytes 8912896 | tf_op jit(solution)/shard_map/dot_general | solution.py:113
  68.7 4.7 %fusion.62 = f32[512,4096]{1,0:T(8,128)S(1)} fusion(bf16[512,512]{0,1:T(8,128)(2,1)S(1)} %bitcast.188, bf16[512,4096]{1,0:T(8,128)(2,1)} %param.10), kind=kOutput, calls=%fused_computation.96 | convolution fusion | flops 2147483648 | bytes 13107200 | tf_op jit(solution)/shard_map/dot_general | solution.py:119
  73.4 3.2 %copy-done.3 = f32[512,4096]{1,0:T(8,128)} copy-done((f32[512,4096]{1,0:T(8,128)}, f32[512,4096]{1,0:T(8,128)S(1)}, u32[]{:S(2)}) %copy-start.3) | copy-done | bytes 8388632
  78.4 10.5 %fusion.6 = bf16[1,4,512,2048]{2,3,1,0:T(8,128)(2,1)} fusion(f32[2048,512,4]{1,0,2:T(8,128)} %copy-done.2, f32[4,512]{1,0:T(4,128)S(1)} %log_add_fusion, pred[512,2048]{0,1:T(8,128)(4,1)S(1)} %fusion.17), kind=kLoop, calls=%fused_computation.10 | loop fusion | flops 16777216 | bytes 26222592 | tf_op jit(solution)/shard_map/convert_element_type | solution.py:147
  89.1 5.9 %convolution_convert_fusion.1 = bf16[512,512]{1,0:T(8,128)(2,1)S(1)} fusion(bf16[512,4096]{1,0:T(8,128)(2,1)} %bitcast.185, bf16[512,4096]{1,0:T(8,128)(2,1)} %param.10), kind=kOutput, calls=%fused_computation.47 | convolution fusion | flops 2147745792 | bytes 8912896 | tf_op jit(solution)/shard_map/dot_general | solution.py:127
  95.0 5.6 %bitcast_add_fusion = f32[2,128,4096]{2,1,0:T(8,128)} fusion(bf16[2,128,4096]{2,1,0:T(8,128)(2,1)} %collective-permute-done.5, f32[2,2,128,4096]{3,2,1,0:T(8,128)} %bitcast.183, s32[]{:T(128)S(6)} %select_n.96), kind=kLoop, calls=%fused_computation.25 | loop fusion | flops 2097152 | bytes 10485764 | tf_op jit(solution)/shard_map/add | solution.py:54
  108.6 5.2 %fusion.22 = bf16[1536,128]{0,1:T(8,128)(2,1)S(1)} fusion(bf16[512,4,128]{0,2,1:T(8,128)(2,1)} %bitcast.194, bf16[1,4,512,2048]{2,3,1,0:T(8,128)(2,1)} %fusion.6), kind=kOutput, calls=%fused_computation.32 | convolution fusion | flops 805502976 | bytes 7208960 | tf_op jit(solution)/shard_map/cgqk,qcgd->kcd/dot_general | solution.py:153
  113.8 9.8 %fusion.2 = bf16[1,4,512,2048]{2,3,1,0:T(8,128)(2,1)S(1)} fusion(f32[2048,512,4]{1,0,2:T(8,128)} %copy-done.2, f32[4,512]{1,0:T(4,128)S(1)} %copy.59, f32[4,512]{1,0:T(4,128)S(1)} %log_add_fusion, pred[512,2048]{0,1:T(8,128)(4,1)S(1)} %fusion.17, bf16[512,4,128]{0,2,1:T(8,128)(2,1)S(1)} %bitcast.196, bf16[2048,256]{1,0:T(8,128)(2,1)S(1)} %copy-done.7), kind=kOutput, calls=%fused_computation.3 | convolution fusion | flops 1103101952 | bytes 27279360 | tf_op jit(solution)/shard_map/qcgd,kcd->cgqk/dot_general | solution.py:143
  129.9 4.6 %collective-permute-start.9 = (bf16[512,256]{0,1:T(8,128)(2,1)}, bf16[512,256]{0,1:T(8,128)(2,1)S(1)}, u32[]{:S(2)}, u32[]{:S(2)}) collective-permute-start(bf16[512,256]{0,1:T(8,128)(2,1)} %get-tuple-element.52), channel_id=1, source_target_pairs={{12,0},{16,4},{20,8},{24,12},{28,16},{32,20},{36,24},{40,28},{44,3... | collective-permute-start | bytes 786440 | tf_op jit(solution)/shard_map/ppermute | solution.py:26
  134.6 3.7 %collective-permute-start.8 = (bf16[512,256]{0,1:T(8,128)(2,1)S(1)}, bf16[512,256]{0,1:T(8,128)(2,1)S(1)}, u32[]{:S(2)}, u32[]{:S(2)}) collective-permute-start(bf16[512,256]{0,1:T(8,128)(2,1)S(1)} %get-tuple-element.53), channel_id=1, source_target_pairs={{8,0},{12,4},{16,8},{20,12},{24,16},{28,20},{32,24},{36,28},{40,32... | collective-permute-start | bytes 786440 | tf_op jit(solution)/shard_map/ppermute | solution.py:26
  140.5 3.3 %fusion.40 = f32[512,128]{0,1:T(8,128)} fusion(bf16[512,4,128]{0,2,1:T(8,128)(2,1)} %bitcast.195, bf16[1,4,512,2048]{2,3,1,0:T(8,128)(2,1)} %fusion.6), kind=kOutput, calls=%fused_computation.50 | convolution fusion | flops 268435456 | bytes 2883584 | tf_op jit(solution)/shard_map/cgqk,qcgd->kcd/dot_general | solution.py:153
  143.8 3.1 %fusion.37 = f32[512,128]{0,1:T(8,128)} fusion(bf16[512,4,128]{0,2,1:T(8,128)(2,1)S(1)} %bitcast.193, bf16[1,4,512,2048]{2,3,1,0:T(8,128)(2,1)} %copy-done.4), kind=kOutput, calls=%fused_computation.49 | convolution fusion | flops 268435456 | bytes 2883584 | tf_op jit(solution)/shard_map/cgqk,qcgd->kcd/dot_general | solution.py:150
  149.0 4.3 %all-to-all-start = ((bf16[8,512,64]{1,2,0:T(8,128)(2,1)}), bf16[8,512,64]{1,2,0:T(8,128)(2,1)S(1)}, u32[]{:S(2)}, u32[]{:S(2)}) async-start(bf16[8,512,64]{1,2,0:T(8,128)(2,1)} %bitcast.51), calls=%async_computation.1 | async-start | bytes 1048576 | tf_op jit(solution)/shard_map/all_to_all | solution.py:122
  156.2 6.2 %all-to-all-done = bf16[8,512,64]{1,2,0:T(8,128)(2,1)S(1)} async-done(((bf16[8,512,64]{1,2,0:T(8,128)(2,1)}), bf16[8,512,64]{1,2,0:T(8,128)(2,1)S(1)}, u32[]{:S(2)}, u32[]{:S(2)}) %all-to-all-start) | async-done | bytes 524320 | tf_op jit(solution)/shard_map/all_to_all | solution.py:122
  (87 shorter events, 44.0 us)
Async XLA Ops:
  7.2 16.1 %copy-start = (s32[256]{0:T(256)S(1)}, s32[256]{0:T(256)}, u32[]{:S(2)}) copy-start(s32[256]{0:T(256)} %param.13) | copy-start | bytes 3076
  7.2 139.7 %reduce-scatter.2.cloned.1.call-start = ((), (), s32[]{:S(2)}) async-start(), calls=%async_computation.2 | async-start | bytes 4718592 | tf_op jit(solution)/shard_map/reduce_scatter | solution.py:117
  9.1 19.5 %collective-permute-start.3 = (bf16[512,256]{1,0:T(8,128)(2,1)S(1)}, bf16[512,256]{1,0:T(8,128)(2,1)S(1)}, u32[]{:S(2)}, u32[]{:S(2)}) collective-permute-start(bf16[512,256]{1,0:T(8,128)(2,1)S(1)} %constant_dynamic-update-slice_fusion), channel_id=1, source_target_pairs={{0,4},{4,8},{8,12},{12,16},{16,20},{20,24},{24,28},{28,32},{32,36}... | collective-permute-start | bytes 786440 | tf_op jit(solution)/shard_map/ppermute | solution.py:21
  12.6 16.0 %collective-permute-start.2 = (bf16[512,256]{1,0:T(8,128)(2,1)S(1)}, bf16[512,256]{1,0:T(8,128)(2,1)S(1)}, u32[]{:S(2)}, u32[]{:S(2)}) collective-permute-start(bf16[512,256]{1,0:T(8,128)(2,1)S(1)} %constant_dynamic-update-slice_fusion), channel_id=1, source_target_pairs={{0,8},{4,12},{8,16},{12,20},{16,24},{20,28},{24,32},{28,36},{32,40... | collective-permute-start | bytes 786440 | tf_op jit(solution)/shard_map/ppermute | solution.py:21
  16.0 17.4 %collective-permute-start.1 = (bf16[512,256]{1,0:T(8,128)(2,1)S(1)}, bf16[512,256]{1,0:T(8,128)(2,1)}, u32[]{:S(2)}, u32[]{:S(2)}) collective-permute-start(bf16[512,256]{1,0:T(8,128)(2,1)S(1)} %constant_dynamic-update-slice_fusion), channel_id=1, source_target_pairs={{0,12},{4,16},{8,20},{12,24},{16,28},{20,32},{24,36},{28,40},{32,4... | collective-permute-start | bytes 786440 | tf_op jit(solution)/shard_map/ppermute | solution.py:21
  19.9 31.5 %collective-permute-start = (bf16[128,4096]{1,0:T(8,128)(2,1)}, bf16[128,4096]{1,0:T(8,128)(2,1)S(1)}, u32[]{:S(2)}, u32[]{:S(2)}) collective-permute-start(bf16[128,4096]{1,0:T(8,128)(2,1)} %param.11), channel_id=1, source_target_pairs={{0,2},{2,0},{1,3},{3,1},{4,6},{6,4},{5,7},{7,5},{8,10},{10,8},{9,1... | collective-permute-start | bytes 3145736 | tf_op jit(solution)/shard_map/ppermute | solution.py:30
  26.3 11.3 %copy-start.12 = (bf16[512,512]{0,1:T(8,128)(2,1)}, bf16[512,512]{0,1:T(8,128)(2,1)S(1)}, u32[]{:S(2)}) copy-start(bf16[512,512]{0,1:T(8,128)(2,1)S(1)} %copy.85) | copy-start | bytes 1572868
  34.4 7.3 %copy-start.6 = (bf16[2048,256]{1,0:T(8,128)(2,1)}, bf16[2048,256]{1,0:T(8,128)(2,1)S(1)}, u32[]{:S(2)}) copy-start(bf16[2048,256]{1,0:T(8,128)(2,1)S(1)} %pad_maximum_fusion.2) | copy-start | bytes 3145732
  37.5 5.7 %copy-start.2 = (f32[2048,512,4]{1,0,2:T(8,128)}, f32[2048,512,4]{1,0,2:T(8,128)S(1)}, u32[]{:S(2)}) copy-start(f32[2048,512,4]{1,0,2:T(8,128)S(1)} %get-tuple-element.58) | copy-start | bytes 50331652
  43.3 9.1 %copy-start.10 = (bf16[128,4096]{1,0:T(8,128)(2,1)S(1)}, bf16[128,4096]{1,0:T(8,128)(2,1)}, u32[]{:S(2)}) copy-start(bf16[128,4096]{1,0:T(8,128)(2,1)} %param.11) | copy-start | bytes 3145732
  55.3 4.5 %collective-permute-start.4 = (bf16[2,128,4096]{2,1,0:T(8,128)(2,1)}, bf16[2,128,4096]{2,1,0:T(8,128)(2,1)}, u32[]{:S(2)}, u32[]{:S(2)}) collective-permute-start(bf16[2,128,4096]{2,1,0:T(8,128)(2,1)} %pad_maximum_fusion.1), channel_id=1, source_target_pairs={{0,1},{1,0},{2,3},{3,2},{4,5},{5,4},{6,7},{7,6},{8,9},{9,8},{10,11... | collective-permute-start | bytes 6291464 | tf_op jit(solution)/shard_map/ppermute | solution.py:30
  78.2 16.8 %collective-permute-start.5 = (bf16[2,128,4096]{2,1,0:T(8,128)(2,1)}, bf16[2,128,4096]{2,1,0:T(8,128)(2,1)}, u32[]{:S(2)}, u32[]{:S(2)}) collective-permute-start(bf16[2,128,4096]{2,1,0:T(8,128)(2,1)} %fusion.23), channel_id=1, source_target_pairs={{0,1},{1,0},{2,3},{3,2},{4,5},{5,4},{6,7},{7,6},{8,9},{9,8},{10,11... | collective-permute-start | bytes 6291464 | tf_op jit(solution)/shard_map/ppermute | solution.py:30
  102.1 11.6 %copy-start.7 = (bf16[2048,256]{1,0:T(8,128)(2,1)S(1)}, bf16[2048,256]{1,0:T(8,128)(2,1)}, u32[]{:S(2)}) copy-start(bf16[2048,256]{1,0:T(8,128)(2,1)} %copy-done.6) | copy-start | bytes 3145732
  102.9 10.9 %copy-start.15 = (bf16[512,512]{0,1:T(8,128)(2,1)S(1)}, bf16[512,512]{0,1:T(8,128)(2,1)}, u32[]{:S(2)}) copy-start(bf16[512,512]{0,1:T(8,128)(2,1)} %copy.86) | copy-start | bytes 1572868
  105.7 47.7 %collective-permute-start.6 = (bf16[128,4096]{1,0:T(8,128)(2,1)}, bf16[128,4096]{1,0:T(8,128)(2,1)S(1)}, u32[]{:S(2)}, u32[]{:S(2)}) collective-permute-start(bf16[128,4096]{1,0:T(8,128)(2,1)} %fusion.43), channel_id=1, source_target_pairs={{0,2},{2,0},{1,3},{3,1},{4,6},{6,4},{5,7},{7,5},{8,10},{10,8},{9,1... | collective-permute-start | bytes 3145736 | tf_op jit(solution)/shard_map/ppermute | solution.py:30
  113.8 9.8 %copy-start.13 = (bf16[512,512]{0,1:T(8,128)(2,1)S(1)}, bf16[512,512]{0,1:T(8,128)(2,1)}, u32[]{:S(2)}) copy-start(bf16[512,512]{0,1:T(8,128)(2,1)} %copy-done.12) | copy-start | bytes 1572868
  126.9 16.9 %copy-start.14 = (bf16[512,512]{0,1:T(8,128)(2,1)S(1)}, bf16[512,512]{0,1:T(8,128)(2,1)}, u32[]{:S(2)}) copy-start(bf16[512,512]{0,1:T(8,128)(2,1)} %copy-done.12) | copy-start | bytes 1572868
  129.9 33.2 %collective-permute-start.9 = (bf16[512,256]{0,1:T(8,128)(2,1)}, bf16[512,256]{0,1:T(8,128)(2,1)S(1)}, u32[]{:S(2)}, u32[]{:S(2)}) collective-permute-start(bf16[512,256]{0,1:T(8,128)(2,1)} %get-tuple-element.52), channel_id=1, source_target_pairs={{12,0},{16,4},{20,8},{24,12},{28,16},{32,20},{36,24},{40,28},{44,3... | collective-permute-start | bytes 786440 | tf_op jit(solution)/shard_map/ppermute | solution.py:26
  134.6 28.6 %collective-permute-start.8 = (bf16[512,256]{0,1:T(8,128)(2,1)S(1)}, bf16[512,256]{0,1:T(8,128)(2,1)S(1)}, u32[]{:S(2)}, u32[]{:S(2)}) collective-permute-start(bf16[512,256]{0,1:T(8,128)(2,1)S(1)} %get-tuple-element.53), channel_id=1, source_target_pairs={{8,0},{12,4},{16,8},{20,12},{24,16},{28,20},{32,24},{36,28},{40,32... | collective-permute-start | bytes 786440 | tf_op jit(solution)/shard_map/ppermute | solution.py:26
  138.3 24.9 %collective-permute-start.7 = (bf16[512,256]{0,1:T(8,128)(2,1)S(1)}, bf16[512,256]{0,1:T(8,128)(2,1)S(1)}, u32[]{:S(2)}, u32[]{:S(2)}) collective-permute-start(bf16[512,256]{0,1:T(8,128)(2,1)S(1)} %get-tuple-element.54), channel_id=1, source_target_pairs={{4,0},{8,4},{12,8},{16,12},{20,16},{24,20},{28,24},{32,28},{36,32}... | collective-permute-start | bytes 786440 | tf_op jit(solution)/shard_map/ppermute | solution.py:26
  140.5 24.4 %copy-start.1 = (s32[256]{0:T(256)S(1)}, s32[256]{0:T(256)}, u32[]{:S(2)}) copy-start(s32[256]{0:T(256)} %param.13) | copy-start | bytes 3076
  146.9 16.2 %copy-start.16 = (f32[512,128]{0,1:T(8,128)S(1)}, f32[512,128]{0,1:T(8,128)}, u32[]{:S(2)}) copy-start(f32[512,128]{0,1:T(8,128)} %fusion.40) | copy-start | bytes 786436
  146.9 16.2 %copy-start.17 = (f32[512,128]{0,1:T(8,128)S(1)}, f32[512,128]{0,1:T(8,128)}, u32[]{:S(2)}) copy-start(f32[512,128]{0,1:T(8,128)} %fusion.37) | copy-start | bytes 786436
  149.0 13.4 %all-to-all-start = ((bf16[8,512,64]{1,2,0:T(8,128)(2,1)}), bf16[8,512,64]{1,2,0:T(8,128)(2,1)S(1)}, u32[]{:S(2)}, u32[]{:S(2)}) async-start(bf16[8,512,64]{1,2,0:T(8,128)(2,1)} %bitcast.51), calls=%async_computation.1 | async-start | bytes 1048576 | tf_op jit(solution)/shard_map/all_to_all | solution.py:122
  (6 other events, 15.1 us)
Sparse Core Ops, SparseCore 0:
  68.9 55.2 reduce-scatter.1

commit v9 on v6

--- a/solution.py
+++ b/solution.py
@@ -142,8 +142,6 @@
         "qcgd,kcd->cgqk", grad_four, value_heads, preferred_element_type=jnp.float32
     )
     d_scores = (probs * (d_probs - delta_rows[..., None]) * score_scale).astype(jnp.bfloat16)
-    layer_received, d_scores = lax.optimization_barrier((layer_received, d_scores))
-    layer_out = (layer_kept + layer_received.astype(jnp.float32)).astype(jnp.bfloat16)
     probs_half = probs.astype(jnp.bfloat16)
 
     def key_side(score_part, prob_part):
@@ -168,6 +166,10 @@
         "cgqk,kcd->qcgd", d_scores, key_heads, preferred_element_type=jnp.float32
     )
     pair_grad = key_side(d_scores[..., span:], probs_half[..., span:])
+    returned, grad_weight, layer_received = lax.optimization_barrier(
+        (returned, grad_weight, layer_received)
+    )
+    layer_out = (layer_kept + layer_received.astype(jnp.float32)).astype(jnp.bfloat16)
     for sent in returned:
         pair_grad = pair_grad + sent.astype(jnp.float32)
     key_grad = pair_grad[:, :kv_width]

time: 184 us -> 175 us (0.951)
  the two profiles are of different devices: /device:TPU:96 before, /device:TPU:111 now
where the time goes in v9:
time: 175 us; the launch traced here: 174 us
  matrix products  43.6 us (25%)
  starting transfers between devices  33.8 us (19%)
  waiting for transfers between devices  32.9 us (19%)
  other arithmetic  28.7 us (16%)
  local copies, waits for them, and re-layouts  20.4 us (12%)
  between operations  14.5 us (8%)
    all_to_all x1, waiting for transfers between devices, on_device(): weight_cols = lax.all_to_all(weight_cols, CTX[1:], 0, 0, tiled=True)  19.2 us
    ppermute x3, starting transfers between devices, from_earlier(): return lax.ppermute(block, CTX, route)  11.8 us
    unnamed x56, local copies, waits for them, and re-layouts  11.8 us
    ppermute x4, waiting for transfers between devices, swapped(): return lax.ppermute(block, axis, [(0, 1), (1, 0)])  10.5 us
    dot_general x1, matrix products, on_device(): jnp.einsum('qcgd,kcd->cgqk', grad_four, value_heads, preferred_element_ty...  9.45 us
    convert_element_type x1, other arithmetic, on_device(): probs_half = probs.astype(jnp.bfloat16)  8.4 us
    dot_general x2, matrix products, key_side(): jnp.einsum('cgqk,qcgd->kcd', score_part, query_four, preferred_element_ty...  8.31 us
    all_to_all x1, starting transfers between devices, on_device(): weight_cols = lax.all_to_all(weight_cols, CTX[1:], 0, 0, tiled=True)  8.29 us
  transfers between devices with their start and end apart: 12, of which 5 were waited for; matrix products, arithmetic and copies ran while one was open for 39% of the time, Pallas kernels for 0%

profile of v9, /device:TPU:111, one launch (start us, length us, event | category | flops | bytes accessed | tf_op | source)
XLA Modules:
  0.0 173.9 jit_solution(15610866302664400387)
XLA Ops:
  9.1 5.5 %collective-permute-start.1 = (bf16[512,256]{1,0:T(8,128)(2,1)S(1)}, bf16[512,256]{1,0:T(8,128)(2,1)S(1)}, u32[]{:S(2)}, u32[]{:S(2)}) collective-permute-start(bf16[512,256]{1,0:T(8,128)(2,1)S(1)} %constant_dynamic-update-slice_fusion), channel_id=1, source_target_pairs={{0,12},{4,16},{8,20},{12,24},{16,28},{20,32},{24,36},{28,40},{32,4... | collective-permute-start | bytes 786440 | tf_op jit(solution)/shard_map/ppermute | solution.py:21
  14.6 3.7 %collective-permute-start.2 = (bf16[512,256]{1,0:T(8,128)(2,1)S(1)}, bf16[512,256]{1,0:T(8,128)(2,1)S(1)}, u32[]{:S(2)}, u32[]{:S(2)}) collective-permute-start(bf16[512,256]{1,0:T(8,128)(2,1)S(1)} %constant_dynamic-update-slice_fusion), channel_id=1, source_target_pairs={{0,8},{4,12},{8,16},{12,20},{16,24},{20,28},{24,32},{28,36},{32,40... | collective-permute-start | bytes 786440 | tf_op jit(solution)/shard_map/ppermute | solution.py:21
  18.3 2.6 %collective-permute-start.3 = (bf16[512,256]{1,0:T(8,128)(2,1)S(1)}, bf16[512,256]{1,0:T(8,128)(2,1)}, u32[]{:S(2)}, u32[]{:S(2)}) collective-permute-start(bf16[512,256]{1,0:T(8,128)(2,1)S(1)} %constant_dynamic-update-slice_fusion), channel_id=1, source_target_pairs={{0,4},{4,8},{8,12},{12,16},{16,20},{20,24},{24,28},{28,32},{32,36}... | collective-permute-start | bytes 786440 | tf_op jit(solution)/shard_map/ppermute | solution.py:21
  26.1 2.3 %fusion.17 = pred[512,2048]{0,1:T(8,128)(4,1)S(1)} fusion(s32[512]{0:T(512)S(1)} %broadcast_bitcast_fusion, s32[2048]{0:T(1024)S(1)} %get-tuple-element.56, s32[512]{0:T(512)S(1)} %get-tuple-element.54, s32[512]{0:T(512)S(1)} %dynamic_slice.23, s32[512]{0:T(512)S(1)} %get-tuple-element.55, s32[2048]{0:T(1024)S(1)} %pad_dynamic-slice_fusion, ...), kind=kLoop, calls=%fused_computation.27 | loop fusion | flops 7340032 | bytes 1083392 | tf_op jit(solution)/shard_map/and | solution.py:89
  28.5 2.3 %collective-permute-done.3 = bf16[512,256]{1,0:T(8,128)(2,1)} collective-permute-done((bf16[512,256]{1,0:T(8,128)(2,1)S(1)}, bf16[512,256]{1,0:T(8,128)(2,1)}, u32[]{:S(2)}, u32[]{:S(2)}) %collective-permute-start.3) | collective-permute-done | bytes 262176 | tf_op jit(solution)/shard_map/ppermute | solution.py:21
  31.8 3.1 %fusion.5 = (f32[4,512]{1,0:T(4,128)S(1)}, f32[2048,512,4]{1,0,2:T(8,128)S(1)}) fusion(pred[512,2048]{0,1:T(8,128)(4,1)S(1)} %fusion.17, bf16[512,4,128]{0,2,1:T(8,128)(2,1)S(1)} %bitcast.196, bf16[2048,256]{1,0:T(8,128)(2,1)S(1)} %pad_maximum_fusion.2), kind=kOutput, calls=%fused_computation.9 | convolution fusion | flops 1086322688 | bytes 18882560 | tf_op jit(solution)/shard_map/qcgd,kcd->cgqk/dot_general | solution.py:97
  35.0 4.2 %fusion.7 = f32[4,512]{1,0:T(4,128)S(1)} fusion(f32[2048,512,4]{1,0,2:T(8,128)S(1)} %get-tuple-element.51, f32[4,512]{1,0:T(4,128)S(1)} %get-tuple-element.50, pred[512,2048]{0,1:T(8,128)(4,1)S(1)} %fusion.17), kind=kLoop, calls=%fused_computation.11 | loop fusion | flops 20969472 | bytes 17842176 | tf_op jit(solution)/shard_map/reduce_sum | solution.py:103
  40.7 5.2 %divide_convert_fusion = bf16[512,1,4,128]{0,3,2,1:T(8,128)(2,1)} fusion(f32[2048,512,4]{1,0,2:T(8,128)S(1)} %get-tuple-element.51, f32[4,512]{1,0:T(4,128)S(1)} %get-tuple-element.50, pred[512,2048]{0,1:T(8,128)(4,1)S(1)} %fusion.17, f32[512,4]{0,1:T(4,128)S(1)} %bitcast.199, bf16[2048,256]{1,0:T(8,128)(2,1)S(1)} %pad_maximum_fusion.2), kind=kOutput, calls=%fused_computation.58 | convolution fusion | flops 1095237632 | bytes 18890752 | tf_op jit(solution)/shard_map/cgqk,kcd->qcgd/dot_general | solution.py:104
  45.9 6.4 %collective-permute-done = bf16[128,4096]{1,0:T(8,128)(2,1)S(1)} collective-permute-done((bf16[128,4096]{1,0:T(8,128)(2,1)}, bf16[128,4096]{1,0:T(8,128)(2,1)S(1)}, u32[]{:S(2)}, u32[]{:S(2)}) %collective-permute-start) | collective-permute-done | bytes 1048608 | tf_op jit(solution)/shard_map/ppermute | solution.py:30
  57.8 4.1 %collective-permute-done.4 = bf16[2,128,4096]{2,1,0:T(8,128)(2,1)} collective-permute-done((bf16[2,128,4096]{2,1,0:T(8,128)(2,1)}, bf16[2,128,4096]{2,1,0:T(8,128)(2,1)}, u32[]{:S(2)}, u32[]{:S(2)}) %collective-permute-start.4) | collective-permute-done | bytes 2097184 | tf_op jit(solution)/shard_map/ppermute | solution.py:30
  66.5 4.4 %convolution_convert_fusion = bf16[512,4096]{1,0:T(8,128)(2,1)} fusion(bf16[512,512]{0,1:T(8,128)(2,1)S(1)} %bitcast.193, bf16[512,4096]{1,0:T(8,128)(2,1)S(1)} %bitcast.190), kind=kOutput, calls=%fused_computation.22 | convolution fusion | flops 2149580800 | bytes 8912896 | tf_op jit(solution)/shard_map/dot_general | solution.py:112
  70.9 8.4 %fusion.6 = bf16[1,4,512,2048]{2,3,1,0:T(8,128)(2,1)S(1)} fusion(f32[2048,512,4]{1,0,2:T(8,128)} %copy-done.2, f32[4,512]{1,0:T(4,128)S(1)} %log_add_fusion, pred[512,2048]{0,1:T(8,128)(4,1)S(1)} %fusion.17), kind=kLoop, calls=%fused_computation.10 | loop fusion | flops 16777216 | bytes 26222592 | tf_op jit(solution)/shard_map/convert_element_type | solution.py:145
  79.4 2.5 %fusion.62 = f32[512,4096]{1,0:T(8,128)S(1)} fusion(bf16[512,512]{0,1:T(8,128)(2,1)S(1)} %bitcast.194, bf16[512,4096]{1,0:T(8,128)(2,1)S(1)} %copy-done.7), kind=kOutput, calls=%fused_computation.97 | convolution fusion | flops 2147483648 | bytes 13107200 | tf_op jit(solution)/shard_map/dot_general | solution.py:118
  84.7 3.2 %bitcast_reduce_fusion = (f32[512,4]{0,1:T(4,128)}, bf16[512,512]{0,1:T(8,128)(2,1)S(1)}) fusion(bf16[512,512]{0,1:T(8,128)(2,1)S(1)} %bitcast.195, bf16[512,4096]{1,0:T(8,128)(2,1)S(1)} %bitcast.191, bf16[512,4096]{1,0:T(8,128)(2,1)S(1)} %copy-done.7), kind=kOutput, calls=%fused_computation.53 | convolution fusion | flops 2148792320 | bytes 9445376 | tf_op jit(solution)/shard_map/dot_general | solution.py:127
  88.1 2.9 %fusion.22 = bf16[1536,128]{0,1:T(8,128)(2,1)} fusion(bf16[512,4,128]{0,2,1:T(8,128)(2,1)S(1)} %bitcast.200, bf16[1,4,512,2048]{2,3,1,0:T(8,128)(2,1)S(1)} %fusion.6), kind=kOutput, calls=%fused_computation.32 | convolution fusion | flops 805502976 | bytes 7208960 | tf_op jit(solution)/shard_map/cgqk,qcgd->kcd/dot_general | solution.py:151
  93.7 9.5 %fusion.2 = bf16[1,4,512,2048]{2,3,1,0:T(8,128)(2,1)} fusion(f32[2048,512,4]{1,0,2:T(8,128)S(1)} %bitcast.185, f32[4,512]{1,0:T(4,128)} %bitcast.203, f32[4,512]{1,0:T(4,128)S(1)} %log_add_fusion, pred[512,2048]{0,1:T(8,128)(4,1)S(1)} %fusion.17, bf16[512,4,128]{0,2,1:T(8,128)(2,1)} %bitcast.201, bf16[2048,256]{1,0:T(8,128)(2,1)} %copy-done.10), kind=kOutput, calls=%fused_computation.3 | convolution fusion | flops 1103101952 | bytes 27279360 | tf_op jit(solution)/shard_map/qcgd,kcd->cgqk/dot_general | solution.py:141
  103.1 5.2 %fusion.21 = bf16[1536,128]{0,1:T(8,128)(2,1)S(1)} fusion(bf16[512,4,128]{0,2,1:T(8,128)(2,1)} %bitcast.197, bf16[1,4,512,2048]{2,3,1,0:T(8,128)(2,1)} %fusion.2), kind=kOutput, calls=%fused_computation.31 | convolution fusion | flops 805502976 | bytes 7208960 | tf_op jit(solution)/shard_map/cgqk,qcgd->kcd/dot_general | solution.py:148
  109.3 2.4 %collective-permute-start.6 = (bf16[512,256]{0,1:T(8,128)(2,1)}, bf16[512,256]{0,1:T(8,128)(2,1)S(1)}, u32[]{:S(2)}, u32[]{:S(2)}) collective-permute-start(bf16[512,256]{0,1:T(8,128)(2,1)} %get-tuple-element.47), channel_id=1, source_target_pairs={{4,0},{8,4},{12,8},{16,12},{20,16},{24,20},{28,24},{32,28},{36,32}... | collective-permute-start | bytes 786440 | tf_op jit(solution)/shard_map/ppermute | solution.py:26
  113.7 3.2 %collective-permute-start.8 = (bf16[512,256]{0,1:T(8,128)(2,1)}, bf16[512,256]{0,1:T(8,128)(2,1)}, u32[]{:S(2)}, u32[]{:S(2)}) collective-permute-start(bf16[512,256]{0,1:T(8,128)(2,1)} %get-tuple-element.45), channel_id=1, source_target_pairs={{12,0},{16,4},{20,8},{24,12},{28,16},{32,20},{36,24},{40,28},{44,3... | collective-permute-start | bytes 786440 | tf_op jit(solution)/shard_map/ppermute | solution.py:26
  126.7 8.3 %all-to-all-start = ((bf16[8,512,64]{1,2,0:T(8,128)(2,1)}), bf16[8,512,64]{1,2,0:T(8,128)(2,1)S(1)}, u32[]{:S(2)}, u32[]{:S(2)}) async-start(bf16[8,512,64]{1,2,0:T(8,128)(2,1)} %bitcast.40), calls=%async_computation.1 | async-start | bytes 1048576 | tf_op jit(solution)/shard_map/all_to_all | solution.py:122
  135.0 3.3 %fusion.40 = f32[512,128]{0,1:T(8,128)} fusion(bf16[512,4,128]{0,2,1:T(8,128)(2,1)} %bitcast.202, bf16[1,4,512,2048]{2,3,1,0:T(8,128)(2,1)} %copy-done.6), kind=kOutput, calls=%fused_computation.50 | convolution fusion | flops 268435456 | bytes 2883584 | tf_op jit(solution)/shard_map/cgqk,qcgd->kcd/dot_general | solution.py:151
  138.3 3.1 %fusion.37 = f32[512,128]{0,1:T(8,128)} fusion(bf16[512,4,128]{0,2,1:T(8,128)(2,1)S(1)} %bitcast.198, bf16[1,4,512,2048]{2,3,1,0:T(8,128)(2,1)} %fusion.2), kind=kOutput, calls=%fused_computation.49 | convolution fusion | flops 268435456 | bytes 2883584 | tf_op jit(solution)/shard_map/cgqk,qcgd->kcd/dot_general | solution.py:148
  141.4 19.2 %all-to-all-done = bf16[8,512,64]{1,2,0:T(8,128)(2,1)S(1)} async-done(((bf16[8,512,64]{1,2,0:T(8,128)(2,1)}), bf16[8,512,64]{1,2,0:T(8,128)(2,1)S(1)}, u32[]{:S(2)}, u32[]{:S(2)}) %all-to-all-start) | async-done | bytes 524320 | tf_op jit(solution)/shard_map/all_to_all | solution.py:122
  164.2 2.8 %fusion.28 = bf16[128,4096]{1,0:T(8,128)(2,1)} fusion(bf16[128,4096]{1,0:T(8,128)(2,1)S(1)} %collective-permute-done.9, f32[2,128,4096]{2,1,0:T(8,128)} %copy-done.5, s32[]{:T(128)S(6)} %select_n.98), kind=kLoop, calls=%fused_computation.40 | loop fusion | flops 1572864 | bytes 4194308 | tf_op jit(solution)/shard_map/convert_element_type | solution.py:172
  (99 shorter events, 41.6 us)
Async XLA Ops:
  7.2 15.9 %copy-start = (s32[256]{0:T(256)S(1)}, s32[256]{0:T(256)}, u32[]{:S(2)}) copy-start(s32[256]{0:T(256)} %param.13) | copy-start | bytes 3076
  7.2 117.4 %reduce-scatter.2.cloned.1.call-start = ((), (), s32[]{:S(2)}) async-start(), calls=%async_computation.2 | async-start | bytes 4718592 | tf_op jit(solution)/shard_map/reduce_scatter | solution.py:116
  9.1 19.3 %collective-permute-start.1 = (bf16[512,256]{1,0:T(8,128)(2,1)S(1)}, bf16[512,256]{1,0:T(8,128)(2,1)S(1)}, u32[]{:S(2)}, u32[]{:S(2)}) collective-permute-start(bf16[512,256]{1,0:T(8,128)(2,1)S(1)} %constant_dynamic-update-slice_fusion), channel_id=1, source_target_pairs={{0,12},{4,16},{8,20},{12,24},{16,28},{20,32},{24,36},{28,40},{32,4... | collective-permute-start | bytes 786440 | tf_op jit(solution)/shard_map/ppermute | solution.py:21
  14.6 13.9 %collective-permute-start.2 = (bf16[512,256]{1,0:T(8,128)(2,1)S(1)}, bf16[512,256]{1,0:T(8,128)(2,1)S(1)}, u32[]{:S(2)}, u32[]{:S(2)}) collective-permute-start(bf16[512,256]{1,0:T(8,128)(2,1)S(1)} %constant_dynamic-update-slice_fusion), channel_id=1, source_target_pairs={{0,8},{4,12},{8,16},{12,20},{16,24},{20,28},{24,32},{28,36},{32,40... | collective-permute-start | bytes 786440 | tf_op jit(solution)/shard_map/ppermute | solution.py:21
  18.3 12.5 %collective-permute-start.3 = (bf16[512,256]{1,0:T(8,128)(2,1)S(1)}, bf16[512,256]{1,0:T(8,128)(2,1)}, u32[]{:S(2)}, u32[]{:S(2)}) collective-permute-start(bf16[512,256]{1,0:T(8,128)(2,1)S(1)} %constant_dynamic-update-slice_fusion), channel_id=1, source_target_pairs={{0,4},{4,8},{8,12},{12,16},{16,20},{20,24},{24,28},{28,32},{32,36}... | collective-permute-start | bytes 786440 | tf_op jit(solution)/shard_map/ppermute | solution.py:21
  20.9 31.4 %collective-permute-start = (bf16[128,4096]{1,0:T(8,128)(2,1)}, bf16[128,4096]{1,0:T(8,128)(2,1)S(1)}, u32[]{:S(2)}, u32[]{:S(2)}) collective-permute-start(bf16[128,4096]{1,0:T(8,128)(2,1)} %param.11), channel_id=1, source_target_pairs={{0,2},{2,0},{1,3},{3,1},{4,6},{6,4},{5,7},{7,5},{8,10},{10,8},{9,1... | collective-permute-start | bytes 3145736 | tf_op jit(solution)/shard_map/ppermute | solution.py:30
  26.1 8.9 %copy-start.16 = (bf16[512,512]{0,1:T(8,128)(2,1)}, bf16[512,512]{0,1:T(8,128)(2,1)S(1)}, u32[]{:S(2)}) copy-start(bf16[512,512]{0,1:T(8,128)(2,1)S(1)} %copy.58) | copy-start | bytes 1572868
  40.7 12.6 %copy-start.12 = (bf16[128,4096]{1,0:T(8,128)(2,1)S(1)}, bf16[128,4096]{1,0:T(8,128)(2,1)}, u32[]{:S(2)}) copy-start(bf16[128,4096]{1,0:T(8,128)(2,1)} %param.11) | copy-start | bytes 3145732
  56.2 5.7 %collective-permute-start.4 = (bf16[2,128,4096]{2,1,0:T(8,128)(2,1)}, bf16[2,128,4096]{2,1,0:T(8,128)(2,1)}, u32[]{:S(2)}, u32[]{:S(2)}) collective-permute-start(bf16[2,128,4096]{2,1,0:T(8,128)(2,1)} %pad_maximum_fusion.1), channel_id=1, source_target_pairs={{0,1},{1,0},{2,3},{3,2},{4,5},{5,4},{6,7},{7,6},{8,9},{9,8},{10,11... | collective-permute-start | bytes 6291464 | tf_op jit(solution)/shard_map/ppermute | solution.py:30
  70.9 8.4 %copy-start.7 = (bf16[512,4096]{1,0:T(8,128)(2,1)S(1)}, bf16[512,4096]{1,0:T(8,128)(2,1)}, u32[]{:S(2)}) copy-start(bf16[512,4096]{1,0:T(8,128)(2,1)} %param.10) | copy-start | bytes 12582916
  70.9 8.4 %copy-start.15 = (bf16[512,1,4,128]{0,3,2,1:T(8,128)(2,1)S(1)}, bf16[512,1,4,128]{0,3,2,1:T(8,128)(2,1)}, u32[]{:S(2)}) copy-start(bf16[512,1,4,128]{0,3,2,1:T(8,128)(2,1)} %divide_convert_fusion) | copy-start | bytes 1572868
  79.4 8.8 %copy-start.6 = (bf16[1,4,512,2048]{2,3,1,0:T(8,128)(2,1)}, bf16[1,4,512,2048]{2,3,1,0:T(8,128)(2,1)S(1)}, u32[]{:S(2)}) copy-start(bf16[1,4,512,2048]{2,3,1,0:T(8,128)(2,1)S(1)} %fusion.6) | copy-start | bytes 25165828
  83.5 33.4 %collective-permute-start.5 = (bf16[2,128,4096]{2,1,0:T(8,128)(2,1)}, bf16[2,128,4096]{2,1,0:T(8,128)(2,1)}, u32[]{:S(2)}, u32[]{:S(2)}) collective-permute-start(bf16[2,128,4096]{2,1,0:T(8,128)(2,1)} %fusion.23), channel_id=1, source_target_pairs={{0,1},{1,0},{2,3},{3,2},{4,5},{5,4},{6,7},{7,6},{8,9},{9,8},{10,11... | collective-permute-start | bytes 6291464 | tf_op jit(solution)/shard_map/ppermute | solution.py:30
  103.1 13.8 %copy-start.4 = (f32[512,4096]{1,0:T(8,128)S(1)}, f32[512,4096]{1,0:T(8,128)}, u32[]{:S(2)}) copy-start(f32[512,4096]{1,0:T(8,128)} %copy-done.3) | copy-start | bytes 25165828
  108.4 13.2 %slice-start.4 = ((s8[8388608]{0:T(1024)(128)(4,1)}), s8[4194304]{0:T(1024)(128)(4,1)S(1)}, s32[]{:S(2)}) async-start(s8[8388608]{0:T(1024)(128)(4,1)} %bitcast.188), calls=%async_computation.7 | async-start | bytes 8388608
  109.3 52.0 %collective-permute-start.6 = (bf16[512,256]{0,1:T(8,128)(2,1)}, bf16[512,256]{0,1:T(8,128)(2,1)S(1)}, u32[]{:S(2)}, u32[]{:S(2)}) collective-permute-start(bf16[512,256]{0,1:T(8,128)(2,1)} %get-tuple-element.47), channel_id=1, source_target_pairs={{4,0},{8,4},{12,8},{16,12},{20,16},{24,20},{28,24},{32,28},{36,32}... | collective-permute-start | bytes 786440 | tf_op jit(solution)/shard_map/ppermute | solution.py:26
  111.7 49.6 %collective-permute-start.7 = (bf16[512,256]{0,1:T(8,128)(2,1)}, bf16[512,256]{0,1:T(8,128)(2,1)}, u32[]{:S(2)}, u32[]{:S(2)}) collective-permute-start(bf16[512,256]{0,1:T(8,128)(2,1)} %get-tuple-element.46), channel_id=1, source_target_pairs={{8,0},{12,4},{16,8},{20,12},{24,16},{28,20},{32,24},{36,28},{40,32... | collective-permute-start | bytes 786440 | tf_op jit(solution)/shard_map/ppermute | solution.py:26
  113.7 7.8 %slice-start.5 = ((s8[8388608]{0:T(1024)(128)(4,1)}), s8[4194304]{0:T(1024)(128)(4,1)S(1)}, s32[]{:S(2)}) async-start(s8[8388608]{0:T(1024)(128)(4,1)} %bitcast.188), calls=%async_computation.8 | async-start | bytes 8388608
  113.7 7.8 %copy-start.11 = (bf16[2048,256]{1,0:T(8,128)(2,1)S(1)}, bf16[2048,256]{1,0:T(8,128)(2,1)}, u32[]{:S(2)}) copy-start(bf16[2048,256]{1,0:T(8,128)(2,1)} %copy-done.10) | copy-start | bytes 3145732
  113.7 47.7 %collective-permute-start.8 = (bf16[512,256]{0,1:T(8,128)(2,1)}, bf16[512,256]{0,1:T(8,128)(2,1)}, u32[]{:S(2)}, u32[]{:S(2)}) collective-permute-start(bf16[512,256]{0,1:T(8,128)(2,1)} %get-tuple-element.45), channel_id=1, source_target_pairs={{12,0},{16,4},{20,8},{24,12},{28,16},{32,20},{36,24},{40,28},{44,3... | collective-permute-start | bytes 786440 | tf_op jit(solution)/shard_map/ppermute | solution.py:26
  119.4 41.9 %collective-permute-start.9 = (bf16[128,4096]{1,0:T(8,128)(2,1)S(1)}, bf16[128,4096]{1,0:T(8,128)(2,1)S(1)}, u32[]{:S(2)}, u32[]{:S(2)}) collective-permute-start(bf16[128,4096]{1,0:T(8,128)(2,1)S(1)} %fusion.43), channel_id=1, source_target_pairs={{0,2},{2,0},{1,3},{3,1},{4,6},{6,4},{5,7},{7,5},{8,10},{10,8},{9,1... | collective-permute-start | bytes 3145736 | tf_op jit(solution)/shard_map/ppermute | solution.py:30
  122.8 15.4 %copy-start.17 = (bf16[512,512]{0,1:T(8,128)(2,1)S(1)}, bf16[512,512]{0,1:T(8,128)(2,1)}, u32[]{:S(2)}) copy-start(bf16[512,512]{0,1:T(8,128)(2,1)} %copy-done.16) | copy-start | bytes 1572868
  126.7 33.9 %all-to-all-start = ((bf16[8,512,64]{1,2,0:T(8,128)(2,1)}), bf16[8,512,64]{1,2,0:T(8,128)(2,1)S(1)}, u32[]{:S(2)}, u32[]{:S(2)}) async-start(bf16[8,512,64]{1,2,0:T(8,128)(2,1)} %bitcast.40), calls=%async_computation.1 | async-start | bytes 1048576 | tf_op jit(solution)/shard_map/all_to_all | solution.py:122
  135.0 32.1 %copy-start.1 = (s32[256]{0:T(256)S(1)}, s32[256]{0:T(256)}, u32[]{:S(2)}) copy-start(s32[256]{0:T(256)} %param.13) | copy-start | bytes 3076
  (14 other events, 67.5 us)
Sparse Core Ops, SparseCore 0:
  71.0 53.5 reduce-scatter.1

commit v10 on v7

--- a/solution.py
+++ b/solution.py
@@ -110,17 +110,17 @@
     grad_piece, attn = gathered_over_tp(out_grad, attn)
 
     weight_part = lax.dot_general(
-        attn, grad_piece, (((0,), (0,)), ((), ())), preferred_element_type=jnp.float32
+        grad_piece, attn, (((0,), (0,)), ((), ())), preferred_element_type=jnp.float32
     ).astype(jnp.bfloat16)
     weight_part, attn, grad_piece = lax.optimization_barrier((weight_part, attn, grad_piece))
-    weight_sum = lax.psum_scatter(weight_part, CTX[0], scatter_dimension=1, tiled=True)
+    weight_sum = lax.psum_scatter(weight_part, CTX[0], scatter_dimension=0, tiled=True)
 
     out_part = jnp.dot(attn, out_weight, preferred_element_type=jnp.float32)
     layer_out = summed_over_tp(out_part).astype(jnp.bfloat16)
     rest_count = ctx_count // lax.axis_size(CTX[0])
-    weight_cols = weight_sum.reshape(weight_sum.shape[0], rest_count, -1).transpose(1, 0, 2)
+    weight_cols = weight_sum.reshape(rest_count, -1, weight_sum.shape[1])
     weight_cols = lax.all_to_all(weight_cols, CTX[1:], 0, 0, tiled=True)
-    weight_sum = jnp.sum(weight_cols.astype(jnp.float32), axis=0)
+    weight_sum = jnp.sum(weight_cols.astype(jnp.float32), axis=0).T
     seq_total = ctx_count * tokens_here
     grad_weight = weight_sum * seq_total ** (-0.5)
 

time: 168 us -> 168 us (level)
  waiting for transfers between devices: 25.7 us -> 27.8 us
  local copies, waits for them, and re-layouts: 21 us -> 19 us
    ppermute x4, waiting for transfers between devices: 21 us -> 23 us  [swapped(): return lax.ppermute(block, axis, [(0, 1), (1, 0)])]
    reduce_scatter x1 -> x0, local copies, waits for them, and re-layouts: 2.04 us -> none  [on_device(): lax.psum_scatter(weight_part, CTX[0], scatter_dimension=1, tiled=True)]
  transfers between devices with their start and end apart: 12 -> 12, of which waited for: 4 -> 4; matrix products, arithmetic and copies ran while one was open for 43% -> 41% of each run, Pallas kernels for 0% -> 0%
where the time goes in v10:
time: 168 us; the launch traced here: 166 us
  matrix products  43.7 us (26%)
  starting transfers between devices  31.9 us (19%)
  other arithmetic  29.3 us (17%)
  waiting for transfers between devices  27.8 us (17%)
  local copies, waits for them, and re-layouts  19 us (11%)
  between operations  14.5 us (9%)
    ppermute x4, waiting for transfers between devices, swapped(): return lax.ppermute(block, axis, [(0, 1), (1, 0)])  23 us
    unnamed x54, local copies, waits for them, and re-layouts  12.4 us
    ppermute x3, starting transfers between devices, from_earlier(): return lax.ppermute(block, CTX, route)  10.8 us
    ppermute x3, starting transfers between devices, to_earlier(): return lax.ppermute(block, CTX, route)  10.6 us
    dot_general x1, matrix products, on_device(): jnp.einsum('qcgd,kcd->cgqk', grad_four, value_heads, preferred_element_ty...  9.44 us
    convert_element_type x1, other arithmetic, on_device(): probs_half = probs.astype(jnp.bfloat16)  8.4 us
    dot_general x2, matrix products, key_side(): jnp.einsum('cgqk,qcgd->kcd', score_part, query_four, preferred_element_ty...  8.38 us
    ppermute x4, starting transfers between devices, swapped(): return lax.ppermute(block, axis, [(0, 1), (1, 0)])  6.39 us
  transfers between devices with their start and end apart: 12, of which 4 were waited for; matrix products, arithmetic and copies ran while one was open for 41% of the time, Pallas kernels for 0%

profile of v10, /device:TPU:96, one launch (start us, length us, event | category | flops | bytes accessed | tf_op | source)
XLA Modules:
  0.0 166.1 jit_solution(6827005361813657679)
XLA Ops:
  9.1 3.5 %collective-permute-start.3 = (bf16[512,256]{1,0:T(8,128)(2,1)S(1)}, bf16[512,256]{1,0:T(8,128)(2,1)S(1)}, u32[]{:S(2)}, u32[]{:S(2)}) collective-permute-start(bf16[512,256]{1,0:T(8,128)(2,1)S(1)} %constant_dynamic-update-slice_fusion), channel_id=1, source_target_pairs={{0,4},{4,8},{8,12},{12,16},{16,20},{20,24},{24,28},{28,32},{32,36}... | collective-permute-start | bytes 786440 | tf_op jit(solution)/shard_map/ppermute | solution.py:21
  12.6 3.4 %collective-permute-start.2 = (bf16[512,256]{1,0:T(8,128)(2,1)S(1)}, bf16[512,256]{1,0:T(8,128)(2,1)S(1)}, u32[]{:S(2)}, u32[]{:S(2)}) collective-permute-start(bf16[512,256]{1,0:T(8,128)(2,1)S(1)} %constant_dynamic-update-slice_fusion), channel_id=1, source_target_pairs={{0,8},{4,12},{8,16},{12,20},{16,24},{20,28},{24,32},{28,36},{32,40... | collective-permute-start | bytes 786440 | tf_op jit(solution)/shard_map/ppermute | solution.py:21
  16.0 3.9 %collective-permute-start.1 = (bf16[512,256]{1,0:T(8,128)(2,1)S(1)}, bf16[512,256]{1,0:T(8,128)(2,1)}, u32[]{:S(2)}, u32[]{:S(2)}) collective-permute-start(bf16[512,256]{1,0:T(8,128)(2,1)S(1)} %constant_dynamic-update-slice_fusion), channel_id=1, source_target_pairs={{0,12},{4,16},{8,20},{12,24},{16,28},{20,32},{24,36},{28,40},{32,4... | collective-permute-start | bytes 786440 | tf_op jit(solution)/shard_map/ppermute | solution.py:21
  19.9 3.3 %collective-permute-start = (bf16[128,4096]{1,0:T(8,128)(2,1)}, bf16[128,4096]{1,0:T(8,128)(2,1)S(1)}, u32[]{:S(2)}, u32[]{:S(2)}) collective-permute-start(bf16[128,4096]{1,0:T(8,128)(2,1)} %param.11), channel_id=1, source_target_pairs={{0,2},{2,0},{1,3},{3,1},{4,6},{6,4},{5,7},{7,5},{8,10},{10,8},{9,1... | collective-permute-start | bytes 3145736 | tf_op jit(solution)/shard_map/ppermute | solution.py:30
  28.6 4.8 %collective-permute-done.1 = bf16[512,256]{1,0:T(8,128)(2,1)} collective-permute-done((bf16[512,256]{1,0:T(8,128)(2,1)S(1)}, bf16[512,256]{1,0:T(8,128)(2,1)}, u32[]{:S(2)}, u32[]{:S(2)}) %collective-permute-start.1) | collective-permute-done | bytes 262176 | tf_op jit(solution)/shard_map/ppermute | solution.py:21
  34.4 3.1 %fusion.5 = (f32[4,512]{1,0:T(4,128)S(1)}, f32[2048,512,4]{1,0,2:T(8,128)S(1)}) fusion(pred[512,2048]{0,1:T(8,128)(4,1)S(1)} %fusion.17, bf16[512,4,128]{0,2,1:T(8,128)(2,1)S(1)} %bitcast.196, bf16[2048,256]{1,0:T(8,128)(2,1)S(1)} %pad_maximum_fusion.2), kind=kOutput, calls=%fused_computation.9 | convolution fusion | flops 1086322688 | bytes 18882560 | tf_op jit(solution)/shard_map/qcgd,kcd->cgqk/dot_general | solution.py:97
  37.6 4.2 %fusion.7 = f32[4,512]{1,0:T(4,128)S(1)} fusion(f32[2048,512,4]{1,0,2:T(8,128)S(1)} %get-tuple-element.49, f32[4,512]{1,0:T(4,128)S(1)} %get-tuple-element.48, pred[512,2048]{0,1:T(8,128)(4,1)S(1)} %fusion.17), kind=kLoop, calls=%fused_computation.11 | loop fusion | flops 20969472 | bytes 17842176 | tf_op jit(solution)/shard_map/reduce_sum | solution.py:103
  43.3 5.2 %divide_convert_fusion = bf16[512,1,4,128]{0,3,2,1:T(8,128)(2,1)} fusion(f32[2048,512,4]{1,0,2:T(8,128)S(1)} %get-tuple-element.49, f32[4,512]{1,0:T(4,128)S(1)} %get-tuple-element.48, pred[512,2048]{0,1:T(8,128)(4,1)S(1)} %fusion.17, f32[512,4]{0,1:T(4,128)S(1)} %bitcast.200, bf16[2048,256]{1,0:T(8,128)(2,1)S(1)} %pad_maximum_fusion.2), kind=kOutput, calls=%fused_computation.58 | convolution fusion | flops 1095237632 | bytes 18890752 | tf_op jit(solution)/shard_map/cgqk,kcd->qcgd/dot_general | solution.py:104
  48.5 2.9 %collective-permute-done = bf16[128,4096]{1,0:T(8,128)(2,1)S(1)} collective-permute-done((bf16[128,4096]{1,0:T(8,128)(2,1)}, bf16[128,4096]{1,0:T(8,128)(2,1)S(1)}, u32[]{:S(2)}, u32[]{:S(2)}) %collective-permute-start) | collective-permute-done | bytes 1048608 | tf_op jit(solution)/shard_map/ppermute | solution.py:30
  55.3 4.5 %collective-permute-done.4 = bf16[2,128,4096]{2,1,0:T(8,128)(2,1)} collective-permute-done((bf16[2,128,4096]{2,1,0:T(8,128)(2,1)}, bf16[2,128,4096]{2,1,0:T(8,128)(2,1)}, u32[]{:S(2)}, u32[]{:S(2)}) %collective-permute-start.4) | collective-permute-done | bytes 2097184 | tf_op jit(solution)/shard_map/ppermute | solution.py:30
  64.3 4.5 %convolution_convert_fusion = bf16[4096,512]{1,0:T(8,128)(2,1)} fusion(bf16[512,4096]{1,0:T(8,128)(2,1)S(1)} %bitcast.190, bf16[512,512]{0,1:T(8,128)(2,1)S(1)} %bitcast.193), kind=kOutput, calls=%fused_computation.22 | convolution fusion | flops 2149580800 | bytes 8912896 | tf_op jit(solution)/shard_map/dot_general | solution.py:112
  68.9 8.4 %fusion.6 = bf16[1,4,512,2048]{2,3,1,0:T(8,128)(2,1)S(1)} fusion(f32[2048,512,4]{1,0,2:T(8,128)} %copy-done.2, f32[4,512]{1,0:T(4,128)S(1)} %log_add_fusion, pred[512,2048]{0,1:T(8,128)(4,1)S(1)} %fusion.17), kind=kLoop, calls=%fused_computation.10 | loop fusion | flops 16777216 | bytes 26222592 | tf_op jit(solution)/shard_map/convert_element_type | solution.py:145
  82.7 3.2 %bitcast_reduce_fusion = (f32[512,4]{0,1:T(4,128)}, bf16[512,512]{0,1:T(8,128)(2,1)S(1)}) fusion(bf16[512,512]{0,1:T(8,128)(2,1)S(1)} %bitcast.195, bf16[512,4096]{1,0:T(8,128)(2,1)S(1)} %bitcast.191, bf16[512,4096]{1,0:T(8,128)(2,1)S(1)} %copy-done.7), kind=kOutput, calls=%fused_computation.53 | convolution fusion | flops 2148792320 | bytes 9445376 | tf_op jit(solution)/shard_map/dot_general | solution.py:127
  86.1 2.9 %fusion.22 = bf16[1536,128]{0,1:T(8,128)(2,1)} fusion(bf16[512,4,128]{0,2,1:T(8,128)(2,1)S(1)} %bitcast.201, bf16[1,4,512,2048]{2,3,1,0:T(8,128)(2,1)S(1)} %fusion.6), kind=kOutput, calls=%fused_computation.32 | convolution fusion | flops 805502976 | bytes 7208960 | tf_op jit(solution)/shard_map/cgqk,qcgd->kcd/dot_general | solution.py:151
  91.6 9.4 %fusion.2 = bf16[1,4,512,2048]{2,3,1,0:T(8,128)(2,1)} fusion(f32[2048,512,4]{1,0,2:T(8,128)S(1)} %bitcast.185, f32[4,512]{1,0:T(4,128)} %bitcast.204, f32[4,512]{1,0:T(4,128)S(1)} %log_add_fusion, pred[512,2048]{0,1:T(8,128)(4,1)S(1)} %fusion.17, bf16[512,4,128]{0,2,1:T(8,128)(2,1)} %bitcast.202, bf16[2048,256]{1,0:T(8,128)(2,1)} %copy-done.10), kind=kOutput, calls=%fused_computation.3 | convolution fusion | flops 1103101952 | bytes 27279360 | tf_op jit(solution)/shard_map/qcgd,kcd->cgqk/dot_general | solution.py:141
  101.1 5.2 %fusion.21 = bf16[1536,128]{0,1:T(8,128)(2,1)S(1)} fusion(bf16[512,4,128]{0,2,1:T(8,128)(2,1)} %bitcast.197, bf16[1,4,512,2048]{2,3,1,0:T(8,128)(2,1)} %fusion.2), kind=kOutput, calls=%fused_computation.31 | convolution fusion | flops 805502976 | bytes 7208960 | tf_op jit(solution)/shard_map/cgqk,qcgd->kcd/dot_general | solution.py:148
  106.7 3.1 %bitcast_add_fusion = f32[2,128,4096]{2,1,0:T(8,128)S(1)} fusion(bf16[2,128,4096]{2,1,0:T(8,128)(2,1)} %collective-permute-done.5, f32[2,2,128,4096]{3,2,1,0:T(8,128)S(1)} %bitcast.187, s32[]{:T(128)S(6)} %select_n.96), kind=kLoop, calls=%fused_computation.25 | loop fusion | flops 2097152 | bytes 10485764 | tf_op jit(solution)/shard_map/add | solution.py:54
  110.0 3.0 %collective-permute-start.6 = (bf16[128,4096]{1,0:T(8,128)(2,1)S(1)}, bf16[128,4096]{1,0:T(8,128)(2,1)S(1)}, u32[]{:S(2)}, u32[]{:S(2)}) collective-permute-start(bf16[128,4096]{1,0:T(8,128)(2,1)S(1)} %fusion.43), channel_id=1, source_target_pairs={{0,2},{2,0},{1,3},{3,1},{4,6},{6,4},{5,7},{7,5},{8,10},{10,8},{9,1... | collective-permute-start | bytes 3145736 | tf_op jit(solution)/shard_map/ppermute | solution.py:30
  116.2 4.7 %collective-permute-start.9 = (bf16[512,256]{0,1:T(8,128)(2,1)}, bf16[512,256]{0,1:T(8,128)(2,1)S(1)}, u32[]{:S(2)}, u32[]{:S(2)}) collective-permute-start(bf16[512,256]{0,1:T(8,128)(2,1)} %get-tuple-element.43), channel_id=1, source_target_pairs={{12,0},{16,4},{20,8},{24,12},{28,16},{32,20},{36,24},{40,28},{44,3... | collective-permute-start | bytes 786440 | tf_op jit(solution)/shard_map/ppermute | solution.py:26
  120.9 3.6 %collective-permute-start.8 = (bf16[512,256]{0,1:T(8,128)(2,1)}, bf16[512,256]{0,1:T(8,128)(2,1)S(1)}, u32[]{:S(2)}, u32[]{:S(2)}) collective-permute-start(bf16[512,256]{0,1:T(8,128)(2,1)} %get-tuple-element.44), channel_id=1, source_target_pairs={{8,0},{12,4},{16,8},{20,12},{24,16},{28,20},{32,24},{36,28},{40,32... | collective-permute-start | bytes 786440 | tf_op jit(solution)/shard_map/ppermute | solution.py:26
  126.9 3.3 %fusion.40 = f32[512,128]{0,1:T(8,128)} fusion(bf16[512,4,128]{0,2,1:T(8,128)(2,1)} %bitcast.203, bf16[1,4,512,2048]{2,3,1,0:T(8,128)(2,1)} %copy-done.6), kind=kOutput, calls=%fused_computation.50 | convolution fusion | flops 268435456 | bytes 2883584 | tf_op jit(solution)/shard_map/cgqk,qcgd->kcd/dot_general | solution.py:151
  130.1 3.2 %fusion.37 = f32[512,128]{0,1:T(8,128)} fusion(bf16[512,4,128]{0,2,1:T(8,128)(2,1)} %bitcast.198, bf16[1,4,512,2048]{2,3,1,0:T(8,128)(2,1)} %fusion.2), kind=kOutput, calls=%fused_computation.49 | convolution fusion | flops 268435456 | bytes 2883584 | tf_op jit(solution)/shard_map/cgqk,qcgd->kcd/dot_general | solution.py:148
  133.3 4.0 %all-to-all-start = ((bf16[8,64,512]{2,1,0:T(8,128)(2,1)}), bf16[8,64,512]{2,1,0:T(8,128)(2,1)S(1)}, u32[]{:S(2)}, u32[]{:S(2)}) async-start(bf16[8,64,512]{2,1,0:T(8,128)(2,1)} %bitcast.199), calls=%async_computation.1 | async-start | bytes 1048576 | tf_op jit(solution)/shard_map/all_to_all | solution.py:122
  137.3 15.6 %collective-permute-done.6 = bf16[128,4096]{1,0:T(8,128)(2,1)S(1)} collective-permute-done((bf16[128,4096]{1,0:T(8,128)(2,1)S(1)}, bf16[128,4096]{1,0:T(8,128)(2,1)S(1)}, u32[]{:S(2)}, u32[]{:S(2)}) %collective-permute-start.6) | collective-permute-done | bytes 1048608 | tf_op jit(solution)/shard_map/ppermute | solution.py:30
  (96 shorter events, 38.9 us)
Async XLA Ops:
  7.2 16.1 %copy-start = (s32[256]{0:T(256)S(1)}, s32[256]{0:T(256)}, u32[]{:S(2)}) copy-start(s32[256]{0:T(256)} %param.13) | copy-start | bytes 3076
  7.2 126.1 %reduce-scatter.2.cloned.1.call-start = ((), (), s32[]{:S(2)}) async-start(), calls=%async_computation.2 | async-start | bytes 4718592 | tf_op jit(solution)/shard_map/reduce_scatter | solution.py:116
  9.1 19.5 %collective-permute-start.3 = (bf16[512,256]{1,0:T(8,128)(2,1)S(1)}, bf16[512,256]{1,0:T(8,128)(2,1)S(1)}, u32[]{:S(2)}, u32[]{:S(2)}) collective-permute-start(bf16[512,256]{1,0:T(8,128)(2,1)S(1)} %constant_dynamic-update-slice_fusion), channel_id=1, source_target_pairs={{0,4},{4,8},{8,12},{12,16},{16,20},{20,24},{24,28},{28,32},{32,36}... | collective-permute-start | bytes 786440 | tf_op jit(solution)/shard_map/ppermute | solution.py:21
  12.6 16.0 %collective-permute-start.2 = (bf16[512,256]{1,0:T(8,128)(2,1)S(1)}, bf16[512,256]{1,0:T(8,128)(2,1)S(1)}, u32[]{:S(2)}, u32[]{:S(2)}) collective-permute-start(bf16[512,256]{1,0:T(8,128)(2,1)S(1)} %constant_dynamic-update-slice_fusion), channel_id=1, source_target_pairs={{0,8},{4,12},{8,16},{12,20},{16,24},{20,28},{24,32},{28,36},{32,40... | collective-permute-start | bytes 786440 | tf_op jit(solution)/shard_map/ppermute | solution.py:21
  16.0 17.4 %collective-permute-start.1 = (bf16[512,256]{1,0:T(8,128)(2,1)S(1)}, bf16[512,256]{1,0:T(8,128)(2,1)}, u32[]{:S(2)}, u32[]{:S(2)}) collective-permute-start(bf16[512,256]{1,0:T(8,128)(2,1)S(1)} %constant_dynamic-update-slice_fusion), channel_id=1, source_target_pairs={{0,12},{4,16},{8,20},{12,24},{16,28},{20,32},{24,36},{28,40},{32,4... | collective-permute-start | bytes 786440 | tf_op jit(solution)/shard_map/ppermute | solution.py:21
  19.9 31.5 %collective-permute-start = (bf16[128,4096]{1,0:T(8,128)(2,1)}, bf16[128,4096]{1,0:T(8,128)(2,1)S(1)}, u32[]{:S(2)}, u32[]{:S(2)}) collective-permute-start(bf16[128,4096]{1,0:T(8,128)(2,1)} %param.11), channel_id=1, source_target_pairs={{0,2},{2,0},{1,3},{3,1},{4,6},{6,4},{5,7},{7,5},{8,10},{10,8},{9,1... | collective-permute-start | bytes 3145736 | tf_op jit(solution)/shard_map/ppermute | solution.py:30
  26.3 11.3 %copy-start.16 = (bf16[512,512]{0,1:T(8,128)(2,1)}, bf16[512,512]{0,1:T(8,128)(2,1)S(1)}, u32[]{:S(2)}) copy-start(bf16[512,512]{0,1:T(8,128)(2,1)S(1)} %copy.57) | copy-start | bytes 1572868
  34.4 7.3 %copy-start.10 = (bf16[2048,256]{1,0:T(8,128)(2,1)}, bf16[2048,256]{1,0:T(8,128)(2,1)S(1)}, u32[]{:S(2)}) copy-start(bf16[2048,256]{1,0:T(8,128)(2,1)S(1)} %pad_maximum_fusion.2) | copy-start | bytes 3145732
  43.3 9.1 %copy-start.12 = (bf16[128,4096]{1,0:T(8,128)(2,1)S(1)}, bf16[128,4096]{1,0:T(8,128)(2,1)}, u32[]{:S(2)}) copy-start(bf16[128,4096]{1,0:T(8,128)(2,1)} %param.11) | copy-start | bytes 3145732
  55.3 4.5 %collective-permute-start.4 = (bf16[2,128,4096]{2,1,0:T(8,128)(2,1)}, bf16[2,128,4096]{2,1,0:T(8,128)(2,1)}, u32[]{:S(2)}, u32[]{:S(2)}) collective-permute-start(bf16[2,128,4096]{2,1,0:T(8,128)(2,1)} %pad_maximum_fusion.1), channel_id=1, source_target_pairs={{0,1},{1,0},{2,3},{3,2},{4,5},{5,4},{6,7},{7,6},{8,9},{9,8},{10,11... | collective-permute-start | bytes 6291464 | tf_op jit(solution)/shard_map/ppermute | solution.py:30
  68.9 8.4 %copy-start.7 = (bf16[512,4096]{1,0:T(8,128)(2,1)S(1)}, bf16[512,4096]{1,0:T(8,128)(2,1)}, u32[]{:S(2)}) copy-start(bf16[512,4096]{1,0:T(8,128)(2,1)} %param.10) | copy-start | bytes 12582916
  68.9 8.4 %copy-start.15 = (bf16[512,1,4,128]{0,3,2,1:T(8,128)(2,1)S(1)}, bf16[512,1,4,128]{0,3,2,1:T(8,128)(2,1)}, u32[]{:S(2)}) copy-start(bf16[512,1,4,128]{0,3,2,1:T(8,128)(2,1)} %divide_convert_fusion) | copy-start | bytes 1572868
  77.4 8.7 %copy-start.6 = (bf16[1,4,512,2048]{2,3,1,0:T(8,128)(2,1)}, bf16[1,4,512,2048]{2,3,1,0:T(8,128)(2,1)S(1)}, u32[]{:S(2)}) copy-start(bf16[1,4,512,2048]{2,3,1,0:T(8,128)(2,1)S(1)} %fusion.6) | copy-start | bytes 25165828
  81.5 24.9 %collective-permute-start.5 = (bf16[2,128,4096]{2,1,0:T(8,128)(2,1)}, bf16[2,128,4096]{2,1,0:T(8,128)(2,1)}, u32[]{:S(2)}, u32[]{:S(2)}) collective-permute-start(bf16[2,128,4096]{2,1,0:T(8,128)(2,1)} %fusion.23), channel_id=1, source_target_pairs={{0,1},{1,0},{2,3},{3,2},{4,5},{5,4},{6,7},{7,6},{8,9},{9,8},{10,11... | collective-permute-start | bytes 6291464 | tf_op jit(solution)/shard_map/ppermute | solution.py:30
  82.7 7.5 %slice-start.2 = ((s8[16777216]{0:T(1024)(128)(4,1)}), s8[4194304]{0:T(1024)(128)(4,1)S(1)}, s32[]{:S(2)}) async-start(s8[16777216]{0:T(1024)(128)(4,1)} %bitcast.184), calls=%async_computation.5 | async-start | bytes 8388608
  101.1 11.9 %slice-start.4 = ((s8[8388608]{0:T(1024)(128)(4,1)}), s8[4194304]{0:T(1024)(128)(4,1)S(1)}, s32[]{:S(2)}) async-start(s8[8388608]{0:T(1024)(128)(4,1)} %bitcast.188), calls=%async_computation.7 | async-start | bytes 8388608
  106.3 6.7 %slice-start.5 = ((s8[8388608]{0:T(1024)(128)(4,1)}), s8[4194304]{0:T(1024)(128)(4,1)S(1)}, s32[]{:S(2)}) async-start(s8[8388608]{0:T(1024)(128)(4,1)} %bitcast.188), calls=%async_computation.8 | async-start | bytes 8388608
  106.4 6.6 %copy-start.11 = (bf16[2048,256]{1,0:T(8,128)(2,1)S(1)}, bf16[2048,256]{1,0:T(8,128)(2,1)}, u32[]{:S(2)}) copy-start(bf16[2048,256]{1,0:T(8,128)(2,1)} %copy-done.10) | copy-start | bytes 3145732
  110.0 43.0 %collective-permute-start.6 = (bf16[128,4096]{1,0:T(8,128)(2,1)S(1)}, bf16[128,4096]{1,0:T(8,128)(2,1)S(1)}, u32[]{:S(2)}, u32[]{:S(2)}) collective-permute-start(bf16[128,4096]{1,0:T(8,128)(2,1)S(1)} %fusion.43), channel_id=1, source_target_pairs={{0,2},{2,0},{1,3},{3,1},{4,6},{6,4},{5,7},{7,5},{8,10},{10,8},{9,1... | collective-permute-start | bytes 3145736 | tf_op jit(solution)/shard_map/ppermute | solution.py:30
  116.2 40.3 %collective-permute-start.9 = (bf16[512,256]{0,1:T(8,128)(2,1)}, bf16[512,256]{0,1:T(8,128)(2,1)S(1)}, u32[]{:S(2)}, u32[]{:S(2)}) collective-permute-start(bf16[512,256]{0,1:T(8,128)(2,1)} %get-tuple-element.43), channel_id=1, source_target_pairs={{12,0},{16,4},{20,8},{24,12},{28,16},{32,20},{36,24},{40,28},{44,3... | collective-permute-start | bytes 786440 | tf_op jit(solution)/shard_map/ppermute | solution.py:26
  120.9 35.6 %collective-permute-start.8 = (bf16[512,256]{0,1:T(8,128)(2,1)}, bf16[512,256]{0,1:T(8,128)(2,1)S(1)}, u32[]{:S(2)}, u32[]{:S(2)}) collective-permute-start(bf16[512,256]{0,1:T(8,128)(2,1)} %get-tuple-element.44), channel_id=1, source_target_pairs={{8,0},{12,4},{16,8},{20,12},{24,16},{28,20},{32,24},{36,28},{40,32... | collective-permute-start | bytes 786440 | tf_op jit(solution)/shard_map/ppermute | solution.py:26
  124.5 32.0 %collective-permute-start.7 = (bf16[512,256]{0,1:T(8,128)(2,1)}, bf16[512,256]{0,1:T(8,128)(2,1)S(1)}, u32[]{:S(2)}, u32[]{:S(2)}) collective-permute-start(bf16[512,256]{0,1:T(8,128)(2,1)} %get-tuple-element.45), channel_id=1, source_target_pairs={{4,0},{8,4},{12,8},{16,12},{20,16},{24,20},{28,24},{32,28},{36,32}... | collective-permute-start | bytes 786440 | tf_op jit(solution)/shard_map/ppermute | solution.py:26
  126.8 32.4 %copy-start.1 = (s32[256]{0:T(256)S(1)}, s32[256]{0:T(256)}, u32[]{:S(2)}) copy-start(s32[256]{0:T(256)} %param.13) | copy-start | bytes 3076
  133.3 22.4 %all-to-all-start = ((bf16[8,64,512]{2,1,0:T(8,128)(2,1)}), bf16[8,64,512]{2,1,0:T(8,128)(2,1)S(1)}, u32[]{:S(2)}, u32[]{:S(2)}) async-start(bf16[8,64,512]{2,1,0:T(8,128)(2,1)} %bitcast.199), calls=%async_computation.1 | async-start | bytes 1048576 | tf_op jit(solution)/shard_map/all_to_all | solution.py:122
  (13 other events, 59.0 us)
Sparse Core Ops, SparseCore 0:
  69.0 55.2 reduce-scatter.1

commit v11 on v10

--- a/solution.py
+++ b/solution.py
@@ -41,8 +41,9 @@
     low = lax.axis_index(TP[1])
     other, after = lax.optimization_barrier((swapped(piece, TP[0]), after))
     by_high = in_order(piece, other, high)
-    both = in_order(by_high, swapped(by_high, TP[1]), low)
-    return jnp.transpose(both, (1, 0, 2, 3)).reshape(-1, piece.shape[1]), after
+    partner = swapped(by_high, TP[1])
+    both = in_order(by_high, partner, low)
+    return jnp.transpose(both, (1, 0, 2, 3)).reshape(-1, piece.shape[1]), after, by_high, partner
 
 
 def summed_over_tp(part):
@@ -107,11 +108,16 @@
     attn_four = summed / jnp.transpose(total, (2, 0, 1))[..., None]
     attn = attn_four.reshape(tokens_here, -1).astype(jnp.bfloat16)
     log_sum = row_max + jnp.log(total)
-    grad_piece, attn = gathered_over_tp(out_grad, attn)
-
+    grad_piece, attn, own_rows, partner_rows = gathered_over_tp(out_grad, attn)
+    low = lax.axis_index(TP[1])
+    attn_quarters = attn.reshape(2, 2, tokens_here // 4, attn.shape[1])
+    own_attn = lax.dynamic_index_in_dim(attn_quarters, low, 1, keepdims=False)
+    partner_attn = lax.dynamic_index_in_dim(attn_quarters, 1 - low, 1, keepdims=False)
+    contract = (((0, 1), (0, 1)), ((), ()))
     weight_part = lax.dot_general(
-        grad_piece, attn, (((0,), (0,)), ((), ())), preferred_element_type=jnp.float32
-    ).astype(jnp.bfloat16)
+        own_rows, own_attn, contract, preferred_element_type=jnp.float32
+    ) + lax.dot_general(partner_rows, partner_attn, contract, preferred_element_type=jnp.float32)
+    weight_part = weight_part.astype(jnp.bfloat16)
     weight_part, attn, grad_piece = lax.optimization_barrier((weight_part, attn, grad_piece))
     weight_sum = lax.psum_scatter(weight_part, CTX[0], scatter_dimension=0, tiled=True)
 

time: 168 us -> 187 us (1.11)
  local copies, waits for them, and re-layouts: 19 us -> 34.2 us
  matrix products: 43.7 us -> 53.4 us
  waiting for transfers between devices: 27.8 us -> 19.5 us
  other arithmetic: 29.3 us -> 31.4 us
    dot_general x1 -> x2, matrix products: 4.54 us -> 12.8 us  [the longest x1 7.32 us: on_device(): lax.dot_general(partner_rows, partner_attn, contract, preferred_element_t...]
    transpose x0 -> x1, local copies, waits for them, and re-layouts: none -> 6.46 us  [gathered_over_tp(): jnp.transpose(both, (1, 0, 2, 3)).reshape(-1, piece.shape[1])]
    ppermute x4, waiting for transfers between devices: 23 us -> 18.5 us  [swapped(): return lax.ppermute(block, axis, [(0, 1), (1, 0)])]
    ppermute x3, waiting for transfers between devices: 4.76 us -> 0.98 us  [from_earlier(): return lax.ppermute(block, CTX, route)]
    dynamic_slice x0 -> x1, local copies, waits for them, and re-layouts: none -> 3.24 us  [on_device(): lax.dynamic_index_in_dim(attn_quarters, 1 - low, 1, keepdims=False)]
    unnamed x54 -> x55, local copies, waits for them, and re-layouts: 12.4 us -> 15.1 us
    transpose x0 -> x1, other arithmetic: none -> 2.37 us  [gathered_over_tp(): jnp.transpose(both, (1, 0, 2, 3)).reshape(-1, piece.shape[1])]
    reshape x0 -> x1, local copies, waits for them, and re-layouts: none -> 1.96 us  [on_device(): attn_quarters = attn.reshape(2, 2, tokens_here // 4, attn.shape[1])]
  transfers between devices with their start and end apart: 12 -> 12, of which waited for: 4 -> 3; matrix products, arithmetic and copies ran while one was open for 41% -> 47% of each run, Pallas kernels for 0% -> 0%
where the time goes in v11:
time: 187 us; the launch traced here: 185 us
  matrix products  53.4 us (29%)
  local copies, waits for them, and re-layouts  34.2 us (18%)
  starting transfers between devices  32.3 us (17%)
  other arithmetic  31.4 us (17%)
  waiting for transfers between devices  19.5 us (10%)
  between operations  14.5 us (8%)
    ppermute x4, waiting for transfers between devices, swapped(): return lax.ppermute(block, axis, [(0, 1), (1, 0)])  18.5 us
    unnamed x55, local copies, waits for them, and re-layouts  15.1 us
    ppermute x3, starting transfers between devices, to_earlier(): return lax.ppermute(block, CTX, route)  11.2 us
    ppermute x3, starting transfers between devices, from_earlier(): return lax.ppermute(block, CTX, route)  10.8 us
    dot_general x1, matrix products, on_device(): jnp.einsum('qcgd,kcd->cgqk', grad_four, value_heads, preferred_element_ty...  9.43 us
    convert_element_type x1, other arithmetic, on_device(): probs_half = probs.astype(jnp.bfloat16)  8.4 us
    dot_general x2, matrix products, key_side(): jnp.einsum('cgqk,qcgd->kcd', score_part, query_four, preferred_element_ty...  8.38 us
    dot_general x1, matrix products, on_device(): lax.dot_general(partner_rows, partner_attn, contract, preferred_element_t...  7.32 us
  transfers between devices with their start and end apart: 12, of which 3 were waited for; matrix products, arithmetic and copies ran while one was open for 47% of the time, Pallas kernels for 0%

profile of v11, /device:TPU:96, one launch (start us, length us, event | category | flops | bytes accessed | tf_op | source)
XLA Modules:
  0.0 185.3 jit_solution(18144058835436313589)
XLA Ops:
  9.1 3.5 %collective-permute-start.3 = (bf16[512,256]{1,0:T(8,128)(2,1)S(1)}, bf16[512,256]{1,0:T(8,128)(2,1)S(1)}, u32[]{:S(2)}, u32[]{:S(2)}) collective-permute-start(bf16[512,256]{1,0:T(8,128)(2,1)S(1)} %constant_dynamic-update-slice_fusion), channel_id=1, source_target_pairs={{0,4},{4,8},{8,12},{12,16},{16,20},{20,24},{24,28},{28,32},{32,36}... | collective-permute-start | bytes 786440 | tf_op jit(solution)/shard_map/ppermute | solution.py:21
  12.6 3.4 %collective-permute-start.2 = (bf16[512,256]{1,0:T(8,128)(2,1)S(1)}, bf16[512,256]{1,0:T(8,128)(2,1)S(1)}, u32[]{:S(2)}, u32[]{:S(2)}) collective-permute-start(bf16[512,256]{1,0:T(8,128)(2,1)S(1)} %constant_dynamic-update-slice_fusion), channel_id=1, source_target_pairs={{0,8},{4,12},{8,16},{12,20},{16,24},{20,28},{24,32},{28,36},{32,40... | collective-permute-start | bytes 786440 | tf_op jit(solution)/shard_map/ppermute | solution.py:21
  16.0 3.9 %collective-permute-start.1 = (bf16[512,256]{1,0:T(8,128)(2,1)S(1)}, bf16[512,256]{1,0:T(8,128)(2,1)}, u32[]{:S(2)}, u32[]{:S(2)}) collective-permute-start(bf16[512,256]{1,0:T(8,128)(2,1)S(1)} %constant_dynamic-update-slice_fusion), channel_id=1, source_target_pairs={{0,12},{4,16},{8,20},{12,24},{16,28},{20,32},{24,36},{28,40},{32,4... | collective-permute-start | bytes 786440 | tf_op jit(solution)/shard_map/ppermute | solution.py:21
  21.6 3.3 %collective-permute-start = (bf16[128,4096]{0,1:T(8,128)(2,1)S(1)}, bf16[128,4096]{0,1:T(8,128)(2,1)}, u32[]{:S(2)}, u32[]{:S(2)}) collective-permute-start(bf16[128,4096]{0,1:T(8,128)(2,1)S(1)} %copy.37), channel_id=1, source_target_pairs={{0,2},{2,0},{1,3},{3,1},{4,6},{6,4},{5,7},{7,5},{8,10},{10,8},{9,1... | collective-permute-start | bytes 3145736 | tf_op jit(solution)/shard_map/ppermute | solution.py:30
  34.6 4.6 %fusion.5 = (f32[4,512]{1,0:T(4,128)S(1)}, f32[2048,512,4]{1,0,2:T(8,128)S(1)}) fusion(pred[512,2048]{0,1:T(8,128)(4,1)S(1)} %fusion.18, bf16[512,4,128]{0,2,1:T(8,128)(2,1)} %bitcast.206, bf16[2048,256]{1,0:T(8,128)(2,1)S(1)} %pad_maximum_fusion.1), kind=kOutput, calls=%fused_computation.9 | convolution fusion | flops 1086322688 | bytes 18882560 | tf_op jit(solution)/shard_map/qcgd,kcd->cgqk/dot_general | solution.py:98
  39.2 4.2 %fusion.7 = f32[4,512]{1,0:T(4,128)S(1)} fusion(f32[2048,512,4]{1,0,2:T(8,128)S(1)} %get-tuple-element.51, f32[4,512]{1,0:T(4,128)S(1)} %get-tuple-element.50, pred[512,2048]{0,1:T(8,128)(4,1)S(1)} %fusion.18), kind=kLoop, calls=%fused_computation.11 | loop fusion | flops 20969472 | bytes 17842176 | tf_op jit(solution)/shard_map/reduce_sum | solution.py:104
  44.9 5.2 %divide_convert_fusion = bf16[512,1,4,128]{0,3,2,1:T(8,128)(2,1)} fusion(f32[2048,512,4]{1,0,2:T(8,128)S(1)} %get-tuple-element.51, f32[4,512]{1,0:T(4,128)S(1)} %get-tuple-element.50, pred[512,2048]{0,1:T(8,128)(4,1)S(1)} %fusion.18, f32[512,4]{0,1:T(4,128)S(1)} %bitcast.210, bf16[2048,256]{1,0:T(8,128)(2,1)S(1)} %pad_maximum_fusion.1), kind=kOutput, calls=%fused_computation.59 | convolution fusion | flops 1095237632 | bytes 18890752 | tf_op jit(solution)/shard_map/cgqk,kcd->qcgd/dot_general | solution.py:105
  50.1 2.8 %collective-permute-done = bf16[128,4096]{0,1:T(8,128)(2,1)} collective-permute-done((bf16[128,4096]{0,1:T(8,128)(2,1)S(1)}, bf16[128,4096]{0,1:T(8,128)(2,1)}, u32[]{:S(2)}, u32[]{:S(2)}) %collective-permute-start) | collective-permute-done | bytes 1048608 | tf_op jit(solution)/shard_map/ppermute | solution.py:30
  57.8 3.2 %constant_dynamic-slice_fusion = (bf16[2,1,128,512]{2,1,0,3:T(2,128)(2,1)}, bf16[2,1,128,512]{2,1,0,3:T(2,128)(2,1)}) fusion(bf16[2,2,128,512]{2,1,0,3:T(2,128)(2,1)} %reshape.242, s32[]{:T(128)S(6)} %select_n.97, s32[]{:T(128)S(6)} %select_n.96), kind=kLoop, calls=%fused_computation.95 | loop fusion | bytes 1048584 | tf_op jit(solution)/shard_map/jit(dynamic_index_in_dim)/dynamic_slice | solution.py:115
  64.2 5.5 %fusion.52 = f32[4096,512,1]{1,0,2:T(8,128)} fusion(bf16[2,1,128,512]{3,2,0,1:T(8,128)(2,1)} %copy.66, bf16[1,128,4096]{1,2,0:T(8,128)(2,1)S(1)} %get-tuple-element.42, bf16[1,128,4096]{1,2,0:T(8,128)(2,1)S(1)} %get-tuple-element.41), kind=kOutput, calls=%fused_computation.69 | convolution fusion | flops 1074790400 | bytes 10747904 | tf_op jit(solution)/shard_map/dot_general | solution.py:117
  74.2 6.5 %copy.41 = bf16[2,2,128,4096]{3,2,1,0:T(8,128)(2,1)} copy(bf16[2,2,128,4096]{2,3,0,1:T(8,128)(2,1)} %maximum_bitcast_fusion) | data formatting | bytes 8388608 | tf_op jit(solution)/shard_map/transpose | solution.py:46
  80.7 7.3 %fusion.12 = bf16[4096,512]{1,0:T(8,128)(2,1)} fusion(f32[4096,512,1]{1,0,2:T(8,128)} %fusion.52, bf16[2,128,4096]{1,2,0:T(8,128)(2,1)} %collective-permute-done.4, bf16[2,1,128,512]{3,2,0,1:T(8,128)(2,1)S(1)} %copy.67), kind=kOutput, calls=%fused_computation.17 | convolution fusion | flops 1077936128 | bytes 14942208 | tf_op jit(solution)/shard_map/dot_general | solution.py:119
  88.0 8.4 %fusion.6 = bf16[1,4,512,2048]{2,3,1,0:T(8,128)(2,1)S(1)} fusion(f32[2048,512,4]{1,0,2:T(8,128)} %copy-done.2, f32[4,512]{1,0:T(4,128)S(1)} %log_add_fusion, pred[512,2048]{0,1:T(8,128)(4,1)S(1)} %fusion.18), kind=kLoop, calls=%fused_computation.10 | loop fusion | flops 16777216 | bytes 26222592 | tf_op jit(solution)/shard_map/convert_element_type | solution.py:151
  101.8 3.2 %bitcast_reduce_fusion = (f32[512,4]{0,1:T(4,128)}, bf16[512,512]{0,1:T(8,128)(2,1)S(1)}) fusion(bf16[512,512]{0,1:T(8,128)(2,1)S(1)} %bitcast.205, bf16[512,4096]{1,0:T(8,128)(2,1)S(1)} %bitcast.201, bf16[512,4096]{1,0:T(8,128)(2,1)S(1)} %copy-done.7), kind=kOutput, calls=%fused_computation.54 | convolution fusion | flops 2148792320 | bytes 9445376 | tf_op jit(solution)/shard_map/dot_general | solution.py:133
  105.2 2.9 %fusion.23 = bf16[1536,128]{0,1:T(8,128)(2,1)} fusion(bf16[512,4,128]{0,2,1:T(8,128)(2,1)S(1)} %bitcast.211, bf16[1,4,512,2048]{2,3,1,0:T(8,128)(2,1)S(1)} %fusion.6), kind=kOutput, calls=%fused_computation.33 | convolution fusion | flops 805502976 | bytes 7208960 | tf_op jit(solution)/shard_map/cgqk,qcgd->kcd/dot_general | solution.py:157
  110.8 9.4 %fusion.2 = bf16[1,4,512,2048]{2,3,1,0:T(8,128)(2,1)} fusion(f32[2048,512,4]{1,0,2:T(8,128)S(1)} %bitcast.196, f32[4,512]{1,0:T(4,128)} %bitcast.214, f32[4,512]{1,0:T(4,128)S(1)} %log_add_fusion, pred[512,2048]{0,1:T(8,128)(4,1)S(1)} %fusion.18, bf16[512,4,128]{0,2,1:T(8,128)(2,1)} %bitcast.212, bf16[2048,256]{1,0:T(8,128)(2,1)} %copy-done.11), kind=kOutput, calls=%fused_computation.3 | convolution fusion | flops 1103101952 | bytes 27279360 | tf_op jit(solution)/shard_map/qcgd,kcd->cgqk/dot_general | solution.py:147
  120.2 5.2 %fusion.22 = bf16[1536,128]{0,1:T(8,128)(2,1)S(1)} fusion(bf16[512,4,128]{0,2,1:T(8,128)(2,1)} %bitcast.207, bf16[1,4,512,2048]{2,3,1,0:T(8,128)(2,1)} %fusion.2), kind=kOutput, calls=%fused_computation.32 | convolution fusion | flops 805502976 | bytes 7208960 | tf_op jit(solution)/shard_map/cgqk,qcgd->kcd/dot_general | solution.py:154
  125.9 3.1 %bitcast_add_fusion.1 = f32[2,128,4096]{2,1,0:T(8,128)S(1)} fusion(bf16[2,128,4096]{2,1,0:T(8,128)(2,1)} %collective-permute-done.5, f32[2,2,128,4096]{3,2,1,0:T(8,128)S(1)} %bitcast.198, s32[]{:T(128)S(6)} %select_n.96), kind=kLoop, calls=%fused_computation.26 | loop fusion | flops 2097152 | bytes 10485764 | tf_op jit(solution)/shard_map/add | solution.py:55
  134.8 5.0 %collective-permute-start.9 = (bf16[512,256]{0,1:T(8,128)(2,1)}, bf16[512,256]{0,1:T(8,128)(2,1)S(1)}, u32[]{:S(2)}, u32[]{:S(2)}) collective-permute-start(bf16[512,256]{0,1:T(8,128)(2,1)} %get-tuple-element.43), channel_id=1, source_target_pairs={{12,0},{16,4},{20,8},{24,12},{28,16},{32,20},{36,24},{40,28},{44,3... | collective-permute-start | bytes 786440 | tf_op jit(solution)/shard_map/ppermute | solution.py:26
  139.8 3.8 %collective-permute-start.8 = (bf16[512,256]{0,1:T(8,128)(2,1)}, bf16[512,256]{0,1:T(8,128)(2,1)S(1)}, u32[]{:S(2)}, u32[]{:S(2)}) collective-permute-start(bf16[512,256]{0,1:T(8,128)(2,1)} %get-tuple-element.44), channel_id=1, source_target_pairs={{8,0},{12,4},{16,8},{20,12},{24,16},{28,20},{32,24},{36,28},{40,32... | collective-permute-start | bytes 786440 | tf_op jit(solution)/shard_map/ppermute | solution.py:26
  146.0 3.3 %fusion.41 = f32[512,128]{0,1:T(8,128)} fusion(bf16[512,4,128]{0,2,1:T(8,128)(2,1)} %bitcast.213, bf16[1,4,512,2048]{2,3,1,0:T(8,128)(2,1)} %copy-done.6), kind=kOutput, calls=%fused_computation.51 | convolution fusion | flops 268435456 | bytes 2883584 | tf_op jit(solution)/shard_map/cgqk,qcgd->kcd/dot_general | solution.py:157
  149.3 3.2 %fusion.38 = f32[512,128]{0,1:T(8,128)} fusion(bf16[512,4,128]{0,2,1:T(8,128)(2,1)} %bitcast.208, bf16[1,4,512,2048]{2,3,1,0:T(8,128)(2,1)} %fusion.2), kind=kOutput, calls=%fused_computation.50 | convolution fusion | flops 268435456 | bytes 2883584 | tf_op jit(solution)/shard_map/cgqk,qcgd->kcd/dot_general | solution.py:154
  152.5 3.9 %all-to-all-start = ((bf16[8,64,512]{2,1,0:T(8,128)(2,1)}), bf16[8,64,512]{2,1,0:T(8,128)(2,1)S(1)}, u32[]{:S(2)}, u32[]{:S(2)}) async-start(bf16[8,64,512]{2,1,0:T(8,128)(2,1)} %bitcast.209), calls=%async_computation.1 | async-start | bytes 1048576 | tf_op jit(solution)/shard_map/all_to_all | solution.py:128
  156.5 15.7 %collective-permute-done.6 = bf16[128,4096]{1,0:T(8,128)(2,1)S(1)} collective-permute-done((bf16[128,4096]{1,0:T(8,128)(2,1)S(1)}, bf16[128,4096]{1,0:T(8,128)(2,1)S(1)}, u32[]{:S(2)}, u32[]{:S(2)}) %collective-permute-start.6) | collective-permute-done | bytes 1048608 | tf_op jit(solution)/shard_map/ppermute | solution.py:30
  (101 shorter events, 50.4 us)
Async XLA Ops:
  7.2 17.8 %copy-start = (s32[256]{0:T(256)S(1)}, s32[256]{0:T(256)}, u32[]{:S(2)}) copy-start(s32[256]{0:T(256)} %param.13) | copy-start | bytes 3076
  7.2 145.3 %reduce-scatter.2.cloned.1.call-start = ((), (), s32[]{:S(2)}) async-start(), calls=%async_computation.2 | async-start | bytes 4718592 | tf_op jit(solution)/shard_map/reduce_scatter | solution.py:122
  9.1 21.9 %collective-permute-start.3 = (bf16[512,256]{1,0:T(8,128)(2,1)S(1)}, bf16[512,256]{1,0:T(8,128)(2,1)S(1)}, u32[]{:S(2)}, u32[]{:S(2)}) collective-permute-start(bf16[512,256]{1,0:T(8,128)(2,1)S(1)} %constant_dynamic-update-slice_fusion), channel_id=1, source_target_pairs={{0,4},{4,8},{8,12},{12,16},{16,20},{20,24},{24,28},{28,32},{32,36}... | collective-permute-start | bytes 786440 | tf_op jit(solution)/shard_map/ppermute | solution.py:21
  12.6 18.4 %collective-permute-start.2 = (bf16[512,256]{1,0:T(8,128)(2,1)S(1)}, bf16[512,256]{1,0:T(8,128)(2,1)S(1)}, u32[]{:S(2)}, u32[]{:S(2)}) collective-permute-start(bf16[512,256]{1,0:T(8,128)(2,1)S(1)} %constant_dynamic-update-slice_fusion), channel_id=1, source_target_pairs={{0,8},{4,12},{8,16},{12,20},{16,24},{20,28},{24,32},{28,36},{32,40... | collective-permute-start | bytes 786440 | tf_op jit(solution)/shard_map/ppermute | solution.py:21
  16.0 17.4 %collective-permute-start.1 = (bf16[512,256]{1,0:T(8,128)(2,1)S(1)}, bf16[512,256]{1,0:T(8,128)(2,1)}, u32[]{:S(2)}, u32[]{:S(2)}) collective-permute-start(bf16[512,256]{1,0:T(8,128)(2,1)S(1)} %constant_dynamic-update-slice_fusion), channel_id=1, source_target_pairs={{0,12},{4,16},{8,20},{12,24},{16,28},{20,32},{24,36},{28,40},{32,4... | collective-permute-start | bytes 786440 | tf_op jit(solution)/shard_map/ppermute | solution.py:21
  21.6 17.6 %copy-start.8 = (bf16[128,4096]{0,1:T(8,128)(2,1)}, bf16[128,4096]{0,1:T(8,128)(2,1)S(1)}, u32[]{:S(2)}) copy-start(bf16[128,4096]{0,1:T(8,128)(2,1)S(1)} %copy.37) | copy-start | bytes 3145732
  21.6 31.4 %collective-permute-start = (bf16[128,4096]{0,1:T(8,128)(2,1)S(1)}, bf16[128,4096]{0,1:T(8,128)(2,1)}, u32[]{:S(2)}, u32[]{:S(2)}) collective-permute-start(bf16[128,4096]{0,1:T(8,128)(2,1)S(1)} %copy.37), channel_id=1, source_target_pairs={{0,2},{2,0},{1,3},{3,1},{4,6},{6,4},{5,7},{7,5},{8,10},{10,8},{9,1... | collective-permute-start | bytes 3145736 | tf_op jit(solution)/shard_map/ppermute | solution.py:30
  34.6 8.8 %copy-start.11 = (bf16[2048,256]{1,0:T(8,128)(2,1)}, bf16[2048,256]{1,0:T(8,128)(2,1)S(1)}, u32[]{:S(2)}) copy-start(bf16[2048,256]{1,0:T(8,128)(2,1)S(1)} %pad_maximum_fusion.1) | copy-start | bytes 3145732
  44.9 8.0 %copy-start.9 = (bf16[128,4096]{0,1:T(8,128)(2,1)S(1)}, bf16[128,4096]{0,1:T(8,128)(2,1)}, u32[]{:S(2)}) copy-start(bf16[128,4096]{0,1:T(8,128)(2,1)} %copy-done.8) | copy-start | bytes 3145732
  55.9 13.8 %collective-permute-start.4 = (bf16[2,128,4096]{1,2,0:T(8,128)(2,1)}, bf16[2,128,4096]{1,2,0:T(8,128)(2,1)}, u32[]{:S(2)}, u32[]{:S(2)}) collective-permute-start(bf16[2,128,4096]{1,2,0:T(8,128)(2,1)} %pad_maximum_fusion), channel_id=1, source_target_pairs={{0,1},{1,0},{2,3},{3,2},{4,5},{5,4},{6,7},{7,6},{8,9},{9,8},{10,11... | collective-permute-start | bytes 6291464 | tf_op jit(solution)/shard_map/ppermute | solution.py:30
  88.0 8.4 %copy-start.7 = (bf16[512,4096]{1,0:T(8,128)(2,1)S(1)}, bf16[512,4096]{1,0:T(8,128)(2,1)}, u32[]{:S(2)}) copy-start(bf16[512,4096]{1,0:T(8,128)(2,1)} %param.10) | copy-start | bytes 12582916
  88.0 8.4 %copy-start.13 = (bf16[512,1,4,128]{0,3,2,1:T(8,128)(2,1)S(1)}, bf16[512,1,4,128]{0,3,2,1:T(8,128)(2,1)}, u32[]{:S(2)}) copy-start(bf16[512,1,4,128]{0,3,2,1:T(8,128)(2,1)} %divide_convert_fusion) | copy-start | bytes 1572868
  96.5 8.8 %copy-start.6 = (bf16[1,4,512,2048]{2,3,1,0:T(8,128)(2,1)}, bf16[1,4,512,2048]{2,3,1,0:T(8,128)(2,1)S(1)}, u32[]{:S(2)}) copy-start(bf16[1,4,512,2048]{2,3,1,0:T(8,128)(2,1)S(1)} %fusion.6) | copy-start | bytes 25165828
  100.6 24.9 %collective-permute-start.5 = (bf16[2,128,4096]{2,1,0:T(8,128)(2,1)}, bf16[2,128,4096]{2,1,0:T(8,128)(2,1)}, u32[]{:S(2)}, u32[]{:S(2)}) collective-permute-start(bf16[2,128,4096]{2,1,0:T(8,128)(2,1)} %fusion.24), channel_id=1, source_target_pairs={{0,1},{1,0},{2,3},{3,2},{4,5},{5,4},{6,7},{7,6},{8,9},{9,8},{10,11... | collective-permute-start | bytes 6291464 | tf_op jit(solution)/shard_map/ppermute | solution.py:30
  101.7 6.4 %slice-start = ((s8[16777216]{0:T(1024)(128)(4,1)}), s8[4194304]{0:T(1024)(128)(4,1)S(1)}, s32[]{:S(2)}) async-start(s8[16777216]{0:T(1024)(128)(4,1)} %bitcast.195), calls=%async_computation.3 | async-start | bytes 8388608
  101.7 6.4 %slice-start.1 = ((s8[16777216]{0:T(1024)(128)(4,1)}), s8[4194304]{0:T(1024)(128)(4,1)S(1)}, s32[]{:S(2)}) async-start(s8[16777216]{0:T(1024)(128)(4,1)} %bitcast.195), calls=%async_computation.4 | async-start | bytes 8388608
  101.8 7.5 %slice-start.2 = ((s8[16777216]{0:T(1024)(128)(4,1)}), s8[4194304]{0:T(1024)(128)(4,1)S(1)}, s32[]{:S(2)}) async-start(s8[16777216]{0:T(1024)(128)(4,1)} %bitcast.195), calls=%async_computation.5 | async-start | bytes 8388608
  120.2 11.3 %slice-start.4 = ((s8[8388608]{0:T(1024)(128)(4,1)}), s8[4194304]{0:T(1024)(128)(4,1)S(1)}, s32[]{:S(2)}) async-start(s8[8388608]{0:T(1024)(128)(4,1)} %bitcast.199), calls=%async_computation.7 | async-start | bytes 8388608
  129.1 43.1 %collective-permute-start.6 = (bf16[128,4096]{1,0:T(8,128)(2,1)S(1)}, bf16[128,4096]{1,0:T(8,128)(2,1)S(1)}, u32[]{:S(2)}, u32[]{:S(2)}) collective-permute-start(bf16[128,4096]{1,0:T(8,128)(2,1)S(1)} %fusion.44), channel_id=1, source_target_pairs={{0,2},{2,0},{1,3},{3,1},{4,6},{6,4},{5,7},{7,5},{8,10},{10,8},{9,1... | collective-permute-start | bytes 3145736 | tf_op jit(solution)/shard_map/ppermute | solution.py:30
  134.8 41.0 %collective-permute-start.9 = (bf16[512,256]{0,1:T(8,128)(2,1)}, bf16[512,256]{0,1:T(8,128)(2,1)S(1)}, u32[]{:S(2)}, u32[]{:S(2)}) collective-permute-start(bf16[512,256]{0,1:T(8,128)(2,1)} %get-tuple-element.43), channel_id=1, source_target_pairs={{12,0},{16,4},{20,8},{24,12},{28,16},{32,20},{36,24},{40,28},{44,3... | collective-permute-start | bytes 786440 | tf_op jit(solution)/shard_map/ppermute | solution.py:26
  139.8 35.9 %collective-permute-start.8 = (bf16[512,256]{0,1:T(8,128)(2,1)}, bf16[512,256]{0,1:T(8,128)(2,1)S(1)}, u32[]{:S(2)}, u32[]{:S(2)}) collective-permute-start(bf16[512,256]{0,1:T(8,128)(2,1)} %get-tuple-element.44), channel_id=1, source_target_pairs={{8,0},{12,4},{16,8},{20,12},{24,16},{28,20},{32,24},{36,28},{40,32... | collective-permute-start | bytes 786440 | tf_op jit(solution)/shard_map/ppermute | solution.py:26
  143.6 32.1 %collective-permute-start.7 = (bf16[512,256]{0,1:T(8,128)(2,1)}, bf16[512,256]{0,1:T(8,128)(2,1)S(1)}, u32[]{:S(2)}, u32[]{:S(2)}) collective-permute-start(bf16[512,256]{0,1:T(8,128)(2,1)} %get-tuple-element.45), channel_id=1, source_target_pairs={{4,0},{8,4},{12,8},{16,12},{20,16},{24,20},{28,24},{32,28},{36,32}... | collective-permute-start | bytes 786440 | tf_op jit(solution)/shard_map/ppermute | solution.py:26
  146.0 32.4 %copy-start.1 = (s32[256]{0:T(256)S(1)}, s32[256]{0:T(256)}, u32[]{:S(2)}) copy-start(s32[256]{0:T(256)} %param.13) | copy-start | bytes 3076
  152.5 22.4 %all-to-all-start = ((bf16[8,64,512]{2,1,0:T(8,128)(2,1)}), bf16[8,64,512]{2,1,0:T(8,128)(2,1)S(1)}, u32[]{:S(2)}, u32[]{:S(2)}) async-start(bf16[8,64,512]{2,1,0:T(8,128)(2,1)} %bitcast.209), calls=%async_computation.1 | async-start | bytes 1048576 | tf_op jit(solution)/shard_map/all_to_all | solution.py:128
  (12 other events, 54.0 us)
Sparse Core Ops, SparseCore 0:
  88.1 55.4 reduce-scatter.1

commit v12 on v10

--- a/solution.py
+++ b/solution.py
@@ -157,7 +157,6 @@
         )
 
     early_grad = key_side(d_scores[..., :span], probs_half[..., :span]).astype(jnp.bfloat16)
-    early_grad, d_scores, probs_half = lax.optimization_barrier((early_grad, d_scores, probs_half))
     returned = []
     for distance in range(1, REACH + 1):
         lo = span - distance * tokens_here

time: 168 us -> 174 us (1.036)
  matrix products: 43.7 us -> 49.6 us
  other arithmetic: 29.3 us -> 33 us
  waiting for transfers between devices: 27.8 us -> 25.8 us
    dot_general x1, matrix products: 1.29 us -> 5 us  [on_device(): jnp.einsum('cgqk,kcd->qcgd', d_scores, key_heads, preferred_element_type=...]
    convert_element_type x1, other arithmetic: 8.4 us -> 10.8 us  [on_device(): probs_half = probs.astype(jnp.bfloat16)]
    ppermute x4, waiting for transfers between devices: 23 us -> 21 us  [swapped(): return lax.ppermute(block, axis, [(0, 1), (1, 0)])]
    dot_general x2, matrix products: 6.15 us -> 8.05 us  [key_side(): jnp.einsum('cgqk,qcgd->kcd', prob_part, grad_four, preferred_element_type...]
    unnamed x54 -> x48, local copies, waits for them, and re-layouts: 12.4 us -> 11.9 us
  transfers between devices with their start and end apart: 12 -> 12, of which waited for: 4 -> 4; matrix products, arithmetic and copies ran while one was open for 41% -> 45% of each run, Pallas kernels for 0% -> 0%
where the time goes in v12:
time: 174 us; the launch traced here: 172 us
  matrix products  49.6 us (29%)
  other arithmetic  33 us (19%)
  starting transfers between devices  31.5 us (18%)
  waiting for transfers between devices  25.8 us (15%)
  local copies, waits for them, and re-layouts  17.6 us (10%)
  between operations  14.4 us (8%)
    ppermute x4, waiting for transfers between devices, swapped(): return lax.ppermute(block, axis, [(0, 1), (1, 0)])  21 us
    unnamed x48, local copies, waits for them, and re-layouts  11.9 us
    convert_element_type x1, other arithmetic, on_device(): probs_half = probs.astype(jnp.bfloat16)  10.8 us
    ppermute x3, starting transfers between devices, from_earlier(): return lax.ppermute(block, CTX, route)  10.8 us
    ppermute x3, starting transfers between devices, to_earlier(): return lax.ppermute(block, CTX, route)  10.7 us
    dot_general x1, matrix products, on_device(): jnp.einsum('qcgd,kcd->cgqk', grad_four, value_heads, preferred_element_ty...  9.48 us
    dot_general x2, matrix products, key_side(): jnp.einsum('cgqk,qcgd->kcd', score_part, query_four, preferred_element_ty...  8.11 us
    dot_general x2, matrix products, key_side(): jnp.einsum('cgqk,qcgd->kcd', prob_part, grad_four, preferred_element_type...  8.05 us
  transfers between devices with their start and end apart: 12, of which 4 were waited for; matrix products, arithmetic and copies ran while one was open for 45% of the time, Pallas kernels for 0%

profile of v12, /device:TPU:96, one launch (start us, length us, event | category | flops | bytes accessed | tf_op | source)
XLA Modules:
  0.0 171.9 jit_solution(8550431574268586687)
XLA Ops:
  9.1 3.5 %collective-permute-start.3 = (bf16[512,256]{1,0:T(8,128)(2,1)S(1)}, bf16[512,256]{1,0:T(8,128)(2,1)S(1)}, u32[]{:S(2)}, u32[]{:S(2)}) collective-permute-start(bf16[512,256]{1,0:T(8,128)(2,1)S(1)} %constant_dynamic-update-slice_fusion), channel_id=1, source_target_pairs={{0,4},{4,8},{8,12},{12,16},{16,20},{20,24},{24,28},{28,32},{32,36}... | collective-permute-start | bytes 786440 | tf_op jit(solution)/shard_map/ppermute | solution.py:21
  12.6 3.4 %collective-permute-start.2 = (bf16[512,256]{1,0:T(8,128)(2,1)S(1)}, bf16[512,256]{1,0:T(8,128)(2,1)S(1)}, u32[]{:S(2)}, u32[]{:S(2)}) collective-permute-start(bf16[512,256]{1,0:T(8,128)(2,1)S(1)} %constant_dynamic-update-slice_fusion), channel_id=1, source_target_pairs={{0,8},{4,12},{8,16},{12,20},{16,24},{20,28},{24,32},{28,36},{32,40... | collective-permute-start | bytes 786440 | tf_op jit(solution)/shard_map/ppermute | solution.py:21
  16.0 3.9 %collective-permute-start.1 = (bf16[512,256]{1,0:T(8,128)(2,1)S(1)}, bf16[512,256]{1,0:T(8,128)(2,1)}, u32[]{:S(2)}, u32[]{:S(2)}) collective-permute-start(bf16[512,256]{1,0:T(8,128)(2,1)S(1)} %constant_dynamic-update-slice_fusion), channel_id=1, source_target_pairs={{0,12},{4,16},{8,20},{12,24},{16,28},{20,32},{24,36},{28,40},{32,4... | collective-permute-start | bytes 786440 | tf_op jit(solution)/shard_map/ppermute | solution.py:21
  19.9 3.3 %collective-permute-start = (bf16[128,4096]{1,0:T(8,128)(2,1)}, bf16[128,4096]{1,0:T(8,128)(2,1)S(1)}, u32[]{:S(2)}, u32[]{:S(2)}) collective-permute-start(bf16[128,4096]{1,0:T(8,128)(2,1)} %param.11), channel_id=1, source_target_pairs={{0,2},{2,0},{1,3},{3,1},{4,6},{6,4},{5,7},{7,5},{8,10},{10,8},{9,1... | collective-permute-start | bytes 3145736 | tf_op jit(solution)/shard_map/ppermute | solution.py:30
  28.6 4.8 %collective-permute-done.1 = bf16[512,256]{1,0:T(8,128)(2,1)} collective-permute-done((bf16[512,256]{1,0:T(8,128)(2,1)S(1)}, bf16[512,256]{1,0:T(8,128)(2,1)}, u32[]{:S(2)}, u32[]{:S(2)}) %collective-permute-start.1) | collective-permute-done | bytes 262176 | tf_op jit(solution)/shard_map/ppermute | solution.py:21
  34.4 3.1 %fusion.5 = (f32[4,512]{1,0:T(4,128)S(1)}, f32[2048,512,4]{1,0,2:T(8,128)S(1)}) fusion(pred[512,2048]{0,1:T(8,128)(4,1)S(1)} %fusion.17, bf16[512,4,128]{0,2,1:T(8,128)(2,1)S(1)} %bitcast.194, bf16[2048,256]{1,0:T(8,128)(2,1)S(1)} %pad_maximum_fusion.2), kind=kOutput, calls=%fused_computation.9 | convolution fusion | flops 1086322688 | bytes 18882560 | tf_op jit(solution)/shard_map/qcgd,kcd->cgqk/dot_general | solution.py:97
  37.6 4.2 %fusion.7 = f32[4,512]{1,0:T(4,128)S(1)} fusion(f32[2048,512,4]{1,0,2:T(8,128)S(1)} %get-tuple-element.43, f32[4,512]{1,0:T(4,128)S(1)} %get-tuple-element.42, pred[512,2048]{0,1:T(8,128)(4,1)S(1)} %fusion.17), kind=kLoop, calls=%fused_computation.11 | loop fusion | flops 20969472 | bytes 17842176 | tf_op jit(solution)/shard_map/reduce_sum | solution.py:103
  43.3 5.2 %divide_convert_fusion = bf16[512,1,4,128]{0,3,2,1:T(8,128)(2,1)} fusion(f32[2048,512,4]{1,0,2:T(8,128)S(1)} %get-tuple-element.43, f32[4,512]{1,0:T(4,128)S(1)} %get-tuple-element.42, pred[512,2048]{0,1:T(8,128)(4,1)S(1)} %fusion.17, f32[512,4]{0,1:T(4,128)S(1)} %bitcast.198, bf16[2048,256]{1,0:T(8,128)(2,1)S(1)} %pad_maximum_fusion.2), kind=kOutput, calls=%fused_computation.56 | convolution fusion | flops 1095237632 | bytes 18890752 | tf_op jit(solution)/shard_map/cgqk,kcd->qcgd/dot_general | solution.py:104
  55.3 4.5 %collective-permute-done.4 = bf16[2,128,4096]{2,1,0:T(8,128)(2,1)} collective-permute-done((bf16[2,128,4096]{2,1,0:T(8,128)(2,1)}, bf16[2,128,4096]{2,1,0:T(8,128)(2,1)}, u32[]{:S(2)}, u32[]{:S(2)}) %collective-permute-start.4) | collective-permute-done | bytes 2097184 | tf_op jit(solution)/shard_map/ppermute | solution.py:30
  64.3 4.5 %convolution_convert_fusion = bf16[4096,512]{1,0:T(8,128)(2,1)} fusion(bf16[512,4096]{1,0:T(8,128)(2,1)S(1)} %bitcast.188, bf16[512,512]{0,1:T(8,128)(2,1)S(1)} %bitcast.191), kind=kOutput, calls=%fused_computation.22 | convolution fusion | flops 2149580800 | bytes 8912896 | tf_op jit(solution)/shard_map/dot_general | solution.py:112
  68.9 10.8 %fusion.6 = bf16[1,4,512,2048]{2,3,1,0:T(8,128)(2,1)} fusion(f32[2048,512,4]{1,0,2:T(8,128)} %copy-done.2, f32[4,512]{1,0:T(4,128)S(1)} %log_add_fusion, pred[512,2048]{0,1:T(8,128)(4,1)S(1)} %fusion.17), kind=kLoop, calls=%fused_computation.10 | loop fusion | flops 16777216 | bytes 26222592 | tf_op jit(solution)/shard_map/convert_element_type | solution.py:145
  84.0 3.8 %bitcast_reduce_fusion = (f32[512,4]{0,1:T(4,128)}, bf16[512,512]{0,1:T(8,128)(2,1)}) fusion(bf16[512,512]{0,1:T(8,128)(2,1)S(1)} %bitcast.193, bf16[512,4096]{1,0:T(8,128)(2,1)S(1)} %bitcast.189, bf16[512,4096]{1,0:T(8,128)(2,1)S(1)} %copy-done.5), kind=kOutput, calls=%fused_computation.51 | convolution fusion | flops 2148792320 | bytes 9445376 | tf_op jit(solution)/shard_map/dot_general | solution.py:127
  91.6 9.5 %fusion.2 = bf16[1,4,512,2048]{2,3,1,0:T(8,128)(2,1)} fusion(f32[2048,512,4]{1,0,2:T(8,128)S(1)} %bitcast.185, f32[4,512]{1,0:T(4,128)} %bitcast.202, f32[4,512]{1,0:T(4,128)S(1)} %log_add_fusion, pred[512,2048]{0,1:T(8,128)(4,1)S(1)} %fusion.17, bf16[512,4,128]{0,2,1:T(8,128)(2,1)} %bitcast.199, bf16[2048,256]{1,0:T(8,128)(2,1)} %copy-done.8), kind=kOutput, calls=%fused_computation.3 | convolution fusion | flops 1103101952 | bytes 27279360 | tf_op jit(solution)/shard_map/qcgd,kcd->cgqk/dot_general | solution.py:141
  101.1 5.0 %fusion.30 = bf16[128,4,512]{2,0,1:T(8,128)(2,1)S(1)} fusion(bf16[1,4,512,2048]{2,3,1,0:T(8,128)(2,1)} %fusion.2, bf16[2048,256]{1,0:T(8,128)(2,1)} %copy-done.8), kind=kOutput, calls=%fused_computation.46 | convolution fusion | flops 1074003968 | bytes 9437184 | tf_op jit(solution)/shard_map/cgqk,kcd->qcgd/dot_general | solution.py:164
  107.1 5.0 %fusion.21 = bf16[1536,128]{0,1:T(8,128)(2,1)S(1)} fusion(bf16[512,4,128]{0,2,1:T(8,128)(2,1)S(1)} %bitcast.195, bf16[1,4,512,2048]{2,3,1,0:T(8,128)(2,1)} %fusion.2), kind=kOutput, calls=%fused_computation.31 | convolution fusion | flops 805502976 | bytes 7208960 | tf_op jit(solution)/shard_map/cgqk,qcgd->kcd/dot_general | solution.py:148
  112.1 3.4 %bitcast_add_fusion = f32[2,128,4096]{2,1,0:T(8,128)S(1)} fusion(bf16[2,128,4096]{2,1,0:T(8,128)(2,1)} %collective-permute-done.5, f32[2,2,128,4096]{3,2,1,0:T(8,128)} %bitcast.187, s32[]{:T(128)S(6)} %select_n.96), kind=kLoop, calls=%fused_computation.25 | loop fusion | flops 2097152 | bytes 10485764 | tf_op jit(solution)/shard_map/add | solution.py:54
  115.7 3.0 %collective-permute-start.6 = (bf16[128,4096]{1,0:T(8,128)(2,1)S(1)}, bf16[128,4096]{1,0:T(8,128)(2,1)S(1)}, u32[]{:S(2)}, u32[]{:S(2)}) collective-permute-start(bf16[128,4096]{1,0:T(8,128)(2,1)S(1)} %fusion.35), channel_id=1, source_target_pairs={{0,2},{2,0},{1,3},{3,1},{4,6},{6,4},{5,7},{7,5},{8,10},{10,8},{9,1... | collective-permute-start | bytes 3145736 | tf_op jit(solution)/shard_map/ppermute | solution.py:30
  118.7 4.9 %fusion.22 = bf16[1536,128]{0,1:T(8,128)(2,1)S(1)} fusion(bf16[512,4,128]{0,2,1:T(8,128)(2,1)S(1)} %bitcast.200, bf16[1,4,512,2048]{2,3,1,0:T(8,128)(2,1)} %fusion.6), kind=kOutput, calls=%fused_computation.32 | convolution fusion | flops 805502976 | bytes 7208960 | tf_op jit(solution)/shard_map/cgqk,qcgd->kcd/dot_general | solution.py:151
  124.5 4.7 %collective-permute-start.9 = (bf16[512,256]{0,1:T(8,128)(2,1)}, bf16[512,256]{0,1:T(8,128)(2,1)}, u32[]{:S(2)}, u32[]{:S(2)}) collective-permute-start(bf16[512,256]{0,1:T(8,128)(2,1)} %get-tuple-element.37), channel_id=1, source_target_pairs={{12,0},{16,4},{20,8},{24,12},{28,16},{32,20},{36,24},{40,28},{44,3... | collective-permute-start | bytes 786440 | tf_op jit(solution)/shard_map/ppermute | solution.py:26
  131.4 3.8 %collective-permute-start.8 = (bf16[512,256]{0,1:T(8,128)(2,1)S(1)}, bf16[512,256]{0,1:T(8,128)(2,1)}, u32[]{:S(2)}, u32[]{:S(2)}) collective-permute-start(bf16[512,256]{0,1:T(8,128)(2,1)S(1)} %get-tuple-element.39), channel_id=1, source_target_pairs={{8,0},{12,4},{16,8},{20,12},{24,16},{28,20},{32,24},{36,28},{40,32... | collective-permute-start | bytes 786440 | tf_op jit(solution)/shard_map/ppermute | solution.py:26
  135.2 3.1 %fusion.34 = f32[512,128]{0,1:T(8,128)} fusion(bf16[512,4,128]{0,2,1:T(8,128)(2,1)S(1)} %bitcast.201, bf16[1,4,512,2048]{2,3,1,0:T(8,128)(2,1)} %fusion.6), kind=kOutput, calls=%fused_computation.48 | convolution fusion | flops 268435456 | bytes 2883584 | tf_op jit(solution)/shard_map/cgqk,qcgd->kcd/dot_general | solution.py:151
  138.3 3.1 %fusion.33 = f32[512,128]{0,1:T(8,128)} fusion(bf16[512,4,128]{0,2,1:T(8,128)(2,1)S(1)} %bitcast.196, bf16[1,4,512,2048]{2,3,1,0:T(8,128)(2,1)} %fusion.2), kind=kOutput, calls=%fused_computation.47 | convolution fusion | flops 268435456 | bytes 2883584 | tf_op jit(solution)/shard_map/cgqk,qcgd->kcd/dot_general | solution.py:148
  141.4 3.6 %all-to-all-start = ((bf16[8,64,512]{2,1,0:T(8,128)(2,1)}), bf16[8,64,512]{2,1,0:T(8,128)(2,1)S(1)}, u32[]{:S(2)}, u32[]{:S(2)}) async-start(bf16[8,64,512]{2,1,0:T(8,128)(2,1)} %bitcast.197), calls=%async_computation.1 | async-start | bytes 1048576 | tf_op jit(solution)/shard_map/all_to_all | solution.py:122
  145.1 13.6 %collective-permute-done.6 = bf16[128,4096]{1,0:T(8,128)(2,1)S(1)} collective-permute-done((bf16[128,4096]{1,0:T(8,128)(2,1)S(1)}, bf16[128,4096]{1,0:T(8,128)(2,1)S(1)}, u32[]{:S(2)}, u32[]{:S(2)}) %collective-permute-start.6) | collective-permute-done | bytes 1048608 | tf_op jit(solution)/shard_map/ppermute | solution.py:30
  (88 shorter events, 39.7 us)
Async XLA Ops:
  7.2 16.1 %copy-start = (s32[256]{0:T(256)S(1)}, s32[256]{0:T(256)}, u32[]{:S(2)}) copy-start(s32[256]{0:T(256)} %param.13) | copy-start | bytes 3076
  7.2 134.2 %reduce-scatter.2.cloned.1.call-start = ((), (), s32[]{:S(2)}) async-start(), calls=%async_computation.2 | async-start | bytes 4718592 | tf_op jit(solution)/shard_map/reduce_scatter | solution.py:116
  9.1 19.5 %collective-permute-start.3 = (bf16[512,256]{1,0:T(8,128)(2,1)S(1)}, bf16[512,256]{1,0:T(8,128)(2,1)S(1)}, u32[]{:S(2)}, u32[]{:S(2)}) collective-permute-start(bf16[512,256]{1,0:T(8,128)(2,1)S(1)} %constant_dynamic-update-slice_fusion), channel_id=1, source_target_pairs={{0,4},{4,8},{8,12},{12,16},{16,20},{20,24},{24,28},{28,32},{32,36}... | collective-permute-start | bytes 786440 | tf_op jit(solution)/shard_map/ppermute | solution.py:21
  12.6 16.0 %collective-permute-start.2 = (bf16[512,256]{1,0:T(8,128)(2,1)S(1)}, bf16[512,256]{1,0:T(8,128)(2,1)S(1)}, u32[]{:S(2)}, u32[]{:S(2)}) collective-permute-start(bf16[512,256]{1,0:T(8,128)(2,1)S(1)} %constant_dynamic-update-slice_fusion), channel_id=1, source_target_pairs={{0,8},{4,12},{8,16},{12,20},{16,24},{20,28},{24,32},{28,36},{32,40... | collective-permute-start | bytes 786440 | tf_op jit(solution)/shard_map/ppermute | solution.py:21
  16.0 17.4 %collective-permute-start.1 = (bf16[512,256]{1,0:T(8,128)(2,1)S(1)}, bf16[512,256]{1,0:T(8,128)(2,1)}, u32[]{:S(2)}, u32[]{:S(2)}) collective-permute-start(bf16[512,256]{1,0:T(8,128)(2,1)S(1)} %constant_dynamic-update-slice_fusion), channel_id=1, source_target_pairs={{0,12},{4,16},{8,20},{12,24},{16,28},{20,32},{24,36},{28,40},{32,4... | collective-permute-start | bytes 786440 | tf_op jit(solution)/shard_map/ppermute | solution.py:21
  19.9 31.5 %collective-permute-start = (bf16[128,4096]{1,0:T(8,128)(2,1)}, bf16[128,4096]{1,0:T(8,128)(2,1)S(1)}, u32[]{:S(2)}, u32[]{:S(2)}) collective-permute-start(bf16[128,4096]{1,0:T(8,128)(2,1)} %param.11), channel_id=1, source_target_pairs={{0,2},{2,0},{1,3},{3,1},{4,6},{6,4},{5,7},{7,5},{8,10},{10,8},{9,1... | collective-permute-start | bytes 3145736 | tf_op jit(solution)/shard_map/ppermute | solution.py:30
  26.3 11.3 %copy-start.13 = (bf16[512,512]{0,1:T(8,128)(2,1)}, bf16[512,512]{0,1:T(8,128)(2,1)S(1)}, u32[]{:S(2)}) copy-start(bf16[512,512]{0,1:T(8,128)(2,1)S(1)} %copy.57) | copy-start | bytes 1572868
  34.4 7.3 %copy-start.8 = (bf16[2048,256]{1,0:T(8,128)(2,1)}, bf16[2048,256]{1,0:T(8,128)(2,1)S(1)}, u32[]{:S(2)}) copy-start(bf16[2048,256]{1,0:T(8,128)(2,1)S(1)} %pad_maximum_fusion.2) | copy-start | bytes 3145732
  43.3 9.1 %copy-start.9 = (bf16[128,4096]{1,0:T(8,128)(2,1)S(1)}, bf16[128,4096]{1,0:T(8,128)(2,1)}, u32[]{:S(2)}) copy-start(bf16[128,4096]{1,0:T(8,128)(2,1)} %param.11) | copy-start | bytes 3145732
  55.3 4.5 %collective-permute-start.4 = (bf16[2,128,4096]{2,1,0:T(8,128)(2,1)}, bf16[2,128,4096]{2,1,0:T(8,128)(2,1)}, u32[]{:S(2)}, u32[]{:S(2)}) collective-permute-start(bf16[2,128,4096]{2,1,0:T(8,128)(2,1)} %pad_maximum_fusion.1), channel_id=1, source_target_pairs={{0,1},{1,0},{2,3},{3,2},{4,5},{5,4},{6,7},{7,6},{8,9},{9,8},{10,11... | collective-permute-start | bytes 6291464 | tf_op jit(solution)/shard_map/ppermute | solution.py:30
  68.9 10.9 %copy-start.5 = (bf16[512,4096]{1,0:T(8,128)(2,1)S(1)}, bf16[512,4096]{1,0:T(8,128)(2,1)}, u32[]{:S(2)}) copy-start(bf16[512,4096]{1,0:T(8,128)(2,1)} %param.10) | copy-start | bytes 12582916
  79.8 8.0 %slice-start = ((s8[16777216]{0:T(1024)(128)(4,1)}), s8[4194304]{0:T(1024)(128)(4,1)S(1)}, s32[]{:S(2)}) async-start(s8[16777216]{0:T(1024)(128)(4,1)} %bitcast.184), calls=%async_computation.3 | async-start | bytes 8388608
  79.8 9.2 %slice-start.1 = ((s8[16777216]{0:T(1024)(128)(4,1)}), s8[4194304]{0:T(1024)(128)(4,1)S(1)}, s32[]{:S(2)}) async-start(s8[16777216]{0:T(1024)(128)(4,1)} %bitcast.184), calls=%async_computation.4 | async-start | bytes 8388608
  83.8 7.8 %slice-start.3 = ((s8[16777216]{0:T(1024)(128)(4,1)}), s8[4194304]{0:T(1024)(128)(4,1)S(1)}, s32[]{:S(2)}) async-start(s8[16777216]{0:T(1024)(128)(4,1)} %bitcast.184), calls=%async_computation.6 | async-start | bytes 8388608
  83.8 28.3 %collective-permute-start.5 = (bf16[2,128,4096]{2,1,0:T(8,128)(2,1)}, bf16[2,128,4096]{2,1,0:T(8,128)(2,1)}, u32[]{:S(2)}, u32[]{:S(2)}) collective-permute-start(bf16[2,128,4096]{2,1,0:T(8,128)(2,1)} %fusion.23), channel_id=1, source_target_pairs={{0,1},{1,0},{2,3},{3,2},{4,5},{5,4},{6,7},{7,6},{8,9},{9,8},{10,11... | collective-permute-start | bytes 6291464 | tf_op jit(solution)/shard_map/ppermute | solution.py:30
  115.6 8.9 %copy-start.4 = (f32[2,128,4096]{2,1,0:T(8,128)}, f32[2,128,4096]{2,1,0:T(8,128)S(1)}, u32[]{:S(2)}) copy-start(f32[2,128,4096]{2,1,0:T(8,128)S(1)} %bitcast_add_fusion) | copy-start | bytes 12582916
  115.7 42.9 %collective-permute-start.6 = (bf16[128,4096]{1,0:T(8,128)(2,1)S(1)}, bf16[128,4096]{1,0:T(8,128)(2,1)S(1)}, u32[]{:S(2)}, u32[]{:S(2)}) collective-permute-start(bf16[128,4096]{1,0:T(8,128)(2,1)S(1)} %fusion.35), channel_id=1, source_target_pairs={{0,2},{2,0},{1,3},{3,1},{4,6},{6,4},{5,7},{7,5},{8,10},{10,8},{9,1... | collective-permute-start | bytes 3145736 | tf_op jit(solution)/shard_map/ppermute | solution.py:30
  124.5 37.7 %collective-permute-start.9 = (bf16[512,256]{0,1:T(8,128)(2,1)}, bf16[512,256]{0,1:T(8,128)(2,1)}, u32[]{:S(2)}, u32[]{:S(2)}) collective-permute-start(bf16[512,256]{0,1:T(8,128)(2,1)} %get-tuple-element.37), channel_id=1, source_target_pairs={{12,0},{16,4},{20,8},{24,12},{28,16},{32,20},{36,24},{40,28},{44,3... | collective-permute-start | bytes 786440 | tf_op jit(solution)/shard_map/ppermute | solution.py:26
  129.2 33.0 %collective-permute-start.7 = (bf16[512,256]{0,1:T(8,128)(2,1)}, bf16[512,256]{0,1:T(8,128)(2,1)}, u32[]{:S(2)}, u32[]{:S(2)}) collective-permute-start(bf16[512,256]{0,1:T(8,128)(2,1)} %get-tuple-element.38), channel_id=1, source_target_pairs={{4,0},{8,4},{12,8},{16,12},{20,16},{24,20},{28,24},{32,28},{36,32}... | collective-permute-start | bytes 786440 | tf_op jit(solution)/shard_map/ppermute | solution.py:26
  131.4 30.9 %collective-permute-start.8 = (bf16[512,256]{0,1:T(8,128)(2,1)S(1)}, bf16[512,256]{0,1:T(8,128)(2,1)}, u32[]{:S(2)}, u32[]{:S(2)}) collective-permute-start(bf16[512,256]{0,1:T(8,128)(2,1)S(1)} %get-tuple-element.39), channel_id=1, source_target_pairs={{8,0},{12,4},{16,8},{20,12},{24,16},{28,20},{32,24},{36,28},{40,32... | collective-permute-start | bytes 786440 | tf_op jit(solution)/shard_map/ppermute | solution.py:26
  135.2 29.9 %copy-start.1 = (s32[256]{0:T(256)S(1)}, s32[256]{0:T(256)}, u32[]{:S(2)}) copy-start(s32[256]{0:T(256)} %param.13) | copy-start | bytes 3076
  141.4 20.8 %copy-start.15 = (f32[512,128]{0,1:T(8,128)S(1)}, f32[512,128]{0,1:T(8,128)}, u32[]{:S(2)}) copy-start(f32[512,128]{0,1:T(8,128)} %fusion.34) | copy-start | bytes 786436
  141.4 20.8 %copy-start.16 = (f32[512,128]{0,1:T(8,128)S(1)}, f32[512,128]{0,1:T(8,128)}, u32[]{:S(2)}) copy-start(f32[512,128]{0,1:T(8,128)} %fusion.33) | copy-start | bytes 786436
  141.4 20.0 %all-to-all-start = ((bf16[8,64,512]{2,1,0:T(8,128)(2,1)}), bf16[8,64,512]{2,1,0:T(8,128)(2,1)S(1)}, u32[]{:S(2)}, u32[]{:S(2)}) async-start(bf16[8,64,512]{2,1,0:T(8,128)(2,1)} %bitcast.197), calls=%async_computation.1 | async-start | bytes 1048576 | tf_op jit(solution)/shard_map/all_to_all | solution.py:122
  (10 other events, 44.2 us)
Sparse Core Ops, SparseCore 0:
  69.0 55.2 reduce-scatter.1

commit v13 on v10

--- a/solution.py
+++ b/solution.py
@@ -49,12 +49,12 @@
     high = lax.axis_index(TP[0])
     low = lax.axis_index(TP[1])
     quarters = part.reshape(2, 2, part.shape[0] // 4, part.shape[1])
-    kept = lax.dynamic_index_in_dim(quarters, low, 1, keepdims=False)
-    given = lax.dynamic_index_in_dim(quarters, 1 - low, 1, keepdims=False)
-    halves = kept + swapped(given.astype(jnp.bfloat16), TP[1]).astype(jnp.float32)
-    kept = lax.dynamic_index_in_dim(halves, high, 0, keepdims=False)
-    given = lax.dynamic_index_in_dim(halves, 1 - high, 0, keepdims=False)
-    return kept + swapped(given.astype(jnp.bfloat16), TP[0]).astype(jnp.float32)
+    kept = lax.dynamic_index_in_dim(quarters, high, 0, keepdims=False)
+    given = lax.dynamic_index_in_dim(quarters, 1 - high, 0, keepdims=False)
+    halves = kept + swapped(given.astype(jnp.bfloat16), TP[0]).astype(jnp.float32)
+    kept = lax.dynamic_index_in_dim(halves, low, 0, keepdims=False)
+    given = lax.dynamic_index_in_dim(halves, 1 - low, 0, keepdims=False)
+    return kept + swapped(given.astype(jnp.bfloat16), TP[1]).astype(jnp.float32)
 
 
 def on_device(query_rows, key_rows, value_rows, out_weight, out_grad, doc_ids, window_blocks):

time: 168 us -> 183 us (1.089)
  waiting for transfers between devices: 27.8 us -> 46.1 us
  local copies, waits for them, and re-layouts: 19 us -> 16.1 us
    ppermute x4, waiting for transfers between devices: 23 us -> 32.2 us  [swapped(): return lax.ppermute(block, axis, [(0, 1), (1, 0)])]
    all_to_all x1, waiting for transfers between devices: 0.01 us -> 9.15 us  [on_device(): weight_cols = lax.all_to_all(weight_cols, CTX[1:], 0, 0, tiled=True)]
    unnamed x54, local copies, waits for them, and re-layouts: 12.4 us -> 9.48 us
  transfers between devices with their start and end apart: 12 -> 12, of which waited for: 4 -> 5; matrix products, arithmetic and copies ran while one was open for 41% -> 37% of each run, Pallas kernels for 0% -> 0%
where the time goes in v13:
time: 183 us; the launch traced here: 181 us
  waiting for transfers between devices  46.1 us (25%)
  matrix products  43.7 us (24%)
  starting transfers between devices  32.3 us (18%)
  other arithmetic  28.5 us (16%)
  local copies, waits for them, and re-layouts  16.1 us (9%)
  between operations  14.5 us (8%)
    ppermute x4, waiting for transfers between devices, swapped(): return lax.ppermute(block, axis, [(0, 1), (1, 0)])  32.2 us
    ppermute x3, starting transfers between devices, from_earlier(): return lax.ppermute(block, CTX, route)  10.8 us
    ppermute x3, starting transfers between devices, to_earlier(): return lax.ppermute(block, CTX, route)  10.8 us
    unnamed x54, local copies, waits for them, and re-layouts  9.48 us
    dot_general x1, matrix products, on_device(): jnp.einsum('qcgd,kcd->cgqk', grad_four, value_heads, preferred_element_ty...  9.43 us
    all_to_all x1, waiting for transfers between devices, on_device(): weight_cols = lax.all_to_all(weight_cols, CTX[1:], 0, 0, tiled=True)  9.15 us
    convert_element_type x1, other arithmetic, on_device(): probs_half = probs.astype(jnp.bfloat16)  8.4 us
    dot_general x2, matrix products, key_side(): jnp.einsum('cgqk,qcgd->kcd', score_part, query_four, preferred_element_ty...  8.38 us
  transfers between devices with their start and end apart: 12, of which 5 were waited for; matrix products, arithmetic and copies ran while one was open for 37% of the time, Pallas kernels for 0%

profile of v13, /device:TPU:96, one launch (start us, length us, event | category | flops | bytes accessed | tf_op | source)
XLA Modules:
  0.0 181.2 jit_solution(4755340507139637482)
XLA Ops:
  9.1 3.5 %collective-permute-start.3 = (bf16[512,256]{1,0:T(8,128)(2,1)S(1)}, bf16[512,256]{1,0:T(8,128)(2,1)S(1)}, u32[]{:S(2)}, u32[]{:S(2)}) collective-permute-start(bf16[512,256]{1,0:T(8,128)(2,1)S(1)} %constant_dynamic-update-slice_fusion), channel_id=1, source_target_pairs={{0,4},{4,8},{8,12},{12,16},{16,20},{20,24},{24,28},{28,32},{32,36}... | collective-permute-start | bytes 786440 | tf_op jit(solution)/shard_map/ppermute | solution.py:21
  12.6 3.4 %collective-permute-start.2 = (bf16[512,256]{1,0:T(8,128)(2,1)S(1)}, bf16[512,256]{1,0:T(8,128)(2,1)S(1)}, u32[]{:S(2)}, u32[]{:S(2)}) collective-permute-start(bf16[512,256]{1,0:T(8,128)(2,1)S(1)} %constant_dynamic-update-slice_fusion), channel_id=1, source_target_pairs={{0,8},{4,12},{8,16},{12,20},{16,24},{20,28},{24,32},{28,36},{32,40... | collective-permute-start | bytes 786440 | tf_op jit(solution)/shard_map/ppermute | solution.py:21
  16.0 3.9 %collective-permute-start.1 = (bf16[512,256]{1,0:T(8,128)(2,1)S(1)}, bf16[512,256]{1,0:T(8,128)(2,1)}, u32[]{:S(2)}, u32[]{:S(2)}) collective-permute-start(bf16[512,256]{1,0:T(8,128)(2,1)S(1)} %constant_dynamic-update-slice_fusion), channel_id=1, source_target_pairs={{0,12},{4,16},{8,20},{12,24},{16,28},{20,32},{24,36},{28,40},{32,4... | collective-permute-start | bytes 786440 | tf_op jit(solution)/shard_map/ppermute | solution.py:21
  19.9 3.3 %collective-permute-start = (bf16[128,4096]{1,0:T(8,128)(2,1)}, bf16[128,4096]{1,0:T(8,128)(2,1)S(1)}, u32[]{:S(2)}, u32[]{:S(2)}) collective-permute-start(bf16[128,4096]{1,0:T(8,128)(2,1)} %param.11), channel_id=1, source_target_pairs={{0,2},{2,0},{1,3},{3,1},{4,6},{6,4},{5,7},{7,5},{8,10},{10,8},{9,1... | collective-permute-start | bytes 3145736 | tf_op jit(solution)/shard_map/ppermute | solution.py:30
  28.6 4.8 %collective-permute-done.1 = bf16[512,256]{1,0:T(8,128)(2,1)} collective-permute-done((bf16[512,256]{1,0:T(8,128)(2,1)S(1)}, bf16[512,256]{1,0:T(8,128)(2,1)}, u32[]{:S(2)}, u32[]{:S(2)}) %collective-permute-start.1) | collective-permute-done | bytes 262176 | tf_op jit(solution)/shard_map/ppermute | solution.py:21
  34.4 3.1 %fusion.5 = (f32[4,512]{1,0:T(4,128)S(1)}, f32[2048,512,4]{1,0,2:T(8,128)S(1)}) fusion(pred[512,2048]{0,1:T(8,128)(4,1)S(1)} %fusion.17, bf16[512,4,128]{0,2,1:T(8,128)(2,1)S(1)} %bitcast.192, bf16[2048,256]{1,0:T(8,128)(2,1)S(1)} %pad_maximum_fusion.2), kind=kOutput, calls=%fused_computation.9 | convolution fusion | flops 1086322688 | bytes 18882560 | tf_op jit(solution)/shard_map/qcgd,kcd->cgqk/dot_general | solution.py:97
  37.6 4.2 %fusion.7 = f32[4,512]{1,0:T(4,128)S(1)} fusion(f32[2048,512,4]{1,0,2:T(8,128)S(1)} %get-tuple-element.49, f32[4,512]{1,0:T(4,128)S(1)} %get-tuple-element.48, pred[512,2048]{0,1:T(8,128)(4,1)S(1)} %fusion.17), kind=kLoop, calls=%fused_computation.11 | loop fusion | flops 20969472 | bytes 17842176 | tf_op jit(solution)/shard_map/reduce_sum | solution.py:103
  43.3 5.2 %divide_convert_fusion = bf16[512,1,4,128]{0,3,2,1:T(8,128)(2,1)} fusion(f32[2048,512,4]{1,0,2:T(8,128)S(1)} %get-tuple-element.49, f32[4,512]{1,0:T(4,128)S(1)} %get-tuple-element.48, pred[512,2048]{0,1:T(8,128)(4,1)S(1)} %fusion.17, f32[512,4]{0,1:T(4,128)S(1)} %bitcast.196, bf16[2048,256]{1,0:T(8,128)(2,1)S(1)} %pad_maximum_fusion.2), kind=kOutput, calls=%fused_computation.58 | convolution fusion | flops 1095237632 | bytes 18890752 | tf_op jit(solution)/shard_map/cgqk,kcd->qcgd/dot_general | solution.py:104
  48.5 2.9 %collective-permute-done = bf16[128,4096]{1,0:T(8,128)(2,1)S(1)} collective-permute-done((bf16[128,4096]{1,0:T(8,128)(2,1)}, bf16[128,4096]{1,0:T(8,128)(2,1)S(1)}, u32[]{:S(2)}, u32[]{:S(2)}) %collective-permute-start) | collective-permute-done | bytes 1048608 | tf_op jit(solution)/shard_map/ppermute | solution.py:30
  55.3 4.5 %collective-permute-done.4 = bf16[2,128,4096]{2,1,0:T(8,128)(2,1)} collective-permute-done((bf16[2,128,4096]{2,1,0:T(8,128)(2,1)}, bf16[2,128,4096]{2,1,0:T(8,128)(2,1)}, u32[]{:S(2)}, u32[]{:S(2)}) %collective-permute-start.4) | collective-permute-done | bytes 2097184 | tf_op jit(solution)/shard_map/ppermute | solution.py:30
  64.3 4.5 %convolution_convert_fusion = bf16[4096,512]{1,0:T(8,128)(2,1)} fusion(bf16[512,4096]{1,0:T(8,128)(2,1)S(1)} %bitcast.186, bf16[512,512]{0,1:T(8,128)(2,1)S(1)} %bitcast.189), kind=kOutput, calls=%fused_computation.22 | convolution fusion | flops 2149580800 | bytes 8912896 | tf_op jit(solution)/shard_map/dot_general | solution.py:112
  68.9 8.4 %fusion.6 = bf16[1,4,512,2048]{2,3,1,0:T(8,128)(2,1)S(1)} fusion(f32[2048,512,4]{1,0,2:T(8,128)} %copy-done.2, f32[4,512]{1,0:T(4,128)S(1)} %log_add_fusion, pred[512,2048]{0,1:T(8,128)(4,1)S(1)} %fusion.17), kind=kLoop, calls=%fused_computation.10 | loop fusion | flops 16777216 | bytes 26222592 | tf_op jit(solution)/shard_map/convert_element_type | solution.py:145
  81.5 2.9 %collective-permute-start.5 = (bf16[2,128,4096]{2,1,0:T(8,128)(2,1)}, bf16[2,128,4096]{2,1,0:T(8,128)(2,1)}, u32[]{:S(2)}, u32[]{:S(2)}) collective-permute-start(bf16[2,128,4096]{2,1,0:T(8,128)(2,1)} %fusion.23), channel_id=1, source_target_pairs={{0,2},{2,0},{1,3},{3,1},{4,6},{6,4},{5,7},{7,5},{8,10},{10,8},{9,1... | collective-permute-start | bytes 6291464 | tf_op jit(solution)/shard_map/ppermute | solution.py:30
  84.4 3.2 %bitcast_reduce_fusion = (f32[512,4]{0,1:T(4,128)}, bf16[512,512]{0,1:T(8,128)(2,1)S(1)}) fusion(bf16[512,512]{0,1:T(8,128)(2,1)S(1)} %bitcast.191, bf16[512,4096]{1,0:T(8,128)(2,1)S(1)} %bitcast.187, bf16[512,4096]{1,0:T(8,128)(2,1)S(1)} %copy-done.7), kind=kOutput, calls=%fused_computation.53 | convolution fusion | flops 2148792320 | bytes 9445376 | tf_op jit(solution)/shard_map/dot_general | solution.py:127
  87.6 2.9 %fusion.22 = bf16[1536,128]{0,1:T(8,128)(2,1)} fusion(bf16[512,4,128]{0,2,1:T(8,128)(2,1)S(1)} %bitcast.197, bf16[1,4,512,2048]{2,3,1,0:T(8,128)(2,1)S(1)} %fusion.6), kind=kOutput, calls=%fused_computation.32 | convolution fusion | flops 805502976 | bytes 7208960 | tf_op jit(solution)/shard_map/cgqk,qcgd->kcd/dot_general | solution.py:151
  91.5 9.4 %fusion.2 = bf16[1,4,512,2048]{2,3,1,0:T(8,128)(2,1)} fusion(f32[2048,512,4]{1,0,2:T(8,128)S(1)} %bitcast.181, f32[4,512]{1,0:T(4,128)} %bitcast.200, f32[4,512]{1,0:T(4,128)S(1)} %log_add_fusion, pred[512,2048]{0,1:T(8,128)(4,1)S(1)} %fusion.17, bf16[512,4,128]{0,2,1:T(8,128)(2,1)} %bitcast.198, bf16[2048,256]{1,0:T(8,128)(2,1)} %copy-done.10), kind=kOutput, calls=%fused_computation.3 | convolution fusion | flops 1103101952 | bytes 27279360 | tf_op jit(solution)/shard_map/qcgd,kcd->cgqk/dot_general | solution.py:141
  100.9 5.2 %fusion.21 = bf16[1536,128]{0,1:T(8,128)(2,1)S(1)} fusion(bf16[512,4,128]{0,2,1:T(8,128)(2,1)} %bitcast.193, bf16[1,4,512,2048]{2,3,1,0:T(8,128)(2,1)} %fusion.2), kind=kOutput, calls=%fused_computation.31 | convolution fusion | flops 805502976 | bytes 7208960 | tf_op jit(solution)/shard_map/cgqk,qcgd->kcd/dot_general | solution.py:148
  106.2 24.8 %collective-permute-done.5 = bf16[2,128,4096]{2,1,0:T(8,128)(2,1)} collective-permute-done((bf16[2,128,4096]{2,1,0:T(8,128)(2,1)}, bf16[2,128,4096]{2,1,0:T(8,128)(2,1)}, u32[]{:S(2)}, u32[]{:S(2)}) %collective-permute-start.5) | collective-permute-done | bytes 2097184 | tf_op jit(solution)/shard_map/ppermute | solution.py:30
  137.2 5.2 %collective-permute-start.9 = (bf16[512,256]{0,1:T(8,128)(2,1)}, bf16[512,256]{0,1:T(8,128)(2,1)S(1)}, u32[]{:S(2)}, u32[]{:S(2)}) collective-permute-start(bf16[512,256]{0,1:T(8,128)(2,1)} %get-tuple-element.43), channel_id=1, source_target_pairs={{12,0},{16,4},{20,8},{24,12},{28,16},{32,20},{36,24},{40,28},{44,3... | collective-permute-start | bytes 786440 | tf_op jit(solution)/shard_map/ppermute | solution.py:26
  142.4 3.7 %collective-permute-start.8 = (bf16[512,256]{0,1:T(8,128)(2,1)}, bf16[512,256]{0,1:T(8,128)(2,1)S(1)}, u32[]{:S(2)}, u32[]{:S(2)}) collective-permute-start(bf16[512,256]{0,1:T(8,128)(2,1)} %get-tuple-element.44), channel_id=1, source_target_pairs={{8,0},{12,4},{16,8},{20,12},{24,16},{28,20},{32,24},{36,28},{40,32... | collective-permute-start | bytes 786440 | tf_op jit(solution)/shard_map/ppermute | solution.py:26
  148.0 3.3 %fusion.40 = f32[512,128]{0,1:T(8,128)} fusion(bf16[512,4,128]{0,2,1:T(8,128)(2,1)} %bitcast.199, bf16[1,4,512,2048]{2,3,1,0:T(8,128)(2,1)} %copy-done.6), kind=kOutput, calls=%fused_computation.50 | convolution fusion | flops 268435456 | bytes 2883584 | tf_op jit(solution)/shard_map/cgqk,qcgd->kcd/dot_general | solution.py:151
  151.3 3.2 %fusion.37 = f32[512,128]{0,1:T(8,128)} fusion(bf16[512,4,128]{0,2,1:T(8,128)(2,1)} %bitcast.194, bf16[1,4,512,2048]{2,3,1,0:T(8,128)(2,1)} %fusion.2), kind=kOutput, calls=%fused_computation.49 | convolution fusion | flops 268435456 | bytes 2883584 | tf_op jit(solution)/shard_map/cgqk,qcgd->kcd/dot_general | solution.py:148
  154.5 4.4 %all-to-all-start = ((bf16[8,64,512]{2,1,0:T(8,128)(2,1)}), bf16[8,64,512]{2,1,0:T(8,128)(2,1)S(1)}, u32[]{:S(2)}, u32[]{:S(2)}) async-start(bf16[8,64,512]{2,1,0:T(8,128)(2,1)} %bitcast.195), calls=%async_computation.1 | async-start | bytes 1048576 | tf_op jit(solution)/shard_map/all_to_all | solution.py:122
  161.7 9.1 %all-to-all-done = bf16[8,64,512]{2,1,0:T(8,128)(2,1)S(1)} async-done(((bf16[8,64,512]{2,1,0:T(8,128)(2,1)}), bf16[8,64,512]{2,1,0:T(8,128)(2,1)S(1)}, u32[]{:S(2)}, u32[]{:S(2)}) %all-to-all-start) | async-done | bytes 524320 | tf_op jit(solution)/shard_map/all_to_all | solution.py:122
  (96 shorter events, 37.8 us)
Async XLA Ops:
  7.2 16.1 %copy-start = (s32[256]{0:T(256)S(1)}, s32[256]{0:T(256)}, u32[]{:S(2)}) copy-start(s32[256]{0:T(256)} %param.13) | copy-start | bytes 3076
  7.2 147.3 %reduce-scatter.2.cloned.1.call-start = ((), (), s32[]{:S(2)}) async-start(), calls=%async_computation.2 | async-start | bytes 4718592 | tf_op jit(solution)/shard_map/reduce_scatter | solution.py:116
  9.1 19.5 %collective-permute-start.3 = (bf16[512,256]{1,0:T(8,128)(2,1)S(1)}, bf16[512,256]{1,0:T(8,128)(2,1)S(1)}, u32[]{:S(2)}, u32[]{:S(2)}) collective-permute-start(bf16[512,256]{1,0:T(8,128)(2,1)S(1)} %constant_dynamic-update-slice_fusion), channel_id=1, source_target_pairs={{0,4},{4,8},{8,12},{12,16},{16,20},{20,24},{24,28},{28,32},{32,36}... | collective-permute-start | bytes 786440 | tf_op jit(solution)/shard_map/ppermute | solution.py:21
  12.6 16.0 %collective-permute-start.2 = (bf16[512,256]{1,0:T(8,128)(2,1)S(1)}, bf16[512,256]{1,0:T(8,128)(2,1)S(1)}, u32[]{:S(2)}, u32[]{:S(2)}) collective-permute-start(bf16[512,256]{1,0:T(8,128)(2,1)S(1)} %constant_dynamic-update-slice_fusion), channel_id=1, source_target_pairs={{0,8},{4,12},{8,16},{12,20},{16,24},{20,28},{24,32},{28,36},{32,40... | collective-permute-start | bytes 786440 | tf_op jit(solution)/shard_map/ppermute | solution.py:21
  16.0 17.4 %collective-permute-start.1 = (bf16[512,256]{1,0:T(8,128)(2,1)S(1)}, bf16[512,256]{1,0:T(8,128)(2,1)}, u32[]{:S(2)}, u32[]{:S(2)}) collective-permute-start(bf16[512,256]{1,0:T(8,128)(2,1)S(1)} %constant_dynamic-update-slice_fusion), channel_id=1, source_target_pairs={{0,12},{4,16},{8,20},{12,24},{16,28},{20,32},{24,36},{28,40},{32,4... | collective-permute-start | bytes 786440 | tf_op jit(solution)/shard_map/ppermute | solution.py:21
  19.9 31.5 %collective-permute-start = (bf16[128,4096]{1,0:T(8,128)(2,1)}, bf16[128,4096]{1,0:T(8,128)(2,1)S(1)}, u32[]{:S(2)}, u32[]{:S(2)}) collective-permute-start(bf16[128,4096]{1,0:T(8,128)(2,1)} %param.11), channel_id=1, source_target_pairs={{0,2},{2,0},{1,3},{3,1},{4,6},{6,4},{5,7},{7,5},{8,10},{10,8},{9,1... | collective-permute-start | bytes 3145736 | tf_op jit(solution)/shard_map/ppermute | solution.py:30
  26.3 11.3 %copy-start.16 = (bf16[512,512]{0,1:T(8,128)(2,1)}, bf16[512,512]{0,1:T(8,128)(2,1)S(1)}, u32[]{:S(2)}) copy-start(bf16[512,512]{0,1:T(8,128)(2,1)S(1)} %copy.54) | copy-start | bytes 1572868
  43.3 9.1 %copy-start.12 = (bf16[128,4096]{1,0:T(8,128)(2,1)S(1)}, bf16[128,4096]{1,0:T(8,128)(2,1)}, u32[]{:S(2)}) copy-start(bf16[128,4096]{1,0:T(8,128)(2,1)} %param.11) | copy-start | bytes 3145732
  55.3 4.5 %collective-permute-start.4 = (bf16[2,128,4096]{2,1,0:T(8,128)(2,1)}, bf16[2,128,4096]{2,1,0:T(8,128)(2,1)}, u32[]{:S(2)}, u32[]{:S(2)}) collective-permute-start(bf16[2,128,4096]{2,1,0:T(8,128)(2,1)} %pad_maximum_fusion.1), channel_id=1, source_target_pairs={{0,1},{1,0},{2,3},{3,2},{4,5},{5,4},{6,7},{7,6},{8,9},{9,8},{10,11... | collective-permute-start | bytes 6291464 | tf_op jit(solution)/shard_map/ppermute | solution.py:30
  68.9 8.4 %copy-start.7 = (bf16[512,4096]{1,0:T(8,128)(2,1)S(1)}, bf16[512,4096]{1,0:T(8,128)(2,1)}, u32[]{:S(2)}) copy-start(bf16[512,4096]{1,0:T(8,128)(2,1)} %param.10) | copy-start | bytes 12582916
  68.9 8.4 %copy-start.15 = (bf16[512,1,4,128]{0,3,2,1:T(8,128)(2,1)S(1)}, bf16[512,1,4,128]{0,3,2,1:T(8,128)(2,1)}, u32[]{:S(2)}) copy-start(bf16[512,1,4,128]{0,3,2,1:T(8,128)(2,1)} %divide_convert_fusion) | copy-start | bytes 1572868
  77.4 10.2 %copy-start.6 = (bf16[1,4,512,2048]{2,3,1,0:T(8,128)(2,1)}, bf16[1,4,512,2048]{2,3,1,0:T(8,128)(2,1)S(1)}, u32[]{:S(2)}) copy-start(bf16[1,4,512,2048]{2,3,1,0:T(8,128)(2,1)S(1)} %fusion.6) | copy-start | bytes 25165828
  79.8 7.7 %copy-start.3 = (f32[512,4096]{1,0:T(8,128)}, f32[512,4096]{1,0:T(8,128)S(1)}, u32[]{:S(2)}) copy-start(f32[512,4096]{1,0:T(8,128)S(1)} %fusion.62) | copy-start | bytes 25165828
  81.5 49.5 %collective-permute-start.5 = (bf16[2,128,4096]{2,1,0:T(8,128)(2,1)}, bf16[2,128,4096]{2,1,0:T(8,128)(2,1)}, u32[]{:S(2)}, u32[]{:S(2)}) collective-permute-start(bf16[2,128,4096]{2,1,0:T(8,128)(2,1)} %fusion.23), channel_id=1, source_target_pairs={{0,2},{2,0},{1,3},{3,1},{4,6},{6,4},{5,7},{7,5},{8,10},{10,8},{9,1... | collective-permute-start | bytes 6291464 | tf_op jit(solution)/shard_map/ppermute | solution.py:30
  100.9 30.1 %copy-start.4 = (f32[512,4096]{1,0:T(8,128)S(1)}, f32[512,4096]{1,0:T(8,128)}, u32[]{:S(2)}) copy-start(f32[512,4096]{1,0:T(8,128)} %copy-done.3) | copy-start | bytes 25165828
  100.9 32.6 %slice-start.4 = ((s8[8388608]{0:T(1024)(128)(4,1)}), s8[4194304]{0:T(1024)(128)(4,1)S(1)}, s32[]{:S(2)}) async-start(s8[8388608]{0:T(1024)(128)(4,1)} %bitcast.184), calls=%async_computation.7 | async-start | bytes 8388608
  106.1 27.4 %slice-start.5 = ((s8[8388608]{0:T(1024)(128)(4,1)}), s8[4194304]{0:T(1024)(128)(4,1)S(1)}, s32[]{:S(2)}) async-start(s8[8388608]{0:T(1024)(128)(4,1)} %bitcast.184), calls=%async_computation.8 | async-start | bytes 8388608
  106.2 27.4 %copy-start.11 = (bf16[2048,256]{1,0:T(8,128)(2,1)S(1)}, bf16[2048,256]{1,0:T(8,128)(2,1)}, u32[]{:S(2)}) copy-start(bf16[2048,256]{1,0:T(8,128)(2,1)} %copy-done.10) | copy-start | bytes 3145732
  133.4 25.5 %collective-permute-start.6 = (bf16[128,4096]{1,0:T(8,128)(2,1)S(1)}, bf16[128,4096]{1,0:T(8,128)(2,1)S(1)}, u32[]{:S(2)}, u32[]{:S(2)}) collective-permute-start(bf16[128,4096]{1,0:T(8,128)(2,1)S(1)} %fusion.43), channel_id=1, source_target_pairs={{0,1},{1,0},{2,3},{3,2},{4,5},{5,4},{6,7},{7,6},{8,9},{9,8},{10,11... | collective-permute-start | bytes 3145736 | tf_op jit(solution)/shard_map/ppermute | solution.py:30
  137.2 34.4 %collective-permute-start.9 = (bf16[512,256]{0,1:T(8,128)(2,1)}, bf16[512,256]{0,1:T(8,128)(2,1)S(1)}, u32[]{:S(2)}, u32[]{:S(2)}) collective-permute-start(bf16[512,256]{0,1:T(8,128)(2,1)} %get-tuple-element.43), channel_id=1, source_target_pairs={{12,0},{16,4},{20,8},{24,12},{28,16},{32,20},{36,24},{40,28},{44,3... | collective-permute-start | bytes 786440 | tf_op jit(solution)/shard_map/ppermute | solution.py:26
  142.4 29.2 %collective-permute-start.8 = (bf16[512,256]{0,1:T(8,128)(2,1)}, bf16[512,256]{0,1:T(8,128)(2,1)S(1)}, u32[]{:S(2)}, u32[]{:S(2)}) collective-permute-start(bf16[512,256]{0,1:T(8,128)(2,1)} %get-tuple-element.44), channel_id=1, source_target_pairs={{8,0},{12,4},{16,8},{20,12},{24,16},{28,20},{32,24},{36,28},{40,32... | collective-permute-start | bytes 786440 | tf_op jit(solution)/shard_map/ppermute | solution.py:26
  146.1 25.5 %collective-permute-start.7 = (bf16[512,256]{0,1:T(8,128)(2,1)}, bf16[512,256]{0,1:T(8,128)(2,1)S(1)}, u32[]{:S(2)}, u32[]{:S(2)}) collective-permute-start(bf16[512,256]{0,1:T(8,128)(2,1)} %get-tuple-element.45), channel_id=1, source_target_pairs={{4,0},{8,4},{12,8},{16,12},{20,16},{24,20},{28,24},{32,28},{36,32}... | collective-permute-start | bytes 786440 | tf_op jit(solution)/shard_map/ppermute | solution.py:26
  148.0 26.4 %copy-start.1 = (s32[256]{0:T(256)S(1)}, s32[256]{0:T(256)}, u32[]{:S(2)}) copy-start(s32[256]{0:T(256)} %param.13) | copy-start | bytes 3076
  154.5 16.4 %all-to-all-start = ((bf16[8,64,512]{2,1,0:T(8,128)(2,1)}), bf16[8,64,512]{2,1,0:T(8,128)(2,1)S(1)}, u32[]{:S(2)}, u32[]{:S(2)}) async-start(bf16[8,64,512]{2,1,0:T(8,128)(2,1)} %bitcast.195), calls=%async_computation.1 | async-start | bytes 1048576 | tf_op jit(solution)/shard_map/all_to_all | solution.py:122
  (13 other events, 57.7 us)
Sparse Core Ops, SparseCore 0:
  69.0 55.2 reduce-scatter.1
